TPU v7x, 32 devices: a whole 2x2x4 slice. The times are simulated.
32 devices in a mesh: groups: 2 (over y), seq: 4 (over z), chan: 4 (over x, core).
Axes of the slice: x: 2, y: 2, z: 4, core: 2. Of those that a mesh axis runs over, the one named last changes fastest.
Arguments:
- value: bfloat16 [1024, 4096], P(('groups', 'seq'), 'chan'), parts along dimension 0, may hold values from -6 to 6
- first_gate: bfloat16 [1024, 4096], P(('groups', 'seq'), 'chan'), parts along dimension 0, may hold values from -6 to 6
- second_gate: bfloat16 [1024, 4096], P(('groups', 'seq'), 'chan'), parts along dimension 0, may hold values from -6 to 6
- first_filter: bfloat16 [256, 512], P('chan'), may hold values from -0.25 to 0.25
- second_filter: bfloat16 [256, 512], P('chan'), may hold values from -0.25 to 0.25
- out_weight: bfloat16 [4096, 4096], P('chan'), may hold values from -0.09375 to 0.09375
- segment_ids: int32 [1024], P(('groups', 'seq')), parts along dimension 0, may hold values from 0 to 1, never falling along the last dimension, each value on 1 to 384 neighbouring positions
Outputs:
- mixed: bfloat16 [1024, 4096], P(('groups', 'seq')), parts along dimension 0
There are 2 independent parts, one for each index of `groups`. A program takes and returns all parts, laid end to end along the dimension named above; an argument that names none is the same for every part. Nothing has to cross between parts.
Inputs may be any that keep to these rules, and one draw needn't show every extreme that they name: `segment_ids`: ids never fall along the window; the 2 contexts each hold 128 to 384 neighbouring positions and together fill the window.
All inputs are finite; a program needn't handle non-finite values.
Results may differ from a plain program's by a relative error of at most 0.0065.
Values may be sent and summed in bfloat16 or wider, within the bound.
No kernel may reach another device: no remote copies, remote signals or barrier semaphores. Data moves between devices by JAX's collectives and lax.ppermute only.
A program may use at most 192 MiB of HBM per device.

v0:
```python
import jax
import jax.numpy as jnp
from jax import lax
from jax.sharding import PartitionSpec as P


def toeplitz_taps(doubled, length, base, rows, cols, row_segs, col_segs):
    filt_count = doubled.shape[0]
    span = rows + cols
    start = jnp.mod(base - cols + 1, length)
    window = lax.dynamic_slice_in_dim(doubled, start, span - 1, 1)
    reversed_win = jnp.concatenate(
        [window[:, ::-1], jnp.zeros((filt_count, 1), doubled.dtype)], axis=1
    )
    tiled = jnp.tile(reversed_win, (1, rows))[:, : rows * (span - 1)]
    skewed = tiled.reshape(filt_count, rows, span - 1)[:, :, rows - 1 : rows - 1 + cols]
    same = (row_segs[:, None] == col_segs[None, :]).astype(doubled.dtype)
    return skewed * same[None, :, :]


def apply_taps(grouped, taps):
    return jnp.einsum("gcs,gts->gct", grouped, taps, preferred_element_type=jnp.float32)


def to_rows(result):
    filt_count, per_filter, rows = result.shape
    return result.transpose(2, 0, 1).reshape(rows, filt_count * per_filter)


def local(value, first_gate, second_gate, first_filter, second_filter, out_weight, segment_ids):
    tok_rows = value.shape[0]
    chans = value.shape[1]
    filt_count = first_filter.shape[0]
    length = first_filter.shape[1]
    per_filter = chans // filt_count
    my_start = lax.axis_index("seq") * tok_rows
    seg_row = segment_ids.reshape(1, tok_rows)

    def long_conv(filters, field):
        doubled = jnp.concatenate([filters, filters], axis=1)
        field_cols = field.T
        empty = jnp.zeros((filt_count, per_filter, tok_rows), jnp.float32)
        piece_field = lax.all_gather(field_cols, "seq", axis=1, tiled=True)
        piece_segs = lax.all_gather(seg_row, "seq", axis=1, tiled=True)
        cols = piece_field.shape[1]
        steps_count = cols // tok_rows

        def one_block(index, acc):
            offset = (index * tok_rows).astype(jnp.int32)
            sub_field = lax.dynamic_slice_in_dim(piece_field, offset, tok_rows, 1)
            sub_segs = lax.dynamic_slice_in_dim(piece_segs[0], offset, tok_rows, 0)
            grouped = sub_field.reshape(filt_count, per_filter, tok_rows)
            taps = toeplitz_taps(
                doubled, length, my_start - offset, tok_rows, tok_rows, segment_ids, sub_segs
            )
            return acc + apply_taps(grouped, taps)

        total = lax.fori_loop(0, steps_count, one_block, empty)
        return to_rows(total)

    first_input = (first_gate.astype(jnp.float32) * value.astype(jnp.float32)).astype(jnp.bfloat16)
    first_mix = long_conv(first_filter, first_input)
    second_input = (second_gate.astype(jnp.float32) * first_mix).astype(jnp.bfloat16)
    second_mix = long_conv(second_filter, second_input).astype(jnp.bfloat16)
    partial_out = jnp.dot(second_mix, out_weight, preferred_element_type=jnp.float32)
    mixed = lax.psum(partial_out, "chan").astype(jnp.bfloat16)
    return mixed


def solution(mesh):
    in_specs = (
        P(("groups", "seq"), "chan"),
        P(("groups", "seq"), "chan"),
        P(("groups", "seq"), "chan"),
        P("chan", None),
        P("chan", None),
        P("chan", None),
        P(("groups", "seq")),
    )
    out_specs = P(("groups", "seq"), None)
    return jax.shard_map(local, mesh=mesh, in_specs=in_specs, out_specs=out_specs, check_vma=False)
```

profile of v0, /device:TPU:0, one launch (start us, length us, event | category | flops | bytes accessed | tf_op | source)
XLA Modules:
  0.0 331.7 jit_solution(859946293358869970)
XLA Ops:
  6.5 1.1 copy.15
  7.7 1.1 copy.16
  8.8 0.8 fusion.9
  9.7 1.1 copy.14
  10.8 12.8 %all-gather.1 = s32[4,1,128]{2,1,0:T(1,128)S(1)} all-gather(s32[1,1,128]{2,1,0:T(1,128)} %bitcast.64), channel_id=2, replica_groups=mesh['groups'=2,'seq'=4,'chan'=4] {'seq'}, dimensions={0}, use_global_device_ids=true | all-gather | bytes 2560 | tf_op jit(solution)/shard_map/all_gather | solution.py:44
  23.6 0.9 pad_maximum_fusion
  24.5 17.9 %all-gather.5.cloned.1.call-done = bf16[1024,512]{1,0:T(8,128)(2,1)} async-done(((bf16[1024,128]{1,0:T(8,128)(2,1)}), bf16[1024,512]{1,0:T(8,128)(2,1)}) %all-gather.5.cloned.1.call-update) | async-done | bytes 1048592 | tf_op jit(solution)/shard_map/all_gather | solution.py:43
  42.4 103.7 %while.36 = (s32[]{:T(128)}, f32[64,16,128]{2,1,0:T(8,128)S(1)}, bf16[1024,512]{1,0:T(8,128)(2,1)}, s32[]{:T(128)}, bf16[64,1024]{1,0:T(8,128)(2,1)S(1)}, /*inde...) while((s32[]{:T(128)}, f32[64,16,128]{2,1,0:T(8,128)S(1)}, ...), condition=%wide.region_1.2_spmd.clone, body=%wide.region_0.1_spmd.clone.sunk | while | flops 34897944 | bytes 33591060 | solution.py:58
  42.8 0.3 tile.60
  43.1 2.6 copy.21
  45.7 2.3 slice.78
  47.9 15.8 %reshape.158 = bf16[64,128,255]{2,1,0:T(8,128)(2,1)} reshape(bf16[64,32640]{1,0:T(8,128)(2,1)} %slice.78) | data formatting | bytes 8355840 | tf_op jit(solution)/shard_map/while/body/eval_jaxpr/reshape | solution.py:16
  63.9 1.0 constant_dynamic-slice_fusion.10
  64.8 3.5 %fusion.23 = f32[64,16,128]{2,1,0:T(8,128)S(1)} fusion(bf16[64,16,128]{2,1,0:T(8,128)(2,1)S(1)} %bitcast.58, bf16[64,128,255]{2,1,0:T(8,128)(2,1)} %reshape.158, bf16[128,128]{1,0:T(8,128)(2,1)S(1)} %compare_convert_fusion.4, f32[64,16,128]{2,1,0:T(8,128)S(1)} %get-tuple-element.645, pred[]{:T(512)S(6)} %compare.16), kind=kOutput, calls=%fused_computation.2.clone.1 | convolution fusion | flops 34865152 | bytes 3440641 | tf_op jit(solution)/shard_map/while/body/eval_jaxpr/gcs,gts->gct/dot_general | solution.py:22
  68.7 0.3 tile.60
  69.0 2.6 copy.21
  71.6 2.3 slice.78
  73.9 15.8 %reshape.158 = bf16[64,128,255]{2,1,0:T(8,128)(2,1)} reshape(bf16[64,32640]{1,0:T(8,128)(2,1)} %slice.78) | data formatting | bytes 8355840 | tf_op jit(solution)/shard_map/while/body/eval_jaxpr/reshape | solution.py:16
  89.8 1.0 constant_dynamic-slice_fusion.10
  90.8 3.5 %fusion.23 = f32[64,16,128]{2,1,0:T(8,128)S(1)} fusion(bf16[64,16,128]{2,1,0:T(8,128)(2,1)S(1)} %bitcast.58, bf16[64,128,255]{2,1,0:T(8,128)(2,1)} %reshape.158, bf16[128,128]{1,0:T(8,128)(2,1)S(1)} %compare_convert_fusion.4, f32[64,16,128]{2,1,0:T(8,128)S(1)} %get-tuple-element.645, pred[]{:T(512)S(6)} %compare.16), kind=kOutput, calls=%fused_computation.2.clone.1 | convolution fusion | flops 34865152 | bytes 3440641 | tf_op jit(solution)/shard_map/while/body/eval_jaxpr/gcs,gts->gct/dot_general | solution.py:22
  94.4 0.2 reverse.4
  94.6 0.3 tile.60
  94.9 2.6 copy.21
  97.5 2.3 slice.78
  99.8 15.8 %reshape.158 = bf16[64,128,255]{2,1,0:T(8,128)(2,1)} reshape(bf16[64,32640]{1,0:T(8,128)(2,1)} %slice.78) | data formatting | bytes 8355840 | tf_op jit(solution)/shard_map/while/body/eval_jaxpr/reshape | solution.py:16
  115.7 1.0 constant_dynamic-slice_fusion.10
  116.7 3.5 %fusion.23 = f32[64,16,128]{2,1,0:T(8,128)S(1)} fusion(bf16[64,16,128]{2,1,0:T(8,128)(2,1)S(1)} %bitcast.58, bf16[64,128,255]{2,1,0:T(8,128)(2,1)} %reshape.158, bf16[128,128]{1,0:T(8,128)(2,1)S(1)} %compare_convert_fusion.4, f32[64,16,128]{2,1,0:T(8,128)S(1)} %get-tuple-element.645, pred[]{:T(512)S(6)} %compare.16), kind=kOutput, calls=%fused_computation.2.clone.1 | convolution fusion | flops 34865152 | bytes 3440641 | tf_op jit(solution)/shard_map/while/body/eval_jaxpr/gcs,gts->gct/dot_general | solution.py:22
  120.3 0.2 reverse.4
  120.6 0.3 tile.60
  120.9 2.6 copy.21
  123.5 2.3 slice.78
  125.7 15.8 %reshape.158 = bf16[64,128,255]{2,1,0:T(8,128)(2,1)} reshape(bf16[64,32640]{1,0:T(8,128)(2,1)} %slice.78) | data formatting | bytes 8355840 | tf_op jit(solution)/shard_map/while/body/eval_jaxpr/reshape | solution.py:16
  141.7 1.0 constant_dynamic-slice_fusion.10
  142.7 3.5 %fusion.23 = f32[64,16,128]{2,1,0:T(8,128)S(1)} fusion(bf16[64,16,128]{2,1,0:T(8,128)(2,1)S(1)} %bitcast.58, bf16[64,128,255]{2,1,0:T(8,128)(2,1)} %reshape.158, bf16[128,128]{1,0:T(8,128)(2,1)S(1)} %compare_convert_fusion.4, f32[64,16,128]{2,1,0:T(8,128)S(1)} %get-tuple-element.645, pred[]{:T(512)S(6)} %compare.16), kind=kOutput, calls=%fused_computation.2.clone.1 | convolution fusion | flops 34865152 | bytes 3440641 | tf_op jit(solution)/shard_map/while/body/eval_jaxpr/gcs,gts->gct/dot_general | solution.py:22
  146.1 0.8 fusion.8
  146.9 28.3 %all-gather.7.cloned.1.call-done = bf16[1024,512]{1,0:T(8,128)(2,1)} async-done(((bf16[1024,128]{1,0:T(8,128)(2,1)}), bf16[1024,512]{1,0:T(8,128)(2,1)}) %all-gather.7.cloned.1.call-update) | async-done | bytes 1048592 | tf_op jit(solution)/shard_map/all_gather | solution.py:43
  175.3 103.7 %while.37 = (s32[]{:T(128)}, f32[64,16,128]{2,1,0:T(8,128)S(1)}, bf16[1024,512]{1,0:T(8,128)(2,1)}, s32[]{:T(128)}, bf16[64,1024]{1,0:T(8,128)(2,1)S(1)}, /*inde...) while((s32[]{:T(128)}, f32[64,16,128]{2,1,0:T(8,128)S(1)}, ...), condition=%wide.region_3.4_spmd.clone, body=%wide.region_2.3_spmd.clone.sunk | while | flops 34897944 | bytes 33591060 | solution.py:58
  175.7 0.3 tile.61
  175.9 2.6 copy.22
  178.6 2.3 slice.81
  180.8 15.8 %reshape.159 = bf16[64,128,255]{2,1,0:T(8,128)(2,1)} reshape(bf16[64,32640]{1,0:T(8,128)(2,1)} %slice.81) | data formatting | bytes 8355840 | tf_op jit(solution)/shard_map/while/body/eval_jaxpr/reshape | solution.py:16
  196.8 1.0 constant_dynamic-slice_fusion.12
  197.7 3.5 %fusion.26 = f32[64,16,128]{2,1,0:T(8,128)S(1)} fusion(bf16[64,16,128]{2,1,0:T(8,128)(2,1)S(1)} %bitcast.59, bf16[64,128,255]{2,1,0:T(8,128)(2,1)} %reshape.159, bf16[128,128]{1,0:T(8,128)(2,1)S(1)} %compare_convert_fusion.5, f32[64,16,128]{2,1,0:T(8,128)S(1)} %get-tuple-element.690, pred[]{:T(512)S(6)} %compare.17), kind=kOutput, calls=%fused_computation.11.clone.1 | convolution fusion | flops 34865152 | bytes 3440641 | tf_op jit(solution)/shard_map/while/body/eval_jaxpr/gcs,gts->gct/dot_general | solution.py:22
  201.3 0.2 reverse.5
  201.6 0.3 tile.61
  201.9 2.6 copy.22
  204.5 2.3 slice.81
  206.7 15.8 %reshape.159 = bf16[64,128,255]{2,1,0:T(8,128)(2,1)} reshape(bf16[64,32640]{1,0:T(8,128)(2,1)} %slice.81) | data formatting | bytes 8355840 | tf_op jit(solution)/shard_map/while/body/eval_jaxpr/reshape | solution.py:16
  222.7 1.0 constant_dynamic-slice_fusion.12
  223.7 3.5 %fusion.26 = f32[64,16,128]{2,1,0:T(8,128)S(1)} fusion(bf16[64,16,128]{2,1,0:T(8,128)(2,1)S(1)} %bitcast.59, bf16[64,128,255]{2,1,0:T(8,128)(2,1)} %reshape.159, bf16[128,128]{1,0:T(8,128)(2,1)S(1)} %compare_convert_fusion.5, f32[64,16,128]{2,1,0:T(8,128)S(1)} %get-tuple-element.690, pred[]{:T(512)S(6)} %compare.17), kind=kOutput, calls=%fused_computation.11.clone.1 | convolution fusion | flops 34865152 | bytes 3440641 | tf_op jit(solution)/shard_map/while/body/eval_jaxpr/gcs,gts->gct/dot_general | solution.py:22
  227.5 0.3 tile.61
  227.8 2.6 copy.22
  230.4 2.3 slice.81
  232.7 15.8 %reshape.159 = bf16[64,128,255]{2,1,0:T(8,128)(2,1)} reshape(bf16[64,32640]{1,0:T(8,128)(2,1)} %slice.81) | data formatting | bytes 8355840 | tf_op jit(solution)/shard_map/while/body/eval_jaxpr/reshape | solution.py:16
  248.6 1.0 constant_dynamic-slice_fusion.12
  249.6 3.5 %fusion.26 = f32[64,16,128]{2,1,0:T(8,128)S(1)} fusion(bf16[64,16,128]{2,1,0:T(8,128)(2,1)S(1)} %bitcast.59, bf16[64,128,255]{2,1,0:T(8,128)(2,1)} %reshape.159, bf16[128,128]{1,0:T(8,128)(2,1)S(1)} %compare_convert_fusion.5, f32[64,16,128]{2,1,0:T(8,128)S(1)} %get-tuple-element.690, pred[]{:T(512)S(6)} %compare.17), kind=kOutput, calls=%fused_computation.11.clone.1 | convolution fusion | flops 34865152 | bytes 3440641 | tf_op jit(solution)/shard_map/while/body/eval_jaxpr/gcs,gts->gct/dot_general | solution.py:22
  253.5 0.3 tile.61
  253.8 2.6 copy.22
  256.4 2.3 slice.81
  258.6 15.8 %reshape.159 = bf16[64,128,255]{2,1,0:T(8,128)(2,1)} reshape(bf16[64,32640]{1,0:T(8,128)(2,1)} %slice.81) | data formatting | bytes 8355840 | tf_op jit(solution)/shard_map/while/body/eval_jaxpr/reshape | solution.py:16
  274.6 1.0 constant_dynamic-slice_fusion.12
  275.5 3.5 %fusion.26 = f32[64,16,128]{2,1,0:T(8,128)S(1)} fusion(bf16[64,16,128]{2,1,0:T(8,128)(2,1)S(1)} %bitcast.59, bf16[64,128,255]{2,1,0:T(8,128)(2,1)} %reshape.159, bf16[128,128]{1,0:T(8,128)(2,1)S(1)} %compare_convert_fusion.5, f32[64,16,128]{2,1,0:T(8,128)S(1)} %get-tuple-element.690, pred[]{:T(512)S(6)} %compare.17), kind=kOutput, calls=%fused_computation.11.clone.1 | convolution fusion | flops 34865152 | bytes 3440641 | tf_op jit(solution)/shard_map/while/body/eval_jaxpr/gcs,gts->gct/dot_general | solution.py:22
  279.1 4.7 %fusion.10 = f32[128,4096]{1,0:T(8,128)S(1)} fusion(bf16[128,1024]{0,1:T(8,128)(2,1)S(1)} %bitcast.62, bf16[1024,4096]{1,0:T(8,128)(2,1)} %param.16), kind=kOutput, calls=%fused_computation.24 | convolution fusion | flops 1073741824 | bytes 10747904 | tf_op jit(solution)/shard_map/dot_general | solution.py:65
  283.7 41.1 %all-reduce.3 = bf16[128,4096]{1,0:T(8,128)(2,1)} all-reduce(f32[128,4096]{1,0:T(8,128)S(1)} %fusion.10), channel_id=1, replica_groups=mesh['groups'=2,'seq'=4,'chan'=4] {'chan'}, use_global_device_ids=true, to_apply=%region_4.5 | all-reduce | flops 524288 | bytes 3145728 | tf_op jit(solution)/shard_map/psum | solution.py:66
  (71 shorter events, 3.2 us)
Async XLA Ops:
  6.5 35.9 %all-gather.5.cloned.1.call-start = ((), (), s32[]{:S(2)}) async-start(), calls=%async_computation | async-start | bytes 1310720 | tf_op jit(solution)/shard_map/all_gather | solution.py:43
  9.6 165.7 %all-gather.7.cloned.1.call-start = ((), (), s32[]{:S(2)}) async-start(), calls=%async_computation.1 | async-start | bytes 1310720 | tf_op jit(solution)/shard_map/all_gather | solution.py:43
  42.4 104.5 %copy-start = (bf16[64,512]{1,0:T(8,128)(2,1)S(1)}, bf16[64,512]{1,0:T(8,128)(2,1)}, u32[]{:S(2)}) copy-start(bf16[64,512]{1,0:T(8,128)(2,1)} %param.15) | copy-start | bytes 196612
  47.9 15.8 %copy-start.1 = (s32[128]{0:T(128)S(1)}, s32[128]{0:T(128)}, u32[]{:S(2)}) copy-start(s32[128]{0:T(128)} %get-tuple-element.664) | copy-start | bytes 1540 | tf_op jit(solution)/shard_map/while
  73.9 15.8 %copy-start.1 = (s32[128]{0:T(128)S(1)}, s32[128]{0:T(128)}, u32[]{:S(2)}) copy-start(s32[128]{0:T(128)} %get-tuple-element.664) | copy-start | bytes 1540 | tf_op jit(solution)/shard_map/while
  99.8 15.8 %copy-start.1 = (s32[128]{0:T(128)S(1)}, s32[128]{0:T(128)}, u32[]{:S(2)}) copy-start(s32[128]{0:T(128)} %get-tuple-element.664) | copy-start | bytes 1540 | tf_op jit(solution)/shard_map/while
  125.7 15.8 %copy-start.1 = (s32[128]{0:T(128)S(1)}, s32[128]{0:T(128)}, u32[]{:S(2)}) copy-start(s32[128]{0:T(128)} %get-tuple-element.664) | copy-start | bytes 1540 | tf_op jit(solution)/shard_map/while
  180.8 15.8 %copy-start.2 = (s32[128]{0:T(128)S(1)}, s32[128]{0:T(128)}, u32[]{:S(2)}) copy-start(s32[128]{0:T(128)} %get-tuple-element.709) | copy-start | bytes 1540 | tf_op jit(solution)/shard_map/while
  206.7 15.8 %copy-start.2 = (s32[128]{0:T(128)S(1)}, s32[128]{0:T(128)}, u32[]{:S(2)}) copy-start(s32[128]{0:T(128)} %get-tuple-element.709) | copy-start | bytes 1540 | tf_op jit(solution)/shard_map/while
  232.7 15.8 %copy-start.2 = (s32[128]{0:T(128)S(1)}, s32[128]{0:T(128)}, u32[]{:S(2)}) copy-start(s32[128]{0:T(128)} %get-tuple-element.709) | copy-start | bytes 1540 | tf_op jit(solution)/shard_map/while
  258.6 15.8 %copy-start.2 = (s32[128]{0:T(128)S(1)}, s32[128]{0:T(128)}, u32[]{:S(2)}) copy-start(s32[128]{0:T(128)} %get-tuple-element.709) | copy-start | bytes 1540 | tf_op jit(solution)/shard_map/while
Sparse Core Ops, SparseCore 0:
  9.7 32.6 all-gather.4
  147.0 28.2 all-gather.6
where the time goes:
time: 333 us; the launch traced here: 332 us
  local copies, waits for them, and re-layouts  182 us (55%)
  blocking collectives  53.9 us (16%)
  waiting for transfers between devices  46.3 us (14%)
  matrix products  32.3 us (10%)
  between operations  13.5 us (4%)
    reshape x8, local copies, waits for them, and re-layouts, toeplitz_taps(): tiled.reshape(filt_count, rows, span - 1)[:, :, rows - 1:rows - 1 + cols]  127 us
    all_gather x2, waiting for transfers between devices, long_conv(): piece_field = lax.all_gather(field_cols, 'seq', axis=1, tiled=True)  46.2 us
    psum x1, blocking collectives, local(): mixed = lax.psum(partial_out, 'chan').astype(jnp.bfloat16)  41.1 us
    dot_general x8, matrix products, apply_taps(): jnp.einsum('gcs,gts->gct', grouped, taps, preferred_element_type=jnp.floa...  27.7 us
    while x40, local copies, waits for them, and re-layouts  23 us
    slice x8, local copies, waits for them, and re-layouts, toeplitz_taps(): tiled = jnp.tile(reversed_win, (1, rows))[:, :rows * (span - 1)]  18 us
    all_gather x1, blocking collectives, long_conv(): piece_segs = lax.all_gather(seg_row, 'seq', axis=1, tiled=True)  12.8 us
    dynamic_slice x8, local copies, waits for them, and re-layouts, one_block(): sub_field = lax.dynamic_slice_in_dim(piece_field, offset, tok_rows, 1)  7.8 us
  transfers between devices with their start and end apart: 2, of which 2 were waited for; matrix products, arithmetic and copies ran while one was open for 1% of the time, Pallas kernels for 0%

commit v1 on v0

v1 whole, which is shorter than its diff:
```python
import numpy as np
import jax
import jax.numpy as jnp
from jax import lax
from jax.sharding import PartitionSpec as P

F32 = jnp.float32
BF16 = jnp.bfloat16


def split_bf16(mat):
    hi = mat.astype(jnp.bfloat16)
    lo = (mat - hi.astype(np.float64)).astype(jnp.bfloat16)
    return hi, lo


def dft_mats(length):
    half = length // 2
    n = np.arange(length)
    f = np.arange(half)
    ang = 2.0 * np.pi * ((f[:, None] * n[None, :]) % length) / length
    fwd = np.zeros((length, length))
    fwd[:half] = np.cos(ang)
    fwd[half] = np.where(n % 2 == 0, 1.0, -1.0)
    fwd[half + 1:] = -np.sin(ang[1:])
    inv = np.zeros((length, length))
    scale = np.full(half, 2.0)
    scale[0] = 1.0
    inv[:, :half] = (np.cos(ang) * scale[:, None]).T / length
    inv[:, half] = np.where(n % 2 == 0, 1.0, -1.0) / length
    inv[:, half + 1:] = (-2.0 * np.sin(ang[1:])).T / length
    return split_bf16(fwd), split_bf16(inv)


def mm(a, b):
    return jnp.dot(a, b, preferred_element_type=F32)


def make_local(nseq):
    def local(value, first_gate, second_gate, first_filter, second_filter, out_weight, segment_ids):
        chans = value.shape[1]
        filt_local, length = first_filter.shape
        group = chans // filt_local
        per = chans // nseq
        fpd = per // group
        half = length // 2
        (f_hi, f_lo), (i_hi, i_lo) = dft_mats(length)
        f_hi, f_lo, i_hi, i_lo = (jnp.asarray(m) for m in (f_hi, f_lo, i_hi, i_lo))
        me = lax.axis_index("seq")

        segs = lax.all_gather(segment_ids, "seq", tiled=True)
        in0 = (segs == 0)[:, None]
        in1 = (segs == 1)[:, None]

        def spectrum(filt):
            mine = lax.dynamic_slice_in_dim(filt, me * fpd, fpd, 0)
            taps = jnp.repeat(mine.T, group, axis=1)
            spec = mm(f_hi, taps) + mm(f_lo, taps)
            re, im = spec[:half], spec[half:]
            row0 = lax.broadcasted_iota(jnp.int32, re.shape, 0) == 0
            a = re
            b = jnp.where(row0, 0.0, im)
            d = jnp.where(row0, im, re)
            two = lambda x: jnp.concatenate([x, x], axis=1)
            return two(a), two(b), two(d)

        def long_conv(spec, field):
            a, b, d = spec
            zero = jnp.zeros_like(field)
            masked = jnp.concatenate(
                [jnp.where(in0, field, zero), jnp.where(in1, field, zero)], axis=1
            )
            x = mm(f_hi, masked) + mm(f_lo, masked)
            xr, xi = x[:half], x[half:]
            y = jnp.concatenate([xr * a - xi * b, xr * b + xi * d], axis=0)
            y_hi32 = lax.reduce_precision(y, exponent_bits=8, mantissa_bits=7)
            y_hi = y_hi32.astype(BF16)
            y_lo = (y - y_hi32).astype(BF16)
            both = mm(i_hi, y_hi) + mm(i_hi, y_lo) + mm(i_lo, y_hi)
            return jnp.where(in0, both[:, :per], 0.0) + jnp.where(in1, both[:, per:], 0.0)

        first_input = (first_gate.astype(F32) * value.astype(F32)).astype(BF16)
        first_cols = lax.all_to_all(first_input, "seq", 1, 0, tiled=True)
        gate_cols = lax.all_to_all(second_gate, "seq", 1, 0, tiled=True)
        first_mix = long_conv(spectrum(first_filter), first_cols)
        second_input = (gate_cols.astype(F32) * first_mix).astype(BF16)
        second_mix = long_conv(spectrum(second_filter), second_input).astype(BF16)
        mix_rows = lax.all_to_all(second_mix, "seq", 0, 1, tiled=True)
        partial_out = mm(mix_rows, out_weight)
        return lax.psum(partial_out, "chan").astype(BF16)

    return local


def solution(mesh):
    in_specs = (
        P(("groups", "seq"), "chan"),
        P(("groups", "seq"), "chan"),
        P(("groups", "seq"), "chan"),
        P("chan", None),
        P("chan", None),
        P("chan", None),
        P(("groups", "seq")),
    )
    out_specs = P(("groups", "seq"), None)
    local = make_local(mesh.shape["seq"])
    return jax.shard_map(local, mesh=mesh, in_specs=in_specs, out_specs=out_specs, check_vma=False)
```

time: 333 us -> 95.9 us (0.29)
  local copies, waits for them, and re-layouts: 182 us -> 2.54 us
  waiting for transfers between devices: 46.3 us -> 2.89 us
  matrix products: 32.3 us -> 11.7 us
  between operations: 13.5 us -> 0.24 us
  starting transfers between devices: 0.04 us -> 9.89 us
  blocking collectives: 53.9 us -> 62.4 us
    reshape x8 -> x0, local copies, waits for them, and re-layouts: 127 us -> none  [toeplitz_taps(): tiled.reshape(filt_count, rows, span - 1)[:, :, rows - 1:rows - 1 + cols]]
    all_gather x2 -> x0, waiting for transfers between devices: 46.2 us -> none  [long_conv(): piece_field = lax.all_gather(field_cols, 'seq', axis=1, tiled=True)]
    while x40 -> x0, local copies, waits for them, and re-layouts: 23 us -> none
    dot_general x9 -> x15, matrix products: 32.3 us -> 11.7 us  [mm(): return jnp.dot(a, b, preferred_element_type=F32)]
    slice x8 -> x0, local copies, waits for them, and re-layouts: 18 us -> none  [toeplitz_taps(): tiled = jnp.tile(reversed_win, (1, rows))[:, :rows * (span - 1)]]
    all_to_all x0 -> x1, blocking collectives: none -> 10.5 us  [local(): mix_rows = lax.all_to_all(second_mix, 'seq', 0, 1, tiled=True)]
    all_to_all x0 -> x2, starting transfers between devices: none -> 9.89 us  [the longest x1 6.36 us: local(): first_cols = lax.all_to_all(first_input, 'seq', 1, 0, tiled=True)]
    dynamic_slice x24 -> x0, local copies, waits for them, and re-layouts: 8.53 us -> none  [the longest x8 7.8 us: one_block(): sub_field = lax.dynamic_slice_in_dim(piece_field, offset, tok_rows, 1)]
  transfers between devices with their start and end apart: 2 -> 2, of which waited for: 2 -> 1; matrix products, arithmetic and copies ran while one was open for 1% -> 13% of each run, Pallas kernels for 0% -> 0%
where the time goes in v1:
time: 95.9 us; the launch traced here: 95.3 us
  blocking collectives  62.4 us (65%)
  matrix products  11.7 us (12%)
  starting transfers between devices  9.89 us (10%)
  other arithmetic  5.69 us (6%)
  waiting for transfers between devices  2.89 us (3%)
  local copies, waits for them, and re-layouts  2.54 us (3%)
    psum x1, blocking collectives, local(): return lax.psum(partial_out, 'chan').astype(BF16)  40.5 us
    dot_general x15, matrix products, mm(): return jnp.dot(a, b, preferred_element_type=F32)  11.7 us
    all_gather x1, blocking collectives, local(): segs = lax.all_gather(segment_ids, 'seq', tiled=True)  11.4 us
    all_to_all x1, blocking collectives, local(): mix_rows = lax.all_to_all(second_mix, 'seq', 0, 1, tiled=True)  10.5 us
    all_to_all x1, starting transfers between devices, local(): first_cols = lax.all_to_all(first_input, 'seq', 1, 0, tiled=True)  6.36 us
    all_to_all x1, starting transfers between devices, local(): gate_cols = lax.all_to_all(second_gate, 'seq', 1, 0, tiled=True)  3.54 us
    sub x2, other arithmetic, long_conv(): y = jnp.concatenate([xr * a - xi * b, xr * b + xi * d], axis=0)  3.13 us
    all_to_all x1, waiting for transfers between devices, local(): gate_cols = lax.all_to_all(second_gate, 'seq', 1, 0, tiled=True)  2.88 us
  transfers between devices with their start and end apart: 2, of which 1 were waited for; matrix products, arithmetic and copies ran while one was open for 13% of the time, Pallas kernels for 0%

profile of v1, /device:TPU:0, one launch (start us, length us, event | category | flops | bytes accessed | tf_op | source)
XLA Modules:
  0.0 95.3 jit_solution(12851788758731247672)
XLA Ops:
  0.0 0.0 copy-start.2
  0.0 0.0 copy-start.1
  0.0 0.0 copy-start.4
  0.0 0.0 copy-start.5
  0.0 1.2 %multiply_convert_fusion = bf16[128,1024]{1,0:T(8,128)(2,1)S(1)} fusion(bf16[128,1024]{1,0:T(8,128)(2,1)} %param.11, bf16[128,1024]{1,0:T(8,128)(2,1)} %param.12), kind=kLoop, calls=%fused_computation.48 | loop fusion | flops 524288 | bytes 786432 | tf_op jit(solution)/shard_map/convert_element_type | solution.py:82
  1.2 0.9 copy.35
  2.1 6.4 %all-to-all-start.1 = ((bf16[128,4,256]{0,2,1:T(8,128)(2,1)}), bf16[128,4,256]{0,2,1:T(8,128)(2,1)S(1)}, u32[]{:S(2)}, u32[]{:S(2)}) async-start(bf16[128,4,256]{0,2,1:T(8,128)(2,1)} %bitcast.3), calls=%async_computation.1 | async-start | bytes 524288 | tf_op jit(solution)/shard_map/all_to_all | solution.py:83
  8.4 0.7 dynamic-slice_bitcast_fusion
  9.2 1.4 %fusion.38 = f32[256,512]{0,1:T(8,128)S(1)} fusion(bf16[512,256]{0,1:T(8,128)(2,1)S(1)} %bitcast.69, bf16[512,512]{1,0:T(8,128)(2,1)} %constant.27.clone), kind=kOutput, calls=%fused_computation.78 | convolution fusion | flops 134217728 | bytes 1310720 | tf_op jit(solution)/shard_map/dot_general | solution.py:36
  10.6 1.4 %fusion.39 = f32[256,512]{0,1:T(8,128)S(1)} fusion(bf16[512,256]{0,1:T(8,128)(2,1)S(1)} %bitcast.71, bf16[512,512]{1,0:T(8,128)(2,1)} %constant.27.clone), kind=kOutput, calls=%fused_computation.79 | convolution fusion | flops 134217728 | bytes 1310720 | tf_op jit(solution)/shard_map/dot_general | solution.py:36
  12.0 0.0 copy-start
  12.0 1.4 %fusion.5 = f32[512,256]{1,0:T(8,128)S(1)} fusion(f32[256,512]{0,1:T(8,128)S(1)} %fusion.38, bf16[512,256]{0,1:T(8,128)(2,1)S(1)} %bitcast.70, bf16[512,512]{1,0:T(8,128)(2,1)} %constant.28.clone), kind=kOutput, calls=%fused_computation.17 | convolution fusion | flops 134348800 | bytes 1835008 | tf_op jit(solution)/shard_map/dot_general | solution.py:36
  13.4 1.4 %fusion.4 = f32[512,256]{1,0:T(8,128)S(1)} fusion(f32[256,512]{0,1:T(8,128)S(1)} %fusion.39, bf16[512,256]{0,1:T(8,128)(2,1)S(1)} %bitcast.72, bf16[512,512]{1,0:T(8,128)(2,1)} %constant.28.clone), kind=kOutput, calls=%fused_computation.15 | convolution fusion | flops 134348800 | bytes 1835008 | tf_op jit(solution)/shard_map/dot_general | solution.py:36
  14.8 0.0 copy-done.4
  14.8 0.9 copy.33
  15.7 0.0 copy-done.5
  15.7 11.4 %all-gather = s32[4,1,128]{2,1,0:T(1,128)S(1)} all-gather(s32[1,1,128]{2,1,0:T(1,128)S(1)} %bitcast.81), channel_id=1, replica_groups=mesh['groups'=2,'seq'=4,'chan'=4] {'seq'}, dimensions={0}, use_global_device_ids=true | all-gather | bytes 2560 | tf_op jit(solution)/shard_map/all_gather | solution.py:51
  27.1 1.0 %slice_select_fusion.6 = (f32[256,256]{1,0:T(8,128)S(1)}, f32[256,256]{1,0:T(8,128)S(1)}, f32[256,256]{1,0:T(8,128)}, f32[256,256]{1,0:T(8,128)}, f32[256,256]{1,0:T(8,128)}, /*index=5*/f32[256,256]{1,0:T(8,128)}) fusion(f32[512,256]{1,0:T(8,128)S(1)} %fusion.5, pred[256]{0:T(512)(128)(4,1)S(1)} %iota_compare_fusion, f32[512,256]{1,0:T(8,128)S(1)} %fusion.4), kind=kLoop, calls=%fused_computation.59 | loop fusion | flops 262144 | bytes 2621696 | tf_op jit(solution)/shard_map/jit(_where)/select_n | solution.py:63
  28.1 0.0 copy-start.3
  28.1 0.0 all-to-all-done.1
  28.1 3.5 %all-to-all-start = ((bf16[128,4,256]{0,2,1:T(8,128)(2,1)}), bf16[128,4,256]{0,2,1:T(8,128)(2,1)S(1)}, u32[]{:S(2)}, u32[]{:S(2)}) async-start(bf16[128,4,256]{0,2,1:T(8,128)(2,1)} %bitcast.1), calls=%async_computation | async-start | bytes 524288 | tf_op jit(solution)/shard_map/all_to_all | solution.py:84
  31.6 0.1 bitcast_select_fusion.1
  31.7 0.0 copy-done.2
  31.7 0.5 fusion.23
  32.2 0.0 copy-done.1
  32.2 0.5 fusion.3
  32.7 1.3 %fusion.14 = (f32[256,512]{1,0:T(8,128)S(1)}, f32[256,512]{1,0:T(8,128)S(1)}) fusion(f32[256,256]{1,0:T(8,128)} %get-tuple-element.18, f32[256,256]{1,0:T(8,128)S(1)} %get-tuple-element.14, f32[512,512]{1,0:T(8,128)S(1)} %fusion.3, f32[256,256]{1,0:T(8,128)S(1)} %get-tuple-element.13), kind=kLoop, calls=%fused_computation.33 | loop fusion | flops 1179648 | bytes 2883584 | tf_op jit(solution)/shard_map/sub | solution.py:75
  34.0 0.0 copy-done
  34.0 0.5 fusion.25
  34.5 0.5 convolution_add_fusion.4
  35.0 0.0 copy-done.3
  35.0 0.5 fusion.2
  35.5 2.9 %all-to-all-done = bf16[128,4,256]{0,2,1:T(8,128)(2,1)S(1)} async-done(((bf16[128,4,256]{0,2,1:T(8,128)(2,1)}), bf16[128,4,256]{0,2,1:T(8,128)(2,1)S(1)}, u32[]{:S(2)}, u32[]{:S(2)}) %all-to-all-start) | async-done | bytes 262176 | tf_op jit(solution)/shard_map/all_to_all | solution.py:84
  38.4 0.1 broadcast_select_fusion.1
  38.6 0.5 fusion.22
  39.0 0.0 slice-start
  39.1 0.5 fusion.1
  39.5 1.9 %fusion.18 = (f32[256,512]{1,0:T(8,128)S(1)}, f32[256,512]{1,0:T(8,128)S(1)}) fusion(f32[256,256]{1,0:T(8,128)} %get-tuple-element.21, f32[256,256]{1,0:T(8,128)} %get-tuple-element.22, f32[512,512]{1,0:T(8,128)S(1)} %fusion.1, f32[256,256]{1,0:T(8,128)} %get-tuple-element.23), kind=kLoop, calls=%fused_computation.41 | loop fusion | flops 1179648 | bytes 2883584 | tf_op jit(solution)/shard_map/sub | solution.py:75
  41.4 0.5 fusion.26
  41.9 0.0 slice-start.1
  41.9 0.5 convolution_add_fusion.1
  42.4 0.5 fusion
  42.9 0.1 copy_bitcast_fusion
  43.0 10.5 %all_to_all.51 = bf16[4,128,256]{1,2,0:T(8,128)(2,1)S(1)} all-to-all(bf16[4,128,256]{1,2,0:T(8,128)(2,1)S(1)} %copy_bitcast_fusion), channel_id=1, replica_groups=mesh['groups'=2,'seq'=4,'chan'=4] {'seq'}, dimensions={0} | all-to-all | bytes 524288 | tf_op jit(solution)/shard_map/all_to_all | solution.py:88
  53.5 0.0 slice-done
  53.5 0.0 slice-done.1
  53.5 1.3 %fusion.40 = f32[128,4096]{1,0:T(8,128)S(1)} fusion(bf16[128,1024]{0,1:T(8,128)(2,1)S(1)} %bitcast.73, bf16[1024,4096]{1,0:T(8,128)(2,1)S(1)} %bitcast.68), kind=kOutput, calls=%fused_computation.80 | convolution fusion | flops 1073741824 | bytes 10747904 | tf_op jit(solution)/shard_map/dot_general | solution.py:36
  54.8 40.5 %all-reduce.1 = bf16[128,4096]{1,0:T(8,128)(2,1)} all-reduce(f32[128,4096]{1,0:T(8,128)S(1)} %fusion.40), channel_id=1, replica_groups=mesh['groups'=2,'seq'=4,'chan'=4] {'chan'}, use_global_device_ids=true, to_apply=%region_0.1 | all-reduce | flops 524288 | bytes 3145728 | tf_op jit(solution)/shard_map/psum | solution.py:90
  (6 shorter events, 0.1 us)
Async XLA Ops:
  0.0 31.7 %copy-start.2 = (bf16[512,512]{1,0:T(8,128)(2,1)S(1)}, bf16[512,512]{1,0:T(8,128)(2,1)}, u32[]{:S(2)}) copy-start(bf16[512,512]{1,0:T(8,128)(2,1)} %constant.27.clone) | copy-start | bytes 1572868
  0.0 32.2 %copy-start.1 = (bf16[512,512]{1,0:T(8,128)(2,1)S(1)}, bf16[512,512]{1,0:T(8,128)(2,1)}, u32[]{:S(2)}) copy-start(bf16[512,512]{1,0:T(8,128)(2,1)} %constant.28.clone) | copy-start | bytes 1572868
  0.0 14.8 %copy-start.4 = (bf16[128,1024]{1,0:T(8,128)(2,1)S(1)}, bf16[128,1024]{1,0:T(8,128)(2,1)}, u32[]{:S(2)}) copy-start(bf16[128,1024]{1,0:T(8,128)(2,1)} %param.13) | copy-start | bytes 786436
  0.0 15.7 %copy-start.5 = (s32[128]{0:T(128)S(1)}, s32[128]{0:T(128)}, u32[]{:S(2)}) copy-start(s32[128]{0:T(128)} %param.17) | copy-start | bytes 1540
  2.1 26.0 %all-to-all-start.1 = ((bf16[128,4,256]{0,2,1:T(8,128)(2,1)}), bf16[128,4,256]{0,2,1:T(8,128)(2,1)S(1)}, u32[]{:S(2)}, u32[]{:S(2)}) async-start(bf16[128,4,256]{0,2,1:T(8,128)(2,1)} %bitcast.3), calls=%async_computation.1 | async-start | bytes 524288 | tf_op jit(solution)/shard_map/all_to_all | solution.py:83
  12.0 22.0 %copy-start = (bf16[512,512]{1,0:T(8,128)(2,1)S(1)}, bf16[512,512]{1,0:T(8,128)(2,1)}, u32[]{:S(2)}) copy-start(bf16[512,512]{1,0:T(8,128)(2,1)} %constant.29.clone) | copy-start | bytes 1572868
  28.1 6.9 %copy-start.3 = (bf16[512,512]{1,0:T(8,128)(2,1)S(1)}, bf16[512,512]{1,0:T(8,128)(2,1)}, u32[]{:S(2)}) copy-start(bf16[512,512]{1,0:T(8,128)(2,1)} %constant.30.clone) | copy-start | bytes 1572868
  28.1 10.3 %all-to-all-start = ((bf16[128,4,256]{0,2,1:T(8,128)(2,1)}), bf16[128,4,256]{0,2,1:T(8,128)(2,1)S(1)}, u32[]{:S(2)}, u32[]{:S(2)}) async-start(bf16[128,4,256]{0,2,1:T(8,128)(2,1)} %bitcast.1), calls=%async_computation | async-start | bytes 524288 | tf_op jit(solution)/shard_map/all_to_all | solution.py:84
  39.0 14.4 %slice-start = ((s8[8388608]{0:T(1024)(128)(4,1)}), s8[4194304]{0:T(1024)(128)(4,1)S(1)}, s32[]{:S(2)}) async-start(s8[8388608]{0:T(1024)(128)(4,1)} %bitcast.67), calls=%async_computation.3 | async-start | bytes 8388608
  41.9 11.6 %slice-start.1 = ((s8[8388608]{0:T(1024)(128)(4,1)}), s8[4194304]{0:T(1024)(128)(4,1)S(1)}, s32[]{:S(2)}) async-start(s8[8388608]{0:T(1024)(128)(4,1)} %bitcast.67), calls=%async_computation.4 | async-start | bytes 8388608

commit v2 on v1

--- a/solution.py
+++ b/solution.py
@@ -36,7 +36,22 @@
     return jnp.dot(a, b, preferred_element_type=F32)
 
 
-def make_local(nseq):
+def swap(x, bit):
+    return lax.ppermute(x, "chan", [(c, c ^ bit) for c in range(4)])
+
+
+def chan_sum(partial_out):
+    core = lax.axis_index("chan") % 2
+    width = partial_out.shape[1] // 2
+    mine = lax.dynamic_slice_in_dim(partial_out, core * width, width, 1)
+    other = lax.dynamic_slice_in_dim(partial_out, (1 - core) * width, width, 1)
+    chip = mine + swap(other.astype(BF16), 1).astype(F32)
+    total = (chip + swap(chip.astype(BF16), 2).astype(F32)).astype(BF16)
+    peer = swap(total, 1)
+    return jnp.where(core == 0, jnp.concatenate([total, peer], 1), jnp.concatenate([peer, total], 1))
+
+
+def make_local(nseq, nchan):
     def local(value, first_gate, second_gate, first_filter, second_filter, out_weight, segment_ids):
         chans = value.shape[1]
         filt_local, length = first_filter.shape
@@ -48,9 +63,6 @@
         f_hi, f_lo, i_hi, i_lo = (jnp.asarray(m) for m in (f_hi, f_lo, i_hi, i_lo))
         me = lax.axis_index("seq")
 
-        segs = lax.all_gather(segment_ids, "seq", tiled=True)
-        in0 = (segs == 0)[:, None]
-        in1 = (segs == 1)[:, None]
 
         def spectrum(filt):
             mine = lax.dynamic_slice_in_dim(filt, me * fpd, fpd, 0)
@@ -79,15 +91,29 @@
             both = mm(i_hi, y_hi) + mm(i_hi, y_lo) + mm(i_lo, y_hi)
             return jnp.where(in0, both[:, :per], 0.0) + jnp.where(in1, both[:, per:], 0.0)
 
+        rows = value.shape[0]
         first_input = (first_gate.astype(F32) * value.astype(F32)).astype(BF16)
-        first_cols = lax.all_to_all(first_input, "seq", 1, 0, tiled=True)
+        id_rows = -(-rows // per)
+        ids = jnp.pad(segment_ids.astype(BF16), (0, id_rows * per - rows)).reshape(id_rows, 1, per)
+        ids = jnp.broadcast_to(ids, (id_rows, nseq, per))
+        pad_rows = -(-id_rows // 16) * 16
+        ids = jnp.pad(ids, ((0, pad_rows - id_rows), (0, 0), (0, 0)))
+        payload = jnp.concatenate([first_input.reshape(rows, nseq, per), ids], axis=0)
+        got = lax.all_to_all(payload.reshape(rows + pad_rows, nseq * per), "seq", 1, 0, tiled=True)
+        got = got.reshape(nseq, rows + pad_rows, per)
+        first_cols = got[:, :rows].reshape(nseq * rows, per)
+        segs = got[:, rows:rows + id_rows].reshape(nseq, id_rows * per)[:, :rows].reshape(nseq * rows)
+        in0 = (segs == 0)[:, None]
+        in1 = (segs == 1)[:, None]
         gate_cols = lax.all_to_all(second_gate, "seq", 1, 0, tiled=True)
         first_mix = long_conv(spectrum(first_filter), first_cols)
         second_input = (gate_cols.astype(F32) * first_mix).astype(BF16)
         second_mix = long_conv(spectrum(second_filter), second_input).astype(BF16)
         mix_rows = lax.all_to_all(second_mix, "seq", 0, 1, tiled=True)
         partial_out = mm(mix_rows, out_weight)
-        return lax.psum(partial_out, "chan").astype(BF16)
+        if nchan != 4:
+            return lax.psum(partial_out, "chan").astype(BF16)
+        return chan_sum(partial_out)
 
     return local
 
@@ -103,5 +129,5 @@
         P(("groups", "seq")),
     )
     out_specs = P(("groups", "seq"), None)
-    local = make_local(mesh.shape["seq"])
+    local = make_local(mesh.shape["seq"], mesh.shape["chan"])
     return jax.shard_map(local, mesh=mesh, in_specs=in_specs, out_specs=out_specs, check_vma=False)

time: 95.9 us -> 69.9 us (0.73)
  blocking collectives: 62.4 us -> 0 us
  waiting for transfers between devices: 2.89 us -> 30.8 us
  starting transfers between devices: 9.89 us -> 15 us
  local copies, waits for them, and re-layouts: 2.54 us -> 7.42 us
    psum x1 -> x0, blocking collectives: 40.5 us -> none  [local(): return lax.psum(partial_out, 'chan').astype(BF16)]
    ppermute x0 -> x3, waiting for transfers between devices: none -> 16.3 us  [swap(): return lax.ppermute(x, 'chan', [(c, c ^ bit) for c in range(4)])]
    all_to_all x1 -> x2, waiting for transfers between devices: 0.01 us -> 12 us  [the longest x1 6.72 us: local(): mix_rows = lax.all_to_all(second_mix, 'seq', 0, 1, tiled=True)]
    all_gather x1 -> x0, blocking collectives: 11.4 us -> none  [local(): segs = lax.all_gather(segment_ids, 'seq', tiled=True)]
    all_to_all x1 -> x0, blocking collectives: 10.5 us -> none  [local(): mix_rows = lax.all_to_all(second_mix, 'seq', 0, 1, tiled=True)]
    unnamed x17 -> x22, local copies, waits for them, and re-layouts: 0.9 us -> 5.37 us
    all_to_all x1 -> x2, starting transfers between devices: 6.36 us -> 9.88 us  [the longest x1 6.48 us: local(): lax.all_to_all(payload.reshape(rows + pad_rows, nseq * per), 'seq', 1, 0,...]
    sub x2, other arithmetic: 3.13 us -> 0.46 us  [long_conv(): y = jnp.concatenate([xr * a - xi * b, xr * b + xi * d], axis=0)]
  transfers between devices with their start and end apart: 2 -> 6, of which waited for: 1 -> 6; matrix products, arithmetic and copies ran while one was open for 13% -> 10% of each run, Pallas kernels for 0% -> 0%
where the time goes in v2:
time: 69.9 us; the launch traced here: 69.3 us
  waiting for transfers between devices  30.8 us (44%)
  starting transfers between devices  15 us (21%)
  matrix products  10.8 us (15%)
  local copies, waits for them, and re-layouts  7.42 us (11%)
  other arithmetic  4.85 us (7%)
    ppermute x3, waiting for transfers between devices, swap(): return lax.ppermute(x, 'chan', [(c, c ^ bit) for c in range(4)])  16.3 us
    dot_general x15, matrix products, mm(): return jnp.dot(a, b, preferred_element_type=F32)  10.8 us
    all_to_all x1, waiting for transfers between devices, local(): mix_rows = lax.all_to_all(second_mix, 'seq', 0, 1, tiled=True)  6.72 us
    all_to_all x1, starting transfers between devices, local(): lax.all_to_all(payload.reshape(rows + pad_rows, nseq * per), 'seq', 1, 0,...  6.48 us
    unnamed x22, local copies, waits for them, and re-layouts  5.37 us
    all_to_all x1, waiting for transfers between devices, local(): lax.all_to_all(payload.reshape(rows + pad_rows, nseq * per), 'seq', 1, 0,...  5.29 us
    all_to_all x1, starting transfers between devices, local(): mix_rows = lax.all_to_all(second_mix, 'seq', 0, 1, tiled=True)  3.41 us
    all_to_all x1, starting transfers between devices, local(): gate_cols = lax.all_to_all(second_gate, 'seq', 1, 0, tiled=True)  3.4 us
  transfers between devices with their start and end apart: 6, of which 6 were waited for; matrix products, arithmetic and copies ran while one was open for 10% of the time, Pallas kernels for 0%

profile of v2, /device:TPU:0, one launch (start us, length us, event | category | flops | bytes accessed | tf_op | source)
XLA Modules:
  0.0 69.3 jit_solution(5097228464414926217)
XLA Ops:
  0.0 1.1 %copy.44 = bf16[128,1024]{0,1:T(8,128)(2,1)S(1)} copy(bf16[128,1024]{1,0:T(8,128)(2,1)} %param.12) | data formatting | bytes 524288 | tf_op args[1]
  1.1 0.0 copy-start.2
  1.1 1.2 %copy.45 = bf16[128,1024]{0,1:T(8,128)(2,1)S(1)} copy(bf16[128,1024]{1,0:T(8,128)(2,1)} %param.11) | data formatting | bytes 524288 | tf_op args[0]
  2.3 0.7 convert_element_type.61
  3.0 0.1 multiply_convert_fusion
  3.1 0.1 broadcast_in_dim.59
  3.2 0.1 fusion.10
  3.3 0.9 %copy.46 = bf16[144,4,256]{2,0,1:T(8,128)(2,1)} copy(bf16[144,4,256]{0,2,1:T(8,128)(2,1)S(1)} %fusion.10) | data formatting | bytes 589824 | tf_op jit(solution)/shard_map/concatenate | solution.py:101
  4.2 0.0 copy-start.1
  4.2 6.5 %all-to-all-start = ((bf16[144,4,256]{2,0,1:T(8,128)(2,1)}), bf16[144,4,256]{2,0,1:T(8,128)(2,1)S(1)}, u32[]{:S(2)}, u32[]{:S(2)}) async-start(bf16[144,4,256]{2,0,1:T(8,128)(2,1)} %copy.46), calls=%async_computation | async-start | bytes 589824 | tf_op jit(solution)/shard_map/all_to_all | solution.py:102
  10.7 0.7 %dynamic-slice_bitcast_fusion = (bf16[512,16]{0,1:T(8,128)(2,1)S(1)}, bf16[512,16]{0,1:T(8,128)(2,1)S(1)}) fusion(bf16[64,512]{1,0:T(8,128)(2,1)} %param.15, s32[]{:T(128)S(6)} %select_n.69, bf16[64,512]{1,0:T(8,128)(2,1)} %param.14), kind=kLoop, calls=%fused_computation.69 | loop fusion | bytes 65540 | tf_op jit(solution)/shard_map/transpose | solution.py:69
  11.5 0.0 copy-done.2
  11.5 0.3 fusion.42
  11.8 0.3 fusion.41
  12.2 0.0 copy-done.1
  12.2 0.0 copy-start.8
  12.2 0.3 fusion.4
  12.5 0.3 fusion.5
  12.9 0.3 copy-done.8
  13.1 0.9 %copy.47 = bf16[128,1024]{0,1:T(8,128)(2,1)} copy(bf16[128,1024]{1,0:T(8,128)(2,1)S(1)} %copy-done.8) | data formatting | bytes 524288 | tf_op args[2]
  14.0 1.0 %slice_select_fusion.6 = (f32[256,256]{1,0:T(8,128)S(1)}, f32[256,256]{1,0:T(8,128)S(1)}, f32[256,256]{1,0:T(8,128)}, f32[256,256]{1,0:T(8,128)}, f32[256,256]{1,0:T(8,128)}, /*index=5*/f32[256,256]{1,0:T(8,128)}) fusion(f32[512,256]{1,0:T(8,128)S(1)} %fusion.5, pred[256]{0:T(512)(128)(4,1)S(1)} %iota_compare_fusion.1, f32[512,256]{1,0:T(8,128)S(1)} %fusion.4), kind=kLoop, calls=%fused_computation.67 | loop fusion | flops 262144 | bytes 2621696 | tf_op jit(solution)/shard_map/jit(_where)/select_n | solution.py:75
  15.0 5.3 %all-to-all-done = bf16[144,4,256]{2,0,1:T(8,128)(2,1)S(1)} async-done(((bf16[144,4,256]{2,0,1:T(8,128)(2,1)}), bf16[144,4,256]{2,0,1:T(8,128)(2,1)S(1)}, u32[]{:S(2)}, u32[]{:S(2)}) %all-to-all-start) | async-done | bytes 294944 | tf_op jit(solution)/shard_map/all_to_all | solution.py:102
  20.3 3.4 %all-to-all-start.1 = ((bf16[128,4,256]{0,2,1:T(8,128)(2,1)}), bf16[128,4,256]{0,2,1:T(8,128)(2,1)S(1)}, u32[]{:S(2)}, u32[]{:S(2)}) async-start(bf16[128,4,256]{0,2,1:T(8,128)(2,1)} %bitcast.3), calls=%async_computation.1 | async-start | bytes 524288 | tf_op jit(solution)/shard_map/all_to_all | solution.py:108
  23.8 0.1 copy.65
  24.0 0.5 fusion.26
  24.4 0.0 copy-start.7
  24.5 0.5 fusion.3
  24.9 0.0 copy-start
  24.9 0.5 copy-done.7
  25.4 0.2 fusion.17
  25.6 0.4 copy-done
  26.0 0.5 fusion.28
  26.5 0.0 copy-start.3
  26.5 0.5 convolution_add_fusion.4
  27.0 0.5 copy-done.3
  27.5 0.5 fusion.2
  28.0 2.5 %all-to-all-done.1 = bf16[128,4,256]{0,2,1:T(8,128)(2,1)S(1)} async-done(((bf16[128,4,256]{0,2,1:T(8,128)(2,1)}), bf16[128,4,256]{0,2,1:T(8,128)(2,1)S(1)}, u32[]{:S(2)}, u32[]{:S(2)}) %all-to-all-start.1) | async-done | bytes 262176 | tf_op jit(solution)/shard_map/all_to_all | solution.py:108
  30.6 0.1 broadcast_select_fusion.2
  30.7 0.5 fusion.25
  31.2 0.0 copy-start.4
  31.2 0.0 copy-start.5
  31.2 0.0 copy-start.6
  31.2 0.5 fusion.1
  31.7 0.4 copy-done.4
  32.2 0.1 copy-done.5
  32.2 0.1 copy-done.6
  32.3 0.2 fusion.21
  32.6 0.5 fusion.29
  33.1 0.5 convolution_add_fusion.1
  33.6 0.5 fusion
  34.1 0.8 %copy_bitcast_fusion = bf16[4,128,256]{1,2,0:T(8,128)(2,1)} fusion(f32[512,512]{0,1:T(8,128)S(1)} %fusion, pred[512]{0:T(512)(128)(4,1)S(1)} %get-tuple-element.19, pred[512]{0:T(512)(128)(4,1)S(1)} %get-tuple-element.20), kind=kLoop, calls=%fused_computation.60 | loop fusion | flops 524288 | bytes 1311744 | tf_op jit(solution)/shard_map/all_to_all | solution.py:112
  34.8 3.4 %all-to-all-start.2 = ((bf16[4,128,256]{1,2,0:T(8,128)(2,1)}), bf16[4,128,256]{1,2,0:T(8,128)(2,1)S(1)}, u32[]{:S(2)}, u32[]{:S(2)}) async-start(bf16[4,128,256]{1,2,0:T(8,128)(2,1)} %copy_bitcast_fusion), calls=%async_computation.2 | async-start | bytes 524288 | tf_op jit(solution)/shard_map/all_to_all | solution.py:112
  38.3 6.7 %all-to-all-done.2 = bf16[4,128,256]{1,2,0:T(8,128)(2,1)S(1)} async-done(((bf16[4,128,256]{1,2,0:T(8,128)(2,1)}), bf16[4,128,256]{1,2,0:T(8,128)(2,1)S(1)}, u32[]{:S(2)}, u32[]{:S(2)}) %all-to-all-start.2) | async-done | bytes 262176 | tf_op jit(solution)/shard_map/all_to_all | solution.py:112
  45.0 4.7 %fusion.43 = f32[128,4096]{1,0:T(8,128)S(1)} fusion(bf16[128,1024]{0,1:T(8,128)(2,1)S(1)} %bitcast.70, bf16[1024,4096]{1,0:T(8,128)(2,1)} %param.16), kind=kOutput, calls=%fused_computation.89 | convolution fusion | flops 1073741824 | bytes 10747904 | tf_op jit(solution)/shard_map/dot_general | solution.py:36
  49.7 0.1 dynamic-slice_convert_fusion
  49.7 0.1 collective-permute-start
  49.8 1.9 %collective-permute-done = bf16[128,2048]{1,0:T(8,128)(2,1)S(1)} collective-permute-done((bf16[128,2048]{1,0:T(8,128)(2,1)S(1)}, bf16[128,2048]{1,0:T(8,128)(2,1)S(1)}, u32[]{:S(2)}, u32[]{:S(2)}) %collective-permute-start) | collective-permute-done | bytes 524320 | tf_op jit(solution)/shard_map/ppermute | solution.py:40
  51.7 0.1 fusion.9
  51.8 1.6 %collective-permute-start.1 = (bf16[128,2048]{1,0:T(8,128)(2,1)S(1)}, bf16[128,2048]{1,0:T(8,128)(2,1)S(1)}, u32[]{:S(2)}, u32[]{:S(2)}) collective-permute-start(bf16[128,2048]{1,0:T(8,128)(2,1)S(1)} %fusion.9), channel_id=1, source_target_pairs={{0,2},{1,3},{2,0},{3,1},{4,6},{5,7},{6,4},{7,5},{8,10},{9,11},{10,... | collective-permute-start | bytes 1572872 | tf_op jit(solution)/shard_map/ppermute | solution.py:40
  53.4 12.5 %collective-permute-done.1 = bf16[128,2048]{1,0:T(8,128)(2,1)S(1)} collective-permute-done((bf16[128,2048]{1,0:T(8,128)(2,1)S(1)}, bf16[128,2048]{1,0:T(8,128)(2,1)S(1)}, u32[]{:S(2)}, u32[]{:S(2)}) %collective-permute-start.1) | collective-permute-done | bytes 524320 | tf_op jit(solution)/shard_map/ppermute | solution.py:40
  65.9 0.2 add_convert_fusion
  66.1 0.1 collective-permute-start.2
  66.1 1.9 %collective-permute-done.2 = bf16[128,2048]{1,0:T(8,128)(2,1)S(1)} collective-permute-done((bf16[128,2048]{1,0:T(8,128)(2,1)S(1)}, bf16[128,2048]{1,0:T(8,128)(2,1)S(1)}, u32[]{:S(2)}, u32[]{:S(2)}) %collective-permute-start.2) | collective-permute-done | bytes 524320 | tf_op jit(solution)/shard_map/ppermute | solution.py:40
  68.0 1.2 %maximum_select_fusion = bf16[128,4096]{1,0:T(8,128)(2,1)} fusion(bf16[128,2048]{1,0:T(8,128)(2,1)S(1)} %collective-permute-done.2, bf16[128,2048]{1,0:T(8,128)(2,1)S(1)} %add_convert_fusion, pred[]{:T(512)S(6)} %eq.42), kind=kLoop, calls=%fused_computation.23 | loop fusion | flops 4718592 | bytes 2097153 | tf_op jit(solution)/shard_map/jit(_where)/select_n | solution.py:51
  (10 shorter events, 0.2 us)
Async XLA Ops:
  1.1 10.3 %copy-start.2 = (bf16[512,512]{1,0:T(8,128)(2,1)S(1)}, bf16[512,512]{1,0:T(8,128)(2,1)}, u32[]{:S(2)}) copy-start(bf16[512,512]{1,0:T(8,128)(2,1)} %constant.47.clone) | copy-start | bytes 1572868
  4.2 8.0 %copy-start.1 = (bf16[512,512]{1,0:T(8,128)(2,1)S(1)}, bf16[512,512]{1,0:T(8,128)(2,1)}, u32[]{:S(2)}) copy-start(bf16[512,512]{1,0:T(8,128)(2,1)} %constant.48.clone) | copy-start | bytes 1572868
  4.2 16.1 %all-to-all-start = ((bf16[144,4,256]{2,0,1:T(8,128)(2,1)}), bf16[144,4,256]{2,0,1:T(8,128)(2,1)S(1)}, u32[]{:S(2)}, u32[]{:S(2)}) async-start(bf16[144,4,256]{2,0,1:T(8,128)(2,1)} %copy.46), calls=%async_computation | async-start | bytes 589824 | tf_op jit(solution)/shard_map/all_to_all | solution.py:102
  12.2 1.0 %copy-start.8 = (bf16[128,1024]{1,0:T(8,128)(2,1)S(1)}, bf16[128,1024]{1,0:T(8,128)(2,1)}, u32[]{:S(2)}) copy-start(bf16[128,1024]{1,0:T(8,128)(2,1)} %param.13) | copy-start | bytes 786436
  20.3 10.3 %all-to-all-start.1 = ((bf16[128,4,256]{0,2,1:T(8,128)(2,1)}), bf16[128,4,256]{0,2,1:T(8,128)(2,1)S(1)}, u32[]{:S(2)}, u32[]{:S(2)}) async-start(bf16[128,4,256]{0,2,1:T(8,128)(2,1)} %bitcast.3), calls=%async_computation.1 | async-start | bytes 524288 | tf_op jit(solution)/shard_map/all_to_all | solution.py:108
  24.4 1.0 %copy-start.7 = (f32[256,256]{1,0:T(8,128)S(1)}, f32[256,256]{1,0:T(8,128)}, u32[]{:S(2)}) copy-start(f32[256,256]{1,0:T(8,128)} %get-tuple-element.16) | copy-start | bytes 786436
  24.9 1.1 %copy-start = (bf16[512,512]{1,0:T(8,128)(2,1)S(1)}, bf16[512,512]{1,0:T(8,128)(2,1)}, u32[]{:S(2)}) copy-start(bf16[512,512]{1,0:T(8,128)(2,1)} %constant.49.clone) | copy-start | bytes 1572868
  26.5 1.0 %copy-start.3 = (bf16[512,512]{1,0:T(8,128)(2,1)S(1)}, bf16[512,512]{1,0:T(8,128)(2,1)}, u32[]{:S(2)}) copy-start(bf16[512,512]{1,0:T(8,128)(2,1)} %constant.50.clone) | copy-start | bytes 1572868
  31.2 1.0 %copy-start.4 = (f32[256,256]{1,0:T(8,128)S(1)}, f32[256,256]{1,0:T(8,128)}, u32[]{:S(2)}) copy-start(f32[256,256]{1,0:T(8,128)} %get-tuple-element.21) | copy-start | bytes 786436
  31.2 1.0 %copy-start.5 = (f32[256,256]{1,0:T(8,128)S(1)}, f32[256,256]{1,0:T(8,128)}, u32[]{:S(2)}) copy-start(f32[256,256]{1,0:T(8,128)} %get-tuple-element.22) | copy-start | bytes 786436
  31.2 1.1 %copy-start.6 = (f32[256,256]{1,0:T(8,128)S(1)}, f32[256,256]{1,0:T(8,128)}, u32[]{:S(2)}) copy-start(f32[256,256]{1,0:T(8,128)} %get-tuple-element.23) | copy-start | bytes 786436
  34.8 10.2 %all-to-all-start.2 = ((bf16[4,128,256]{1,2,0:T(8,128)(2,1)}), bf16[4,128,256]{1,2,0:T(8,128)(2,1)S(1)}, u32[]{:S(2)}, u32[]{:S(2)}) async-start(bf16[4,128,256]{1,2,0:T(8,128)(2,1)} %copy_bitcast_fusion), calls=%async_computation.2 | async-start | bytes 524288 | tf_op jit(solution)/shard_map/all_to_all | solution.py:112
  49.7 2.0 %collective-permute-start = (bf16[128,2048]{1,0:T(8,128)(2,1)S(1)}, bf16[128,2048]{1,0:T(8,128)(2,1)S(1)}, u32[]{:S(2)}, u32[]{:S(2)}) collective-permute-start(bf16[128,2048]{1,0:T(8,128)(2,1)S(1)} %dynamic-slice_convert_fusion), channel_id=1, source_target_pairs={{0,1},{1,0},{2,3},{3,2},{4,5},{5,4},{6,7},{7,6},{8,9},{9,8},{10,11... | collective-permute-start | bytes 1572872 | tf_op jit(solution)/shard_map/ppermute | solution.py:40
  51.8 14.0 %collective-permute-start.1 = (bf16[128,2048]{1,0:T(8,128)(2,1)S(1)}, bf16[128,2048]{1,0:T(8,128)(2,1)S(1)}, u32[]{:S(2)}, u32[]{:S(2)}) collective-permute-start(bf16[128,2048]{1,0:T(8,128)(2,1)S(1)} %fusion.9), channel_id=1, source_target_pairs={{0,2},{1,3},{2,0},{3,1},{4,6},{5,7},{6,4},{7,5},{8,10},{9,11},{10,... | collective-permute-start | bytes 1572872 | tf_op jit(solution)/shard_map/ppermute | solution.py:40
  66.1 2.0 %collective-permute-start.2 = (bf16[128,2048]{1,0:T(8,128)(2,1)S(1)}, bf16[128,2048]{1,0:T(8,128)(2,1)S(1)}, u32[]{:S(2)}, u32[]{:S(2)}) collective-permute-start(bf16[128,2048]{1,0:T(8,128)(2,1)S(1)} %add_convert_fusion), channel_id=1, source_target_pairs={{0,1},{1,0},{2,3},{3,2},{4,5},{5,4},{6,7},{7,6},{8,9},{9,8},{10,11... | collective-permute-start | bytes 1572872 | tf_op jit(solution)/shard_map/ppermute | solution.py:40

commit v3 on v2

v3 whole, which is shorter than its diff:
```python
import numpy as np
import jax
import jax.numpy as jnp
from jax import lax
from jax.sharding import PartitionSpec as P

F32 = jnp.float32
BF16 = jnp.bfloat16


def split_bf16(mat):
    hi = mat.astype(jnp.bfloat16)
    lo = (mat - hi.astype(np.float64)).astype(jnp.bfloat16)
    return hi, lo


def dft_mats(length):
    half = length // 2
    n = np.arange(length)
    f = np.arange(half)
    ang = 2.0 * np.pi * ((f[:, None] * n[None, :]) % length) / length
    fwd = np.zeros((length, length))
    fwd[:half] = np.cos(ang)
    fwd[half] = np.where(n % 2 == 0, 1.0, -1.0)
    fwd[half + 1:] = -np.sin(ang[1:])
    return split_bf16(fwd)


def mm(a, b):
    return jnp.dot(a, b, preferred_element_type=F32)


def swap(x, bit):
    return lax.ppermute(x, "chan", [(c, c ^ bit) for c in range(4)])


def chan_sum(partial_out):
    core = lax.axis_index("chan") % 2
    width = partial_out.shape[1] // 2
    mine = lax.dynamic_slice_in_dim(partial_out, core * width, width, 1)
    other = lax.dynamic_slice_in_dim(partial_out, (1 - core) * width, width, 1)
    chip = mine + swap(other.astype(BF16), 1).astype(F32)
    total = (chip + swap(chip.astype(BF16), 2).astype(F32)).astype(BF16)
    peer = swap(total, 1)
    return jnp.where(core == 0, jnp.concatenate([total, peer], 1), jnp.concatenate([peer, total], 1))


def make_local(nseq, nchan):
    def local(value, first_gate, second_gate, first_filter, second_filter, out_weight, segment_ids):
        rows, chans = value.shape
        filt_local, length = first_filter.shape
        group = chans // filt_local
        per = chans // nseq
        fpd = per // group
        half = length // 2
        f_hi, f_lo = dft_mats(length)
        f_blocks = np.stack(
            [np.concatenate([f_hi[:, b * rows:(b + 1) * rows], f_lo[:, b * rows:(b + 1) * rows]], axis=1)
             for b in range(nseq)]
        )
        f_blocks = jnp.asarray(f_blocks)
        me = lax.axis_index("seq")
        srcs = [(me - k) % nseq for k in range(nseq)]

        def shift(x, k):
            return lax.ppermute(x, "seq", [(i, (i + k) % nseq) for i in range(nseq)])

        def scatter_cols(x):
            out = [lax.dynamic_index_in_dim(x, me, 0, keepdims=False)]
            for k in range(1, nseq):
                out.append(shift(lax.dynamic_index_in_dim(x, (me + k) % nseq, 0, keepdims=False), k))
            return out

        def spectrum(filt):
            mine = lax.dynamic_slice_in_dim(filt, me * fpd, fpd, 0)
            taps = jnp.repeat(mine.T, group, axis=1)
            spec = None
            for b in range(nseq):
                blk = taps[b * rows:(b + 1) * rows]
                term = mm(f_blocks[b], jnp.concatenate([blk, blk], axis=0))
                spec = term if spec is None else spec + term
            re, im = spec[:half], spec[half:]
            row0 = lax.broadcasted_iota(jnp.int32, re.shape, 0) == 0
            two = lambda x: jnp.concatenate([x, x], axis=1)
            return two(re), two(jnp.where(row0, 0.0, im)), two(jnp.where(row0, im, re))

        def forward(pieces, piece_segs):
            x = None
            for k in range(nseq):
                z, sg = pieces[k], piece_segs[k][:, None]
                zero = jnp.zeros_like(z)
                masked = jnp.concatenate([jnp.where(sg == 0, z, zero), jnp.where(sg == 1, z, zero)], axis=1)
                term = mm(lax.dynamic_index_in_dim(f_blocks, srcs[k], 0, keepdims=False),
                          jnp.concatenate([masked, masked], axis=0))
                x = term if x is None else x + term
            return x

        weight = np.full((length, 1), 2.0 / length, np.float32)
        weight[0] = weight[half] = 1.0 / length
        weight = jnp.asarray(weight)

        def multiply(spec, x):
            a, b, d = spec
            xr, xi = x[:half], x[half:]
            y = jnp.concatenate([xr * a - xi * b, xr * b + xi * d], axis=0) * weight
            y_hi32 = lax.reduce_precision(y, exponent_bits=8, mantissa_bits=7)
            return y_hi32.astype(BF16), (y - y_hi32).astype(BF16)

        def mm_t(a, b):
            return lax.dot_general(a, b, (((0,), (0,)), ((), ())), preferred_element_type=F32)

        def inverse_block(y, dest):
            y_hi, y_lo = y
            blk = lax.dynamic_index_in_dim(f_blocks, dest, 0, keepdims=False)
            inv_hi, inv_lo = blk[:, :rows], blk[:, rows:]
            both = mm_t(inv_hi, y_hi) + mm_t(inv_hi, y_lo) + mm_t(inv_lo, y_hi)
            m0 = lax.dynamic_slice_in_dim(in0, dest * rows, rows, 0)
            m1 = lax.dynamic_slice_in_dim(in1, dest * rows, rows, 0)
            return jnp.where(m0, both[:, :per], 0.0) + jnp.where(m1, both[:, per:], 0.0)

        first_input = (first_gate.astype(F32) * value.astype(F32)).astype(BF16)
        first_input = first_input.reshape(rows, nseq, per).transpose(1, 0, 2)
        id_rows = -(-rows // per)
        pad_rows = -(-id_rows // 16) * 16
        ids = jnp.pad(segment_ids.astype(BF16), (0, pad_rows * per - rows)).reshape(1, pad_rows, per)
        payload = jnp.concatenate([first_input, jnp.broadcast_to(ids, (nseq, pad_rows, per))], axis=1)
        got = scatter_cols(payload)
        pieces1 = [g[:rows] for g in got]
        piece_segs = [g[rows:].reshape(pad_rows * per)[:rows] for g in got]
        gate_pieces = scatter_cols(second_gate.reshape(rows, nseq, per).transpose(1, 0, 2))

        by_shift = jnp.stack(piece_segs[::-1])
        segs = jnp.roll(by_shift, me + 1, axis=0).reshape(nseq * rows)
        in0 = (segs == 0)[:, None]
        in1 = (segs == 1)[:, None]

        spec1 = spectrum(first_filter)
        spec2 = spectrum(second_filter)
        y1 = multiply(spec1, forward(pieces1, piece_segs))
        first_mix = jnp.concatenate([inverse_block(y1, b) for b in range(nseq)], axis=0)

        pieces2 = []
        for k in range(nseq):
            fm = lax.dynamic_slice_in_dim(first_mix, srcs[k] * rows, rows, 0)
            pieces2.append((gate_pieces[k].astype(F32) * fm).astype(BF16))
        y2 = multiply(spec2, forward(pieces2, piece_segs))

        def out_block(dest):
            return inverse_block(y2, dest).astype(BF16)

        mix_pieces = [out_block(me)]
        for k in range(1, nseq):
            mix_pieces.append(shift(out_block((me + k) % nseq), k))

        def project(cols_lo, width):
            acc = None
            for k in range(nseq):
                w = lax.dynamic_slice(out_weight, (srcs[k] * per, cols_lo), (per, width))
                term = mm(mix_pieces[k], w)
                acc = term if acc is None else acc + term
            return acc

        if nchan != 4:
            return lax.psum(project(0, out_weight.shape[1]), "chan").astype(BF16)
        core = lax.axis_index("chan") % 2
        width = out_weight.shape[1] // 2
        other = project((1 - core) * width, width)
        got_other = swap(other.astype(BF16), 1)
        chip = project(core * width, width) + got_other.astype(F32)
        total = (chip + swap(chip.astype(BF16), 2).astype(F32)).astype(BF16)
        peer = swap(total, 1)
        return jnp.where(core == 0, jnp.concatenate([total, peer], 1), jnp.concatenate([peer, total], 1))

    return local


def solution(mesh):
    in_specs = (
        P(("groups", "seq"), "chan"),
        P(("groups", "seq"), "chan"),
        P(("groups", "seq"), "chan"),
        P("chan", None),
        P("chan", None),
        P("chan", None),
        P(("groups", "seq")),
    )
    out_specs = P(("groups", "seq"), None)
    local = make_local(mesh.shape["seq"], mesh.shape["chan"])
    return jax.shard_map(local, mesh=mesh, in_specs=in_specs, out_specs=out_specs, check_vma=False)
```

time: 69.9 us -> 99.8 us (1.43)
  matrix products: 10.8 us -> 33.8 us
  waiting for transfers between devices: 30.8 us -> 18.3 us
  other arithmetic: 4.85 us -> 13.3 us
  local copies, waits for them, and re-layouts: 7.42 us -> 15.5 us
  starting transfers between devices: 15 us -> 16.9 us
    ppermute x0 -> x9, starting transfers between devices: none -> 15.2 us  [shift(): return lax.ppermute(x, 'seq', [(i, (i + k) % nseq) for i in range(nseq)])]
    all_to_all x3 -> x0, waiting for transfers between devices: 14.5 us -> none  [the longest x1 6.72 us: local(): mix_rows = lax.all_to_all(second_mix, 'seq', 0, 1, tiled=True)]
    dot_general x0 -> x24, matrix products: none -> 13.8 us  [mm_t(): lax.dot_general(a, b, (((0,), (0,)), ((), ())), preferred_element_type=F32)]
    all_to_all x3 -> x0, starting transfers between devices: 13.3 us -> none  [the longest x1 6.48 us: local(): lax.all_to_all(payload.reshape(rows + pad_rows, nseq * per), 'seq', 1, 0,...]
    dot_general x15 -> x32, matrix products: 10.8 us -> 19.9 us  [mm(): return jnp.dot(a, b, preferred_element_type=F32)]
    select_n x5 -> x11, other arithmetic: 2.46 us -> 9.06 us  [the longest x5 4.01 us: forward(): jnp.where(sg == 0, z, zero)]
    another operation x0 -> x8, local copies, waits for them, and re-layouts: none -> 5.04 us
    ppermute x0 -> x9, waiting for transfers between devices: none -> 2.61 us  [shift(): return lax.ppermute(x, 'seq', [(i, (i + k) % nseq) for i in range(nseq)])]
  transfers between devices with their start and end apart: 6 -> 12, of which waited for: 6 -> 4; matrix products, arithmetic and copies ran while one was open for 10% -> 50% of each run, Pallas kernels for 0% -> 0%
where the time goes in v3:
time: 99.8 us; the launch traced here: 98.9 us
  matrix products  33.8 us (34%)
  waiting for transfers between devices  18.3 us (18%)
  starting transfers between devices  16.9 us (17%)
  local copies, waits for them, and re-layouts  15.5 us (16%)
  other arithmetic  13.3 us (13%)
  between operations  1.11 us (1%)
    dot_general x32, matrix products, mm(): return jnp.dot(a, b, preferred_element_type=F32)  19.9 us
    ppermute x3, waiting for transfers between devices, swap(): return lax.ppermute(x, 'chan', [(c, c ^ bit) for c in range(4)])  15.6 us
    ppermute x9, starting transfers between devices, shift(): return lax.ppermute(x, 'seq', [(i, (i + k) % nseq) for i in range(nseq)])  15.2 us
    dot_general x24, matrix products, mm_t(): lax.dot_general(a, b, (((0,), (0,)), ((), ())), preferred_element_type=F32)  13.8 us
    unnamed x68, local copies, waits for them, and re-layouts  7.88 us
    select_n x5, other arithmetic, forward(): jnp.where(sg == 0, z, zero)  4.01 us
    another operation x6, local copies, waits for them, and re-layouts  3.92 us
    select_n x4, other arithmetic, forward(): jnp.where(sg == 1, z, zero)  2.88 us
  transfers between devices with their start and end apart: 12, of which 4 were waited for; matrix products, arithmetic and copies ran while one was open for 50% of the time, Pallas kernels for 0%

profile of v3, /device:TPU:0, one launch (start us, length us, event | category | flops | bytes accessed | tf_op | source)
XLA Modules:
  0.0 98.9 jit_solution(4741808315067612121)
XLA Ops:
  0.0 1.2 %copy.34 = bf16[128,1024]{0,1:T(8,128)(2,1)S(1)} copy(bf16[128,1024]{1,0:T(8,128)(2,1)} %param.10) | data formatting | bytes 524288 | tf_op args[1]
  1.2 1.2 %copy.35 = bf16[128,1024]{0,1:T(8,128)(2,1)S(1)} copy(bf16[128,1024]{1,0:T(8,128)(2,1)} %param.9) | data formatting | bytes 524288 | tf_op args[0]
  2.6 0.7 convert_element_type.83
  3.3 0.7 fusion.147
  4.0 5.1 %collective-permute-start = (bf16[144,256]{1,0:T(8,128)(2,1)}, bf16[144,256]{1,0:T(8,128)(2,1)}, u32[]{:S(2)}, u32[]{:S(2)}) collective-permute-start(bf16[144,256]{1,0:T(8,128)(2,1)} %get-tuple-element.37), channel_id=1, source_target_pairs={{0,12},{4,0},{8,4},{12,8},{1,13},{5,1},{9,5},{13,9},{2,14},{6,2},{... | collective-permute-start | bytes 221192 | tf_op jit(solution)/shard_map/ppermute | solution.py:66
  9.1 1.0 %collective-permute-start.2 = (bf16[144,256]{1,0:T(8,128)(2,1)}, bf16[144,256]{1,0:T(8,128)(2,1)}, u32[]{:S(2)}, u32[]{:S(2)}) collective-permute-start(bf16[144,256]{1,0:T(8,128)(2,1)} %get-tuple-element.39), channel_id=1, source_target_pairs={{0,4},{4,8},{8,12},{12,0},{1,5},{5,9},{9,13},{13,1},{2,6},{6,10},{... | collective-permute-start | bytes 221192 | tf_op jit(solution)/shard_map/ppermute | solution.py:66
  10.1 1.1 %copy.37 = bf16[128,1024]{0,1:T(8,128)(2,1)S(1)} copy(bf16[128,1024]{1,0:T(8,128)(2,1)} %param.11) | data formatting | bytes 524288 | tf_op args[2]
  11.2 0.7 constant_dynamic-slice_fusion
  11.9 0.7 copy.47
  12.7 2.5 %collective-permute-start.3 = (bf16[128,256]{1,0:T(8,128)(2,1)}, bf16[128,256]{1,0:T(8,128)(2,1)}, u32[]{:S(2)}, u32[]{:S(2)}) collective-permute-start(bf16[128,256]{1,0:T(8,128)(2,1)} %bitcast.36), channel_id=1, source_target_pairs={{0,4},{4,8},{8,12},{12,0},{1,5},{5,9},{9,13},{13,1},{2,6},{6,10},{... | collective-permute-start | bytes 196616 | tf_op jit(solution)/shard_map/ppermute | solution.py:66
  15.1 0.8 copy.48
  15.9 0.9 collective-permute-start.4
  16.8 0.8 dynamic-slice_bitcast_fusion.4
  17.6 1.1 %fusion.182 = f32[256,512]{0,1:T(8,128)S(1)} fusion(bf16[128,256]{0,1:T(8,128)(2,1)S(1)} %bitcast.197, bf16[512,128]{1,0:T(8,128)(2,1)} %constant.197), kind=kOutput, calls=%fused_computation.316 | convolution fusion | flops 33554432 | bytes 720896 | tf_op jit(solution)/shard_map/dot_general | solution.py:30
  18.8 1.1 %fusion.174 = f32[256,512]{0,1:T(8,128)S(1)} fusion(bf16[128,256]{0,1:T(8,128)(2,1)S(1)} %bitcast.199, bf16[512,128]{1,0:T(8,128)(2,1)} %constant.197), kind=kOutput, calls=%fused_computation.308 | convolution fusion | flops 33554432 | bytes 720896 | tf_op jit(solution)/shard_map/dot_general | solution.py:30
  19.9 1.1 %convolution_add_fusion.11 = f32[256,512]{0,1:T(8,128)S(1)} fusion(f32[256,512]{0,1:T(8,128)S(1)} %fusion.182, bf16[128,256]{0,1:T(8,128)(2,1)S(1)} %bitcast.198, bf16[512,128]{1,0:T(8,128)(2,1)} %constant.198), kind=kOutput, calls=%fused_computation.19 | convolution fusion | flops 33685504 | bytes 1245184 | tf_op jit(solution)/shard_map/dot_general | solution.py:30
  21.1 1.1 %convolution_add_fusion.15 = f32[256,512]{0,1:T(8,128)S(1)} fusion(f32[256,512]{0,1:T(8,128)S(1)} %fusion.174, bf16[128,256]{0,1:T(8,128)(2,1)S(1)} %bitcast.200, bf16[512,128]{1,0:T(8,128)(2,1)} %constant.198), kind=kOutput, calls=%fused_computation.23 | convolution fusion | flops 33685504 | bytes 1245184 | tf_op jit(solution)/shard_map/dot_general | solution.py:30
  22.7 1.2 %convolution_add_fusion.12 = f32[256,512]{0,1:T(8,128)S(1)} fusion(f32[256,512]{0,1:T(8,128)S(1)} %fusion.181, bf16[128,256]{0,1:T(8,128)(2,1)S(1)} %bitcast.202, bf16[512,128]{1,0:T(8,128)(2,1)} %constant.196), kind=kOutput, calls=%fused_computation.20 | convolution fusion | flops 33685504 | bytes 1245184 | tf_op jit(solution)/shard_map/dot_general | solution.py:30
  24.0 1.1 %convolution_add_fusion.16 = f32[256,512]{0,1:T(8,128)S(1)} fusion(f32[256,512]{0,1:T(8,128)S(1)} %fusion.173, bf16[128,256]{0,1:T(8,128)(2,1)S(1)} %bitcast.204, bf16[512,128]{1,0:T(8,128)(2,1)} %constant.196), kind=kOutput, calls=%fused_computation.24 | convolution fusion | flops 33685504 | bytes 1245184 | tf_op jit(solution)/shard_map/dot_general | solution.py:30
  25.6 1.0 %convolution_add_fusion.10 = f32[256,512]{0,1:T(8,128)} fusion(f32[256,512]{0,1:T(8,128)S(1)} %fusion.183, bf16[128,256]{0,1:T(8,128)(2,1)S(1)} %bitcast.206, bf16[512,128]{1,0:T(8,128)(2,1)S(1)} %copy-done.6), kind=kOutput, calls=%fused_computation.18 | convolution fusion | flops 33685504 | bytes 1245184 | tf_op jit(solution)/shard_map/dot_general | solution.py:30
  26.6 1.0 %convolution_add_fusion.14 = f32[256,512]{0,1:T(8,128)} fusion(f32[256,512]{0,1:T(8,128)S(1)} %fusion.175, bf16[128,256]{0,1:T(8,128)(2,1)S(1)} %bitcast.208, bf16[512,128]{1,0:T(8,128)(2,1)S(1)} %copy-done.6), kind=kOutput, calls=%fused_computation.22 | convolution fusion | flops 33685504 | bytes 1245184 | tf_op jit(solution)/shard_map/dot_general | solution.py:30
  27.7 1.0 %fusion.180 = f32[256,512]{0,1:T(8,128)} fusion(bf16[128,256]{0,1:T(8,128)(2,1)S(1)} %bitcast.195, bf16[512,128]{1,0:T(8,128)(2,1)S(1)} %copy-done.4), kind=kOutput, calls=%fused_computation.314 | convolution fusion | flops 33554432 | bytes 720896 | tf_op jit(solution)/shard_map/dot_general | solution.py:30
  28.7 0.6 copy-done.12
  29.4 1.0 %fusion.172 = f32[256,512]{0,1:T(8,128)} fusion(bf16[128,256]{0,1:T(8,128)(2,1)S(1)} %bitcast.193, bf16[512,128]{1,0:T(8,128)(2,1)S(1)} %copy-done.4), kind=kOutput, calls=%fused_computation.306 | convolution fusion | flops 33554432 | bytes 720896 | tf_op jit(solution)/shard_map/dot_general | solution.py:30
  30.4 1.6 %copy.49 = bf16[128,1,256]{2,0,1:T(8,128)(2,1)} copy(bf16[128,1,256]{0,2,1:T(8,128)(2,1)} %get-tuple-element.41) | data formatting | bytes 131072 | tf_op jit(solution)/shard_map/dynamic-slice.4
  32.0 1.6 %copy.74 = bf16[128,1,256]{2,0,1:T(8,128)(2,1)} copy(bf16[128,1,256]{0,2,1:T(8,128)(2,1)} %get-tuple-element.44) | data formatting | bytes 131072
  33.5 1.6 %fusion.11 = f32[512,256]{1,0:T(8,128)S(1)} fusion(f32[256,512]{0,1:T(8,128)} %convolution_add_fusion.10, f32[256,512]{0,1:T(8,128)S(1)} %convolution_add_fusion.11, f32[256,512]{0,1:T(8,128)S(1)} %convolution_add_fusion.12, f32[256,512]{0,1:T(8,128)} %fusion.180, bf16[128,256]{0,1:T(8,128)(2,1)} %bitcast.196, bf16[512,128]{1,0:T(8,128)(2,1)} %constant.194), kind=kOutput, calls=%fused_computation.33 | convolution fusion | flops 34078720 | bytes 2818048 | tf_op jit(solution)/shard_map/dot_general | solution.py:30
  35.1 1.6 %fusion.7 = f32[512,256]{1,0:T(8,128)S(1)} fusion(f32[256,512]{0,1:T(8,128)} %convolution_add_fusion.14, f32[256,512]{0,1:T(8,128)S(1)} %convolution_add_fusion.15, f32[256,512]{0,1:T(8,128)S(1)} %convolution_add_fusion.16, f32[256,512]{0,1:T(8,128)} %fusion.172, bf16[128,256]{0,1:T(8,128)(2,1)} %bitcast.194, bf16[512,128]{1,0:T(8,128)(2,1)} %constant.194), kind=kOutput, calls=%fused_computation.29 | convolution fusion | flops 34078720 | bytes 2818048 | tf_op jit(solution)/shard_map/dot_general | solution.py:30
  36.7 1.0 slice_select_fusion.2
  37.6 0.8 dynamic-slice_bitcast_fusion.1
  38.4 1.5 %collective-permute-start.5 = (bf16[128,256]{1,0:T(8,128)(2,1)}, bf16[128,256]{1,0:T(8,128)(2,1)}, u32[]{:S(2)}, u32[]{:S(2)}) collective-permute-start(bf16[128,256]{1,0:T(8,128)(2,1)} %bitcast.38), channel_id=1, source_target_pairs={{0,12},{4,0},{8,4},{12,8},{1,13},{5,1},{9,5},{13,9},{2,14},{6,2},{... | collective-permute-start | bytes 196616 | tf_op jit(solution)/shard_map/ppermute | solution.py:66
  39.9 0.7 slice_bitcast_fusion.4
  40.6 0.7 slice_bitcast_fusion.3
  41.3 0.7 slice_bitcast_fusion.2
  42.1 0.6 slice_bitcast_fusion.15
  42.7 0.5 slice_bitcast_fusion.13
  43.7 0.9 broadcast_select_fusion.11
  44.9 0.9 broadcast_select_fusion.7
  46.2 0.9 broadcast_select_fusion.3
  48.3 1.0 fusion.177
  49.2 1.0 %fusion.178 = f32[512,128]{0,1:T(8,128)} fusion(bf16[512,512]{1,0:T(8,128)(2,1)S(1)} %get-tuple-element.20, bf16[512,128]{1,0:T(8,128)(2,1)S(1)} %copy-done.2), kind=kOutput, calls=%fused_computation.312 | convolution fusion | flops 67108864 | bytes 917504 | tf_op jit(solution)/shard_map/dot_general | solution.py:110
  50.2 1.0 fusion.179
  51.5 1.0 fusion.15
  52.5 0.8 concatenate.114
  53.3 1.2 %convolution_add_fusion.31 = f32[512,128]{0,1:T(8,128)S(1)} fusion(f32[512,128]{0,1:T(8,128)} %fusion.177, bf16[512,512]{1,0:T(8,128)(2,1)S(1)} %get-tuple-element.19, bf16[512,128]{1,0:T(8,128)(2,1)S(1)} %copy-done.3), kind=kOutput, calls=%fused_computation.50 | convolution fusion | flops 67174400 | bytes 1179648 | tf_op jit(solution)/shard_map/dot_general | solution.py:110
  54.5 1.2 %fusion.14 = f32[128,512]{1,0:T(8,128)S(1)} fusion(f32[512,128]{0,1:T(8,128)S(1)} %convolution_add_fusion.31, bf16[512,512]{1,0:T(8,128)(2,1)S(1)} %get-tuple-element.20, bf16[512,128]{1,0:T(8,128)(2,1)} %constant.196), kind=kOutput, calls=%fused_computation.49 | convolution fusion | flops 67174400 | bytes 1179648 | tf_op jit(solution)/shard_map/dot_general | solution.py:110
  55.7 1.2 %convolution_add_fusion.29 = f32[512,128]{0,1:T(8,128)S(1)} fusion(f32[512,128]{0,1:T(8,128)} %fusion.178, bf16[512,512]{1,0:T(8,128)(2,1)S(1)} %get-tuple-element.19, bf16[512,128]{1,0:T(8,128)(2,1)S(1)} %copy-done.2), kind=kOutput, calls=%fused_computation.47 | convolution fusion | flops 67174400 | bytes 1179648 | tf_op jit(solution)/shard_map/dot_general | solution.py:110
  57.0 1.2 %fusion.13 = f32[128,512]{1,0:T(8,128)S(1)} fusion(f32[512,128]{0,1:T(8,128)S(1)} %convolution_add_fusion.29, bf16[512,512]{1,0:T(8,128)(2,1)S(1)} %get-tuple-element.20, bf16[512,128]{1,0:T(8,128)(2,1)} %constant.198), kind=kOutput, calls=%fused_computation.46 | convolution fusion | flops 67174400 | bytes 1179648 | tf_op jit(solution)/shard_map/dot_general | solution.py:110
  58.2 1.2 %convolution_add_fusion.27 = f32[512,128]{0,1:T(8,128)S(1)} fusion(f32[512,128]{0,1:T(8,128)} %fusion.179, bf16[512,512]{1,0:T(8,128)(2,1)S(1)} %get-tuple-element.19, bf16[512,128]{1,0:T(8,128)(2,1)S(1)} %copy-done.1), kind=kOutput, calls=%fused_computation.44 | convolution fusion | flops 67174400 | bytes 1179648 | tf_op jit(solution)/shard_map/dot_general | solution.py:110
  59.7 1.1 %fusion.127 = f32[128,256]{1,0:T(8,128)S(1)} fusion(f32[128,512]{1,0:T(8,128)} %fusion.15, pred[128]{0:T(512)(128)(4,1)S(1)} %get-tuple-element.86, pred[128]{0:T(512)(128)(4,1)S(1)} %get-tuple-element.82), kind=kLoop, calls=%fused_computation.208 | loop fusion | flops 98304 | bytes 393472 | tf_op jit(solution)/shard_map/add | solution.py:119
  61.2 1.1 %broadcast_select_fusion.2 = (bf16[128,256]{1,0:T(8,128)(2,1)S(1)}, bf16[128,256]{1,0:T(8,128)(2,1)S(1)}, bf16[128,256]{1,0:T(8,128)(2,1)S(1)}, bf16[128,256]{1,...) fusion(pred[128]{0:T(512)(128)(4,1)S(1)} %copy-done.18, ...), kind=kLoop, calls=%fused_computation.237 | loop fusion | flops 524288 | bytes 1311248 | tf_op jit(solution)/shard_map/jit(_where)/select_n | solution.py:92
  62.3 0.7 broadcast_select_fusion
  63.1 0.7 broadcast_select_fusion.4
  63.8 0.7 broadcast_select_fusion.8
  64.5 0.8 broadcast_select_fusion.12
  68.0 0.6 collective-permute-start.6
  70.3 2.1 %collective-permute-start.7 = (bf16[128,256]{1,0:T(8,128)(2,1)S(1)}, bf16[128,256]{1,0:T(8,128)(2,1)S(1)}, u32[]{:S(2)}, u32[]{:S(2)}) collective-permute-start(bf16[128,256]{1,0:T(8,128)(2,1)S(1)} %fusion.116), channel_id=1, source_target_pairs={{0,8},{4,12},{8,0},{12,4},{1,9},{5,13},{9,1},{13,5},{2,10},{6,14},... | collective-permute-start | bytes 196616 | tf_op jit(solution)/shard_map/ppermute | solution.py:66
  74.1 1.6 %collective-permute-start.8 = (bf16[128,256]{1,0:T(8,128)(2,1)S(1)}, bf16[128,256]{1,0:T(8,128)(2,1)S(1)}, u32[]{:S(2)}, u32[]{:S(2)}) collective-permute-start(bf16[128,256]{1,0:T(8,128)(2,1)S(1)} %fusion.113), channel_id=1, source_target_pairs={{0,12},{4,0},{8,4},{12,8},{1,13},{5,1},{9,5},{13,9},{2,14},{6,2},{... | collective-permute-start | bytes 196616 | tf_op jit(solution)/shard_map/ppermute | solution.py:66
  76.0 2.6 %collective-permute-done.8 = bf16[128,256]{1,0:T(8,128)(2,1)S(1)} collective-permute-done((bf16[128,256]{1,0:T(8,128)(2,1)S(1)}, bf16[128,256]{1,0:T(8,128)(2,1)S(1)}, u32[]{:S(2)}, u32[]{:S(2)}) %collective-permute-start.8) | collective-permute-done | bytes 65568 | tf_op jit(solution)/shard_map/ppermute | solution.py:66
  80.0 1.2 %collective-permute-done.9 = bf16[128,2048]{1,0:T(8,128)(2,1)S(1)} collective-permute-done((bf16[128,2048]{1,0:T(8,128)(2,1)S(1)}, bf16[128,2048]{1,0:T(8,128)(2,1)S(1)}, u32[]{:S(2)}, u32[]{:S(2)}) %collective-permute-start.9) | collective-permute-done | bytes 524320 | tf_op jit(solution)/shard_map/ppermute | solution.py:34
  81.6 1.5 %collective-permute-start.10 = (bf16[128,2048]{1,0:T(8,128)(2,1)S(1)}, bf16[128,2048]{1,0:T(8,128)(2,1)S(1)}, u32[]{:S(2)}, u32[]{:S(2)}) collective-permute-start(bf16[128,2048]{1,0:T(8,128)(2,1)S(1)} %get-tuple-element.90), channel_id=1, source_target_pairs={{0,2},{1,3},{2,0},{3,1},{4,6},{5,7},{6,4},{7,5},{8,10},{9,11},{10,... | collective-permute-start | bytes 1572872 | tf_op jit(solution)/shard_map/ppermute | solution.py:34
  83.1 12.5 %collective-permute-done.10 = bf16[128,2048]{1,0:T(8,128)(2,1)S(1)} collective-permute-done((bf16[128,2048]{1,0:T(8,128)(2,1)S(1)}, bf16[128,2048]{1,0:T(8,128)(2,1)S(1)}, u32[]{:S(2)}, u32[]{:S(2)}) %collective-permute-start.10) | collective-permute-done | bytes 524320 | tf_op jit(solution)/shard_map/ppermute | solution.py:34
  95.8 1.9 %collective-permute-done.11 = bf16[128,2048]{1,0:T(8,128)(2,1)S(1)} collective-permute-done((bf16[128,2048]{1,0:T(8,128)(2,1)S(1)}, bf16[128,2048]{1,0:T(8,128)(2,1)S(1)}, u32[]{:S(2)}, u32[]{:S(2)}) %collective-permute-start.11) | collective-permute-done | bytes 524320 | tf_op jit(solution)/shard_map/ppermute | solution.py:34
  97.7 1.2 %maximum_select_fusion = bf16[128,4096]{1,0:T(8,128)(2,1)} fusion(bf16[128,2048]{1,0:T(8,128)(2,1)S(1)} %collective-permute-done.11, bf16[128,2048]{1,0:T(8,128)(2,1)S(1)} %add_convert_fusion, pred[]{:T(512)S(6)} %eq.90), kind=kLoop, calls=%fused_computation.58 | loop fusion | flops 4718592 | bytes 2097153 | tf_op jit(solution)/shard_map/jit(_where)/select_n | solution.py:172
  (144 shorter events, 12.4 us)
Async XLA Ops:
  0.0 22.2 %copy-start.3 = (bf16[512,128]{1,0:T(8,128)(2,1)S(1)}, bf16[512,128]{1,0:T(8,128)(2,1)}, u32[]{:S(2)}) copy-start(bf16[512,128]{1,0:T(8,128)(2,1)} %constant.195) | copy-start | bytes 393220
  0.0 25.1 %copy-start.1 = (bf16[512,128]{1,0:T(8,128)(2,1)S(1)}, bf16[512,128]{1,0:T(8,128)(2,1)}, u32[]{:S(2)}) copy-start(bf16[512,128]{1,0:T(8,128)(2,1)} %constant.199) | copy-start | bytes 393220
  1.2 26.5 %copy-start.4 = (bf16[512,128]{1,0:T(8,128)(2,1)S(1)}, bf16[512,128]{1,0:T(8,128)(2,1)}, u32[]{:S(2)}) copy-start(bf16[512,128]{1,0:T(8,128)(2,1)} %constant.193) | copy-start | bytes 393220
  4.0 18.5 %copy-start.14 = (bf16[1,144,256]{2,1,0:T(8,128)(2,1)}, bf16[1,144,256]{2,1,0:T(8,128)(2,1)S(1)}, u32[]{:S(2)}) copy-start(bf16[1,144,256]{2,1,0:T(8,128)(2,1)S(1)} %get-tuple-element.40) | copy-start | bytes 221188
  4.0 34.4 %collective-permute-start = (bf16[144,256]{1,0:T(8,128)(2,1)}, bf16[144,256]{1,0:T(8,128)(2,1)}, u32[]{:S(2)}, u32[]{:S(2)}) collective-permute-start(bf16[144,256]{1,0:T(8,128)(2,1)} %get-tuple-element.37), channel_id=1, source_target_pairs={{0,12},{4,0},{8,4},{12,8},{1,13},{5,1},{9,5},{13,9},{2,14},{6,2},{... | collective-permute-start | bytes 221192 | tf_op jit(solution)/shard_map/ppermute | solution.py:66
  9.1 31.5 %collective-permute-start.1 = (bf16[144,256]{1,0:T(8,128)(2,1)}, bf16[144,256]{1,0:T(8,128)(2,1)}, u32[]{:S(2)}, u32[]{:S(2)}) collective-permute-start(bf16[144,256]{1,0:T(8,128)(2,1)} %get-tuple-element.38), channel_id=1, source_target_pairs={{0,8},{4,12},{8,0},{12,4},{1,9},{5,13},{9,1},{13,5},{2,10},{6,14},... | collective-permute-start | bytes 221192 | tf_op jit(solution)/shard_map/ppermute | solution.py:66
  9.1 32.2 %collective-permute-start.2 = (bf16[144,256]{1,0:T(8,128)(2,1)}, bf16[144,256]{1,0:T(8,128)(2,1)}, u32[]{:S(2)}, u32[]{:S(2)}) collective-permute-start(bf16[144,256]{1,0:T(8,128)(2,1)} %get-tuple-element.39), channel_id=1, source_target_pairs={{0,4},{4,8},{8,12},{12,0},{1,5},{5,9},{9,13},{13,1},{2,6},{6,10},{... | collective-permute-start | bytes 221192 | tf_op jit(solution)/shard_map/ppermute | solution.py:66
  12.7 48.5 %collective-permute-start.3 = (bf16[128,256]{1,0:T(8,128)(2,1)}, bf16[128,256]{1,0:T(8,128)(2,1)}, u32[]{:S(2)}, u32[]{:S(2)}) collective-permute-start(bf16[128,256]{1,0:T(8,128)(2,1)} %bitcast.36), channel_id=1, source_target_pairs={{0,4},{4,8},{8,12},{12,0},{1,5},{5,9},{9,13},{13,1},{2,6},{6,10},{... | collective-permute-start | bytes 196616 | tf_op jit(solution)/shard_map/ppermute | solution.py:66
  15.9 45.3 %collective-permute-start.4 = (bf16[128,256]{1,0:T(8,128)(2,1)}, bf16[128,256]{1,0:T(8,128)(2,1)}, u32[]{:S(2)}, u32[]{:S(2)}) collective-permute-start(bf16[128,256]{1,0:T(8,128)(2,1)} %bitcast.37), channel_id=1, source_target_pairs={{0,8},{4,12},{8,0},{12,4},{1,9},{5,13},{9,1},{13,5},{2,10},{6,14},... | collective-permute-start | bytes 196616 | tf_op jit(solution)/shard_map/ppermute | solution.py:66
  16.8 8.8 %copy-start.6 = (bf16[512,128]{1,0:T(8,128)(2,1)S(1)}, bf16[512,128]{1,0:T(8,128)(2,1)}, u32[]{:S(2)}) copy-start(bf16[512,128]{1,0:T(8,128)(2,1)} %constant.200) | copy-start | bytes 393220
  22.7 14.9 %copy-start = (bf16[4,512,256]{2,1,0:T(8,128)(2,1)S(1)}, bf16[4,512,256]{2,1,0:T(8,128)(2,1)}, u32[]{:S(2)}) copy-start(bf16[4,512,256]{2,1,0:T(8,128)(2,1)} %constant.180.clone) | copy-start | bytes 3145732
  27.7 1.0 %copy-start.13 = (bf16[128,16,16]{0,2,1:T(8,128)(2,1)}, bf16[128,16,16]{0,2,1:T(8,128)(2,1)S(1)}, u32[]{:S(2)}) copy-start(bf16[128,16,16]{0,2,1:T(8,128)(2,1)S(1)} %broadcast_in_dim.234) | copy-start | bytes 196612
  28.7 0.6 copy-start.12
  33.5 9.7 %copy-start.15 = (bf16[1,144,256]{2,1,0:T(8,128)(2,1)S(1)}, bf16[1,144,256]{2,1,0:T(8,128)(2,1)}, u32[]{:S(2)}) copy-start(bf16[1,144,256]{2,1,0:T(8,128)(2,1)} %copy-done.14) | copy-start | bytes 221188
  36.7 11.1 %copy-start.16 = (f32[512]{0:T(512)S(1)}, f32[512]{0:T(512)}, u32[]{:S(2)}) copy-start(f32[512]{0:T(512)} %constant.192) | copy-start | bytes 6148
  38.4 10.8 %copy-start.2 = (bf16[512,128]{1,0:T(8,128)(2,1)S(1)}, bf16[512,128]{1,0:T(8,128)(2,1)}, u32[]{:S(2)}) copy-start(bf16[512,128]{1,0:T(8,128)(2,1)} %constant.197) | copy-start | bytes 393220
  38.4 22.8 %collective-permute-start.5 = (bf16[128,256]{1,0:T(8,128)(2,1)}, bf16[128,256]{1,0:T(8,128)(2,1)}, u32[]{:S(2)}, u32[]{:S(2)}) collective-permute-start(bf16[128,256]{1,0:T(8,128)(2,1)} %bitcast.38), channel_id=1, source_target_pairs={{0,12},{4,0},{8,4},{12,8},{1,13},{5,1},{9,5},{13,9},{2,14},{6,2},{... | collective-permute-start | bytes 196616 | tf_op jit(solution)/shard_map/ppermute | solution.py:66
  42.0 5.4 %copy-start.17 = (pred[128]{0:T(512)(128)(4,1)}, pred[128]{0:T(512)(128)(4,1)S(1)}, u32[]{:S(2)}) copy-start(pred[128]{0:T(512)(128)(4,1)S(1)} %get-tuple-element.99) | copy-start | bytes 388
  42.0 5.4 %copy-start.22 = (pred[128]{0:T(512)(128)(4,1)}, pred[128]{0:T(512)(128)(4,1)S(1)}, u32[]{:S(2)}) copy-start(pred[128]{0:T(512)(128)(4,1)S(1)} %get-tuple-element.67) | copy-start | bytes 388
  42.1 5.4 %copy-start.23 = (pred[128]{0:T(512)(128)(4,1)}, pred[128]{0:T(512)(128)(4,1)S(1)}, u32[]{:S(2)}) copy-start(pred[128]{0:T(512)(128)(4,1)S(1)} %get-tuple-element.98) | copy-start | bytes 388
  42.7 4.8 %copy-start.19 = (pred[128]{0:T(512)(128)(4,1)}, pred[128]{0:T(512)(128)(4,1)S(1)}, u32[]{:S(2)}) copy-start(pred[128]{0:T(512)(128)(4,1)S(1)} %get-tuple-element.63) | copy-start | bytes 388
  42.7 4.8 %copy-start.21 = (pred[128]{0:T(512)(128)(4,1)}, pred[128]{0:T(512)(128)(4,1)S(1)}, u32[]{:S(2)}) copy-start(pred[128]{0:T(512)(128)(4,1)S(1)} %get-tuple-element.101) | copy-start | bytes 388
  42.7 4.8 %copy-start.24 = (pred[128]{0:T(512)(128)(4,1)}, pred[128]{0:T(512)(128)(4,1)S(1)}, u32[]{:S(2)}) copy-start(pred[128]{0:T(512)(128)(4,1)S(1)} %get-tuple-element.100) | copy-start | bytes 388
  42.7 4.8 %copy-start.25 = (pred[128]{0:T(512)(128)(4,1)}, pred[128]{0:T(512)(128)(4,1)S(1)}, u32[]{:S(2)}) copy-start(pred[128]{0:T(512)(128)(4,1)S(1)} %get-tuple-element.64) | copy-start | bytes 388
  44.6 6.9 %copy-start.8 = (bf16[512,128]{1,0:T(8,128)(2,1)S(1)}, bf16[512,128]{1,0:T(8,128)(2,1)}, u32[]{:S(2)}) copy-start(bf16[512,128]{1,0:T(8,128)(2,1)} %constant.194) | copy-start | bytes 393220
  47.5 11.9 %copy-start.7 = (bf16[512,128]{1,0:T(8,128)(2,1)S(1)}, bf16[512,128]{1,0:T(8,128)(2,1)}, u32[]{:S(2)}) copy-start(bf16[512,128]{1,0:T(8,128)(2,1)} %constant.200) | copy-start | bytes 393220
  48.0 13.2 %copy-start.18 = (pred[128]{0:T(512)(128)(4,1)S(1)}, pred[128]{0:T(512)(128)(4,1)}, u32[]{:S(2)}) copy-start(pred[128]{0:T(512)(128)(4,1)} %copy-done.17) | copy-start | bytes 388
  48.0 13.2 %copy-start.20 = (pred[128]{0:T(512)(128)(4,1)S(1)}, pred[128]{0:T(512)(128)(4,1)}, u32[]{:S(2)}) copy-start(pred[128]{0:T(512)(128)(4,1)} %copy-done.19) | copy-start | bytes 388
  56.9 9.5 %copy-start.9 = (f32[256,256]{1,0:T(8,128)S(1)}, f32[256,256]{1,0:T(8,128)}, u32[]{:S(2)}) copy-start(f32[256,256]{1,0:T(8,128)} %get-tuple-element.71) | copy-start | bytes 786436
  56.9 9.5 %copy-start.10 = (f32[256,256]{1,0:T(8,128)S(1)}, f32[256,256]{1,0:T(8,128)}, u32[]{:S(2)}) copy-start(f32[256,256]{1,0:T(8,128)} %get-tuple-element.72) | copy-start | bytes 786436
  56.9 9.5 %copy-start.11 = (f32[256,256]{1,0:T(8,128)S(1)}, f32[256,256]{1,0:T(8,128)}, u32[]{:S(2)}) copy-start(f32[256,256]{1,0:T(8,128)} %get-tuple-element.73) | copy-start | bytes 786436
  61.1 5.8 %copy-start.5 = (bf16[512,256]{1,0:T(8,128)(2,1)S(1)}, bf16[512,256]{1,0:T(8,128)(2,1)}, u32[]{:S(2)}) copy-start(bf16[512,256]{1,0:T(8,128)(2,1)} %get-tuple-element.22) | copy-start | bytes 786436
  66.4 6.0 %slice-start = ((s8[8388608]{0:T(1024)(128)(4,1)}), s8[4194304]{0:T(1024)(128)(4,1)S(1)}, s32[]{:S(2)}) async-start(s8[8388608]{0:T(1024)(128)(4,1)} %bitcast.188), calls=%async_computation | async-start | bytes 8388608
  67.4 5.0 %slice-start.1 = ((s8[8388608]{0:T(1024)(128)(4,1)}), s8[4194304]{0:T(1024)(128)(4,1)S(1)}, s32[]{:S(2)}) async-start(s8[8388608]{0:T(1024)(128)(4,1)} %bitcast.188), calls=%async_computation.1 | async-start | bytes 8388608
  68.0 7.6 %collective-permute-start.6 = (bf16[128,256]{1,0:T(8,128)(2,1)S(1)}, bf16[128,256]{1,0:T(8,128)(2,1)S(1)}, u32[]{:S(2)}, u32[]{:S(2)}) collective-permute-start(bf16[128,256]{1,0:T(8,128)(2,1)S(1)} %fusion.119), channel_id=1, source_target_pairs={{0,4},{4,8},{8,12},{12,0},{1,5},{5,9},{9,13},{13,1},{2,6},{6,10},{... | collective-permute-start | bytes 196616 | tf_op jit(solution)/shard_map/ppermute | solution.py:66
  70.3 8.6 %collective-permute-start.7 = (bf16[128,256]{1,0:T(8,128)(2,1)S(1)}, bf16[128,256]{1,0:T(8,128)(2,1)S(1)}, u32[]{:S(2)}, u32[]{:S(2)}) collective-permute-start(bf16[128,256]{1,0:T(8,128)(2,1)S(1)} %fusion.116), channel_id=1, source_target_pairs={{0,8},{4,12},{8,0},{12,4},{1,9},{5,13},{9,1},{13,5},{2,10},{6,14},... | collective-permute-start | bytes 196616 | tf_op jit(solution)/shard_map/ppermute | solution.py:66
  74.1 4.5 %collective-permute-start.8 = (bf16[128,256]{1,0:T(8,128)(2,1)S(1)}, bf16[128,256]{1,0:T(8,128)(2,1)S(1)}, u32[]{:S(2)}, u32[]{:S(2)}) collective-permute-start(bf16[128,256]{1,0:T(8,128)(2,1)S(1)} %fusion.113), channel_id=1, source_target_pairs={{0,12},{4,0},{8,4},{12,8},{1,13},{5,1},{9,5},{13,9},{2,14},{6,2},{... | collective-permute-start | bytes 196616 | tf_op jit(solution)/shard_map/ppermute | solution.py:66
  79.2 2.0 %collective-permute-start.9 = (bf16[128,2048]{1,0:T(8,128)(2,1)S(1)}, bf16[128,2048]{1,0:T(8,128)(2,1)S(1)}, u32[]{:S(2)}, u32[]{:S(2)}) collective-permute-start(bf16[128,2048]{1,0:T(8,128)(2,1)S(1)} %fusion.3), channel_id=1, source_target_pairs={{0,1},{1,0},{2,3},{3,2},{4,5},{5,4},{6,7},{7,6},{8,9},{9,8},{10,11... | collective-permute-start | bytes 1572872 | tf_op jit(solution)/shard_map/ppermute | solution.py:34
  81.6 14.0 %collective-permute-start.10 = (bf16[128,2048]{1,0:T(8,128)(2,1)S(1)}, bf16[128,2048]{1,0:T(8,128)(2,1)S(1)}, u32[]{:S(2)}, u32[]{:S(2)}) collective-permute-start(bf16[128,2048]{1,0:T(8,128)(2,1)S(1)} %get-tuple-element.90), channel_id=1, source_target_pairs={{0,2},{1,3},{2,0},{3,1},{4,6},{5,7},{6,4},{7,5},{8,10},{9,11},{10,... | collective-permute-start | bytes 1572872 | tf_op jit(solution)/shard_map/ppermute | solution.py:34
  95.7 2.0 %collective-permute-start.11 = (bf16[128,2048]{1,0:T(8,128)(2,1)S(1)}, bf16[128,2048]{1,0:T(8,128)(2,1)S(1)}, u32[]{:S(2)}, u32[]{:S(2)}) collective-permute-start(bf16[128,2048]{1,0:T(8,128)(2,1)S(1)} %add_convert_fusion), channel_id=1, source_target_pairs={{0,1},{1,0},{2,3},{3,2},{4,5},{5,4},{6,7},{7,6},{8,9},{9,8},{10,11... | collective-permute-start | bytes 1572872 | tf_op jit(solution)/shard_map/ppermute | solution.py:34

commit v4 on v2

--- a/solution.py
+++ b/solution.py
@@ -38,17 +38,6 @@
 
 def swap(x, bit):
     return lax.ppermute(x, "chan", [(c, c ^ bit) for c in range(4)])
-
-
-def chan_sum(partial_out):
-    core = lax.axis_index("chan") % 2
-    width = partial_out.shape[1] // 2
-    mine = lax.dynamic_slice_in_dim(partial_out, core * width, width, 1)
-    other = lax.dynamic_slice_in_dim(partial_out, (1 - core) * width, width, 1)
-    chip = mine + swap(other.astype(BF16), 1).astype(F32)
-    total = (chip + swap(chip.astype(BF16), 2).astype(F32)).astype(BF16)
-    peer = swap(total, 1)
-    return jnp.where(core == 0, jnp.concatenate([total, peer], 1), jnp.concatenate([peer, total], 1))
 
 
 def make_local(nseq, nchan):
@@ -93,27 +82,40 @@
 
         rows = value.shape[0]
         first_input = (first_gate.astype(F32) * value.astype(F32)).astype(BF16)
+        first_input = first_input.reshape(rows, nseq, per).transpose(1, 0, 2)
         id_rows = -(-rows // per)
-        ids = jnp.pad(segment_ids.astype(BF16), (0, id_rows * per - rows)).reshape(id_rows, 1, per)
-        ids = jnp.broadcast_to(ids, (id_rows, nseq, per))
         pad_rows = -(-id_rows // 16) * 16
-        ids = jnp.pad(ids, ((0, pad_rows - id_rows), (0, 0), (0, 0)))
-        payload = jnp.concatenate([first_input.reshape(rows, nseq, per), ids], axis=0)
-        got = lax.all_to_all(payload.reshape(rows + pad_rows, nseq * per), "seq", 1, 0, tiled=True)
-        got = got.reshape(nseq, rows + pad_rows, per)
+        ids = jnp.pad(segment_ids.astype(BF16), (0, pad_rows * per - rows)).reshape(1, pad_rows, per)
+        payload = jnp.concatenate([first_input, jnp.broadcast_to(ids, (nseq, pad_rows, per))], axis=1)
+        got = lax.all_to_all(payload, "seq", 0, 0, tiled=True)
         first_cols = got[:, :rows].reshape(nseq * rows, per)
-        segs = got[:, rows:rows + id_rows].reshape(nseq, id_rows * per)[:, :rows].reshape(nseq * rows)
+        segs = got[:, rows:].reshape(nseq, pad_rows * per)[:, :rows].reshape(nseq * rows)
         in0 = (segs == 0)[:, None]
         in1 = (segs == 1)[:, None]
-        gate_cols = lax.all_to_all(second_gate, "seq", 1, 0, tiled=True)
+        gate_blocks = second_gate.reshape(rows, nseq, per).transpose(1, 0, 2)
+        gate_cols = lax.all_to_all(gate_blocks, "seq", 0, 0, tiled=True).reshape(nseq * rows, per)
         first_mix = long_conv(spectrum(first_filter), first_cols)
         second_input = (gate_cols.astype(F32) * first_mix).astype(BF16)
         second_mix = long_conv(spectrum(second_filter), second_input).astype(BF16)
-        mix_rows = lax.all_to_all(second_mix, "seq", 0, 1, tiled=True)
-        partial_out = mm(mix_rows, out_weight)
+        mix_blocks = lax.all_to_all(second_mix.reshape(nseq, rows, per), "seq", 0, 0, tiled=True)
+        out_cols = out_weight.shape[1]
+        w_blocks = out_weight.reshape(nseq, per, out_cols)
+
+        def project(w):
+            return lax.dot_general(mix_blocks, w, (((0, 2), (0, 1)), ((), ())), preferred_element_type=F32)
+
         if nchan != 4:
-            return lax.psum(partial_out, "chan").astype(BF16)
-        return chan_sum(partial_out)
+            return lax.psum(project(w_blocks), "chan").astype(BF16)
+        core = lax.axis_index("chan") % 2
+        width = out_cols // 2
+        w_halves = w_blocks.reshape(nseq, per, 2, width)
+        other = project(lax.dynamic_index_in_dim(w_halves, 1 - core, 2, keepdims=False))
+        got_other = swap(other.astype(BF16), 1)
+        mine = project(lax.dynamic_index_in_dim(w_halves, core, 2, keepdims=False))
+        chip = mine + got_other.astype(F32)
+        total = (chip + swap(chip.astype(BF16), 2).astype(F32)).astype(BF16)
+        peer = swap(total, 1)
+        return jnp.where(core == 0, jnp.concatenate([total, peer], 1), jnp.concatenate([peer, total], 1))
 
     return local
 

time: 69.9 us -> 108 us (1.55)
  local copies, waits for them, and re-layouts: 7.42 us -> 37.8 us
  matrix products: 10.8 us -> 22.4 us
  waiting for transfers between devices: 30.8 us -> 20.3 us
  other arithmetic: 4.85 us -> 9.49 us
  starting transfers between devices: 15 us -> 16.8 us
    dynamic_slice x0 -> x1, local copies, waits for them, and re-layouts: none -> 20.5 us  [local(): lax.dynamic_index_in_dim(w_halves, 1 - core, 2, keepdims=False)]
    another operation x0 -> x1, local copies, waits for them, and re-layouts: none -> 14.6 us  [local(): w_halves = w_blocks.reshape(nseq, per, 2, width)]
    dot_general x0 -> x2, matrix products: none -> 12.1 us  [project(): lax.dot_general(mix_blocks, w, (((0, 2), (0, 1)), ((), ())), preferred_el...]
    all_to_all x3, waiting for transfers between devices: 14.5 us -> 4.03 us  [the longest x1 4.02 us: local(): lax.all_to_all(gate_blocks, 'seq', 0, 0, tiled=True)]
    unnamed x22 -> x15, local copies, waits for them, and re-layouts: 5.37 us -> 0.9 us
    sub x2, other arithmetic: 0.46 us -> 3.08 us  [long_conv(): y = jnp.concatenate([xr * a - xi * b, xr * b + xi * d], axis=0)]
    all_to_all x3, starting transfers between devices: 13.3 us -> 15.2 us  [the longest x1 6.35 us: local(): got = lax.all_to_all(payload, 'seq', 0, 0, tiled=True)]
    dot_general x15 -> x14, matrix products: 10.8 us -> 10.3 us  [mm(): return jnp.dot(a, b, preferred_element_type=F32)]
  transfers between devices with their start and end apart: 6 -> 6, of which waited for: 6 -> 4; matrix products, arithmetic and copies ran while one was open for 10% -> 45% of each run, Pallas kernels for 0% -> 0%
where the time goes in v4:
time: 108 us; the launch traced here: 107 us
  local copies, waits for them, and re-layouts  37.8 us (35%)
  matrix products  22.4 us (21%)
  waiting for transfers between devices  20.3 us (19%)
  starting transfers between devices  16.8 us (16%)
  other arithmetic  9.49 us (9%)
    dynamic_slice x1, local copies, waits for them, and re-layouts, local(): lax.dynamic_index_in_dim(w_halves, 1 - core, 2, keepdims=False)  20.5 us
    ppermute x3, waiting for transfers between devices, swap(): return lax.ppermute(x, 'chan', [(c, c ^ bit) for c in range(4)])  16.3 us
    another operation x1, local copies, waits for them, and re-layouts, local(): w_halves = w_blocks.reshape(nseq, per, 2, width)  14.6 us
    dot_general x2, matrix products, project(): lax.dot_general(mix_blocks, w, (((0, 2), (0, 1)), ((), ())), preferred_el...  12.1 us
    dot_general x14, matrix products, mm(): return jnp.dot(a, b, preferred_element_type=F32)  10.3 us
    all_to_all x1, starting transfers between devices, local(): got = lax.all_to_all(payload, 'seq', 0, 0, tiled=True)  6.35 us
    all_to_all x1, starting transfers between devices, local(): lax.all_to_all(gate_blocks, 'seq', 0, 0, tiled=True)  5.22 us
    all_to_all x1, waiting for transfers between devices, local(): lax.all_to_all(gate_blocks, 'seq', 0, 0, tiled=True)  4.02 us
  transfers between devices with their start and end apart: 6, of which 4 were waited for; matrix products, arithmetic and copies ran while one was open for 45% of the time, Pallas kernels for 0%

profile of v4, /device:TPU:0, one launch (start us, length us, event | category | flops | bytes accessed | tf_op | source)
XLA Modules:
  0.0 107.2 jit_solution(14408337115999331326)
XLA Ops:
  0.0 1.1 %multiply_convert_fusion = bf16[128,1024]{1,0:T(8,128)(2,1)S(1)} fusion(bf16[128,1024]{1,0:T(8,128)(2,1)} %param.11, bf16[128,1024]{1,0:T(8,128)(2,1)} %param.12), kind=kLoop, calls=%fused_computation.59 | loop fusion | flops 524288 | bytes 786432 | tf_op jit(solution)/shard_map/convert_element_type | solution.py:84
  1.1 0.7 convert_element_type.56
  1.8 0.7 pad_maximum_fusion.10
  2.6 6.3 %all-to-all-start = ((bf16[4,144,256]{2,1,0:T(8,128)(2,1)}), bf16[4,144,256]{2,1,0:T(8,128)(2,1)S(1)}, u32[]{:S(2)}, u32[]{:S(2)}) async-start(bf16[4,144,256]{2,1,0:T(8,128)(2,1)} %pad_maximum_fusion.10), calls=%async_computation | async-start | bytes 589824 | tf_op jit(solution)/shard_map/all_to_all | solution.py:90
  8.9 0.7 dynamic-slice_bitcast_fusion
  9.7 1.4 %fusion.44 = f32[256,512]{0,1:T(8,128)S(1)} fusion(bf16[512,256]{0,1:T(8,128)(2,1)S(1)} %bitcast.85, bf16[512,512]{1,0:T(8,128)(2,1)} %constant.51.clone), kind=kOutput, calls=%fused_computation.93 | convolution fusion | flops 134217728 | bytes 1310720 | tf_op jit(solution)/shard_map/dot_general | solution.py:36
  11.1 1.4 %fusion.43 = f32[256,512]{0,1:T(8,128)S(1)} fusion(bf16[512,256]{0,1:T(8,128)(2,1)S(1)} %bitcast.87, bf16[512,512]{1,0:T(8,128)(2,1)} %constant.51.clone), kind=kOutput, calls=%fused_computation.92 | convolution fusion | flops 134217728 | bytes 1310720 | tf_op jit(solution)/shard_map/dot_general | solution.py:36
  12.5 1.4 %fusion.9 = f32[512,256]{1,0:T(8,128)S(1)} fusion(f32[256,512]{0,1:T(8,128)S(1)} %fusion.44, bf16[512,256]{0,1:T(8,128)(2,1)S(1)} %bitcast.86, bf16[512,512]{1,0:T(8,128)(2,1)} %constant.52.clone), kind=kOutput, calls=%fused_computation.22 | convolution fusion | flops 134348800 | bytes 1835008 | tf_op jit(solution)/shard_map/dot_general | solution.py:36
  13.8 1.4 %fusion.10 = f32[512,256]{1,0:T(8,128)S(1)} fusion(f32[256,512]{0,1:T(8,128)S(1)} %fusion.43, bf16[512,256]{0,1:T(8,128)(2,1)S(1)} %bitcast.88, bf16[512,512]{1,0:T(8,128)(2,1)} %constant.52.clone), kind=kOutput, calls=%fused_computation.24 | convolution fusion | flops 134348800 | bytes 1835008 | tf_op jit(solution)/shard_map/dot_general | solution.py:36
  15.2 0.0 copy-start.5
  15.2 0.0 copy-start.2
  15.3 0.0 copy-start.1
  15.3 14.6 %reshape_reshape.3 = bf16[4,256,2,2048]{3,2,1,0:T(2,128)(2,1)} reshape(bf16[1024,4096]{1,0:T(8,128)(2,1)} %param.16) | data formatting | bytes 16777216 | tf_op jit(solution)/shard_map/reshape;reshape | solution.py:111
  29.9 0.0 copy-done.5
  29.9 0.0 copy-start
  29.9 0.8 copy.40
  30.7 1.2 %slice_select_fusion.6 = (f32[256,256]{1,0:T(8,128)}, f32[256,256]{1,0:T(8,128)}, f32[256,256]{1,0:T(8,128)}, f32[256,256]{1,0:T(8,128)}, f32[256,256]{1,0:T(8,128)}, /*index=5*/f32[256,256]{1,0:T(8,128)}) fusion(f32[512,256]{1,0:T(8,128)S(1)} %fusion.10, pred[256]{0:T(512)(128)(4,1)S(1)} %iota_compare_fusion, f32[512,256]{1,0:T(8,128)S(1)} %fusion.9), kind=kLoop, calls=%fused_computation.70 | loop fusion | flops 262144 | bytes 2621696 | tf_op jit(solution)/shard_map/jit(_where)/select_n | solution.py:64
  32.0 0.0 all-to-all-done
  32.0 0.0 copy-start.3
  32.0 5.2 %all-to-all-start.1 = ((bf16[4,128,256]{1,2,0:T(8,128)(2,1)}), bf16[4,128,256]{1,2,0:T(8,128)(2,1)}, u32[]{:S(2)}, u32[]{:S(2)}) async-start(bf16[4,128,256]{1,2,0:T(8,128)(2,1)} %bitcast.90), calls=%async_computation.1 | async-start | bytes 524288 | tf_op jit(solution)/shard_map/all_to_all | solution.py:96
  37.2 0.1 copy.60
  37.4 0.0 copy-done.2
  37.4 0.5 fusion.29
  37.9 0.0 copy-done.1
  37.9 0.5 fusion.8
  38.4 1.6 %fusion.20 = (f32[256,512]{1,0:T(8,128)S(1)}, f32[256,512]{1,0:T(8,128)S(1)}) fusion(f32[256,256]{1,0:T(8,128)} %get-tuple-element.18, f32[256,256]{1,0:T(8,128)} %get-tuple-element.14, f32[512,512]{1,0:T(8,128)S(1)} %fusion.8, f32[256,256]{1,0:T(8,128)} %get-tuple-element.13), kind=kLoop, calls=%fused_computation.44 | loop fusion | flops 1179648 | bytes 2883584 | tf_op jit(solution)/shard_map/sub | solution.py:76
  40.0 0.0 copy-done
  40.1 0.0 copy-start.4
  40.1 0.5 fusion.30
  40.6 0.5 convolution_add_fusion.4
  41.1 0.0 copy-done.3
  41.1 0.5 fusion.7
  41.6 4.0 %all-to-all-done.1 = bf16[4,128,256]{1,2,0:T(8,128)(2,1)} async-done(((bf16[4,128,256]{1,2,0:T(8,128)(2,1)}), bf16[4,128,256]{1,2,0:T(8,128)(2,1)}, u32[]{:S(2)}, u32[]{:S(2)}) %all-to-all-start.1) | async-done | bytes 262176 | tf_op jit(solution)/shard_map/all_to_all | solution.py:96
  45.6 1.1 %broadcast_select_fusion.2 = (bf16[512,256]{0,1:T(8,128)(2,1)S(1)}, bf16[512,256]{0,1:T(8,128)(2,1)S(1)}) fusion(pred[512]{0:T(512)(128)(4,1)S(1)} %get-tuple-element.22, f32[512,512]{0,1:T(8,128)S(1)} %fusion.7, pred[512]{0:T(512)(128)(4,1)S(1)} %get-tuple-element.21, bf16[4,128,256]{1,2,0:T(8,128)(2,1)} %all-to-all-done.1), kind=kLoop, calls=%fused_computation.66 | loop fusion | flops 917504 | bytes 1836032 | tf_op jit(solution)/shard_map/jit(_where)/select_n | solution.py:72
  46.7 0.5 fusion.28
  47.2 0.5 fusion.6
  47.7 0.0 copy-done.4
  47.7 1.4 %fusion.24 = (f32[256,512]{1,0:T(8,128)S(1)}, f32[256,512]{1,0:T(8,128)S(1)}) fusion(f32[256,256]{1,0:T(8,128)S(1)} %copy-done.4, f32[256,256]{1,0:T(8,128)} %get-tuple-element.24, f32[512,512]{1,0:T(8,128)S(1)} %fusion.6, f32[256,256]{1,0:T(8,128)} %get-tuple-element.25), kind=kLoop, calls=%fused_computation.52 | loop fusion | flops 1179648 | bytes 2883584 | tf_op jit(solution)/shard_map/sub | solution.py:76
  49.1 0.5 fusion.31
  49.6 0.5 convolution_add_fusion.1
  50.1 0.5 fusion.5
  50.6 0.1 fusion.18
  50.8 0.8 copy.61
  51.6 3.6 %all-to-all-start.2 = ((bf16[4,128,256]{2,1,0:T(8,128)(2,1)}), bf16[4,128,256]{2,1,0:T(8,128)(2,1)S(1)}, u32[]{:S(2)}, u32[]{:S(2)}) async-start(bf16[4,128,256]{2,1,0:T(8,128)(2,1)} %bitcast.16), calls=%async_computation.2 | async-start | bytes 524288 | tf_op jit(solution)/shard_map/all_to_all | solution.py:100
  55.2 20.5 %constant_dynamic-slice_fusion = (bf16[4,256,1,2048]{3,2,1,0:T(2,128)(2,1)}, bf16[4,256,1,2048]{3,2,1,0:T(2,128)(2,1)}) fusion(bf16[4,256,2,2048]{3,2,1,0:T(2,128)(2,1)} %reshape_reshape.3, s32[]{:T(128)S(6)} %select_n.82, s32[]{:T(128)S(6)} %select_n.81), kind=kLoop, calls=%fused_computation.80 | loop fusion | bytes 16777224 | tf_op jit(solution)/shard_map/jit(dynamic_index_in_dim)/dynamic_slice | solution.py:112
  75.7 0.0 all-to-all-done.2
  75.7 6.0 %fusion.4 = bf16[128,2048]{1,0:T(8,128)(2,1)S(1)} fusion(bf16[4,128,256]{2,1,0:T(8,128)(2,1)S(1)} %all-to-all-done.2, bf16[4,256,1,2048]{3,2,1,0:T(2,128)(2,1)} %get-tuple-element.7), kind=kOutput, calls=%fused_computation.6 | convolution fusion | flops 537133056 | bytes 4980736 | tf_op jit(solution)/shard_map/dot_general | solution.py:105
  81.7 0.1 collective-permute-start
  81.8 1.9 %collective-permute-done = bf16[128,2048]{1,0:T(8,128)(2,1)S(1)} collective-permute-done((bf16[128,2048]{1,0:T(8,128)(2,1)S(1)}, bf16[128,2048]{1,0:T(8,128)(2,1)S(1)}, u32[]{:S(2)}, u32[]{:S(2)}) %collective-permute-start) | collective-permute-done | bytes 524320 | tf_op jit(solution)/shard_map/ppermute | solution.py:40
  83.7 6.1 %fusion.13 = (bf16[128,2048]{1,0:T(8,128)(2,1)S(1)}, f32[128,2048]{1,0:T(8,128)S(1)}) fusion(bf16[128,2048]{1,0:T(8,128)(2,1)S(1)} %collective-permute-done, bf16[4,128,256]{2,1,0:T(8,128)(2,1)S(1)} %all-to-all-done.2, bf16[4,256,1,2048]{3,2,1,0:T(2,128)(2,1)} %get-tuple-element.8), kind=kOutput, calls=%fused_computation.32 | convolution fusion | flops 537657344 | bytes 6553600 | tf_op jit(solution)/shard_map/dot_general | solution.py:105
  89.8 1.5 %collective-permute-start.1 = (bf16[128,2048]{1,0:T(8,128)(2,1)S(1)}, bf16[128,2048]{1,0:T(8,128)(2,1)S(1)}, u32[]{:S(2)}, u32[]{:S(2)}) collective-permute-start(bf16[128,2048]{1,0:T(8,128)(2,1)S(1)} %get-tuple-element.26), channel_id=1, source_target_pairs={{0,2},{1,3},{2,0},{3,1},{4,6},{5,7},{6,4},{7,5},{8,10},{9,11},{10,... | collective-permute-start | bytes 1572872 | tf_op jit(solution)/shard_map/ppermute | solution.py:40
  91.3 12.5 %collective-permute-done.1 = bf16[128,2048]{1,0:T(8,128)(2,1)S(1)} collective-permute-done((bf16[128,2048]{1,0:T(8,128)(2,1)S(1)}, bf16[128,2048]{1,0:T(8,128)(2,1)S(1)}, u32[]{:S(2)}, u32[]{:S(2)}) %collective-permute-start.1) | collective-permute-done | bytes 524320 | tf_op jit(solution)/shard_map/ppermute | solution.py:40
  103.8 0.2 add_convert_fusion
  104.0 0.1 collective-permute-start.2
  104.1 1.9 %collective-permute-done.2 = bf16[128,2048]{1,0:T(8,128)(2,1)S(1)} collective-permute-done((bf16[128,2048]{1,0:T(8,128)(2,1)S(1)}, bf16[128,2048]{1,0:T(8,128)(2,1)S(1)}, u32[]{:S(2)}, u32[]{:S(2)}) %collective-permute-start.2) | collective-permute-done | bytes 524320 | tf_op jit(solution)/shard_map/ppermute | solution.py:40
  106.0 1.2 %maximum_select_fusion = bf16[128,4096]{1,0:T(8,128)(2,1)} fusion(bf16[128,2048]{1,0:T(8,128)(2,1)S(1)} %collective-permute-done.2, bf16[128,2048]{1,0:T(8,128)(2,1)S(1)} %add_convert_fusion, pred[]{:T(512)S(6)} %eq.42), kind=kLoop, calls=%fused_computation.29 | loop fusion | flops 4718592 | bytes 2097153 | tf_op jit(solution)/shard_map/jit(_where)/select_n | solution.py:118
  (13 shorter events, 0.2 us)
Async XLA Ops:
  2.6 29.4 %all-to-all-start = ((bf16[4,144,256]{2,1,0:T(8,128)(2,1)}), bf16[4,144,256]{2,1,0:T(8,128)(2,1)S(1)}, u32[]{:S(2)}, u32[]{:S(2)}) async-start(bf16[4,144,256]{2,1,0:T(8,128)(2,1)} %pad_maximum_fusion.10), calls=%async_computation | async-start | bytes 589824 | tf_op jit(solution)/shard_map/all_to_all | solution.py:90
  15.2 14.6 %copy-start.5 = (bf16[128,1024]{1,0:T(8,128)(2,1)S(1)}, bf16[128,1024]{1,0:T(8,128)(2,1)}, u32[]{:S(2)}) copy-start(bf16[128,1024]{1,0:T(8,128)(2,1)} %param.13) | copy-start | bytes 786436
  15.2 22.2 %copy-start.2 = (bf16[512,512]{1,0:T(8,128)(2,1)S(1)}, bf16[512,512]{1,0:T(8,128)(2,1)}, u32[]{:S(2)}) copy-start(bf16[512,512]{1,0:T(8,128)(2,1)} %constant.51.clone) | copy-start | bytes 1572868
  15.3 22.7 %copy-start.1 = (bf16[512,512]{1,0:T(8,128)(2,1)S(1)}, bf16[512,512]{1,0:T(8,128)(2,1)}, u32[]{:S(2)}) copy-start(bf16[512,512]{1,0:T(8,128)(2,1)} %constant.52.clone) | copy-start | bytes 1572868
  29.9 10.2 %copy-start = (bf16[512,512]{1,0:T(8,128)(2,1)S(1)}, bf16[512,512]{1,0:T(8,128)(2,1)}, u32[]{:S(2)}) copy-start(bf16[512,512]{1,0:T(8,128)(2,1)} %constant.53.clone) | copy-start | bytes 1572868
  32.0 9.1 %copy-start.3 = (bf16[512,512]{1,0:T(8,128)(2,1)S(1)}, bf16[512,512]{1,0:T(8,128)(2,1)}, u32[]{:S(2)}) copy-start(bf16[512,512]{1,0:T(8,128)(2,1)} %constant.54.clone) | copy-start | bytes 1572868
  32.0 13.7 %all-to-all-start.1 = ((bf16[4,128,256]{1,2,0:T(8,128)(2,1)}), bf16[4,128,256]{1,2,0:T(8,128)(2,1)}, u32[]{:S(2)}, u32[]{:S(2)}) async-start(bf16[4,128,256]{1,2,0:T(8,128)(2,1)} %bitcast.90), calls=%async_computation.1 | async-start | bytes 524288 | tf_op jit(solution)/shard_map/all_to_all | solution.py:96
  40.1 7.6 %copy-start.4 = (f32[256,256]{1,0:T(8,128)S(1)}, f32[256,256]{1,0:T(8,128)}, u32[]{:S(2)}) copy-start(f32[256,256]{1,0:T(8,128)} %get-tuple-element.23) | copy-start | bytes 786436
  51.6 24.1 %all-to-all-start.2 = ((bf16[4,128,256]{2,1,0:T(8,128)(2,1)}), bf16[4,128,256]{2,1,0:T(8,128)(2,1)S(1)}, u32[]{:S(2)}, u32[]{:S(2)}) async-start(bf16[4,128,256]{2,1,0:T(8,128)(2,1)} %bitcast.16), calls=%async_computation.2 | async-start | bytes 524288 | tf_op jit(solution)/shard_map/all_to_all | solution.py:100
  81.7 2.0 %collective-permute-start = (bf16[128,2048]{1,0:T(8,128)(2,1)S(1)}, bf16[128,2048]{1,0:T(8,128)(2,1)S(1)}, u32[]{:S(2)}, u32[]{:S(2)}) collective-permute-start(bf16[128,2048]{1,0:T(8,128)(2,1)S(1)} %fusion.4), channel_id=1, source_target_pairs={{0,1},{1,0},{2,3},{3,2},{4,5},{5,4},{6,7},{7,6},{8,9},{9,8},{10,11... | collective-permute-start | bytes 1572872 | tf_op jit(solution)/shard_map/ppermute | solution.py:40
  89.8 14.0 %collective-permute-start.1 = (bf16[128,2048]{1,0:T(8,128)(2,1)S(1)}, bf16[128,2048]{1,0:T(8,128)(2,1)S(1)}, u32[]{:S(2)}, u32[]{:S(2)}) collective-permute-start(bf16[128,2048]{1,0:T(8,128)(2,1)S(1)} %get-tuple-element.26), channel_id=1, source_target_pairs={{0,2},{1,3},{2,0},{3,1},{4,6},{5,7},{6,4},{7,5},{8,10},{9,11},{10,... | collective-permute-start | bytes 1572872 | tf_op jit(solution)/shard_map/ppermute | solution.py:40
  104.0 2.0 %collective-permute-start.2 = (bf16[128,2048]{1,0:T(8,128)(2,1)S(1)}, bf16[128,2048]{1,0:T(8,128)(2,1)S(1)}, u32[]{:S(2)}, u32[]{:S(2)}) collective-permute-start(bf16[128,2048]{1,0:T(8,128)(2,1)S(1)} %add_convert_fusion), channel_id=1, source_target_pairs={{0,1},{1,0},{2,3},{3,2},{4,5},{5,4},{6,7},{7,6},{8,9},{9,8},{10,11... | collective-permute-start | bytes 1572872 | tf_op jit(solution)/shard_map/ppermute | solution.py:40

commit v5 on v4

--- a/solution.py
+++ b/solution.py
@@ -99,19 +99,18 @@
         second_mix = long_conv(spectrum(second_filter), second_input).astype(BF16)
         mix_blocks = lax.all_to_all(second_mix.reshape(nseq, rows, per), "seq", 0, 0, tiled=True)
         out_cols = out_weight.shape[1]
-        w_blocks = out_weight.reshape(nseq, per, out_cols)
+        mix_rows = mix_blocks.transpose(1, 0, 2).reshape(rows, nseq * per)
 
         def project(w):
-            return lax.dot_general(mix_blocks, w, (((0, 2), (0, 1)), ((), ())), preferred_element_type=F32)
+            return mm(mix_rows, w)
 
         if nchan != 4:
-            return lax.psum(project(w_blocks), "chan").astype(BF16)
+            return lax.psum(project(out_weight), "chan").astype(BF16)
         core = lax.axis_index("chan") % 2
         width = out_cols // 2
-        w_halves = w_blocks.reshape(nseq, per, 2, width)
-        other = project(lax.dynamic_index_in_dim(w_halves, 1 - core, 2, keepdims=False))
+        other = project(lax.dynamic_slice_in_dim(out_weight, (1 - core) * width, width, 1))
         got_other = swap(other.astype(BF16), 1)
-        mine = project(lax.dynamic_index_in_dim(w_halves, core, 2, keepdims=False))
+        mine = project(lax.dynamic_slice_in_dim(out_weight, core * width, width, 1))
         chip = mine + got_other.astype(F32)
         total = (chip + swap(chip.astype(BF16), 2).astype(F32)).astype(BF16)
         peer = swap(total, 1)

time: 108 us -> 68.6 us (0.64)
  local copies, waits for them, and re-layouts: 37.8 us -> 1.9 us
  waiting for transfers between devices: 20.3 us -> 31.1 us
  matrix products: 22.4 us -> 13.1 us
  other arithmetic: 9.49 us -> 6.71 us
  starting transfers between devices: 16.8 us -> 14.9 us
    dynamic_slice x1 -> x0, local copies, waits for them, and re-layouts: 20.5 us -> none  [local(): lax.dynamic_index_in_dim(w_halves, 1 - core, 2, keepdims=False)]
    another operation x1 -> x0, local copies, waits for them, and re-layouts: 14.6 us -> none  [local(): w_halves = w_blocks.reshape(nseq, per, 2, width)]
    dot_general x2 -> x0, matrix products: 12.1 us -> none  [project(): lax.dot_general(mix_blocks, w, (((0, 2), (0, 1)), ((), ())), preferred_el...]
    all_to_all x1, waiting for transfers between devices: 0.01 us -> 6.72 us  [local(): lax.all_to_all(second_mix.reshape(nseq, rows, per), 'seq', 0, 0, tiled=True)]
    all_to_all x1, waiting for transfers between devices: 0.01 us -> 4.33 us  [local(): got = lax.all_to_all(payload, 'seq', 0, 0, tiled=True)]
    dot_general x14 -> x16, matrix products: 10.3 us -> 13.1 us  [mm(): return jnp.dot(a, b, preferred_element_type=F32)]
    sub x2, other arithmetic: 3.08 us -> 0.45 us  [long_conv(): y = jnp.concatenate([xr * a - xi * b, xr * b + xi * d], axis=0)]
    all_to_all x1, starting transfers between devices: 5.22 us -> 3.4 us  [local(): lax.all_to_all(gate_blocks, 'seq', 0, 0, tiled=True)]
  transfers between devices with their start and end apart: 6 -> 6, of which waited for: 4 -> 6; matrix products, arithmetic and copies ran while one was open for 45% -> 12% of each run, Pallas kernels for 0% -> 0%
where the time goes in v5:
time: 68.6 us; the launch traced here: 68 us
  waiting for transfers between devices  31.1 us (45%)
  starting transfers between devices  14.9 us (22%)
  matrix products  13.1 us (19%)
  other arithmetic  6.71 us (10%)
  local copies, waits for them, and re-layouts  1.9 us (3%)
    ppermute x3, waiting for transfers between devices, swap(): return lax.ppermute(x, 'chan', [(c, c ^ bit) for c in range(4)])  16.3 us
    dot_general x16, matrix products, mm(): return jnp.dot(a, b, preferred_element_type=F32)  13.1 us
    all_to_all x1, waiting for transfers between devices, local(): lax.all_to_all(second_mix.reshape(nseq, rows, per), 'seq', 0, 0, tiled=True)  6.72 us
    all_to_all x1, starting transfers between devices, local(): got = lax.all_to_all(payload, 'seq', 0, 0, tiled=True)  6.35 us
    all_to_all x1, waiting for transfers between devices, local(): got = lax.all_to_all(payload, 'seq', 0, 0, tiled=True)  4.33 us
    all_to_all x1, waiting for transfers between devices, local(): lax.all_to_all(gate_blocks, 'seq', 0, 0, tiled=True)  3.8 us
    all_to_all x1, starting transfers between devices, local(): lax.all_to_all(second_mix.reshape(nseq, rows, per), 'seq', 0, 0, tiled=True)  3.41 us
    all_to_all x1, starting transfers between devices, local(): lax.all_to_all(gate_blocks, 'seq', 0, 0, tiled=True)  3.4 us
  transfers between devices with their start and end apart: 6, of which 6 were waited for; matrix products, arithmetic and copies ran while one was open for 12% of the time, Pallas kernels for 0%

profile of v5, /device:TPU:0, one launch (start us, length us, event | category | flops | bytes accessed | tf_op | source)
XLA Modules:
  0.0 68.0 jit_solution(18219645642936342804)
XLA Ops:
  0.0 0.0 copy-start.2
  0.0 0.0 copy-start.1
  0.0 1.2 %multiply_convert_fusion = bf16[128,1024]{1,0:T(8,128)(2,1)S(1)} fusion(bf16[128,1024]{1,0:T(8,128)(2,1)} %param.11, bf16[128,1024]{1,0:T(8,128)(2,1)} %param.12), kind=kLoop, calls=%fused_computation.57 | loop fusion | flops 524288 | bytes 786432 | tf_op jit(solution)/shard_map/convert_element_type | solution.py:84
  1.2 0.0 copy-start.10
  1.2 0.7 %convert_element_type.56 = bf16[128]{0:T(256)(128)(2,1)S(1)} convert(s32[128]{0:T(128)} %param.17) | non-fusion elementwise | flops 128 | bytes 768 | tf_op jit(solution)/shard_map/convert_element_type | solution.py:88
  2.0 0.7 %pad_maximum_fusion.10 = bf16[4,144,256]{2,1,0:T(8,128)(2,1)} fusion(bf16[4,16,256]{2,1,0:T(8,128)(2,1)S(1)} %broadcast_in_dim.62, bf16[4,128,256]{2,1,0:T(8,128)(2,1)S(1)} %bitcast.79), kind=kLoop, calls=%fused_computation.60 | loop fusion | flops 589824 | bytes 589824 | tf_op jit(solution)/shard_map/concatenate | solution.py:89
  2.7 6.3 %all-to-all-start = ((bf16[4,144,256]{2,1,0:T(8,128)(2,1)}), bf16[4,144,256]{2,1,0:T(8,128)(2,1)S(1)}, u32[]{:S(2)}, u32[]{:S(2)}) async-start(bf16[4,144,256]{2,1,0:T(8,128)(2,1)} %pad_maximum_fusion.10), calls=%async_computation | async-start | bytes 589824 | tf_op jit(solution)/shard_map/all_to_all | solution.py:90
  9.0 0.7 %dynamic-slice_bitcast_fusion = (bf16[512,16]{0,1:T(8,128)(2,1)S(1)}, bf16[512,16]{0,1:T(8,128)(2,1)S(1)}) fusion(bf16[64,512]{1,0:T(8,128)(2,1)} %param.15, s32[]{:T(128)S(6)} %select_n.69, bf16[64,512]{1,0:T(8,128)(2,1)} %param.14), kind=kLoop, calls=%fused_computation.73 | loop fusion | bytes 65540 | tf_op jit(solution)/shard_map/transpose | solution.py:58
  9.8 1.4 %fusion.49 = f32[256,512]{0,1:T(8,128)S(1)} fusion(bf16[512,256]{0,1:T(8,128)(2,1)S(1)} %bitcast.72, bf16[512,512]{1,0:T(8,128)(2,1)} %constant.47.clone), kind=kOutput, calls=%fused_computation.93 | convolution fusion | flops 134217728 | bytes 1310720 | tf_op jit(solution)/shard_map/dot_general | solution.py:36
  11.2 0.0 copy-done.2
  11.2 0.3 fusion.48
  11.6 0.0 copy-done.1
  11.6 0.3 fusion.11
  11.9 0.3 fusion.12
  12.3 0.0 copy-done.10
  12.3 0.8 %copy.35 = bf16[128,1024]{0,1:T(8,128)(2,1)} copy(bf16[128,1024]{1,0:T(8,128)(2,1)S(1)} %copy-done.10) | data formatting | bytes 524288 | tf_op args[2]
  13.1 1.2 %slice_select_fusion.6 = (f32[256,256]{1,0:T(8,128)}, f32[256,256]{1,0:T(8,128)}, f32[256,256]{1,0:T(8,128)}, f32[256,256]{1,0:T(8,128)}, f32[256,256]{1,0:T(8,128)}, /*index=5*/f32[256,256]{1,0:T(8,128)}) fusion(f32[512,256]{1,0:T(8,128)S(1)} %fusion.12, pred[256]{0:T(512)(128)(4,1)S(1)} %iota_compare_fusion, f32[512,256]{1,0:T(8,128)S(1)} %fusion.11), kind=kLoop, calls=%fused_computation.70 | loop fusion | flops 262144 | bytes 2621696 | tf_op jit(solution)/shard_map/jit(_where)/select_n | solution.py:64
  14.3 0.0 copy-start.7
  14.3 0.0 copy-start.8
  14.3 4.3 %all-to-all-done = bf16[4,144,256]{2,1,0:T(8,128)(2,1)S(1)} async-done(((bf16[4,144,256]{2,1,0:T(8,128)(2,1)}), bf16[4,144,256]{2,1,0:T(8,128)(2,1)S(1)}, u32[]{:S(2)}, u32[]{:S(2)}) %all-to-all-start) | async-done | bytes 294944 | tf_op jit(solution)/shard_map/all_to_all | solution.py:90
  18.7 3.4 %all-to-all-start.1 = ((bf16[4,128,256]{1,2,0:T(8,128)(2,1)}), bf16[4,128,256]{1,2,0:T(8,128)(2,1)S(1)}, u32[]{:S(2)}, u32[]{:S(2)}) async-start(bf16[4,128,256]{1,2,0:T(8,128)(2,1)} %bitcast.3), calls=%async_computation.1 | async-start | bytes 524288 | tf_op jit(solution)/shard_map/all_to_all | solution.py:96
  22.2 0.0 copy-start.9
  22.2 0.1 copy.53
  22.4 0.0 copy-start
  22.4 0.5 fusion.31
  22.8 0.5 fusion.10
  23.3 0.0 copy-done.7
  23.3 0.0 copy-done.8
  23.3 0.0 copy-done.9
  23.3 0.0 copy-start.3
  23.4 0.2 fusion.22
  23.6 0.0 copy-done
  23.6 0.5 fusion.33
  24.1 0.5 convolution_add_fusion.4
  24.6 0.0 copy-done.3
  24.6 0.5 fusion.9
  25.1 3.8 %all-to-all-done.1 = bf16[4,128,256]{1,2,0:T(8,128)(2,1)S(1)} async-done(((bf16[4,128,256]{1,2,0:T(8,128)(2,1)}), bf16[4,128,256]{1,2,0:T(8,128)(2,1)S(1)}, u32[]{:S(2)}, u32[]{:S(2)}) %all-to-all-start.1) | async-done | bytes 262176 | tf_op jit(solution)/shard_map/all_to_all | solution.py:96
  28.9 0.0 copy-start.4
  28.9 0.0 copy-start.5
  28.9 0.0 copy-start.6
  28.9 0.1 broadcast_select_fusion.2
  29.1 0.5 fusion.30
  29.6 0.5 fusion.8
  30.1 0.0 copy-done.4
  30.1 0.0 copy-done.5
  30.1 0.0 copy-done.6
  30.1 0.2 fusion.26
  30.3 0.5 fusion.34
  30.8 0.5 convolution_add_fusion.1
  31.3 0.5 fusion.7
  31.8 0.8 %copy_bitcast_fusion = bf16[4,128,256]{1,2,0:T(8,128)(2,1)} fusion(f32[512,512]{0,1:T(8,128)S(1)} %fusion.7, pred[512]{0:T(512)(128)(4,1)S(1)} %get-tuple-element.19, pred[512]{0:T(512)(128)(4,1)S(1)} %get-tuple-element.20), kind=kLoop, calls=%fused_computation.62 | loop fusion | flops 524288 | bytes 1311744 | tf_op jit(solution)/shard_map/reshape | solution.py:100
  32.6 3.4 %all-to-all-start.2 = ((bf16[4,128,256]{1,2,0:T(8,128)(2,1)}), bf16[4,128,256]{1,2,0:T(8,128)(2,1)S(1)}, u32[]{:S(2)}, u32[]{:S(2)}) async-start(bf16[4,128,256]{1,2,0:T(8,128)(2,1)} %copy_bitcast_fusion), calls=%async_computation.2 | async-start | bytes 524288 | tf_op jit(solution)/shard_map/all_to_all | solution.py:100
  36.0 6.7 %all-to-all-done.2 = bf16[4,128,256]{1,2,0:T(8,128)(2,1)S(1)} async-done(((bf16[4,128,256]{1,2,0:T(8,128)(2,1)}), bf16[4,128,256]{1,2,0:T(8,128)(2,1)S(1)}, u32[]{:S(2)}, u32[]{:S(2)}) %all-to-all-start.2) | async-done | bytes 262176 | tf_op jit(solution)/shard_map/all_to_all | solution.py:100
  42.7 2.9 %fusion.4 = bf16[128,2048]{1,0:T(8,128)(2,1)S(1)} fusion(bf16[128,1024]{0,1:T(8,128)(2,1)S(1)} %bitcast.76, bf16[1024,4096]{1,0:T(8,128)(2,1)} %param.16, s32[]{:T(128)S(6)} %select_n.81), kind=kOutput, calls=%fused_computation.4 | convolution fusion | flops 537133056 | bytes 4980740 | tf_op jit(solution)/shard_map/dot_general | solution.py:36
  45.7 0.1 collective-permute-start
  45.8 1.9 %collective-permute-done = bf16[128,2048]{1,0:T(8,128)(2,1)S(1)} collective-permute-done((bf16[128,2048]{1,0:T(8,128)(2,1)S(1)}, bf16[128,2048]{1,0:T(8,128)(2,1)S(1)}, u32[]{:S(2)}, u32[]{:S(2)}) %collective-permute-start) | collective-permute-done | bytes 524320 | tf_op jit(solution)/shard_map/ppermute | solution.py:40
  47.7 2.9 %fusion.15 = (bf16[128,2048]{1,0:T(8,128)(2,1)S(1)}, f32[128,2048]{1,0:T(8,128)S(1)}) fusion(bf16[128,2048]{1,0:T(8,128)(2,1)S(1)} %collective-permute-done, bf16[128,1024]{0,1:T(8,128)(2,1)S(1)} %bitcast.77, bf16[1024,4096]{1,0:T(8,128)(2,1)} %param.16, s32[]{:T(128)S(6)} %select_n.80), kind=kOutput, calls=%fused_computation.30 | convolution fusion | flops 537657344 | bytes 6553604 | tf_op jit(solution)/shard_map/dot_general | solution.py:36
  50.6 1.6 %collective-permute-start.1 = (bf16[128,2048]{1,0:T(8,128)(2,1)S(1)}, bf16[128,2048]{1,0:T(8,128)(2,1)S(1)}, u32[]{:S(2)}, u32[]{:S(2)}) collective-permute-start(bf16[128,2048]{1,0:T(8,128)(2,1)S(1)} %get-tuple-element.24), channel_id=1, source_target_pairs={{0,2},{1,3},{2,0},{3,1},{4,6},{5,7},{6,4},{7,5},{8,10},{9,11},{10,... | collective-permute-start | bytes 1572872 | tf_op jit(solution)/shard_map/ppermute | solution.py:40
  52.1 12.5 %collective-permute-done.1 = bf16[128,2048]{1,0:T(8,128)(2,1)S(1)} collective-permute-done((bf16[128,2048]{1,0:T(8,128)(2,1)S(1)}, bf16[128,2048]{1,0:T(8,128)(2,1)S(1)}, u32[]{:S(2)}, u32[]{:S(2)}) %collective-permute-start.1) | collective-permute-done | bytes 524320 | tf_op jit(solution)/shard_map/ppermute | solution.py:40
  64.6 0.2 add_convert_fusion
  64.8 0.1 collective-permute-start.2
  64.9 1.9 %collective-permute-done.2 = bf16[128,2048]{1,0:T(8,128)(2,1)S(1)} collective-permute-done((bf16[128,2048]{1,0:T(8,128)(2,1)S(1)}, bf16[128,2048]{1,0:T(8,128)(2,1)S(1)}, u32[]{:S(2)}, u32[]{:S(2)}) %collective-permute-start.2) | collective-permute-done | bytes 524320 | tf_op jit(solution)/shard_map/ppermute | solution.py:40
  66.8 1.2 %maximum_select_fusion = bf16[128,4096]{1,0:T(8,128)(2,1)} fusion(bf16[128,2048]{1,0:T(8,128)(2,1)S(1)} %collective-permute-done.2, bf16[128,2048]{1,0:T(8,128)(2,1)S(1)} %add_convert_fusion, pred[]{:T(512)S(6)} %eq.42), kind=kLoop, calls=%fused_computation.27 | loop fusion | flops 4718592 | bytes 2097153 | tf_op jit(solution)/shard_map/jit(_where)/select_n | solution.py:117
  (13 shorter events, 0.2 us)
Async XLA Ops:
  0.0 11.2 %copy-start.2 = (bf16[512,512]{1,0:T(8,128)(2,1)S(1)}, bf16[512,512]{1,0:T(8,128)(2,1)}, u32[]{:S(2)}) copy-start(bf16[512,512]{1,0:T(8,128)(2,1)} %constant.47.clone) | copy-start | bytes 1572868
  0.0 11.6 %copy-start.1 = (bf16[512,512]{1,0:T(8,128)(2,1)S(1)}, bf16[512,512]{1,0:T(8,128)(2,1)}, u32[]{:S(2)}) copy-start(bf16[512,512]{1,0:T(8,128)(2,1)} %constant.48.clone) | copy-start | bytes 1572868
  1.2 11.0 %copy-start.10 = (bf16[128,1024]{1,0:T(8,128)(2,1)S(1)}, bf16[128,1024]{1,0:T(8,128)(2,1)}, u32[]{:S(2)}) copy-start(bf16[128,1024]{1,0:T(8,128)(2,1)} %param.13) | copy-start | bytes 786436
  2.7 16.0 %all-to-all-start = ((bf16[4,144,256]{2,1,0:T(8,128)(2,1)}), bf16[4,144,256]{2,1,0:T(8,128)(2,1)S(1)}, u32[]{:S(2)}, u32[]{:S(2)}) async-start(bf16[4,144,256]{2,1,0:T(8,128)(2,1)} %pad_maximum_fusion.10), calls=%async_computation | async-start | bytes 589824 | tf_op jit(solution)/shard_map/all_to_all | solution.py:90
  14.3 9.0 %copy-start.7 = (f32[256,256]{1,0:T(8,128)S(1)}, f32[256,256]{1,0:T(8,128)}, u32[]{:S(2)}) copy-start(f32[256,256]{1,0:T(8,128)} %get-tuple-element.11) | copy-start | bytes 786436
  14.3 9.0 %copy-start.8 = (f32[256,256]{1,0:T(8,128)S(1)}, f32[256,256]{1,0:T(8,128)}, u32[]{:S(2)}) copy-start(f32[256,256]{1,0:T(8,128)} %get-tuple-element.12) | copy-start | bytes 786436
  18.7 10.3 %all-to-all-start.1 = ((bf16[4,128,256]{1,2,0:T(8,128)(2,1)}), bf16[4,128,256]{1,2,0:T(8,128)(2,1)S(1)}, u32[]{:S(2)}, u32[]{:S(2)}) async-start(bf16[4,128,256]{1,2,0:T(8,128)(2,1)} %bitcast.3), calls=%async_computation.1 | async-start | bytes 524288 | tf_op jit(solution)/shard_map/all_to_all | solution.py:96
  22.2 1.2 %copy-start.9 = (f32[256,256]{1,0:T(8,128)S(1)}, f32[256,256]{1,0:T(8,128)}, u32[]{:S(2)}) copy-start(f32[256,256]{1,0:T(8,128)} %get-tuple-element.16) | copy-start | bytes 786436
  22.4 1.2 %copy-start = (bf16[512,512]{1,0:T(8,128)(2,1)S(1)}, bf16[512,512]{1,0:T(8,128)(2,1)}, u32[]{:S(2)}) copy-start(bf16[512,512]{1,0:T(8,128)(2,1)} %constant.49.clone) | copy-start | bytes 1572868
  23.3 1.3 %copy-start.3 = (bf16[512,512]{1,0:T(8,128)(2,1)S(1)}, bf16[512,512]{1,0:T(8,128)(2,1)}, u32[]{:S(2)}) copy-start(bf16[512,512]{1,0:T(8,128)(2,1)} %constant.50.clone) | copy-start | bytes 1572868
  28.9 1.1 %copy-start.4 = (f32[256,256]{1,0:T(8,128)S(1)}, f32[256,256]{1,0:T(8,128)}, u32[]{:S(2)}) copy-start(f32[256,256]{1,0:T(8,128)} %get-tuple-element.21) | copy-start | bytes 786436
  28.9 1.1 %copy-start.5 = (f32[256,256]{1,0:T(8,128)S(1)}, f32[256,256]{1,0:T(8,128)}, u32[]{:S(2)}) copy-start(f32[256,256]{1,0:T(8,128)} %get-tuple-element.22) | copy-start | bytes 786436
  28.9 1.2 %copy-start.6 = (f32[256,256]{1,0:T(8,128)S(1)}, f32[256,256]{1,0:T(8,128)}, u32[]{:S(2)}) copy-start(f32[256,256]{1,0:T(8,128)} %get-tuple-element.23) | copy-start | bytes 786436
  32.6 10.2 %all-to-all-start.2 = ((bf16[4,128,256]{1,2,0:T(8,128)(2,1)}), bf16[4,128,256]{1,2,0:T(8,128)(2,1)S(1)}, u32[]{:S(2)}, u32[]{:S(2)}) async-start(bf16[4,128,256]{1,2,0:T(8,128)(2,1)} %copy_bitcast_fusion), calls=%async_computation.2 | async-start | bytes 524288 | tf_op jit(solution)/shard_map/all_to_all | solution.py:100
  45.7 2.0 %collective-permute-start = (bf16[128,2048]{1,0:T(8,128)(2,1)S(1)}, bf16[128,2048]{1,0:T(8,128)(2,1)S(1)}, u32[]{:S(2)}, u32[]{:S(2)}) collective-permute-start(bf16[128,2048]{1,0:T(8,128)(2,1)S(1)} %fusion.4), channel_id=1, source_target_pairs={{0,1},{1,0},{2,3},{3,2},{4,5},{5,4},{6,7},{7,6},{8,9},{9,8},{10,11... | collective-permute-start | bytes 1572872 | tf_op jit(solution)/shard_map/ppermute | solution.py:40
  50.6 14.0 %collective-permute-start.1 = (bf16[128,2048]{1,0:T(8,128)(2,1)S(1)}, bf16[128,2048]{1,0:T(8,128)(2,1)S(1)}, u32[]{:S(2)}, u32[]{:S(2)}) collective-permute-start(bf16[128,2048]{1,0:T(8,128)(2,1)S(1)} %get-tuple-element.24), channel_id=1, source_target_pairs={{0,2},{1,3},{2,0},{3,1},{4,6},{5,7},{6,4},{7,5},{8,10},{9,11},{10,... | collective-permute-start | bytes 1572872 | tf_op jit(solution)/shard_map/ppermute | solution.py:40
  64.8 2.0 %collective-permute-start.2 = (bf16[128,2048]{1,0:T(8,128)(2,1)S(1)}, bf16[128,2048]{1,0:T(8,128)(2,1)S(1)}, u32[]{:S(2)}, u32[]{:S(2)}) collective-permute-start(bf16[128,2048]{1,0:T(8,128)(2,1)S(1)} %add_convert_fusion), channel_id=1, source_target_pairs={{0,1},{1,0},{2,3},{3,2},{4,5},{5,4},{6,7},{7,6},{8,9},{9,8},{10,11... | collective-permute-start | bytes 1572872 | tf_op jit(solution)/shard_map/ppermute | solution.py:40

commit v6 on v5

--- a/solution.py
+++ b/solution.py
@@ -50,8 +50,6 @@
         half = length // 2
         (f_hi, f_lo), (i_hi, i_lo) = dft_mats(length)
         f_hi, f_lo, i_hi, i_lo = (jnp.asarray(m) for m in (f_hi, f_lo, i_hi, i_lo))
-        me = lax.axis_index("seq")
-
 
         def spectrum(filt):
             mine = lax.dynamic_slice_in_dim(filt, me * fpd, fpd, 0)
@@ -81,36 +79,56 @@
             return jnp.where(in0, both[:, :per], 0.0) + jnp.where(in1, both[:, per:], 0.0)
 
         rows = value.shape[0]
+        me = lax.axis_index("seq")
+        order = [0] + [k for k in (1, nseq - 1) if k < nseq] + [k for k in range(2, nseq - 1)]
+        order = list(dict.fromkeys(order))
+
+        def exchange(blocks):
+            got = {0: lax.dynamic_index_in_dim(blocks, me, 0, keepdims=False)}
+            for k in order[1:]:
+                piece = lax.dynamic_index_in_dim(blocks, (me + k) % nseq, 0, keepdims=False)
+                got[k] = lax.ppermute(piece, "seq", [(i, (i + k) % nseq) for i in range(nseq)])
+            return got
+
+        def in_source_order(got):
+            by_shift = jnp.stack([got[k] for k in reversed(range(nseq))])
+            return jnp.roll(by_shift, me + 1, axis=0)
+
         first_input = (first_gate.astype(F32) * value.astype(F32)).astype(BF16)
         first_input = first_input.reshape(rows, nseq, per).transpose(1, 0, 2)
+        gate_blocks = second_gate.reshape(rows, nseq, per).transpose(1, 0, 2)
         id_rows = -(-rows // per)
         pad_rows = -(-id_rows // 16) * 16
         ids = jnp.pad(segment_ids.astype(BF16), (0, pad_rows * per - rows)).reshape(1, pad_rows, per)
-        payload = jnp.concatenate([first_input, jnp.broadcast_to(ids, (nseq, pad_rows, per))], axis=1)
-        got = lax.all_to_all(payload, "seq", 0, 0, tiled=True)
+        payload = jnp.concatenate(
+            [first_input, gate_blocks, jnp.broadcast_to(ids, (nseq, pad_rows, per))], axis=1)
+        got = in_source_order(exchange(payload))
         first_cols = got[:, :rows].reshape(nseq * rows, per)
-        segs = got[:, rows:].reshape(nseq, pad_rows * per)[:, :rows].reshape(nseq * rows)
+        gate_cols = got[:, rows:2 * rows].reshape(nseq * rows, per)
+        segs = got[:, 2 * rows:].reshape(nseq, pad_rows * per)[:, :rows].reshape(nseq * rows)
         in0 = (segs == 0)[:, None]
         in1 = (segs == 1)[:, None]
-        gate_blocks = second_gate.reshape(rows, nseq, per).transpose(1, 0, 2)
-        gate_cols = lax.all_to_all(gate_blocks, "seq", 0, 0, tiled=True).reshape(nseq * rows, per)
         first_mix = long_conv(spectrum(first_filter), first_cols)
         second_input = (gate_cols.astype(F32) * first_mix).astype(BF16)
         second_mix = long_conv(spectrum(second_filter), second_input).astype(BF16)
-        mix_blocks = lax.all_to_all(second_mix.reshape(nseq, rows, per), "seq", 0, 0, tiled=True)
+        mix_pieces = exchange(second_mix.reshape(nseq, rows, per))
         out_cols = out_weight.shape[1]
-        mix_rows = mix_blocks.transpose(1, 0, 2).reshape(rows, nseq * per)
 
-        def project(w):
-            return mm(mix_rows, w)
+        def project(cols_lo, width):
+            acc = None
+            for k in order:
+                w = lax.dynamic_slice(out_weight, (((me - k) % nseq) * per, cols_lo), (per, width))
+                term = mm(mix_pieces[k], w)
+                acc = term if acc is None else acc + term
+            return acc
 
         if nchan != 4:
-            return lax.psum(project(out_weight), "chan").astype(BF16)
+            return lax.psum(project(0, out_cols), "chan").astype(BF16)
         core = lax.axis_index("chan") % 2
         width = out_cols // 2
-        other = project(lax.dynamic_slice_in_dim(out_weight, (1 - core) * width, width, 1))
+        other = project((1 - core) * width, width)
         got_other = swap(other.astype(BF16), 1)
-        mine = project(lax.dynamic_slice_in_dim(out_weight, core * width, width, 1))
+        mine = project(core * width, width)
         chip = mine + got_other.astype(F32)
         total = (chip + swap(chip.astype(BF16), 2).astype(F32)).astype(BF16)
         peer = swap(total, 1)

time: 68.6 us -> 74.2 us (1.082)
  local copies, waits for them, and re-layouts: 1.9 us -> 15.3 us
  waiting for transfers between devices: 31.1 us -> 21.2 us
  matrix products: 13.1 us -> 18.5 us
  starting transfers between devices: 14.9 us -> 13 us
  other arithmetic: 6.71 us -> 4.93 us
    all_to_all x3 -> x0, waiting for transfers between devices: 14.9 us -> none  [the longest x1 6.72 us: local(): lax.all_to_all(second_mix.reshape(nseq, rows, per), 'seq', 0, 0, tiled=True)]
    all_to_all x3 -> x0, starting transfers between devices: 13.2 us -> none  [the longest x1 6.35 us: local(): got = lax.all_to_all(payload, 'seq', 0, 0, tiled=True)]
    ppermute x0 -> x6, starting transfers between devices: none -> 11.3 us  [exchange(): lax.ppermute(piece, 'seq', [(i, (i + k) % nseq) for i in range(nseq)])]
    unnamed x25 -> x23, local copies, waits for them, and re-layouts: 0.91 us -> 9.97 us
    ppermute x0 -> x6, waiting for transfers between devices: none -> 6.5 us  [exchange(): lax.ppermute(piece, 'seq', [(i, (i + k) % nseq) for i in range(nseq)])]
    dot_general x16 -> x22, matrix products: 13.1 us -> 18.5 us  [mm(): return jnp.dot(a, b, preferred_element_type=F32)]
    ppermute x3, waiting for transfers between devices: 16.3 us -> 14.7 us  [swap(): return lax.ppermute(x, 'chan', [(c, c ^ bit) for c in range(4)])]
    another operation x0 -> x3, local copies, waits for them, and re-layouts: none -> 1.39 us  [in_source_order(): by_shift = jnp.stack([got[k] for k in reversed(range(nseq))])]
  transfers between devices with their start and end apart: 6 -> 9, of which waited for: 6 -> 3; matrix products, arithmetic and copies ran while one was open for 12% -> 19% of each run, Pallas kernels for 0% -> 0%
where the time goes in v6:
time: 74.2 us; the launch traced here: 73.4 us
  waiting for transfers between devices  21.2 us (29%)
  matrix products  18.5 us (25%)
  local copies, waits for them, and re-layouts  15.3 us (21%)
  starting transfers between devices  13 us (18%)
  other arithmetic  4.93 us (7%)
    dot_general x22, matrix products, mm(): return jnp.dot(a, b, preferred_element_type=F32)  18.5 us
    ppermute x3, waiting for transfers between devices, swap(): return lax.ppermute(x, 'chan', [(c, c ^ bit) for c in range(4)])  14.7 us
    ppermute x6, starting transfers between devices, exchange(): lax.ppermute(piece, 'seq', [(i, (i + k) % nseq) for i in range(nseq)])  11.3 us
    unnamed x23, local copies, waits for them, and re-layouts  9.97 us
    ppermute x6, waiting for transfers between devices, exchange(): lax.ppermute(piece, 'seq', [(i, (i + k) % nseq) for i in range(nseq)])  6.5 us
    ppermute x3, starting transfers between devices, swap(): return lax.ppermute(x, 'chan', [(c, c ^ bit) for c in range(4)])  1.7 us
  transfers between devices with their start and end apart: 9, of which 3 were waited for; matrix products, arithmetic and copies ran while one was open for 19% of the time, Pallas kernels for 0%

profile of v6, /device:TPU:0, one launch (start us, length us, event | category | flops | bytes accessed | tf_op | source)
XLA Modules:
  0.0 73.4 jit_solution(15576799438945041181)
XLA Ops:
  0.0 1.1 %copy.36 = bf16[128,1024]{0,1:T(8,128)(2,1)S(1)} copy(bf16[128,1024]{1,0:T(8,128)(2,1)} %param.12) | data formatting | bytes 524288 | tf_op args[1]
  1.1 1.1 %copy.37 = bf16[128,1024]{0,1:T(8,128)(2,1)S(1)} copy(bf16[128,1024]{1,0:T(8,128)(2,1)} %param.11) | data formatting | bytes 524288 | tf_op args[0]
  2.3 0.7 convert_element_type.56
  2.9 0.1 copy.39
  3.1 1.1 %copy.38 = bf16[128,1024]{0,1:T(8,128)(2,1)S(1)} copy(bf16[128,1024]{1,0:T(8,128)(2,1)} %param.13) | data formatting | bytes 524288 | tf_op args[2]
  4.3 0.1 pad_maximum_fusion.2
  4.7 5.1 %collective-permute-start = (bf16[272,256]{1,0:T(8,128)(2,1)S(1)}, bf16[272,256]{1,0:T(8,128)(2,1)S(1)}, u32[]{:S(2)}, u32[]{:S(2)}) collective-permute-start(bf16[272,256]{1,0:T(8,128)(2,1)S(1)} %bitcast.93), channel_id=1, source_target_pairs={{0,12},{4,0},{8,4},{12,8},{1,13},{5,1},{9,5},{13,9},{2,14},{6,2},{... | collective-permute-start | bytes 417800 | tf_op jit(solution)/shard_map/ppermute | solution.py:90
  10.0 0.8 %copy.42 = bf16[1,272,256]{2,1,0:T(8,128)(2,1)} copy(bf16[1,272,256]{1,2,0:T(8,128)(2,1)S(1)} %get-tuple-element.13) | data formatting | bytes 278528 | tf_op jit(solution)/shard_map/jit(dynamic_index_in_dim)/dynamic_slice | solution.py:89
  10.8 1.0 %collective-permute-start.2 = (bf16[272,256]{1,0:T(8,128)(2,1)}, bf16[272,256]{1,0:T(8,128)(2,1)}, u32[]{:S(2)}, u32[]{:S(2)}) collective-permute-start(bf16[272,256]{1,0:T(8,128)(2,1)} %bitcast.8), channel_id=1, source_target_pairs={{0,4},{4,8},{8,12},{12,0},{1,5},{5,9},{9,13},{13,1},{2,6},{6,10},{... | collective-permute-start | bytes 417800 | tf_op jit(solution)/shard_map/ppermute | solution.py:90
  11.8 0.7 %dynamic-slice_bitcast_fusion.4 = (bf16[512,16]{0,1:T(8,128)(2,1)S(1)}, bf16[512,16]{0,1:T(8,128)(2,1)S(1)}) fusion(bf16[64,512]{1,0:T(8,128)(2,1)} %param.15, s32[]{:T(128)S(6)} %select_n.169, bf16[64,512]{1,0:T(8,128)(2,1)} %param.14), kind=kLoop, calls=%fused_computation.98 | loop fusion | bytes 65540 | tf_op jit(solution)/shard_map/transpose | solution.py:56
  12.5 0.3 fusion.61
  12.9 0.3 fusion.60
  13.2 0.3 copy-done.1
  13.5 0.3 fusion.8
  13.9 0.3 fusion.9
  14.2 0.8 %slice_select_fusion.6 = (f32[256,256]{1,0:T(8,128)S(1)}, f32[256,256]{1,0:T(8,128)}, f32[256,256]{1,0:T(8,128)}, f32[256,256]{1,0:T(8,128)S(1)}, f32[256,256]{1,0:T(8,128)S(1)}, /*index=5*/f32[256,256]{1,0:T(8,128)S(1)}) fusion(f32[512,256]{1,0:T(8,128)S(1)} %fusion.9, pred[256]{0:T(512)(128)(4,1)S(1)} %iota_compare_fusion, f32[512,256]{1,0:T(8,128)S(1)} %fusion.8), kind=kLoop, calls=%fused_computation.81 | loop fusion | flops 262144 | bytes 2621696 | tf_op jit(solution)/shard_map/jit(_where)/select_n | solution.py:62
  15.1 0.2 copy.43
  15.2 6.5 %collective-permute-done.1 = bf16[272,256]{1,0:T(8,128)(2,1)S(1)} collective-permute-done((bf16[272,256]{1,0:T(8,128)(2,1)S(1)}, bf16[272,256]{1,0:T(8,128)(2,1)S(1)}, u32[]{:S(2)}, u32[]{:S(2)}) %collective-permute-start.1) | collective-permute-done | bytes 139296 | tf_op jit(solution)/shard_map/ppermute | solution.py:90
  21.7 0.2 copy.44
  21.9 0.7 constant_dynamic-update-slice_fusion.5
  22.6 1.1 %copy.45 = bf16[1,272,256]{1,2,0:T(8,128)(2,1)S(1)} copy(bf16[1,272,256]{2,1,0:T(8,128)(2,1)} %bitcast.9) | data formatting | bytes 278528 | tf_op jit(solution)/shard_map/stack | solution.py:94
  23.7 0.7 constant_dynamic-update-slice_fusion.4
  24.3 0.7 constant_dynamic-update-slice_fusion.3
  25.0 0.7 dynamic-slice_dynamic-update-slice_fusion
  25.7 0.7 constant_dynamic-update-slice_fusion.2
  26.4 0.7 constant_dynamic-update-slice_fusion.1
  27.1 0.7 constant_dynamic-update-slice_fusion
  27.8 0.7 dynamic-slice_dynamic-update-slice_fusion.1
  28.5 1.1 %convert_bitcast_fusion = (f32[4,32,8,128]{3,2,1,0:T(8,128)S(1)}, bf16[4,32,8,128]{3,2,1,0:T(8,128)(2,1)S(1)}) fusion(bf16[8,272,256]{1,2,0:T(8,128)(2,1)} %dynamic-slice_dynamic-update-slice_fusion.1, s32[]{:T(128)S(6)} %select_n.166, s32[]{:T(128)S(6)} %add.238), kind=kLoop, calls=%fused_computation.70 | loop fusion | flops 131072 | bytes 1310728
  29.6 1.0 %constant_dynamic-slice_fusion = bf16[4,16,256]{1,2,0:T(8,128)(2,1)S(1)} fusion(bf16[8,272,256]{1,2,0:T(8,128)(2,1)} %dynamic-slice_dynamic-update-slice_fusion.1, s32[]{:T(128)S(6)} %select_n.166, s32[]{:T(128)S(6)} %add.237), kind=kLoop, calls=%fused_computation.103 | loop fusion | bytes 65544 | tf_op jit(solution)/shard_map/slice | solution.py:108
  30.8 0.5 fusion.39
  31.3 0.5 fusion.7
  31.8 0.4 copy-done.4
  32.3 0.2 fusion.30
  32.5 0.3 copy-done
  32.9 0.5 fusion.44
  33.4 0.5 convolution_add_fusion.8
  33.9 0.5 copy-done.3
  34.4 0.5 fusion.6
  34.9 0.1 broadcast_select_fusion.1
  35.1 0.5 fusion.38
  35.5 0.5 fusion.5
  36.0 0.2 fusion.34
  36.3 0.5 fusion.45
  36.7 0.5 convolution_add_fusion.5
  37.3 0.5 fusion.4
  37.8 0.1 fusion.28
  37.9 0.1 copy.70
  38.1 0.2 collective-permute-start.3
  38.2 1.5 %fusion.22 = f32[128,2048]{1,0:T(8,128)S(1)} fusion(bf16[1024,4096]{1,0:T(8,128)(2,1)} %param.16, s32[]{:T(128)S(6)} %select_n.181, s32[]{:T(128)S(6)} %select_n.182, bf16[4,128,256]{2,1,0:T(8,128)(2,1)S(1)} %bitcast.89, s32[]{:T(128)S(6)} %select_n.165), kind=kOutput, calls=%fused_computation.42 | convolution fusion | flops 134217728 | bytes 2162700 | tf_op jit(solution)/shard_map/dot_general | solution.py:36
  39.8 1.5 %fusion.16 = f32[128,2048]{1,0:T(8,128)S(1)} fusion(bf16[1024,4096]{1,0:T(8,128)(2,1)} %param.16, s32[]{:T(128)S(6)} %select_n.181, s32[]{:T(128)S(6)} %select_n.189, bf16[4,128,256]{2,1,0:T(8,128)(2,1)S(1)} %bitcast.90, s32[]{:T(128)S(6)} %select_n.165), kind=kOutput, calls=%fused_computation.36 | convolution fusion | flops 134217728 | bytes 2162700 | tf_op jit(solution)/shard_map/dot_general | solution.py:36
  41.3 2.0 %collective-permute-start.5 = (bf16[128,256]{1,0:T(8,128)(2,1)S(1)}, bf16[128,256]{1,0:T(8,128)(2,1)S(1)}, u32[]{:S(2)}, u32[]{:S(2)}) collective-permute-start(bf16[128,256]{1,0:T(8,128)(2,1)S(1)} %get-tuple-element.23), channel_id=1, source_target_pairs={{0,8},{4,12},{8,0},{12,4},{1,9},{5,13},{9,1},{13,5},{2,10},{6,14},... | collective-permute-start | bytes 196616 | tf_op jit(solution)/shard_map/ppermute | solution.py:90
  43.3 2.9 %collective-permute-start.4 = (bf16[128,256]{1,0:T(8,128)(2,1)S(1)}, bf16[128,256]{1,0:T(8,128)(2,1)S(1)}, u32[]{:S(2)}, u32[]{:S(2)}) collective-permute-start(bf16[128,256]{1,0:T(8,128)(2,1)S(1)} %get-tuple-element.22), channel_id=1, source_target_pairs={{0,12},{4,0},{8,4},{12,8},{1,13},{5,1},{9,5},{13,9},{2,14},{6,2},{... | collective-permute-start | bytes 196616 | tf_op jit(solution)/shard_map/ppermute | solution.py:90
  46.2 1.5 %convolution_add_fusion.1 = f32[128,2048]{1,0:T(8,128)S(1)} fusion(f32[128,2048]{1,0:T(8,128)S(1)} %fusion.16, bf16[128,256]{1,0:T(8,128)(2,1)S(1)} %collective-permute-done.3, bf16[1024,4096]{1,0:T(8,128)(2,1)} %param.16, s32[]{:T(128)S(6)} %select_n.184, s32[]{:T(128)S(6)} %select_n.189), kind=kOutput, calls=%fused_computation.2 | convolution fusion | flops 134479872 | bytes 3211272 | tf_op jit(solution)/shard_map/dot_general | solution.py:36
  47.8 1.5 %fusion.12 = f32[128,2048]{1,0:T(8,128)S(1)} fusion(bf16[128,256]{1,0:T(8,128)(2,1)S(1)} %collective-permute-done.5, bf16[1024,4096]{1,0:T(8,128)(2,1)} %param.16, s32[]{:T(128)S(6)} %select_n.188, s32[]{:T(128)S(6)} %select_n.189), kind=kOutput, calls=%fused_computation.32 | convolution fusion | flops 134217728 | bytes 2162696 | tf_op jit(solution)/shard_map/dot_general | solution.py:36
  49.3 1.5 %fusion.3 = bf16[128,2048]{1,0:T(8,128)(2,1)S(1)} fusion(f32[128,2048]{1,0:T(8,128)S(1)} %fusion.12, f32[128,2048]{1,0:T(8,128)S(1)} %convolution_add_fusion.1, bf16[128,256]{1,0:T(8,128)(2,1)S(1)} %collective-permute-done.4, bf16[1024,4096]{1,0:T(8,128)(2,1)} %param.16, s32[]{:T(128)S(6)} %select_n.186, s32[]{:T(128)S(6)} %select_n.189), kind=kOutput, calls=%fused_computation.7 | convolution fusion | flops 135004160 | bytes 3735560 | tf_op jit(solution)/shard_map/dot_general | solution.py:36
  51.0 1.5 %fusion.18 = f32[128,2048]{1,0:T(8,128)S(1)} fusion(bf16[128,256]{1,0:T(8,128)(2,1)S(1)} %collective-permute-done.5, bf16[1024,4096]{1,0:T(8,128)(2,1)} %param.16, s32[]{:T(128)S(6)} %select_n.188, s32[]{:T(128)S(6)} %select_n.182), kind=kOutput, calls=%fused_computation.38 | convolution fusion | flops 134217728 | bytes 2162696 | tf_op jit(solution)/shard_map/dot_general | solution.py:36
  52.5 1.5 %convolution_add_fusion.3 = f32[128,2048]{1,0:T(8,128)S(1)} fusion(f32[128,2048]{1,0:T(8,128)S(1)} %fusion.22, bf16[128,256]{1,0:T(8,128)(2,1)S(1)} %collective-permute-done.3, bf16[1024,4096]{1,0:T(8,128)(2,1)} %param.16, s32[]{:T(128)S(6)} %select_n.184, s32[]{:T(128)S(6)} %select_n.182), kind=kOutput, calls=%fused_computation.6 | convolution fusion | flops 134479872 | bytes 3211272 | tf_op jit(solution)/shard_map/dot_general | solution.py:36
  54.1 1.6 %fusion.59 = (bf16[128,2048]{1,0:T(8,128)(2,1)S(1)}, f32[128,2048]{1,0:T(8,128)S(1)}) fusion(bf16[128,2048]{1,0:T(8,128)(2,1)S(1)} %collective-permute-done.6, f32[128,2048]{1,0:T(8,128)S(1)} %fusion.18, f32[128,2048]{1,0:T(8,128)S(1)} %convolution_add_fusion.3, bf16[128,256]{1,0:T(8,128)(2,1)S(1)} %collective-permute-done.4, ...), kind=kOutput, calls=%fused_computation.121 | convolution fusion | flops 135528448 | bytes 5308424 | tf_op jit(solution)/shard_map/dot_general | solution.py:36
  55.7 1.6 %collective-permute-start.7 = (bf16[128,2048]{1,0:T(8,128)(2,1)S(1)}, bf16[128,2048]{1,0:T(8,128)(2,1)S(1)}, u32[]{:S(2)}, u32[]{:S(2)}) collective-permute-start(bf16[128,2048]{1,0:T(8,128)(2,1)S(1)} %get-tuple-element.32), channel_id=1, source_target_pairs={{0,2},{1,3},{2,0},{3,1},{4,6},{5,7},{6,4},{7,5},{8,10},{9,11},{10,... | collective-permute-start | bytes 1572872 | tf_op jit(solution)/shard_map/ppermute | solution.py:40
  57.2 12.8 %collective-permute-done.7 = bf16[128,2048]{1,0:T(8,128)(2,1)S(1)} collective-permute-done((bf16[128,2048]{1,0:T(8,128)(2,1)S(1)}, bf16[128,2048]{1,0:T(8,128)(2,1)S(1)}, u32[]{:S(2)}, u32[]{:S(2)}) %collective-permute-start.7) | collective-permute-done | bytes 524320 | tf_op jit(solution)/shard_map/ppermute | solution.py:40
  70.1 0.1 add_convert_fusion
  70.3 1.9 %collective-permute-done.8 = bf16[128,2048]{1,0:T(8,128)(2,1)S(1)} collective-permute-done((bf16[128,2048]{1,0:T(8,128)(2,1)S(1)}, bf16[128,2048]{1,0:T(8,128)(2,1)S(1)}, u32[]{:S(2)}, u32[]{:S(2)}) %collective-permute-start.8) | collective-permute-done | bytes 524320 | tf_op jit(solution)/shard_map/ppermute | solution.py:40
  72.2 1.2 %maximum_select_fusion = bf16[128,4096]{1,0:T(8,128)(2,1)} fusion(bf16[128,2048]{1,0:T(8,128)(2,1)S(1)} %collective-permute-done.8, bf16[128,2048]{1,0:T(8,128)(2,1)S(1)} %add_convert_fusion, pred[]{:T(512)S(6)} %eq.59), kind=kLoop, calls=%fused_computation.30 | loop fusion | flops 4718592 | bytes 2097153 | tf_op jit(solution)/shard_map/jit(_where)/select_n | solution.py:135
  (33 shorter events, 1.0 us)
Async XLA Ops:
  4.5 8.1 %copy-start.2 = (bf16[512,512]{1,0:T(8,128)(2,1)S(1)}, bf16[512,512]{1,0:T(8,128)(2,1)}, u32[]{:S(2)}) copy-start(bf16[512,512]{1,0:T(8,128)(2,1)} %constant.140.clone) | copy-start | bytes 1572868
  4.7 10.4 %collective-permute-start = (bf16[272,256]{1,0:T(8,128)(2,1)S(1)}, bf16[272,256]{1,0:T(8,128)(2,1)S(1)}, u32[]{:S(2)}, u32[]{:S(2)}) collective-permute-start(bf16[272,256]{1,0:T(8,128)(2,1)S(1)} %bitcast.93), channel_id=1, source_target_pairs={{0,12},{4,0},{8,4},{12,8},{1,13},{5,1},{9,5},{13,9},{2,14},{6,2},{... | collective-permute-start | bytes 417800 | tf_op jit(solution)/shard_map/ppermute | solution.py:90
  9.9 11.8 %collective-permute-start.1 = (bf16[272,256]{1,0:T(8,128)(2,1)S(1)}, bf16[272,256]{1,0:T(8,128)(2,1)S(1)}, u32[]{:S(2)}, u32[]{:S(2)}) collective-permute-start(bf16[272,256]{1,0:T(8,128)(2,1)S(1)} %bitcast.95), channel_id=1, source_target_pairs={{0,8},{4,12},{8,0},{12,4},{1,9},{5,13},{9,1},{13,5},{2,10},{6,14},... | collective-permute-start | bytes 417800 | tf_op jit(solution)/shard_map/ppermute | solution.py:90
  10.8 11.8 %collective-permute-start.2 = (bf16[272,256]{1,0:T(8,128)(2,1)}, bf16[272,256]{1,0:T(8,128)(2,1)}, u32[]{:S(2)}, u32[]{:S(2)}) collective-permute-start(bf16[272,256]{1,0:T(8,128)(2,1)} %bitcast.8), channel_id=1, source_target_pairs={{0,4},{4,8},{8,12},{12,0},{1,5},{5,9},{9,13},{13,1},{2,6},{6,10},{... | collective-permute-start | bytes 417800 | tf_op jit(solution)/shard_map/ppermute | solution.py:90
  12.5 1.0 %copy-start.1 = (bf16[512,512]{1,0:T(8,128)(2,1)S(1)}, bf16[512,512]{1,0:T(8,128)(2,1)}, u32[]{:S(2)}) copy-start(bf16[512,512]{1,0:T(8,128)(2,1)} %constant.141.clone) | copy-start | bytes 1572868
  31.3 1.0 %copy-start.4 = (f32[256,256]{1,0:T(8,128)S(1)}, f32[256,256]{1,0:T(8,128)}, u32[]{:S(2)}) copy-start(f32[256,256]{1,0:T(8,128)} %get-tuple-element.17) | copy-start | bytes 786436
  31.3 1.0 %copy-start.5 = (f32[256,256]{1,0:T(8,128)S(1)}, f32[256,256]{1,0:T(8,128)}, u32[]{:S(2)}) copy-start(f32[256,256]{1,0:T(8,128)} %get-tuple-element.21) | copy-start | bytes 786436
  31.8 1.1 %copy-start = (bf16[512,512]{1,0:T(8,128)(2,1)S(1)}, bf16[512,512]{1,0:T(8,128)(2,1)}, u32[]{:S(2)}) copy-start(bf16[512,512]{1,0:T(8,128)(2,1)} %constant.142.clone) | copy-start | bytes 1572868
  33.3 1.0 %copy-start.3 = (bf16[512,512]{1,0:T(8,128)(2,1)S(1)}, bf16[512,512]{1,0:T(8,128)(2,1)}, u32[]{:S(2)}) copy-start(bf16[512,512]{1,0:T(8,128)(2,1)} %constant.143.clone) | copy-start | bytes 1572868
  38.1 8.2 %collective-permute-start.3 = (bf16[128,256]{1,0:T(8,128)(2,1)S(1)}, bf16[128,256]{1,0:T(8,128)(2,1)S(1)}, u32[]{:S(2)}, u32[]{:S(2)}) collective-permute-start(bf16[128,256]{1,0:T(8,128)(2,1)S(1)} %get-tuple-element.24), channel_id=1, source_target_pairs={{0,4},{4,8},{8,12},{12,0},{1,5},{5,9},{9,13},{13,1},{2,6},{6,10},{... | collective-permute-start | bytes 196616 | tf_op jit(solution)/shard_map/ppermute | solution.py:90
  41.3 6.5 %collective-permute-start.5 = (bf16[128,256]{1,0:T(8,128)(2,1)S(1)}, bf16[128,256]{1,0:T(8,128)(2,1)S(1)}, u32[]{:S(2)}, u32[]{:S(2)}) collective-permute-start(bf16[128,256]{1,0:T(8,128)(2,1)S(1)} %get-tuple-element.23), channel_id=1, source_target_pairs={{0,8},{4,12},{8,0},{12,4},{1,9},{5,13},{9,1},{13,5},{2,10},{6,14},... | collective-permute-start | bytes 196616 | tf_op jit(solution)/shard_map/ppermute | solution.py:90
  43.3 6.0 %collective-permute-start.4 = (bf16[128,256]{1,0:T(8,128)(2,1)S(1)}, bf16[128,256]{1,0:T(8,128)(2,1)S(1)}, u32[]{:S(2)}, u32[]{:S(2)}) collective-permute-start(bf16[128,256]{1,0:T(8,128)(2,1)S(1)} %get-tuple-element.22), channel_id=1, source_target_pairs={{0,12},{4,0},{8,4},{12,8},{1,13},{5,1},{9,5},{13,9},{2,14},{6,2},{... | collective-permute-start | bytes 196616 | tf_op jit(solution)/shard_map/ppermute | solution.py:90
  50.9 3.2 %collective-permute-start.6 = (bf16[128,2048]{1,0:T(8,128)(2,1)S(1)}, bf16[128,2048]{1,0:T(8,128)(2,1)S(1)}, u32[]{:S(2)}, u32[]{:S(2)}) collective-permute-start(bf16[128,2048]{1,0:T(8,128)(2,1)S(1)} %fusion.3), channel_id=1, source_target_pairs={{0,1},{1,0},{2,3},{3,2},{4,5},{5,4},{6,7},{7,6},{8,9},{9,8},{10,11... | collective-permute-start | bytes 1572872 | tf_op jit(solution)/shard_map/ppermute | solution.py:40
  55.7 14.4 %collective-permute-start.7 = (bf16[128,2048]{1,0:T(8,128)(2,1)S(1)}, bf16[128,2048]{1,0:T(8,128)(2,1)S(1)}, u32[]{:S(2)}, u32[]{:S(2)}) collective-permute-start(bf16[128,2048]{1,0:T(8,128)(2,1)S(1)} %get-tuple-element.32), channel_id=1, source_target_pairs={{0,2},{1,3},{2,0},{3,1},{4,6},{5,7},{6,4},{7,5},{8,10},{9,11},{10,... | collective-permute-start | bytes 1572872 | tf_op jit(solution)/shard_map/ppermute | solution.py:40
  70.2 2.0 %collective-permute-start.8 = (bf16[128,2048]{1,0:T(8,128)(2,1)S(1)}, bf16[128,2048]{1,0:T(8,128)(2,1)S(1)}, u32[]{:S(2)}, u32[]{:S(2)}) collective-permute-start(bf16[128,2048]{1,0:T(8,128)(2,1)S(1)} %add_convert_fusion), channel_id=1, source_target_pairs={{0,1},{1,0},{2,3},{3,2},{4,5},{5,4},{6,7},{7,6},{8,9},{9,8},{10,11... | collective-permute-start | bytes 1572872 | tf_op jit(solution)/shard_map/ppermute | solution.py:40

commit v7 on v6

--- a/solution.py
+++ b/solution.py
@@ -83,26 +83,22 @@
         order = [0] + [k for k in (1, nseq - 1) if k < nseq] + [k for k in range(2, nseq - 1)]
         order = list(dict.fromkeys(order))
 
-        def exchange(blocks):
-            got = {0: lax.dynamic_index_in_dim(blocks, me, 0, keepdims=False)}
-            for k in order[1:]:
-                piece = lax.dynamic_index_in_dim(blocks, (me + k) % nseq, 0, keepdims=False)
-                got[k] = lax.ppermute(piece, "seq", [(i, (i + k) % nseq) for i in range(nseq)])
-            return got
-
-        def in_source_order(got):
-            by_shift = jnp.stack([got[k] for k in reversed(range(nseq))])
-            return jnp.roll(by_shift, me + 1, axis=0)
+        def rotated(got):
+            return jnp.concatenate([got[(nseq - j) % nseq] for j in range(nseq)], axis=0)
 
         first_input = (first_gate.astype(F32) * value.astype(F32)).astype(BF16)
-        first_input = first_input.reshape(rows, nseq, per).transpose(1, 0, 2)
-        gate_blocks = second_gate.reshape(rows, nseq, per).transpose(1, 0, 2)
         id_rows = -(-rows // per)
         pad_rows = -(-id_rows // 16) * 16
-        ids = jnp.pad(segment_ids.astype(BF16), (0, pad_rows * per - rows)).reshape(1, pad_rows, per)
-        payload = jnp.concatenate(
-            [first_input, gate_blocks, jnp.broadcast_to(ids, (nseq, pad_rows, per))], axis=1)
-        got = in_source_order(exchange(payload))
+        ids = jnp.pad(segment_ids.astype(BF16), (0, pad_rows * per - rows)).reshape(pad_rows, per)
+
+        def block_for(dest):
+            cols = lambda x: lax.dynamic_slice_in_dim(x, dest * per, per, 1)
+            return jnp.concatenate([cols(first_input), cols(second_gate), ids], axis=0)
+
+        got = {0: block_for(me)}
+        for k in order[1:]:
+            got[k] = lax.ppermute(block_for((me + k) % nseq), "seq", [(i, (i + k) % nseq) for i in range(nseq)])
+        got = rotated(got).reshape(nseq, 2 * rows + pad_rows, per)
         first_cols = got[:, :rows].reshape(nseq * rows, per)
         gate_cols = got[:, rows:2 * rows].reshape(nseq * rows, per)
         segs = got[:, 2 * rows:].reshape(nseq, pad_rows * per)[:, :rows].reshape(nseq * rows)
@@ -111,7 +107,10 @@
         first_mix = long_conv(spectrum(first_filter), first_cols)
         second_input = (gate_cols.astype(F32) * first_mix).astype(BF16)
         second_mix = long_conv(spectrum(second_filter), second_input).astype(BF16)
-        mix_pieces = exchange(second_mix.reshape(nseq, rows, per))
+        mix_pieces = {0: second_mix[:rows]}
+        for k in order[1:]:
+            mix_pieces[k] = lax.ppermute(second_mix[k * rows:(k + 1) * rows], "seq",
+                                         [(i, (i + k) % nseq) for i in range(nseq)])
         out_cols = out_weight.shape[1]
 
         def project(cols_lo, width):

time: 74.2 us -> 63.8 us (0.86)
  local copies, waits for them, and re-layouts: 15.3 us -> 4.21 us
  other arithmetic: 4.93 us -> 8.42 us
  matrix products: 18.5 us -> 15.3 us
  starting transfers between devices: 13 us -> 14.4 us
  waiting for transfers between devices: 21.2 us -> 20.4 us
    unnamed x23 -> x22, local copies, waits for them, and re-layouts: 9.97 us -> 2.15 us
    dot_general x22, matrix products: 18.5 us -> 15.3 us  [mm(): return jnp.dot(a, b, preferred_element_type=F32)]
    ppermute x6, waiting for transfers between devices: 6.5 us -> 4.86 us  [the longest x3 3.3 us: local(): lax.ppermute(block_for((me + k) % nseq), 'seq', [(i, (i + k) % nseq) for...]
    ppermute x6, starting transfers between devices: 11.3 us -> 12.7 us  [the longest x3 6.6 us: local(): lax.ppermute(second_mix[k * rows:(k + 1) * rows], 'seq', [(i, (i + k) % n...]
    another operation x3 -> x0, local copies, waits for them, and re-layouts: 1.39 us -> none  [in_source_order(): by_shift = jnp.stack([got[k] for k in reversed(range(nseq))])]
    sub x2, other arithmetic: 0.46 us -> 1.84 us  [long_conv(): y = jnp.concatenate([xr * a - xi * b, xr * b + xi * d], axis=0)]
    unnamed x1, other arithmetic: 1.08 us -> 0.01 us
    select_n x2, other arithmetic: 0.2 us -> 1.28 us  [long_conv(): jnp.where(in0, field, zero)]
  transfers between devices with their start and end apart: 9 -> 9, of which waited for: 3 -> 5; matrix products, arithmetic and copies ran while one was open for 19% -> 15% of each run, Pallas kernels for 0% -> 0%
where the time goes in v7:
time: 63.8 us; the launch traced here: 63.3 us
  waiting for transfers between devices  20.4 us (32%)
  matrix products  15.3 us (24%)
  starting transfers between devices  14.4 us (23%)
  other arithmetic  8.42 us (13%)
  local copies, waits for them, and re-layouts  4.21 us (7%)
    ppermute x3, waiting for transfers between devices, swap(): return lax.ppermute(x, 'chan', [(c, c ^ bit) for c in range(4)])  15.6 us
    dot_general x22, matrix products, mm(): return jnp.dot(a, b, preferred_element_type=F32)  15.3 us
    ppermute x3, starting transfers between devices, local(): lax.ppermute(second_mix[k * rows:(k + 1) * rows], 'seq', [(i, (i + k) % n...  6.6 us
    ppermute x3, starting transfers between devices, local(): lax.ppermute(block_for((me + k) % nseq), 'seq', [(i, (i + k) % nseq) for...  6.14 us
    ppermute x3, waiting for transfers between devices, local(): lax.ppermute(block_for((me + k) % nseq), 'seq', [(i, (i + k) % nseq) for...  3.3 us
    unnamed x22, local copies, waits for them, and re-layouts  2.15 us
    sub x2, other arithmetic, long_conv(): y = jnp.concatenate([xr * a - xi * b, xr * b + xi * d], axis=0)  1.84 us
    ppermute x3, starting transfers between devices, swap(): return lax.ppermute(x, 'chan', [(c, c ^ bit) for c in range(4)])  1.7 us
  transfers between devices with their start and end apart: 9, of which 5 were waited for; matrix products, arithmetic and copies ran while one was open for 15% of the time, Pallas kernels for 0%

profile of v7, /device:TPU:0, one launch (start us, length us, event | category | flops | bytes accessed | tf_op | source)
XLA Modules:
  0.0 63.3 jit_solution(8431312435303230362)
XLA Ops:
  0.0 0.7 %convert_element_type.56 = bf16[128]{0:T(256)(128)(2,1)S(1)} convert(s32[128]{0:T(128)} %param.17) | non-fusion elementwise | flops 128 | bytes 768 | tf_op jit(solution)/shard_map/convert_element_type | solution.py:92
  0.7 1.1 %multiply_convert_fusion = bf16[128,1024]{1,0:T(8,128)(2,1)S(1)} fusion(bf16[128,1024]{1,0:T(8,128)(2,1)} %param.11, bf16[128,1024]{1,0:T(8,128)(2,1)} %param.12), kind=kLoop, calls=%fused_computation.69 | loop fusion | flops 524288 | bytes 786432 | tf_op jit(solution)/shard_map/convert_element_type | solution.py:89
  1.9 0.0 copy-start.1
  1.9 1.0 %constant_dynamic-slice_fusion = (bf16[128,256]{1,0:T(8,128)(2,1)S(1)}, bf16[128,256]{1,0:T(8,128)(2,1)S(1)}, bf16[1088,256]{1,0:T(8,128)(2,1)S(1)}, bf16[128,256]{1,0:T(8,128)(2,1)S(1)}) fusion(bf16[128,1024]{1,0:T(8,128)(2,1)} %param.13, s32[]{:T(128)S(6)} %select_n.147, s32[]{:T(128)S(6)} %select_n.143, bf16[1088,256]{1,0:T(8,128)(2,1)S(1)} %get-tuple-element.27, ...), kind=kLoop, calls=%fused_computation.97 | loop fusion | bytes 524304 | tf_op jit(solution)/shard_map/dynamic_slice | solution.py:95
  3.0 5.1 %collective-permute-start = (bf16[272,256]{1,0:T(8,128)(2,1)S(1)}, bf16[272,256]{1,0:T(8,128)(2,1)S(1)}, u32[]{:S(2)}, u32[]{:S(2)}) collective-permute-start(bf16[272,256]{1,0:T(8,128)(2,1)S(1)} %get-tuple-element.36), channel_id=1, source_target_pairs={{0,12},{4,0},{8,4},{12,8},{1,13},{5,1},{9,5},{13,9},{2,14},{6,2},{... | collective-permute-start | bytes 417800 | tf_op jit(solution)/shard_map/ppermute | solution.py:100
  8.1 0.0 collective-permute-start.1
  8.1 1.0 %collective-permute-start.2 = (bf16[272,256]{1,0:T(8,128)(2,1)S(1)}, bf16[272,256]{1,0:T(8,128)(2,1)S(1)}, u32[]{:S(2)}, u32[]{:S(2)}) collective-permute-start(bf16[272,256]{1,0:T(8,128)(2,1)S(1)} %get-tuple-element.34), channel_id=1, source_target_pairs={{0,4},{4,8},{8,12},{12,0},{1,5},{5,9},{9,13},{13,1},{2,6},{6,10},{... | collective-permute-start | bytes 417800 | tf_op jit(solution)/shard_map/ppermute | solution.py:100
  9.1 0.7 %dynamic-slice_bitcast_fusion = (bf16[512,16]{0,1:T(8,128)(2,1)S(1)}, bf16[512,16]{0,1:T(8,128)(2,1)S(1)}) fusion(bf16[64,512]{1,0:T(8,128)(2,1)} %param.15, s32[]{:T(128)S(6)} %select_n.150, bf16[64,512]{1,0:T(8,128)(2,1)} %param.14), kind=kLoop, calls=%fused_computation.89 | loop fusion | bytes 65540 | tf_op jit(solution)/shard_map/transpose | solution.py:56
  9.9 1.4 %fusion.57 = f32[256,512]{0,1:T(8,128)S(1)} fusion(bf16[512,256]{0,1:T(8,128)(2,1)S(1)} %bitcast.61, bf16[512,512]{1,0:T(8,128)(2,1)} %constant.100.clone), kind=kOutput, calls=%fused_computation.118 | convolution fusion | flops 134217728 | bytes 1310720 | tf_op jit(solution)/shard_map/dot_general | solution.py:36
  11.3 1.4 %fusion.58 = f32[256,512]{0,1:T(8,128)S(1)} fusion(bf16[512,256]{0,1:T(8,128)(2,1)S(1)} %bitcast.63, bf16[512,512]{1,0:T(8,128)(2,1)} %constant.100.clone), kind=kOutput, calls=%fused_computation.119 | convolution fusion | flops 134217728 | bytes 1310720 | tf_op jit(solution)/shard_map/dot_general | solution.py:36
  12.7 1.4 %fusion.9 = f32[512,256]{1,0:T(8,128)S(1)} fusion(f32[256,512]{0,1:T(8,128)S(1)} %fusion.57, bf16[512,256]{0,1:T(8,128)(2,1)S(1)} %bitcast.62, bf16[512,512]{1,0:T(8,128)(2,1)} %constant.101.clone), kind=kOutput, calls=%fused_computation.25 | convolution fusion | flops 134348800 | bytes 1835008 | tf_op jit(solution)/shard_map/dot_general | solution.py:36
  14.1 0.0 copy-start
  14.1 1.4 %fusion.8 = f32[512,256]{1,0:T(8,128)S(1)} fusion(f32[256,512]{0,1:T(8,128)S(1)} %fusion.58, bf16[512,256]{0,1:T(8,128)(2,1)S(1)} %bitcast.64, bf16[512,512]{1,0:T(8,128)(2,1)} %constant.101.clone), kind=kOutput, calls=%fused_computation.23 | convolution fusion | flops 134348800 | bytes 1835008 | tf_op jit(solution)/shard_map/dot_general | solution.py:36
  15.5 1.1 %slice_select_fusion.6 = (f32[256,256]{1,0:T(8,128)}, f32[256,256]{1,0:T(8,128)}, f32[256,256]{1,0:T(8,128)}, f32[256,256]{1,0:T(8,128)S(1)}, f32[256,256]{1,0:T(8,128)}, /*index=5*/f32[256,256]{1,0:T(8,128)}) fusion(f32[512,256]{1,0:T(8,128)S(1)} %fusion.9, pred[256]{0:T(512)(128)(4,1)S(1)} %iota_compare_fusion, f32[512,256]{1,0:T(8,128)S(1)} %fusion.8), kind=kLoop, calls=%fused_computation.79 | loop fusion | flops 262144 | bytes 2621696 | tf_op jit(solution)/shard_map/jit(_where)/select_n | solution.py:62
  16.6 0.0 collective-permute-done
  16.7 3.3 %collective-permute-done.1 = bf16[272,256]{1,0:T(8,128)(2,1)S(1)} collective-permute-done((bf16[272,256]{1,0:T(8,128)(2,1)S(1)}, bf16[272,256]{1,0:T(8,128)(2,1)S(1)}, u32[]{:S(2)}, u32[]{:S(2)}) %collective-permute-start.1) | collective-permute-done | bytes 139296 | tf_op jit(solution)/shard_map/ppermute | solution.py:100
  20.0 0.0 collective-permute-done.2
  20.0 0.9 %slice_convert_fusion = (f32[4,128,256]{2,1,0:T(8,128)}, bf16[4,128,256]{2,1,0:T(8,128)(2,1)S(1)}) fusion(bf16[4,272,256]{2,1,0:T(8,128)(2,1)S(1)} %bitcast.68), kind=kLoop, calls=%fused_computation.72 | loop fusion | flops 131072 | bytes 1310720 | tf_op jit(solution)/shard_map/convert_element_type | solution.py:108
  20.9 0.0 copy-start.3
  20.9 0.1 copy.32
  21.1 0.0 copy-done.2
  21.1 0.5 fusion.39
  21.6 0.0 copy-done.1
  21.6 0.5 fusion.7
  22.1 1.6 %fusion.30 = (f32[256,512]{1,0:T(8,128)S(1)}, f32[256,512]{1,0:T(8,128)S(1)}) fusion(f32[256,256]{1,0:T(8,128)} %get-tuple-element.18, f32[256,256]{1,0:T(8,128)} %get-tuple-element.14, f32[512,512]{1,0:T(8,128)S(1)} %fusion.7, f32[256,256]{1,0:T(8,128)} %get-tuple-element.13), kind=kLoop, calls=%fused_computation.55 | loop fusion | flops 1179648 | bytes 2883584 | tf_op jit(solution)/shard_map/sub | solution.py:74
  23.7 0.0 copy-done
  23.7 0.5 fusion.42
  24.2 1.5 %convolution_add_fusion.8 = f32[512,512]{1,0:T(8,128)} fusion(f32[512,512]{1,0:T(8,128)S(1)} %fusion.42, bf16[512,512]{1,0:T(8,128)(2,1)S(1)} %copy-done, f32[256,512]{1,0:T(8,128)S(1)} %get-tuple-element.10, f32[256,512]{1,0:T(8,128)S(1)} %get-tuple-element.9), kind=kOutput, calls=%fused_computation.19 | convolution fusion | flops 269746176 | bytes 3670016 | tf_op jit(solution)/shard_map/dot_general | solution.py:36
  25.7 2.1 %copy.35 = f32[4,128,256]{1,0,2:T(4,128)} copy(f32[4,128,256]{2,1,0:T(8,128)} %get-tuple-element.11) | data formatting | bytes 1048576
  27.7 0.0 copy-done.3
  27.7 1.8 %fusion.6 = f32[512,512]{0,1:T(8,128)S(1)} fusion(f32[512,512]{1,0:T(8,128)} %convolution_add_fusion.8, bf16[512,512]{1,0:T(8,128)(2,1)S(1)} %copy-done.3, f32[256,512]{1,0:T(8,128)S(1)} %get-tuple-element.10, f32[256,512]{1,0:T(8,128)S(1)} %get-tuple-element.9), kind=kOutput, calls=%fused_computation.18 | convolution fusion | flops 269484032 | bytes 3670016 | tf_op jit(solution)/shard_map/dot_general | solution.py:36
  29.5 1.2 %broadcast_select_fusion.2 = (bf16[512,256]{0,1:T(8,128)(2,1)S(1)}, bf16[512,256]{0,1:T(8,128)(2,1)S(1)}) fusion(pred[512]{0:T(512)(128)(4,1)S(1)} %get-tuple-element.33, f32[512,512]{0,1:T(8,128)S(1)} %fusion.6, pred[512]{0:T(512)(128)(4,1)S(1)} %get-tuple-element.32, f32[32,8,4,128]{3,2,1,0:T(4,128)} %bitcast.65), kind=kLoop, calls=%fused_computation.75 | loop fusion | flops 786432 | bytes 2098176 | tf_op jit(solution)/shard_map/jit(_where)/select_n | solution.py:70
  30.8 0.5 fusion.38
  31.2 0.0 slice-start
  31.3 0.5 fusion.5
  31.8 0.2 fusion.34
  32.0 0.5 fusion.43
  32.5 0.0 slice-start.1
  32.5 0.5 convolution_add_fusion.5
  33.0 0.5 fusion.4
  33.5 0.1 fusion.28
  33.6 2.8 %collective-permute-start.5 = (bf16[128,256]{0,1:T(8,128)(2,1)S(1)}, bf16[128,256]{0,1:T(8,128)(2,1)S(1)}, u32[]{:S(2)}, u32[]{:S(2)}) collective-permute-start(bf16[128,256]{0,1:T(8,128)(2,1)S(1)} %get-tuple-element.20), channel_id=1, source_target_pairs={{0,8},{4,12},{8,0},{12,4},{1,9},{5,13},{9,1},{13,5},{2,10},{6,14},... | collective-permute-start | bytes 196616 | tf_op jit(solution)/shard_map/ppermute | solution.py:112
  36.4 0.0 collective-permute-start.3
  36.4 3.8 %collective-permute-start.4 = (bf16[128,256]{0,1:T(8,128)(2,1)S(1)}, bf16[128,256]{0,1:T(8,128)(2,1)S(1)}, u32[]{:S(2)}, u32[]{:S(2)}) collective-permute-start(bf16[128,256]{0,1:T(8,128)(2,1)S(1)} %get-tuple-element.19), channel_id=1, source_target_pairs={{0,12},{4,0},{8,4},{12,8},{1,13},{5,1},{9,5},{13,9},{2,14},{6,2},{... | collective-permute-start | bytes 196616 | tf_op jit(solution)/shard_map/ppermute | solution.py:112
  40.2 0.0 slice-done.1
  40.2 0.3 fusion.16
  40.6 0.3 fusion.22
  40.9 1.6 %collective-permute-done.3 = bf16[128,256]{0,1:T(8,128)(2,1)S(1)} collective-permute-done((bf16[128,256]{0,1:T(8,128)(2,1)S(1)}, bf16[128,256]{0,1:T(8,128)(2,1)S(1)}, u32[]{:S(2)}, u32[]{:S(2)}) %collective-permute-start.3) | collective-permute-done | bytes 65568 | tf_op jit(solution)/shard_map/ppermute | solution.py:112
  42.5 0.3 convolution_add_fusion.1
  42.8 0.0 collective-permute-done.5
  42.8 0.3 fusion.12
  43.2 0.0 collective-permute-done.4
  43.2 0.4 fusion.3
  43.6 0.1 collective-permute-start.6
  43.6 0.3 fusion.18
  44.0 0.3 convolution_add_fusion.3
  44.3 1.2 %collective-permute-done.6 = bf16[128,2048]{1,0:T(8,128)(2,1)S(1)} collective-permute-done((bf16[128,2048]{1,0:T(8,128)(2,1)S(1)}, bf16[128,2048]{1,0:T(8,128)(2,1)S(1)}, u32[]{:S(2)}, u32[]{:S(2)}) %collective-permute-start.6) | collective-permute-done | bytes 524320 | tf_op jit(solution)/shard_map/ppermute | solution.py:40
  45.5 0.4 fusion.56
  45.9 1.6 %collective-permute-start.7 = (bf16[128,2048]{1,0:T(8,128)(2,1)S(1)}, bf16[128,2048]{1,0:T(8,128)(2,1)S(1)}, u32[]{:S(2)}, u32[]{:S(2)}) collective-permute-start(bf16[128,2048]{1,0:T(8,128)(2,1)S(1)} %get-tuple-element.40), channel_id=1, source_target_pairs={{0,2},{1,3},{2,0},{3,1},{4,6},{5,7},{6,4},{7,5},{8,10},{9,11},{10,... | collective-permute-start | bytes 1572872 | tf_op jit(solution)/shard_map/ppermute | solution.py:40
  47.5 12.5 %collective-permute-done.7 = bf16[128,2048]{1,0:T(8,128)(2,1)S(1)} collective-permute-done((bf16[128,2048]{1,0:T(8,128)(2,1)S(1)}, bf16[128,2048]{1,0:T(8,128)(2,1)S(1)}, u32[]{:S(2)}, u32[]{:S(2)}) %collective-permute-start.7) | collective-permute-done | bytes 524320 | tf_op jit(solution)/shard_map/ppermute | solution.py:40
  60.0 0.1 add_convert_fusion
  60.1 0.1 collective-permute-start.8
  60.2 1.9 %collective-permute-done.8 = bf16[128,2048]{1,0:T(8,128)(2,1)S(1)} collective-permute-done((bf16[128,2048]{1,0:T(8,128)(2,1)S(1)}, bf16[128,2048]{1,0:T(8,128)(2,1)S(1)}, u32[]{:S(2)}, u32[]{:S(2)}) %collective-permute-start.8) | collective-permute-done | bytes 524320 | tf_op jit(solution)/shard_map/ppermute | solution.py:40
  62.0 1.2 %maximum_select_fusion = bf16[128,4096]{1,0:T(8,128)(2,1)} fusion(bf16[128,2048]{1,0:T(8,128)(2,1)S(1)} %collective-permute-done.8, bf16[128,2048]{1,0:T(8,128)(2,1)S(1)} %add_convert_fusion, pred[]{:T(512)S(6)} %eq.53), kind=kLoop, calls=%fused_computation.30 | loop fusion | flops 4718592 | bytes 2097153 | tf_op jit(solution)/shard_map/jit(_where)/select_n | solution.py:134
  (24 shorter events, 0.3 us)
Async XLA Ops:
  0.0 21.1 %copy-start.2 = (bf16[512,512]{1,0:T(8,128)(2,1)S(1)}, bf16[512,512]{1,0:T(8,128)(2,1)}, u32[]{:S(2)}) copy-start(bf16[512,512]{1,0:T(8,128)(2,1)} %constant.100.clone) | copy-start | bytes 1572868
  1.9 19.7 %copy-start.1 = (bf16[512,512]{1,0:T(8,128)(2,1)S(1)}, bf16[512,512]{1,0:T(8,128)(2,1)}, u32[]{:S(2)}) copy-start(bf16[512,512]{1,0:T(8,128)(2,1)} %constant.101.clone) | copy-start | bytes 1572868
  3.0 13.7 %collective-permute-start = (bf16[272,256]{1,0:T(8,128)(2,1)S(1)}, bf16[272,256]{1,0:T(8,128)(2,1)S(1)}, u32[]{:S(2)}, u32[]{:S(2)}) collective-permute-start(bf16[272,256]{1,0:T(8,128)(2,1)S(1)} %get-tuple-element.36), channel_id=1, source_target_pairs={{0,12},{4,0},{8,4},{12,8},{1,13},{5,1},{9,5},{13,9},{2,14},{6,2},{... | collective-permute-start | bytes 417800 | tf_op jit(solution)/shard_map/ppermute | solution.py:100
  8.1 11.8 %collective-permute-start.1 = (bf16[272,256]{1,0:T(8,128)(2,1)S(1)}, bf16[272,256]{1,0:T(8,128)(2,1)S(1)}, u32[]{:S(2)}, u32[]{:S(2)}) collective-permute-start(bf16[272,256]{1,0:T(8,128)(2,1)S(1)} %get-tuple-element.35), channel_id=1, source_target_pairs={{0,8},{4,12},{8,0},{12,4},{1,9},{5,13},{9,1},{13,5},{2,10},{6,14},... | collective-permute-start | bytes 417800 | tf_op jit(solution)/shard_map/ppermute | solution.py:100
  8.1 11.8 %collective-permute-start.2 = (bf16[272,256]{1,0:T(8,128)(2,1)S(1)}, bf16[272,256]{1,0:T(8,128)(2,1)S(1)}, u32[]{:S(2)}, u32[]{:S(2)}) collective-permute-start(bf16[272,256]{1,0:T(8,128)(2,1)S(1)} %get-tuple-element.34), channel_id=1, source_target_pairs={{0,4},{4,8},{8,12},{12,0},{1,5},{5,9},{9,13},{13,1},{2,6},{6,10},{... | collective-permute-start | bytes 417800 | tf_op jit(solution)/shard_map/ppermute | solution.py:100
  14.1 9.6 %copy-start = (bf16[512,512]{1,0:T(8,128)(2,1)S(1)}, bf16[512,512]{1,0:T(8,128)(2,1)}, u32[]{:S(2)}) copy-start(bf16[512,512]{1,0:T(8,128)(2,1)} %constant.102.clone) | copy-start | bytes 1572868
  20.9 6.8 %copy-start.3 = (bf16[512,512]{1,0:T(8,128)(2,1)S(1)}, bf16[512,512]{1,0:T(8,128)(2,1)}, u32[]{:S(2)}) copy-start(bf16[512,512]{1,0:T(8,128)(2,1)} %constant.103.clone) | copy-start | bytes 1572868
  27.7 4.0 %copy-start.4 = (f32[256,256]{1,0:T(8,128)S(1)}, f32[256,256]{1,0:T(8,128)}, u32[]{:S(2)}) copy-start(f32[256,256]{1,0:T(8,128)} %get-tuple-element.38) | copy-start | bytes 786436
  27.7 4.0 %copy-start.5 = (f32[256,256]{1,0:T(8,128)S(1)}, f32[256,256]{1,0:T(8,128)}, u32[]{:S(2)}) copy-start(f32[256,256]{1,0:T(8,128)} %get-tuple-element.39) | copy-start | bytes 786436
  31.2 9.0 %slice-start = ((s8[8388608]{0:T(1024)(128)(4,1)}), s8[4194304]{0:T(1024)(128)(4,1)S(1)}, s32[]{:S(2)}) async-start(s8[8388608]{0:T(1024)(128)(4,1)} %bitcast.59), calls=%async_computation | async-start | bytes 8388608
  32.5 7.8 %slice-start.1 = ((s8[8388608]{0:T(1024)(128)(4,1)}), s8[4194304]{0:T(1024)(128)(4,1)S(1)}, s32[]{:S(2)}) async-start(s8[8388608]{0:T(1024)(128)(4,1)} %bitcast.59), calls=%async_computation.1 | async-start | bytes 8388608
  33.6 9.2 %collective-permute-start.5 = (bf16[128,256]{0,1:T(8,128)(2,1)S(1)}, bf16[128,256]{0,1:T(8,128)(2,1)S(1)}, u32[]{:S(2)}, u32[]{:S(2)}) collective-permute-start(bf16[128,256]{0,1:T(8,128)(2,1)S(1)} %get-tuple-element.20), channel_id=1, source_target_pairs={{0,8},{4,12},{8,0},{12,4},{1,9},{5,13},{9,1},{13,5},{2,10},{6,14},... | collective-permute-start | bytes 196616 | tf_op jit(solution)/shard_map/ppermute | solution.py:112
  36.4 6.1 %collective-permute-start.3 = (bf16[128,256]{0,1:T(8,128)(2,1)S(1)}, bf16[128,256]{0,1:T(8,128)(2,1)S(1)}, u32[]{:S(2)}, u32[]{:S(2)}) collective-permute-start(bf16[128,256]{0,1:T(8,128)(2,1)S(1)} %get-tuple-element.21), channel_id=1, source_target_pairs={{0,4},{4,8},{8,12},{12,0},{1,5},{5,9},{9,13},{13,1},{2,6},{6,10},{... | collective-permute-start | bytes 196616 | tf_op jit(solution)/shard_map/ppermute | solution.py:112
  36.4 6.8 %collective-permute-start.4 = (bf16[128,256]{0,1:T(8,128)(2,1)S(1)}, bf16[128,256]{0,1:T(8,128)(2,1)S(1)}, u32[]{:S(2)}, u32[]{:S(2)}) collective-permute-start(bf16[128,256]{0,1:T(8,128)(2,1)S(1)} %get-tuple-element.19), channel_id=1, source_target_pairs={{0,12},{4,0},{8,4},{12,8},{1,13},{5,1},{9,5},{13,9},{2,14},{6,2},{... | collective-permute-start | bytes 196616 | tf_op jit(solution)/shard_map/ppermute | solution.py:112
  43.6 2.0 %collective-permute-start.6 = (bf16[128,2048]{1,0:T(8,128)(2,1)S(1)}, bf16[128,2048]{1,0:T(8,128)(2,1)S(1)}, u32[]{:S(2)}, u32[]{:S(2)}) collective-permute-start(bf16[128,2048]{1,0:T(8,128)(2,1)S(1)} %fusion.3), channel_id=1, source_target_pairs={{0,1},{1,0},{2,3},{3,2},{4,5},{5,4},{6,7},{7,6},{8,9},{9,8},{10,11... | collective-permute-start | bytes 1572872 | tf_op jit(solution)/shard_map/ppermute | solution.py:40
  45.9 14.0 %collective-permute-start.7 = (bf16[128,2048]{1,0:T(8,128)(2,1)S(1)}, bf16[128,2048]{1,0:T(8,128)(2,1)S(1)}, u32[]{:S(2)}, u32[]{:S(2)}) collective-permute-start(bf16[128,2048]{1,0:T(8,128)(2,1)S(1)} %get-tuple-element.40), channel_id=1, source_target_pairs={{0,2},{1,3},{2,0},{3,1},{4,6},{5,7},{6,4},{7,5},{8,10},{9,11},{10,... | collective-permute-start | bytes 1572872 | tf_op jit(solution)/shard_map/ppermute | solution.py:40
  60.1 2.0 %collective-permute-start.8 = (bf16[128,2048]{1,0:T(8,128)(2,1)S(1)}, bf16[128,2048]{1,0:T(8,128)(2,1)S(1)}, u32[]{:S(2)}, u32[]{:S(2)}) collective-permute-start(bf16[128,2048]{1,0:T(8,128)(2,1)S(1)} %add_convert_fusion), channel_id=1, source_target_pairs={{0,1},{1,0},{2,3},{3,2},{4,5},{5,4},{6,7},{7,6},{8,9},{9,8},{10,11... | collective-permute-start | bytes 1572872 | tf_op jit(solution)/shard_map/ppermute | solution.py:40

commit v8 on v7

--- a/solution.py
+++ b/solution.py
@@ -3,6 +3,8 @@
 import jax.numpy as jnp
 from jax import lax
 from jax.sharding import PartitionSpec as P
+from jax.experimental import pallas as pl
+from jax.experimental.pallas import tpu as pltpu
 
 F32 = jnp.float32
 BF16 = jnp.bfloat16
@@ -30,6 +32,44 @@
     inv[:, half] = np.where(n % 2 == 0, 1.0, -1.0) / length
     inv[:, half + 1:] = (-2.0 * np.sin(ang[1:])).T / length
     return split_bf16(fwd), split_bf16(inv)
+
+
+def conv_kernel(z_ref, m0_ref, m1_ref, a_ref, b_ref, d_ref, fhi_ref, flo_ref, ihi_ref, ilo_ref, o_ref):
+    length, per = z_ref.shape
+    half = length // 2
+    z = z_ref[...].astype(F32)
+    m0 = m0_ref[...]
+    m1 = m1_ref[...]
+    masked = jnp.concatenate([z * m0, z * m1], axis=1).astype(BF16)
+    x = (jnp.dot(fhi_ref[...], masked, preferred_element_type=F32)
+         + jnp.dot(flo_ref[...], masked, preferred_element_type=F32))
+    a = a_ref[...]
+    b = b_ref[...]
+    d = d_ref[...]
+    a2 = jnp.concatenate([a, a], axis=1)
+    b2 = jnp.concatenate([b, b], axis=1)
+    d2 = jnp.concatenate([d, d], axis=1)
+    xr = x[:half]
+    xi = x[half:]
+    y = jnp.concatenate([xr * a2 - xi * b2, xr * b2 + xi * d2], axis=0)
+    y_hi = y.astype(BF16)
+    y_lo = (y - y_hi.astype(F32)).astype(BF16)
+    ihi = ihi_ref[...]
+    both = (jnp.dot(ihi, y_hi, preferred_element_type=F32)
+            + jnp.dot(ihi, y_lo, preferred_element_type=F32)
+            + jnp.dot(ilo_ref[...], y_hi, preferred_element_type=F32))
+    o_ref[...] = (both[:, :per] * m0 + both[:, per:] * m1).astype(o_ref.dtype)
+
+
+def conv_call(field, m0, m1, spec, mats, out_dtype):
+    length, per = field.shape
+    flops = 2 * length * length * 2 * per * 5
+    return pl.pallas_call(
+        conv_kernel,
+        out_shape=jax.ShapeDtypeStruct((length, per), out_dtype),
+        compiler_params=pltpu.CompilerParams(vmem_limit_bytes=48 * 1024 * 1024),
+        cost_estimate=pl.CostEstimate(flops=flops, transcendentals=0, bytes_accessed=4 * length * length * 2 + 6 * length * per),
+    )(field, m0, m1, *spec, *mats)
 
 
 def mm(a, b):
@@ -60,23 +100,10 @@
             a = re
             b = jnp.where(row0, 0.0, im)
             d = jnp.where(row0, im, re)
-            two = lambda x: jnp.concatenate([x, x], axis=1)
-            return two(a), two(b), two(d)
+            return a, b, d
 
-        def long_conv(spec, field):
-            a, b, d = spec
-            zero = jnp.zeros_like(field)
-            masked = jnp.concatenate(
-                [jnp.where(in0, field, zero), jnp.where(in1, field, zero)], axis=1
-            )
-            x = mm(f_hi, masked) + mm(f_lo, masked)
-            xr, xi = x[:half], x[half:]
-            y = jnp.concatenate([xr * a - xi * b, xr * b + xi * d], axis=0)
-            y_hi32 = lax.reduce_precision(y, exponent_bits=8, mantissa_bits=7)
-            y_hi = y_hi32.astype(BF16)
-            y_lo = (y - y_hi32).astype(BF16)
-            both = mm(i_hi, y_hi) + mm(i_hi, y_lo) + mm(i_lo, y_hi)
-            return jnp.where(in0, both[:, :per], 0.0) + jnp.where(in1, both[:, per:], 0.0)
+        def long_conv(spec, field, out_dtype=F32):
+            return conv_call(field, in0, in1, spec, (f_hi, f_lo, i_hi, i_lo), out_dtype)
 
         rows = value.shape[0]
         me = lax.axis_index("seq")
@@ -102,11 +129,11 @@
         first_cols = got[:, :rows].reshape(nseq * rows, per)
         gate_cols = got[:, rows:2 * rows].reshape(nseq * rows, per)
         segs = got[:, 2 * rows:].reshape(nseq, pad_rows * per)[:, :rows].reshape(nseq * rows)
-        in0 = (segs == 0)[:, None]
-        in1 = (segs == 1)[:, None]
+        in0 = (segs == 0).astype(F32)[:, None]
+        in1 = (segs == 1).astype(F32)[:, None]
         first_mix = long_conv(spectrum(first_filter), first_cols)
         second_input = (gate_cols.astype(F32) * first_mix).astype(BF16)
-        second_mix = long_conv(spectrum(second_filter), second_input).astype(BF16)
+        second_mix = long_conv(spectrum(second_filter), second_input, BF16)
         mix_pieces = {0: second_mix[:rows]}
         for k in order[1:]:
             mix_pieces[k] = lax.ppermute(second_mix[k * rows:(k + 1) * rows], "seq",

time: 63.8 us -> 63.1 us (0.989)
  local copies, waits for them, and re-layouts: 4.21 us -> 9.82 us
  matrix products: 15.3 us -> 10.5 us
  Pallas kernels: 0 us -> 3.8 us
  other arithmetic: 8.42 us -> 5.04 us
  waiting for transfers between devices: 20.4 us -> 19.2 us
  starting transfers between devices: 14.4 us -> 13.5 us
    dot_general x22 -> x12, matrix products: 15.3 us -> 10.5 us  [mm(): return jnp.dot(a, b, preferred_element_type=F32)]
    unnamed x22 -> x19, local copies, waits for them, and re-layouts: 2.15 us -> 6.03 us
    pallas_call x0 -> x2, Pallas kernels: none -> 3.8 us  [conv_call(): pl.pallas_call(conv_kernel, out_shape=jax.ShapeDtypeStruct((length, per),...]
    sub x2 -> x0, other arithmetic: 1.84 us -> none  [long_conv(): y = jnp.concatenate([xr * a - xi * b, xr * b + xi * d], axis=0)]
    ppermute x3, waiting for transfers between devices: 1.56 us -> 0.01 us  [local(): lax.ppermute(second_mix[k * rows:(k + 1) * rows], 'seq', [(i, (i + k) % n...]
    select_n x3 -> x0, other arithmetic: 1.31 us -> none  [the longest x2 1.28 us: long_conv(): jnp.where(in0, field, zero)]
    select_n x1, other arithmetic: 1.11 us -> 0.14 us  [spectrum(): d = jnp.where(row0, im, re)]
    concatenate x1, local copies, waits for them, and re-layouts: 0.01 us -> 0.92 us  [rotated(): jnp.concatenate([got[(nseq - j) % nseq] for j in range(nseq)], axis=0)]
  transfers between devices with their start and end apart: 9 -> 9, of which waited for: 5 -> 4; matrix products, arithmetic and copies ran while one was open for 15% -> 20% of each run, Pallas kernels for 0% -> 0%
where the time goes in v8:
time: 63.1 us; the launch traced here: 62.3 us
  waiting for transfers between devices  19.2 us (30%)
  starting transfers between devices  13.5 us (21%)
  matrix products  10.5 us (17%)
  local copies, waits for them, and re-layouts  9.82 us (16%)
  other arithmetic  5.04 us (8%)
  Pallas kernels  3.8 us (6%)
    ppermute x3, waiting for transfers between devices, swap(): return lax.ppermute(x, 'chan', [(c, c ^ bit) for c in range(4)])  15.6 us
    dot_general x12, matrix products, mm(): return jnp.dot(a, b, preferred_element_type=F32)  10.5 us
    ppermute x3, starting transfers between devices, local(): lax.ppermute(block_for((me + k) % nseq), 'seq', [(i, (i + k) % nseq) for...  6.09 us
    unnamed x19, local copies, waits for them, and re-layouts  6.03 us
    ppermute x3, starting transfers between devices, local(): lax.ppermute(second_mix[k * rows:(k + 1) * rows], 'seq', [(i, (i + k) % n...  5.71 us
    pallas_call x2, Pallas kernels, conv_call(): pl.pallas_call(conv_kernel, out_shape=jax.ShapeDtypeStruct((length, per),...  3.8 us
    ppermute x3, waiting for transfers between devices, local(): lax.ppermute(block_for((me + k) % nseq), 'seq', [(i, (i + k) % nseq) for...  3.62 us
    ppermute x3, starting transfers between devices, swap(): return lax.ppermute(x, 'chan', [(c, c ^ bit) for c in range(4)])  1.7 us
  transfers between devices with their start and end apart: 9, of which 4 were waited for; matrix products, arithmetic and copies ran while one was open for 20% of the time, Pallas kernels for 0%

profile of v8, /device:TPU:0, one launch (start us, length us, event | category | flops | bytes accessed | tf_op | source)
XLA Modules:
  0.0 62.3 jit_solution(3856722900726135055)
XLA Ops:
  0.0 0.0 copy-start.1
  0.0 0.0 copy-start
  0.0 0.7 %convert_element_type.67 = bf16[128]{0:T(256)(128)(2,1)S(1)} convert(s32[128]{0:T(128)} %param.17) | non-fusion elementwise | flops 128 | bytes 768 | tf_op jit(solution)/shard_map/convert_element_type | solution.py:119
  0.8 1.1 %multiply_convert_fusion = bf16[128,1024]{1,0:T(8,128)(2,1)S(1)} fusion(bf16[128,1024]{1,0:T(8,128)(2,1)} %param.11, bf16[128,1024]{1,0:T(8,128)(2,1)} %param.12), kind=kLoop, calls=%fused_computation.28 | loop fusion | flops 524288 | bytes 786432 | tf_op jit(solution)/shard_map/convert_element_type | solution.py:116
  1.9 1.0 %constant_dynamic-slice_fusion = (bf16[128,256]{1,0:T(8,128)(2,1)S(1)}, bf16[128,256]{1,0:T(8,128)(2,1)S(1)}, bf16[1088,256]{1,0:T(8,128)(2,1)S(1)}, bf16[128,256]{1,0:T(8,128)(2,1)S(1)}) fusion(bf16[128,1024]{1,0:T(8,128)(2,1)} %param.13, s32[]{:T(128)S(6)} %select_n.121, s32[]{:T(128)S(6)} %select_n.117, bf16[1088,256]{1,0:T(8,128)(2,1)S(1)} %get-tuple-element.19, ...), kind=kLoop, calls=%fused_computation.47 | loop fusion | bytes 524304 | tf_op jit(solution)/shard_map/dynamic_slice | solution.py:122
  2.9 0.7 %pad_maximum_fusion = (bf16[272,256]{1,0:T(8,128)(2,1)S(1)}, bf16[272,256]{1,0:T(8,128)(2,1)}, bf16[272,256]{1,0:T(8,128)(2,1)}) fusion(bf16[16,256]{1,0:T(8,128)(2,1)S(1)} %reshape.56, bf16[128,256]{1,0:T(8,128)(2,1)S(1)} %get-tuple-element.20, bf16[128,256]{1,0:T(8,128)(2,1)S(1)} %get-tuple-element.16, bf16[128,256]{1,0:T(8,128)(2,1)S(1)} %get-tuple-element.23, ...), kind=kLoop, calls=%fused_computation.33 | loop fusion | flops 1114112 | bytes 819200 | tf_op jit(solution)/shard_map/concatenate | solution.py:123
  3.6 5.1 %collective-permute-start = (bf16[272,256]{1,0:T(8,128)(2,1)}, bf16[272,256]{1,0:T(8,128)(2,1)}, u32[]{:S(2)}, u32[]{:S(2)}) collective-permute-start(bf16[272,256]{1,0:T(8,128)(2,1)} %get-tuple-element.28), channel_id=1, source_target_pairs={{0,12},{4,0},{8,4},{12,8},{1,13},{5,1},{9,5},{13,9},{2,14},{6,2},{... | collective-permute-start | bytes 417800 | tf_op jit(solution)/shard_map/ppermute | solution.py:127
  8.7 0.0 collective-permute-start.1
  8.7 1.0 %collective-permute-start.2 = (bf16[272,256]{1,0:T(8,128)(2,1)S(1)}, bf16[272,256]{1,0:T(8,128)(2,1)}, u32[]{:S(2)}, u32[]{:S(2)}) collective-permute-start(bf16[272,256]{1,0:T(8,128)(2,1)S(1)} %get-tuple-element.26), channel_id=1, source_target_pairs={{0,4},{4,8},{8,12},{12,0},{1,5},{5,9},{9,13},{13,1},{2,6},{6,10},{... | collective-permute-start | bytes 417800 | tf_op jit(solution)/shard_map/ppermute | solution.py:127
  9.7 0.7 %dynamic-slice_bitcast_fusion = (bf16[512,16]{0,1:T(8,128)(2,1)S(1)}, bf16[512,16]{0,1:T(8,128)(2,1)S(1)}) fusion(bf16[64,512]{1,0:T(8,128)(2,1)} %param.15, s32[]{:T(128)S(6)} %select_n.122, bf16[64,512]{1,0:T(8,128)(2,1)} %param.14), kind=kLoop, calls=%fused_computation.41 | loop fusion | bytes 65540 | tf_op jit(solution)/shard_map/transpose | solution.py:96
  10.5 1.4 %fusion.25 = f32[256,512]{0,1:T(8,128)S(1)} fusion(bf16[512,256]{0,1:T(8,128)(2,1)S(1)} %bitcast.35, bf16[512,512]{1,0:T(8,128)(2,1)} %constant.99.clone.fhi_ref), kind=kOutput, calls=%fused_computation.60 | convolution fusion | flops 134217728 | bytes 1310720 | tf_op jit(solution)/shard_map/dot_general | solution.py:76
  11.9 1.4 %fusion.24 = f32[256,512]{0,1:T(8,128)S(1)} fusion(bf16[512,256]{0,1:T(8,128)(2,1)S(1)} %bitcast.37, bf16[512,512]{1,0:T(8,128)(2,1)} %constant.99.clone.fhi_ref), kind=kOutput, calls=%fused_computation.59 | convolution fusion | flops 134217728 | bytes 1310720 | tf_op jit(solution)/shard_map/dot_general | solution.py:76
  13.3 1.4 %fusion.4 = f32[512,256]{1,0:T(8,128)S(1)} fusion(f32[256,512]{0,1:T(8,128)S(1)} %fusion.25, bf16[512,256]{0,1:T(8,128)(2,1)S(1)} %bitcast.36, bf16[512,512]{1,0:T(8,128)(2,1)} %constant.100.clone.flo_ref), kind=kOutput, calls=%fused_computation.9 | convolution fusion | flops 134348800 | bytes 1835008 | tf_op jit(solution)/shard_map/dot_general | solution.py:76
  14.7 1.4 %fusion.5 = f32[512,256]{1,0:T(8,128)S(1)} fusion(f32[256,512]{0,1:T(8,128)S(1)} %fusion.24, bf16[512,256]{0,1:T(8,128)(2,1)S(1)} %bitcast.38, bf16[512,512]{1,0:T(8,128)(2,1)} %constant.100.clone.flo_ref), kind=kOutput, calls=%fused_computation.11 | convolution fusion | flops 134348800 | bytes 1835008 | tf_op jit(solution)/shard_map/dot_general | solution.py:76
  16.1 0.1 slice_select_fusion
  16.3 0.0 collective-permute-done
  16.3 0.9 %constant_dynamic-update-slice_fusion.2 = bf16[1088,256]{1,0:T(8,128)(2,1)S(1)} fusion(bf16[1088,256]{1,0:T(8,128)(2,1)S(1)} %constant_dynamic-update-slice_fusion.3, bf16[272,256]{1,0:T(8,128)(2,1)} %collective-permute-done), kind=kLoop, calls=%fused_computation.45 | loop fusion | bytes 278528
  17.2 3.6 %collective-permute-done.1 = bf16[272,256]{1,0:T(8,128)(2,1)} collective-permute-done((bf16[272,256]{1,0:T(8,128)(2,1)}, bf16[272,256]{1,0:T(8,128)(2,1)}, u32[]{:S(2)}, u32[]{:S(2)}) %collective-permute-start.1) | collective-permute-done | bytes 139296 | tf_op jit(solution)/shard_map/ppermute | solution.py:127
  20.9 0.9 %constant_dynamic-update-slice_fusion.1 = bf16[1088,256]{1,0:T(8,128)(2,1)S(1)} fusion(bf16[1088,256]{1,0:T(8,128)(2,1)S(1)} %constant_dynamic-update-slice_fusion.2, bf16[272,256]{1,0:T(8,128)(2,1)} %collective-permute-done.1), kind=kLoop, calls=%fused_computation.44 | loop fusion | bytes 278528
  21.8 0.0 collective-permute-done.2
  21.8 0.9 %constant_dynamic-update-slice_fusion = bf16[1088,256]{1,0:T(8,128)(2,1)S(1)} fusion(bf16[1088,256]{1,0:T(8,128)(2,1)S(1)} %constant_dynamic-update-slice_fusion.1, bf16[272,256]{1,0:T(8,128)(2,1)} %collective-permute-done.2), kind=kLoop, calls=%fused_computation.43 | loop fusion | bytes 278528 | tf_op jit(solution)/shard_map/concatenate | solution.py:114
  22.7 0.7 %fusion.21 = (bf16[4,128,256]{2,1,0:T(8,128)(2,1)}, bf16[4,128,256]{2,1,0:T(8,128)(2,1)S(1)}) fusion(bf16[4,272,256]{2,1,0:T(8,128)(2,1)S(1)} %bitcast.39), kind=kLoop, calls=%fused_computation.56 | loop fusion | bytes 1048576 | tf_op jit(solution)/shard_map/slice | solution.py:130
  23.5 0.1 copy.20.m0_ref
  23.6 0.1 copy.21.m1_ref
  23.8 0.0 copy-done.1
  23.8 0.0 copy-done
  23.8 0.0 copy-start.2
  23.8 1.0 %copy-done.2 = bf16[512,512]{1,0:T(8,128)(2,1)S(1)} copy-done((bf16[512,512]{1,0:T(8,128)(2,1)S(1)}, bf16[512,512]{1,0:T(8,128)(2,1)}, u32[]{:S(2)}) %copy-start.2) | copy-done | bytes 524312
  24.9 0.0 copy-start.4
  24.9 1.0 %copy-done.4 = bf16[512,512]{1,0:T(8,128)(2,1)S(1)} copy-done((bf16[512,512]{1,0:T(8,128)(2,1)S(1)}, bf16[512,512]{1,0:T(8,128)(2,1)}, u32[]{:S(2)}) %copy-start.4) | copy-done | bytes 524312
  25.9 1.9 %shard_map.109 = f32[512,256]{1,0:T(8,128)S(1)} custom-call(bf16[512,256]{1,0:T(8,128)(2,1)S(1)} %bitcast.34, f32[512,1]{1,0:T(8,128)S(1)} %copy.20.m0_ref, f32[512,1]{1,0:T(8,128)S(1)} %copy.21.m1_ref, f32[256,256]{1,0:T(8,128)S(1)} %get-tuple-element.29.a_ref, f32[256,256]{1,0:T(8,128)S(1)} %get-tuple-element.30.b_ref, ...), custom_call_target="tpu_custom_call" | custom-call | flops 1342177280 | bytes 2883584 | tf_op jit(solution)/shard_map/pallas_call | solution.py:67
  27.8 1.0 %fusion.18.z_ref = bf16[512,256]{1,0:T(8,128)(2,1)S(1)} fusion(f32[512,256]{1,0:T(8,128)S(1)} %shard_map.109, bf16[4,128,256]{2,1,0:T(8,128)(2,1)} %get-tuple-element.5), kind=kLoop, calls=%fused_computation.27 | loop fusion | flops 393216 | bytes 1048576 | tf_op jit(solution)/shard_map/convert_element_type | solution.py:135
  28.8 0.0 copy-start.3
  28.8 1.0 %copy-done.3 = bf16[512,512]{1,0:T(8,128)(2,1)S(1)} copy-done((bf16[512,512]{1,0:T(8,128)(2,1)S(1)}, bf16[512,512]{1,0:T(8,128)(2,1)}, u32[]{:S(2)}) %copy-start.3) | copy-done | bytes 524312
  29.9 0.0 copy-start.5
  29.9 1.0 %copy-done.5 = bf16[512,512]{1,0:T(8,128)(2,1)S(1)} copy-done((bf16[512,512]{1,0:T(8,128)(2,1)S(1)}, bf16[512,512]{1,0:T(8,128)(2,1)}, u32[]{:S(2)}) %copy-start.5) | copy-done | bytes 524312
  30.9 0.0 copy-start.6
  30.9 1.9 %shard_map.110 = bf16[512,256]{1,0:T(8,128)(2,1)S(1)} custom-call(bf16[512,256]{1,0:T(8,128)(2,1)S(1)} %fusion.18.z_ref, f32[512,1]{1,0:T(8,128)S(1)} %copy.20.m0_ref, f32[512,1]{1,0:T(8,128)S(1)} %copy.21.m1_ref, f32[256,256]{1,0:T(8,128)S(1)} %get-tuple-element.11.a_ref, f32[256,256]{1,0:T(8,128)S(1)} %get-tuple-element.8.b_ref, ...), custom_call_target="tpu_custom_call" | custom-call | flops 1342177280 | bytes 2883584 | tf_op jit(solution)/shard_map/pallas_call | solution.py:67
  32.8 1.9 %collective-permute-start.5 = (bf16[128,256]{1,0:T(8,128)(2,1)S(1)}, bf16[128,256]{1,0:T(8,128)(2,1)S(1)}, u32[]{:S(2)}, u32[]{:S(2)}) collective-permute-start(bf16[128,256]{1,0:T(8,128)(2,1)S(1)} %get-tuple-element.14), channel_id=1, source_target_pairs={{0,8},{4,12},{8,0},{12,4},{1,9},{5,13},{9,1},{13,5},{2,10},{6,14},... | collective-permute-start | bytes 196616 | tf_op jit(solution)/shard_map/ppermute | solution.py:139
  34.7 0.2 collective-permute-start.3
  35.0 3.6 %collective-permute-start.4 = (bf16[128,256]{1,0:T(8,128)(2,1)S(1)}, bf16[128,256]{1,0:T(8,128)(2,1)S(1)}, u32[]{:S(2)}, u32[]{:S(2)}) collective-permute-start(bf16[128,256]{1,0:T(8,128)(2,1)S(1)} %get-tuple-element.13), channel_id=1, source_target_pairs={{0,12},{4,0},{8,4},{12,8},{1,13},{5,1},{9,5},{13,9},{2,14},{6,2},{... | collective-permute-start | bytes 196616 | tf_op jit(solution)/shard_map/ppermute | solution.py:139
  38.5 1.5 %fusion.10 = f32[128,2048]{1,0:T(8,128)S(1)} fusion(bf16[1024,4096]{1,0:T(8,128)(2,1)} %param.16, s32[]{:T(128)S(6)} %select_n.128, s32[]{:T(128)S(6)} %select_n.136, bf16[512,256]{1,0:T(8,128)(2,1)S(1)} %shard_map.110), kind=kOutput, calls=%fused_computation.18 | convolution fusion | flops 134217728 | bytes 2162696 | tf_op jit(solution)/shard_map/dot_general | solution.py:76
  40.1 1.5 %fusion.16 = f32[128,2048]{1,0:T(8,128)S(1)} fusion(bf16[1024,4096]{1,0:T(8,128)(2,1)} %param.16, s32[]{:T(128)S(6)} %select_n.128, s32[]{:T(128)S(6)} %select_n.129, bf16[512,256]{1,0:T(8,128)(2,1)S(1)} %shard_map.110), kind=kOutput, calls=%fused_computation.24 | convolution fusion | flops 134217728 | bytes 2162696 | tf_op jit(solution)/shard_map/dot_general | solution.py:76
  41.6 0.0 collective-permute-done.3
  41.6 0.0 copy-done.6
  41.6 0.3 convolution_add_fusion.1
  42.0 0.0 collective-permute-done.5
  42.0 0.3 fusion.6
  42.3 0.0 collective-permute-done.4
  42.3 0.3 fusion.3
  42.6 0.1 collective-permute-start.6
  42.7 0.3 fusion.12
  43.1 0.3 convolution_add_fusion.3
  43.4 1.2 %collective-permute-done.6 = bf16[128,2048]{1,0:T(8,128)(2,1)S(1)} collective-permute-done((bf16[128,2048]{1,0:T(8,128)(2,1)S(1)}, bf16[128,2048]{1,0:T(8,128)(2,1)S(1)}, u32[]{:S(2)}, u32[]{:S(2)}) %collective-permute-start.6) | collective-permute-done | bytes 524320 | tf_op jit(solution)/shard_map/ppermute | solution.py:80
  44.6 0.4 fusion.23
  45.0 1.6 %collective-permute-start.7 = (bf16[128,2048]{1,0:T(8,128)(2,1)S(1)}, bf16[128,2048]{1,0:T(8,128)(2,1)S(1)}, u32[]{:S(2)}, u32[]{:S(2)}) collective-permute-start(bf16[128,2048]{1,0:T(8,128)(2,1)S(1)} %get-tuple-element.32), channel_id=1, source_target_pairs={{0,2},{1,3},{2,0},{3,1},{4,6},{5,7},{6,4},{7,5},{8,10},{9,11},{10,... | collective-permute-start | bytes 1572872 | tf_op jit(solution)/shard_map/ppermute | solution.py:80
  46.5 12.5 %collective-permute-done.7 = bf16[128,2048]{1,0:T(8,128)(2,1)S(1)} collective-permute-done((bf16[128,2048]{1,0:T(8,128)(2,1)S(1)}, bf16[128,2048]{1,0:T(8,128)(2,1)S(1)}, u32[]{:S(2)}, u32[]{:S(2)}) %collective-permute-start.7) | collective-permute-done | bytes 524320 | tf_op jit(solution)/shard_map/ppermute | solution.py:80
  59.0 0.1 add_convert_fusion
  59.1 0.1 collective-permute-start.8
  59.2 1.9 %collective-permute-done.8 = bf16[128,2048]{1,0:T(8,128)(2,1)S(1)} collective-permute-done((bf16[128,2048]{1,0:T(8,128)(2,1)S(1)}, bf16[128,2048]{1,0:T(8,128)(2,1)S(1)}, u32[]{:S(2)}, u32[]{:S(2)}) %collective-permute-start.8) | collective-permute-done | bytes 524320 | tf_op jit(solution)/shard_map/ppermute | solution.py:80
  61.1 1.2 %maximum_select_fusion = bf16[128,4096]{1,0:T(8,128)(2,1)} fusion(bf16[128,2048]{1,0:T(8,128)(2,1)S(1)} %collective-permute-done.8, bf16[128,2048]{1,0:T(8,128)(2,1)S(1)} %add_convert_fusion, pred[]{:T(512)S(6)} %eq.55), kind=kLoop, calls=%fused_computation.12 | loop fusion | flops 4718592 | bytes 2097153 | tf_op jit(solution)/shard_map/jit(_where)/select_n | solution.py:161
  (11 shorter events, 0.2 us)
Async XLA Ops:
  0.0 23.8 %copy-start.1 = (bf16[512,512]{1,0:T(8,128)(2,1)S(1)}, bf16[512,512]{1,0:T(8,128)(2,1)}, u32[]{:S(2)}) copy-start(bf16[512,512]{1,0:T(8,128)(2,1)} %constant.99.clone.fhi_ref) | copy-start | bytes 1572868
  0.0 23.8 %copy-start = (bf16[512,512]{1,0:T(8,128)(2,1)S(1)}, bf16[512,512]{1,0:T(8,128)(2,1)}, u32[]{:S(2)}) copy-start(bf16[512,512]{1,0:T(8,128)(2,1)} %constant.100.clone.flo_ref) | copy-start | bytes 1572868
  3.6 12.7 %collective-permute-start = (bf16[272,256]{1,0:T(8,128)(2,1)}, bf16[272,256]{1,0:T(8,128)(2,1)}, u32[]{:S(2)}, u32[]{:S(2)}) collective-permute-start(bf16[272,256]{1,0:T(8,128)(2,1)} %get-tuple-element.28), channel_id=1, source_target_pairs={{0,12},{4,0},{8,4},{12,8},{1,13},{5,1},{9,5},{13,9},{2,14},{6,2},{... | collective-permute-start | bytes 417800 | tf_op jit(solution)/shard_map/ppermute | solution.py:127
  8.7 12.1 %collective-permute-start.1 = (bf16[272,256]{1,0:T(8,128)(2,1)}, bf16[272,256]{1,0:T(8,128)(2,1)}, u32[]{:S(2)}, u32[]{:S(2)}) collective-permute-start(bf16[272,256]{1,0:T(8,128)(2,1)} %get-tuple-element.27), channel_id=1, source_target_pairs={{0,8},{4,12},{8,0},{12,4},{1,9},{5,13},{9,1},{13,5},{2,10},{6,14},... | collective-permute-start | bytes 417800 | tf_op jit(solution)/shard_map/ppermute | solution.py:127
  8.7 13.1 %collective-permute-start.2 = (bf16[272,256]{1,0:T(8,128)(2,1)S(1)}, bf16[272,256]{1,0:T(8,128)(2,1)}, u32[]{:S(2)}, u32[]{:S(2)}) collective-permute-start(bf16[272,256]{1,0:T(8,128)(2,1)S(1)} %get-tuple-element.26), channel_id=1, source_target_pairs={{0,4},{4,8},{8,12},{12,0},{1,5},{5,9},{9,13},{13,1},{2,6},{6,10},{... | collective-permute-start | bytes 417800 | tf_op jit(solution)/shard_map/ppermute | solution.py:127
  23.8 1.0 %copy-start.2 = (bf16[512,512]{1,0:T(8,128)(2,1)S(1)}, bf16[512,512]{1,0:T(8,128)(2,1)}, u32[]{:S(2)}) copy-start(bf16[512,512]{1,0:T(8,128)(2,1)} %constant.101.clone.ihi_ref) | copy-start | bytes 1572868
  24.9 1.0 %copy-start.4 = (bf16[512,512]{1,0:T(8,128)(2,1)S(1)}, bf16[512,512]{1,0:T(8,128)(2,1)}, u32[]{:S(2)}) copy-start(bf16[512,512]{1,0:T(8,128)(2,1)} %constant.102.clone.ilo_ref) | copy-start | bytes 1572868
  28.8 1.0 %copy-start.3 = (bf16[512,512]{1,0:T(8,128)(2,1)S(1)}, bf16[512,512]{1,0:T(8,128)(2,1)}, u32[]{:S(2)}) copy-start(bf16[512,512]{1,0:T(8,128)(2,1)} %constant.101.clone.ihi_ref) | copy-start | bytes 1572868
  29.9 1.0 %copy-start.5 = (bf16[512,512]{1,0:T(8,128)(2,1)S(1)}, bf16[512,512]{1,0:T(8,128)(2,1)}, u32[]{:S(2)}) copy-start(bf16[512,512]{1,0:T(8,128)(2,1)} %constant.102.clone.ilo_ref) | copy-start | bytes 1572868
  30.9 10.7 %copy-start.6 = (bf16[1024,4096]{1,0:T(8,128)(2,1)S(1)}, bf16[1024,4096]{1,0:T(8,128)(2,1)}, u32[]{:S(2)}) copy-start(bf16[1024,4096]{1,0:T(8,128)(2,1)} %param.16) | copy-start | bytes 25165828
  32.8 9.1 %collective-permute-start.5 = (bf16[128,256]{1,0:T(8,128)(2,1)S(1)}, bf16[128,256]{1,0:T(8,128)(2,1)S(1)}, u32[]{:S(2)}, u32[]{:S(2)}) collective-permute-start(bf16[128,256]{1,0:T(8,128)(2,1)S(1)} %get-tuple-element.14), channel_id=1, source_target_pairs={{0,8},{4,12},{8,0},{12,4},{1,9},{5,13},{9,1},{13,5},{2,10},{6,14},... | collective-permute-start | bytes 196616 | tf_op jit(solution)/shard_map/ppermute | solution.py:139
  34.7 6.9 %collective-permute-start.3 = (bf16[128,256]{1,0:T(8,128)(2,1)S(1)}, bf16[128,256]{1,0:T(8,128)(2,1)S(1)}, u32[]{:S(2)}, u32[]{:S(2)}) collective-permute-start(bf16[128,256]{1,0:T(8,128)(2,1)S(1)} %get-tuple-element.15), channel_id=1, source_target_pairs={{0,4},{4,8},{8,12},{12,0},{1,5},{5,9},{9,13},{13,1},{2,6},{6,10},{... | collective-permute-start | bytes 196616 | tf_op jit(solution)/shard_map/ppermute | solution.py:139
  35.0 7.3 %collective-permute-start.4 = (bf16[128,256]{1,0:T(8,128)(2,1)S(1)}, bf16[128,256]{1,0:T(8,128)(2,1)S(1)}, u32[]{:S(2)}, u32[]{:S(2)}) collective-permute-start(bf16[128,256]{1,0:T(8,128)(2,1)S(1)} %get-tuple-element.13), channel_id=1, source_target_pairs={{0,12},{4,0},{8,4},{12,8},{1,13},{5,1},{9,5},{13,9},{2,14},{6,2},{... | collective-permute-start | bytes 196616 | tf_op jit(solution)/shard_map/ppermute | solution.py:139
  42.6 2.0 %collective-permute-start.6 = (bf16[128,2048]{1,0:T(8,128)(2,1)S(1)}, bf16[128,2048]{1,0:T(8,128)(2,1)S(1)}, u32[]{:S(2)}, u32[]{:S(2)}) collective-permute-start(bf16[128,2048]{1,0:T(8,128)(2,1)S(1)} %fusion.3), channel_id=1, source_target_pairs={{0,1},{1,0},{2,3},{3,2},{4,5},{5,4},{6,7},{7,6},{8,9},{9,8},{10,11... | collective-permute-start | bytes 1572872 | tf_op jit(solution)/shard_map/ppermute | solution.py:80
  45.0 14.0 %collective-permute-start.7 = (bf16[128,2048]{1,0:T(8,128)(2,1)S(1)}, bf16[128,2048]{1,0:T(8,128)(2,1)S(1)}, u32[]{:S(2)}, u32[]{:S(2)}) collective-permute-start(bf16[128,2048]{1,0:T(8,128)(2,1)S(1)} %get-tuple-element.32), channel_id=1, source_target_pairs={{0,2},{1,3},{2,0},{3,1},{4,6},{5,7},{6,4},{7,5},{8,10},{9,11},{10,... | collective-permute-start | bytes 1572872 | tf_op jit(solution)/shard_map/ppermute | solution.py:80
  59.1 2.0 %collective-permute-start.8 = (bf16[128,2048]{1,0:T(8,128)(2,1)S(1)}, bf16[128,2048]{1,0:T(8,128)(2,1)S(1)}, u32[]{:S(2)}, u32[]{:S(2)}) collective-permute-start(bf16[128,2048]{1,0:T(8,128)(2,1)S(1)} %add_convert_fusion), channel_id=1, source_target_pairs={{0,1},{1,0},{2,3},{3,2},{4,5},{5,4},{6,7},{7,6},{8,9},{9,8},{10,11... | collective-permute-start | bytes 1572872 | tf_op jit(solution)/shard_map/ppermute | solution.py:80

commit v9 on v7

--- a/solution.py
+++ b/solution.py
@@ -1,8 +1,11 @@
+import functools
 import numpy as np
 import jax
 import jax.numpy as jnp
 from jax import lax
 from jax.sharding import PartitionSpec as P
+from jax.experimental import pallas as pl
+from jax.experimental.pallas import tpu as pltpu
 
 F32 = jnp.float32
 BF16 = jnp.bfloat16
@@ -32,6 +35,90 @@
     return split_bf16(fwd), split_bf16(inv)
 
 
+def round_bf16(x, in_kernel):
+    if in_kernel:
+        return x.astype(BF16).astype(F32)
+    return lax.reduce_precision(x, exponent_bits=8, mantissa_bits=7)
+
+
+def hyena_math(pieces, m0, m1, spec1, spec2, mats, rows, wait, in_kernel):
+    nseq = len(pieces)
+    per = pieces[0].shape[1]
+    length = m0.shape[0]
+    half = length // 2
+    order = [(nseq - j) % nseq for j in range(nseq)]
+    first = jnp.concatenate([pieces[k][0:rows, :] for k in order], axis=0).astype(F32)
+    gate = jnp.concatenate([pieces[k][rows:2 * rows, :] for k in order], axis=0).astype(F32)
+
+    def conv(z, spec, first_call):
+        masked = jnp.concatenate([z * m0, z * m1], axis=1).astype(BF16)
+        if first_call:
+            wait(0)
+            wait(1)
+        x = (jnp.dot(mats[0](), masked, preferred_element_type=F32)
+             + jnp.dot(mats[1](), masked, preferred_element_type=F32))
+        a, b, d = (jnp.concatenate([v, v], axis=1) for v in (f() for f in spec))
+        xr = x[:half]
+        xi = x[half:]
+        y = jnp.concatenate([xr * a - xi * b, xr * b + xi * d], axis=0)
+        y_hi32 = round_bf16(y, in_kernel)
+        y_hi = y_hi32.astype(BF16)
+        y_lo = (y - y_hi32).astype(BF16)
+        if first_call:
+            wait(2)
+            wait(3)
+        ihi = mats[2]()
+        both = (jnp.dot(ihi, y_hi, preferred_element_type=F32)
+                + jnp.dot(ihi, y_lo, preferred_element_type=F32)
+                + jnp.dot(mats[3](), y_hi, preferred_element_type=F32))
+        return both[:, :per] * m0 + both[:, per:] * m1
+
+    first_mix = conv(first, spec1, True)
+    second_input = round_bf16(gate * first_mix, in_kernel)
+    return conv(second_input, spec2, False).astype(BF16)
+
+
+def hyena_kernel(*refs, nseq, rows):
+    pieces = [r[...] for r in refs[:nseq]]
+    m0_ref, m1_ref = refs[nseq:nseq + 2]
+    spec_refs = refs[nseq + 2:nseq + 8]
+    mats_hbm = refs[nseq + 8:nseq + 12]
+    o_ref = refs[nseq + 12]
+    mats = refs[nseq + 13:nseq + 17]
+    sem = refs[nseq + 17]
+    copies = [pltpu.make_async_copy(mats_hbm[i], mats[i], sem.at[i]) for i in range(4)]
+    for c in copies:
+        c.start()
+    loader = lambda r: (lambda: r[...])
+    spec1 = [loader(r) for r in spec_refs[:3]]
+    spec2 = [loader(r) for r in spec_refs[3:]]
+    o_ref[...] = hyena_math(pieces, m0_ref[...], m1_ref[...], spec1, spec2,
+                            [loader(r) for r in mats], rows, lambda i: copies[i].wait(), True)
+
+
+def hyena_call(pieces, m0, m1, spec1, spec2, mats, rows):
+    nseq = len(pieces)
+    length = m0.shape[0]
+    per = pieces[0].shape[1]
+    if 4 * length * length * 2 > 8 * 1024 * 1024:
+        const = lambda v: (lambda: v)
+        return hyena_math(pieces, m0, m1, [const(v) for v in spec1], [const(v) for v in spec2],
+                          [const(v) for v in mats], rows, lambda i: None, False)
+    vmem = pl.BlockSpec(memory_space=pltpu.VMEM)
+    hbm = pl.BlockSpec(memory_space=pl.ANY)
+    flops = 2 * (2 * length * length * 2 * per * 5)
+    return pl.pallas_call(
+        functools.partial(hyena_kernel, nseq=nseq, rows=rows),
+        out_shape=jax.ShapeDtypeStruct((length, per), BF16),
+        in_specs=[vmem] * (nseq + 8) + [hbm] * 4,
+        out_specs=vmem,
+        scratch_shapes=[pltpu.VMEM((length, length), BF16) for _ in range(4)]
+        + [pltpu.SemaphoreType.DMA((4,))],
+        compiler_params=pltpu.CompilerParams(vmem_limit_bytes=56 * 1024 * 1024),
+        cost_estimate=pl.CostEstimate(flops=flops, transcendentals=0,
+                                      bytes_accessed=4 * length * length * 2 + 8 * length * per),
+    )(*pieces, m0, m1, *spec1, *spec2, *mats)
+
 def mm(a, b):
     return jnp.dot(a, b, preferred_element_type=F32)
 
@@ -60,32 +147,13 @@
             a = re
             b = jnp.where(row0, 0.0, im)
             d = jnp.where(row0, im, re)
-            two = lambda x: jnp.concatenate([x, x], axis=1)
-            return two(a), two(b), two(d)
-
-        def long_conv(spec, field):
-            a, b, d = spec
-            zero = jnp.zeros_like(field)
-            masked = jnp.concatenate(
-                [jnp.where(in0, field, zero), jnp.where(in1, field, zero)], axis=1
-            )
-            x = mm(f_hi, masked) + mm(f_lo, masked)
-            xr, xi = x[:half], x[half:]
-            y = jnp.concatenate([xr * a - xi * b, xr * b + xi * d], axis=0)
-            y_hi32 = lax.reduce_precision(y, exponent_bits=8, mantissa_bits=7)
-            y_hi = y_hi32.astype(BF16)
-            y_lo = (y - y_hi32).astype(BF16)
-            both = mm(i_hi, y_hi) + mm(i_hi, y_lo) + mm(i_lo, y_hi)
-            return jnp.where(in0, both[:, :per], 0.0) + jnp.where(in1, both[:, per:], 0.0)
+            return a, b, d
 
         rows = value.shape[0]
         me = lax.axis_index("seq")
         order = [0] + [k for k in (1, nseq - 1) if k < nseq] + [k for k in range(2, nseq - 1)]
         order = list(dict.fromkeys(order))
 
-        def rotated(got):
-            return jnp.concatenate([got[(nseq - j) % nseq] for j in range(nseq)], axis=0)
-
         first_input = (first_gate.astype(F32) * value.astype(F32)).astype(BF16)
         id_rows = -(-rows // per)
         pad_rows = -(-id_rows // 16) * 16
@@ -98,15 +166,12 @@
         got = {0: block_for(me)}
         for k in order[1:]:
             got[k] = lax.ppermute(block_for((me + k) % nseq), "seq", [(i, (i + k) % nseq) for i in range(nseq)])
-        got = rotated(got).reshape(nseq, 2 * rows + pad_rows, per)
-        first_cols = got[:, :rows].reshape(nseq * rows, per)
-        gate_cols = got[:, rows:2 * rows].reshape(nseq * rows, per)
-        segs = got[:, 2 * rows:].reshape(nseq, pad_rows * per)[:, :rows].reshape(nseq * rows)
-        in0 = (segs == 0)[:, None]
-        in1 = (segs == 1)[:, None]
-        first_mix = long_conv(spectrum(first_filter), first_cols)
-        second_input = (gate_cols.astype(F32) * first_mix).astype(BF16)
-        second_mix = long_conv(spectrum(second_filter), second_input).astype(BF16)
+        seg_blocks = jnp.stack([got[(nseq - j) % nseq][2 * rows:] for j in range(nseq)])
+        segs = seg_blocks.reshape(nseq, pad_rows * per)[:, :rows].reshape(nseq * rows)
+        in0 = (segs == 0).astype(F32)[:, None]
+        in1 = (segs == 1).astype(F32)[:, None]
+        second_mix = hyena_call([got[k] for k in range(nseq)], in0, in1, spectrum(first_filter),
+                                spectrum(second_filter), (f_hi, f_lo, i_hi, i_lo), rows)
         mix_pieces = {0: second_mix[:rows]}
         for k in order[1:]:
             mix_pieces[k] = lax.ppermute(second_mix[k * rows:(k + 1) * rows], "seq",

time: 63.8 us -> 67.7 us (1.061)
  Pallas kernels: 0 us -> 7.23 us
  other arithmetic: 8.42 us -> 5.04 us
  starting transfers between devices: 14.4 us -> 12.6 us
  matrix products: 15.3 us -> 16.9 us
    pallas_call x0 -> x1, Pallas kernels: none -> 7.23 us  [hyena_call(): pl.pallas_call(functools.partial(hyena_kernel, nseq=nseq, rows=rows), out...]
    unnamed x22 -> x14, local copies, waits for them, and re-layouts: 2.15 us -> 0.07 us
    sub x2 -> x0, other arithmetic: 1.84 us -> none  [long_conv(): y = jnp.concatenate([xr * a - xi * b, xr * b + xi * d], axis=0)]
    ppermute x3, starting transfers between devices: 6.6 us -> 4.76 us  [local(): lax.ppermute(second_mix[k * rows:(k + 1) * rows], 'seq', [(i, (i + k) % n...]
    convert_element_type x0 -> x2, local copies, waits for them, and re-layouts: none -> 1.71 us  [the longest x1 0.86 us: local(): in0 = (segs == 0).astype(F32)[:, None]]
    dot_general x22 -> x12, matrix products: 15.3 us -> 16.9 us  [mm(): return jnp.dot(a, b, preferred_element_type=F32)]
    select_n x3 -> x0, other arithmetic: 1.31 us -> none  [the longest x2 1.28 us: long_conv(): jnp.where(in0, field, zero)]
    ppermute x3, waiting for transfers between devices: 3.3 us -> 4.28 us  [local(): lax.ppermute(block_for((me + k) % nseq), 'seq', [(i, (i + k) % nseq) for...]
  transfers between devices with their start and end apart: 9 -> 9, of which waited for: 5 -> 4; matrix products, arithmetic and copies ran while one was open for 15% -> 21% of each run, Pallas kernels for 0% -> 0%
where the time goes in v9:
time: 67.7 us; the launch traced here: 66.9 us
  waiting for transfers between devices  20.4 us (30%)
  matrix products  16.9 us (25%)
  starting transfers between devices  12.6 us (19%)
  Pallas kernels  7.23 us (11%)
  other arithmetic  5.04 us (7%)
  local copies, waits for them, and re-layouts  4.51 us (7%)
    dot_general x12, matrix products, mm(): return jnp.dot(a, b, preferred_element_type=F32)  16.9 us
    ppermute x3, waiting for transfers between devices, swap(): return lax.ppermute(x, 'chan', [(c, c ^ bit) for c in range(4)])  14.7 us
    pallas_call x1, Pallas kernels, hyena_call(): pl.pallas_call(functools.partial(hyena_kernel, nseq=nseq, rows=rows), out...  7.23 us
    ppermute x3, starting transfers between devices, local(): lax.ppermute(block_for((me + k) % nseq), 'seq', [(i, (i + k) % nseq) for...  6.09 us
    ppermute x3, starting transfers between devices, local(): lax.ppermute(second_mix[k * rows:(k + 1) * rows], 'seq', [(i, (i + k) % n...  4.76 us
    ppermute x3, waiting for transfers between devices, local(): lax.ppermute(block_for((me + k) % nseq), 'seq', [(i, (i + k) % nseq) for...  4.28 us
    ppermute x3, starting transfers between devices, swap(): return lax.ppermute(x, 'chan', [(c, c ^ bit) for c in range(4)])  1.7 us
    ppermute x3, waiting for transfers between devices, local(): lax.ppermute(second_mix[k * rows:(k + 1) * rows], 'seq', [(i, (i + k) % n...  1.35 us
  transfers between devices with their start and end apart: 9, of which 4 were waited for; matrix products, arithmetic and copies ran while one was open for 21% of the time, Pallas kernels for 0%

profile of v9, /device:TPU:0, one launch (start us, length us, event | category | flops | bytes accessed | tf_op | source)
XLA Modules:
  0.0 66.9 jit_solution(6723884919764526229)
XLA Ops:
  0.0 0.0 copy-start
  0.0 0.7 %convert_element_type.58 = bf16[128]{0:T(256)(128)(2,1)S(1)} convert(s32[128]{0:T(128)} %param.17) | non-fusion elementwise | flops 128 | bytes 768 | tf_op jit(solution)/shard_map/convert_element_type | solution.py:160
  0.8 1.1 %multiply_convert_fusion = bf16[128,1024]{1,0:T(8,128)(2,1)S(1)} fusion(bf16[128,1024]{1,0:T(8,128)(2,1)} %param.11, bf16[128,1024]{1,0:T(8,128)(2,1)} %param.12), kind=kLoop, calls=%fused_computation.28 | loop fusion | flops 524288 | bytes 786432 | tf_op jit(solution)/shard_map/convert_element_type | solution.py:157
  1.9 1.0 %constant_dynamic-slice_fusion = (bf16[128,256]{1,0:T(8,128)(2,1)S(1)}, bf16[128,256]{1,0:T(8,128)(2,1)S(1)}, bf16[128,256]{1,0:T(8,128)(2,1)S(1)}, bf16[128,256...) fusion(bf16[128,1024]{1,0:T(8,128)(2,1)} %param.13, ...), kind=kLoop, calls=%fused_computation.44 | loop fusion | bytes 1048592 | tf_op jit(solution)/shard_map/dynamic_slice | solution.py:163
  2.9 0.7 %pad_maximum_fusion = (bf16[272,256]{1,0:T(8,128)(2,1)S(1)}, bf16[272,256]{1,0:T(8,128)(2,1)S(1)}, bf16[272,256]{1,0:T(8,128)(2,1)S(1)}, bf16[272,256]{1,0:T(8,128)(2,1)}) fusion(bf16[16,256]{1,0:T(8,128)(2,1)S(1)} %reshape.53, bf16[128,256]{1,0:T(8,128)(2,1)S(1)} %get-tuple-element.20, bf16[128,256]{1,0:T(8,128)(2,1)S(1)} %get-tuple-element.38, ...), kind=kLoop, calls=%fused_computation.29 | loop fusion | flops 1462272 | bytes 1089536 | tf_op jit(solution)/shard_map/concatenate | solution.py:164
  3.5 5.1 %collective-permute-start.2 = (bf16[272,256]{1,0:T(8,128)(2,1)S(1)}, bf16[272,256]{1,0:T(8,128)(2,1)S(1)}, u32[]{:S(2)}, u32[]{:S(2)}) collective-permute-start(bf16[272,256]{1,0:T(8,128)(2,1)S(1)} %get-tuple-element.24), channel_id=1, source_target_pairs={{0,12},{4,0},{8,4},{12,8},{1,13},{5,1},{9,5},{13,9},{2,14},{6,2},{... | collective-permute-start | bytes 417800 | tf_op jit(solution)/shard_map/ppermute | solution.py:168
  8.6 0.0 collective-permute-start.1
  8.6 1.0 %collective-permute-start = (bf16[272,256]{1,0:T(8,128)(2,1)S(1)}, bf16[272,256]{1,0:T(8,128)(2,1)S(1)}, u32[]{:S(2)}, u32[]{:S(2)}) collective-permute-start(bf16[272,256]{1,0:T(8,128)(2,1)S(1)} %get-tuple-element.25), channel_id=1, source_target_pairs={{0,4},{4,8},{8,12},{12,0},{1,5},{5,9},{9,13},{13,1},{2,6},{6,10},{... | collective-permute-start | bytes 417800 | tf_op jit(solution)/shard_map/ppermute | solution.py:168
  9.7 0.7 %dynamic-slice_bitcast_fusion = (bf16[512,16]{0,1:T(8,128)(2,1)S(1)}, bf16[512,16]{0,1:T(8,128)(2,1)S(1)}) fusion(bf16[64,512]{1,0:T(8,128)(2,1)} %param.15, s32[]{:T(128)S(6)} %select_n.122, bf16[64,512]{1,0:T(8,128)(2,1)} %param.14), kind=kLoop, calls=%fused_computation.39 | loop fusion | bytes 65540 | tf_op jit(solution)/shard_map/transpose | solution.py:143
  10.4 1.4 %fusion.27 = f32[256,512]{0,1:T(8,128)S(1)} fusion(bf16[512,256]{0,1:T(8,128)(2,1)S(1)} %bitcast.38, bf16[512,512]{1,0:T(8,128)(2,1)} %constant.99.clone.refs_12_), kind=kOutput, calls=%fused_computation.61 | convolution fusion | flops 134217728 | bytes 1310720 | tf_op jit(solution)/shard_map/dot_general | solution.py:123
  11.9 1.4 %fusion.26 = f32[256,512]{0,1:T(8,128)S(1)} fusion(bf16[512,256]{0,1:T(8,128)(2,1)S(1)} %bitcast.40, bf16[512,512]{1,0:T(8,128)(2,1)} %constant.99.clone.refs_12_), kind=kOutput, calls=%fused_computation.60 | convolution fusion | flops 134217728 | bytes 1310720 | tf_op jit(solution)/shard_map/dot_general | solution.py:123
  13.2 1.4 %fusion.6 = f32[512,256]{1,0:T(8,128)S(1)} fusion(f32[256,512]{0,1:T(8,128)S(1)} %fusion.27, bf16[512,256]{0,1:T(8,128)(2,1)S(1)} %bitcast.39, bf16[512,512]{1,0:T(8,128)(2,1)} %constant.100.clone.refs_13_), kind=kOutput, calls=%fused_computation.9 | convolution fusion | flops 134348800 | bytes 1835008 | tf_op jit(solution)/shard_map/dot_general | solution.py:123
  14.6 0.0 copy-done
  14.6 0.3 fusion.7
  15.0 1.2 %slice_select_fusion = (f32[256,256]{1,0:T(8,128)}, f32[256,256]{1,0:T(8,128)}, f32[256,256]{1,0:T(8,128)}, f32[256,256]{1,0:T(8,128)}, f32[256,256]{1,0:T(8,128)}, /*index=5*/f32[256,256]{1,0:T(8,128)}) fusion(f32[512,256]{1,0:T(8,128)S(1)} %fusion.6, pred[256]{0:T(512)(128)(4,1)S(1)} %iota_compare_fusion, f32[512,256]{1,0:T(8,128)S(1)} %fusion.7), kind=kLoop, calls=%fused_computation.33 | loop fusion | flops 262144 | bytes 2621696 | tf_op jit(solution)/shard_map/jit(_where)/select_n | solution.py:149
  16.1 0.0 collective-permute-done.2.refs_3_
  16.1 0.0 copy-start.1
  16.2 4.3 %collective-permute-done.1.refs_2_ = bf16[272,256]{1,0:T(8,128)(2,1)S(1)} collective-permute-done((bf16[272,256]{1,0:T(8,128)(2,1)S(1)}, bf16[272,256]{1,0:T(8,128)(2,1)S(1)}, u32[]{:S(2)}, u32[]{:S(2)}) %collective-permute-start.1) | collective-permute-done | bytes 139296 | tf_op jit(solution)/shard_map/ppermute | solution.py:168
  20.5 0.0 copy-start.2
  20.5 0.0 collective-permute-done.refs_1_
  20.5 0.0 copy-start.3
  20.6 0.9 %copy.22.refs_4_ = f32[512,1]{1,0:T(8,128)} copy(f32[512,1]{0,1:T(1,128)S(1)} %bitcast.46) | data formatting | bytes 4096 | tf_op jit(solution)/shard_map/convert_element_type | solution.py:171
  21.4 0.8 %copy.23.refs_5_ = f32[512,1]{1,0:T(8,128)} copy(f32[512,1]{0,1:T(1,128)S(1)} %bitcast.45) | data formatting | bytes 4096 | tf_op jit(solution)/shard_map/convert_element_type | solution.py:172
  22.3 0.0 copy-done.1
  22.3 0.0 copy-done.2
  22.3 0.0 copy-done.3
  22.3 7.2 %shard_map.109 = bf16[512,256]{1,0:T(8,128)(2,1)} custom-call(bf16[272,256]{1,0:T(8,128)(2,1)} %get-tuple-element.27.refs_0_, bf16[272,256]{1,0:T(8,128)(2,1)} %copy-done.3, bf16[272,256]{1,0:T(8,128)(2,1)} %copy-done.2, bf16[272,256]{1,0:T(8,128)(2,1)} %copy-done.1, f32[512,1]{1,0:T(8,128)} %copy.22.refs_4_, f32[512,1]{1,0:T(8,128)} %copy.23.refs_5_, ...), custom_call_target="tpu_custom_call" | custom-call | flops 2684354560 | bytes 3145728 | tf_op jit(solution)/shard_map/pallas_call | solution.py:110
  29.5 0.9 %fusion.24 = (bf16[128,256]{1,0:T(8,128)(2,1)S(1)}, bf16[128,256]{1,0:T(8,128)(2,1)S(1)}, bf16[128,256]{1,0:T(8,128)(2,1)S(1)}) fusion(bf16[512,256]{1,0:T(8,128)(2,1)} %shard_map.109), kind=kLoop, calls=%fused_computation.58 | loop fusion | bytes 393216 | tf_op jit(solution)/shard_map/slice | solution.py:177
  30.4 1.5 %collective-permute-start.4 = (bf16[128,256]{1,0:T(8,128)(2,1)S(1)}, bf16[128,256]{1,0:T(8,128)(2,1)S(1)}, u32[]{:S(2)}, u32[]{:S(2)}) collective-permute-start(bf16[128,256]{1,0:T(8,128)(2,1)S(1)} %get-tuple-element.15), channel_id=1, source_target_pairs={{0,12},{4,0},{8,4},{12,8},{1,13},{5,1},{9,5},{13,9},{2,14},{6,2},{... | collective-permute-start | bytes 196616 | tf_op jit(solution)/shard_map/ppermute | solution.py:177
  32.0 0.6 collective-permute-start.3
  32.5 2.7 %collective-permute-start.5 = (bf16[128,256]{1,0:T(8,128)(2,1)S(1)}, bf16[128,256]{1,0:T(8,128)(2,1)S(1)}, u32[]{:S(2)}, u32[]{:S(2)}) collective-permute-start(bf16[128,256]{1,0:T(8,128)(2,1)S(1)} %get-tuple-element.14), channel_id=1, source_target_pairs={{0,8},{4,12},{8,0},{12,4},{1,9},{5,13},{9,1},{13,5},{2,10},{6,14},... | collective-permute-start | bytes 196616 | tf_op jit(solution)/shard_map/ppermute | solution.py:177
  35.2 0.0 collective-permute-done.4
  35.2 1.5 %fusion.10 = f32[128,2048]{1,0:T(8,128)S(1)} fusion(bf16[128,256]{1,0:T(8,128)(2,1)S(1)} %collective-permute-done.4, bf16[1024,4096]{1,0:T(8,128)(2,1)} %param.16, s32[]{:T(128)S(6)} %select_n.133, s32[]{:T(128)S(6)} %select_n.136), kind=kOutput, calls=%fused_computation.16 | convolution fusion | flops 134217728 | bytes 2162696 | tf_op jit(solution)/shard_map/dot_general | solution.py:123
  36.7 1.3 %collective-permute-done.3 = bf16[128,256]{1,0:T(8,128)(2,1)S(1)} collective-permute-done((bf16[128,256]{1,0:T(8,128)(2,1)S(1)}, bf16[128,256]{1,0:T(8,128)(2,1)S(1)}, u32[]{:S(2)}, u32[]{:S(2)}) %collective-permute-start.3) | collective-permute-done | bytes 65568 | tf_op jit(solution)/shard_map/ppermute | solution.py:177
  38.1 1.5 %fusion.12 = f32[128,2048]{1,0:T(8,128)S(1)} fusion(bf16[128,256]{1,0:T(8,128)(2,1)S(1)} %collective-permute-done.3, bf16[1024,4096]{1,0:T(8,128)(2,1)} %param.16, s32[]{:T(128)S(6)} %select_n.131, s32[]{:T(128)S(6)} %select_n.136), kind=kOutput, calls=%fused_computation.18 | convolution fusion | flops 134217728 | bytes 2162696 | tf_op jit(solution)/shard_map/dot_general | solution.py:123
  39.6 0.0 collective-permute-done.5
  39.6 1.5 %fusion.8 = f32[128,2048]{1,0:T(8,128)S(1)} fusion(bf16[128,256]{1,0:T(8,128)(2,1)S(1)} %collective-permute-done.5, bf16[1024,4096]{1,0:T(8,128)(2,1)} %param.16, s32[]{:T(128)S(6)} %select_n.135, s32[]{:T(128)S(6)} %select_n.136), kind=kOutput, calls=%fused_computation.14 | convolution fusion | flops 134217728 | bytes 2162696 | tf_op jit(solution)/shard_map/dot_general | solution.py:123
  41.2 1.6 %fusion.5 = bf16[128,2048]{1,0:T(8,128)(2,1)S(1)} fusion(f32[128,2048]{1,0:T(8,128)S(1)} %fusion.8, f32[128,2048]{1,0:T(8,128)S(1)} %fusion.10, f32[128,2048]{1,0:T(8,128)S(1)} %fusion.12, bf16[1024,4096]{1,0:T(8,128)(2,1)} %param.16, s32[]{:T(128)S(6)} %select_n.128, s32[]{:T(128)S(6)} %select_n.136, bf16[512,256]{1,0:T(8,128)(2,1)} %shard_map.109), kind=kOutput, calls=%fused_computation.7 | convolution fusion | flops 135266304 | bytes 4784136 | tf_op jit(solution)/shard_map/dot_general | solution.py:123
  42.8 0.1 collective-permute-start.6
  42.9 1.5 %fusion.15 = f32[128,2048]{1,0:T(8,128)S(1)} fusion(bf16[128,256]{1,0:T(8,128)(2,1)S(1)} %collective-permute-done.5, bf16[1024,4096]{1,0:T(8,128)(2,1)} %param.16, s32[]{:T(128)S(6)} %select_n.135, s32[]{:T(128)S(6)} %select_n.129), kind=kOutput, calls=%fused_computation.21 | convolution fusion | flops 134217728 | bytes 2162696 | tf_op jit(solution)/shard_map/dot_general | solution.py:123
  44.4 1.5 %fusion.17 = f32[128,2048]{1,0:T(8,128)S(1)} fusion(bf16[128,256]{1,0:T(8,128)(2,1)S(1)} %collective-permute-done.4, bf16[1024,4096]{1,0:T(8,128)(2,1)} %param.16, s32[]{:T(128)S(6)} %select_n.133, s32[]{:T(128)S(6)} %select_n.129), kind=kOutput, calls=%fused_computation.23 | convolution fusion | flops 134217728 | bytes 2162696 | tf_op jit(solution)/shard_map/dot_general | solution.py:123
  45.9 1.5 %fusion.19 = f32[128,2048]{1,0:T(8,128)S(1)} fusion(bf16[128,256]{1,0:T(8,128)(2,1)S(1)} %collective-permute-done.3, bf16[1024,4096]{1,0:T(8,128)(2,1)} %param.16, s32[]{:T(128)S(6)} %select_n.131, s32[]{:T(128)S(6)} %select_n.129), kind=kOutput, calls=%fused_computation.25 | convolution fusion | flops 134217728 | bytes 2162696 | tf_op jit(solution)/shard_map/dot_general | solution.py:123
  47.5 0.0 collective-permute-done.6
  47.5 1.7 %fusion.25 = (bf16[128,2048]{1,0:T(8,128)(2,1)S(1)}, f32[128,2048]{1,0:T(8,128)S(1)}) fusion(bf16[128,2048]{1,0:T(8,128)(2,1)S(1)} %collective-permute-done.6, f32[128,2048]{1,0:T(8,128)S(1)} %fusion.15, f32[128,2048]{1,0:T(8,128)S(1)} %fusion.17, f32[128,2048]{1,0:T(8,128)S(1)} %fusion.19, bf16[1024,4096]{1,0:T(8,128)(2,1)} %param.16, s32[]{:T(128)S(6)} %select_n.128, ...), kind=kOutput, calls=%fused_computation.59 | convolution fusion | flops 135790592 | bytes 6357000 | tf_op jit(solution)/shard_map/dot_general | solution.py:123
  49.2 1.6 %collective-permute-start.7 = (bf16[128,2048]{1,0:T(8,128)(2,1)S(1)}, bf16[128,2048]{1,0:T(8,128)(2,1)S(1)}, u32[]{:S(2)}, u32[]{:S(2)}) collective-permute-start(bf16[128,2048]{1,0:T(8,128)(2,1)S(1)} %get-tuple-element.31), channel_id=1, source_target_pairs={{0,2},{1,3},{2,0},{3,1},{4,6},{5,7},{6,4},{7,5},{8,10},{9,11},{10,... | collective-permute-start | bytes 1572872 | tf_op jit(solution)/shard_map/ppermute | solution.py:127
  50.7 12.8 %collective-permute-done.7 = bf16[128,2048]{1,0:T(8,128)(2,1)S(1)} collective-permute-done((bf16[128,2048]{1,0:T(8,128)(2,1)S(1)}, bf16[128,2048]{1,0:T(8,128)(2,1)S(1)}, u32[]{:S(2)}, u32[]{:S(2)}) %collective-permute-start.7) | collective-permute-done | bytes 524320 | tf_op jit(solution)/shard_map/ppermute | solution.py:127
  63.5 0.1 add_convert_fusion
  63.7 0.1 collective-permute-start.8
  63.8 1.9 %collective-permute-done.8 = bf16[128,2048]{1,0:T(8,128)(2,1)S(1)} collective-permute-done((bf16[128,2048]{1,0:T(8,128)(2,1)S(1)}, bf16[128,2048]{1,0:T(8,128)(2,1)S(1)}, u32[]{:S(2)}, u32[]{:S(2)}) %collective-permute-start.8) | collective-permute-done | bytes 524320 | tf_op jit(solution)/shard_map/ppermute | solution.py:127
  65.7 1.2 %maximum_select_fusion = bf16[128,4096]{1,0:T(8,128)(2,1)} fusion(bf16[128,2048]{1,0:T(8,128)(2,1)S(1)} %collective-permute-done.8, bf16[128,2048]{1,0:T(8,128)(2,1)S(1)} %add_convert_fusion, pred[]{:T(512)S(6)} %eq.55), kind=kLoop, calls=%fused_computation.12 | loop fusion | flops 4718592 | bytes 2097153 | tf_op jit(solution)/shard_map/jit(_where)/select_n | solution.py:199
  (14 shorter events, 0.2 us)
Async XLA Ops:
  0.0 14.6 %copy-start = (bf16[512,512]{1,0:T(8,128)(2,1)S(1)}, bf16[512,512]{1,0:T(8,128)(2,1)}, u32[]{:S(2)}) copy-start(bf16[512,512]{1,0:T(8,128)(2,1)} %constant.100.clone.refs_13_) | copy-start | bytes 1572868
  3.5 12.6 %collective-permute-start.2 = (bf16[272,256]{1,0:T(8,128)(2,1)S(1)}, bf16[272,256]{1,0:T(8,128)(2,1)S(1)}, u32[]{:S(2)}, u32[]{:S(2)}) collective-permute-start(bf16[272,256]{1,0:T(8,128)(2,1)S(1)} %get-tuple-element.24), channel_id=1, source_target_pairs={{0,12},{4,0},{8,4},{12,8},{1,13},{5,1},{9,5},{13,9},{2,14},{6,2},{... | collective-permute-start | bytes 417800 | tf_op jit(solution)/shard_map/ppermute | solution.py:168
  8.6 11.8 %collective-permute-start.1 = (bf16[272,256]{1,0:T(8,128)(2,1)S(1)}, bf16[272,256]{1,0:T(8,128)(2,1)S(1)}, u32[]{:S(2)}, u32[]{:S(2)}) collective-permute-start(bf16[272,256]{1,0:T(8,128)(2,1)S(1)} %get-tuple-element.26), channel_id=1, source_target_pairs={{0,8},{4,12},{8,0},{12,4},{1,9},{5,13},{9,1},{13,5},{2,10},{6,14},... | collective-permute-start | bytes 417800 | tf_op jit(solution)/shard_map/ppermute | solution.py:168
  8.6 11.9 %collective-permute-start = (bf16[272,256]{1,0:T(8,128)(2,1)S(1)}, bf16[272,256]{1,0:T(8,128)(2,1)S(1)}, u32[]{:S(2)}, u32[]{:S(2)}) collective-permute-start(bf16[272,256]{1,0:T(8,128)(2,1)S(1)} %get-tuple-element.25), channel_id=1, source_target_pairs={{0,4},{4,8},{8,12},{12,0},{1,5},{5,9},{9,13},{13,1},{2,6},{6,10},{... | collective-permute-start | bytes 417800 | tf_op jit(solution)/shard_map/ppermute | solution.py:168
  16.1 6.1 %copy-start.1 = (bf16[272,256]{1,0:T(8,128)(2,1)}, bf16[272,256]{1,0:T(8,128)(2,1)S(1)}, u32[]{:S(2)}) copy-start(bf16[272,256]{1,0:T(8,128)(2,1)S(1)} %collective-permute-done.2.refs_3_) | copy-start | bytes 417796
  20.5 1.8 %copy-start.2 = (bf16[272,256]{1,0:T(8,128)(2,1)}, bf16[272,256]{1,0:T(8,128)(2,1)S(1)}, u32[]{:S(2)}) copy-start(bf16[272,256]{1,0:T(8,128)(2,1)S(1)} %collective-permute-done.1.refs_2_) | copy-start | bytes 417796
  20.5 1.8 %copy-start.3 = (bf16[272,256]{1,0:T(8,128)(2,1)}, bf16[272,256]{1,0:T(8,128)(2,1)S(1)}, u32[]{:S(2)}) copy-start(bf16[272,256]{1,0:T(8,128)(2,1)S(1)} %collective-permute-done.refs_1_) | copy-start | bytes 417796
  30.4 4.8 %collective-permute-start.4 = (bf16[128,256]{1,0:T(8,128)(2,1)S(1)}, bf16[128,256]{1,0:T(8,128)(2,1)S(1)}, u32[]{:S(2)}, u32[]{:S(2)}) collective-permute-start(bf16[128,256]{1,0:T(8,128)(2,1)S(1)} %get-tuple-element.15), channel_id=1, source_target_pairs={{0,12},{4,0},{8,4},{12,8},{1,13},{5,1},{9,5},{13,9},{2,14},{6,2},{... | collective-permute-start | bytes 196616 | tf_op jit(solution)/shard_map/ppermute | solution.py:177
  32.0 6.1 %collective-permute-start.3 = (bf16[128,256]{1,0:T(8,128)(2,1)S(1)}, bf16[128,256]{1,0:T(8,128)(2,1)S(1)}, u32[]{:S(2)}, u32[]{:S(2)}) collective-permute-start(bf16[128,256]{1,0:T(8,128)(2,1)S(1)} %get-tuple-element.13), channel_id=1, source_target_pairs={{0,4},{4,8},{8,12},{12,0},{1,5},{5,9},{9,13},{13,1},{2,6},{6,10},{... | collective-permute-start | bytes 196616 | tf_op jit(solution)/shard_map/ppermute | solution.py:177
  32.5 7.1 %collective-permute-start.5 = (bf16[128,256]{1,0:T(8,128)(2,1)S(1)}, bf16[128,256]{1,0:T(8,128)(2,1)S(1)}, u32[]{:S(2)}, u32[]{:S(2)}) collective-permute-start(bf16[128,256]{1,0:T(8,128)(2,1)S(1)} %get-tuple-element.14), channel_id=1, source_target_pairs={{0,8},{4,12},{8,0},{12,4},{1,9},{5,13},{9,1},{13,5},{2,10},{6,14},... | collective-permute-start | bytes 196616 | tf_op jit(solution)/shard_map/ppermute | solution.py:177
  42.8 4.7 %collective-permute-start.6 = (bf16[128,2048]{1,0:T(8,128)(2,1)S(1)}, bf16[128,2048]{1,0:T(8,128)(2,1)S(1)}, u32[]{:S(2)}, u32[]{:S(2)}) collective-permute-start(bf16[128,2048]{1,0:T(8,128)(2,1)S(1)} %fusion.5), channel_id=1, source_target_pairs={{0,1},{1,0},{2,3},{3,2},{4,5},{5,4},{6,7},{7,6},{8,9},{9,8},{10,11... | collective-permute-start | bytes 1572872 | tf_op jit(solution)/shard_map/ppermute | solution.py:127
  49.2 14.4 %collective-permute-start.7 = (bf16[128,2048]{1,0:T(8,128)(2,1)S(1)}, bf16[128,2048]{1,0:T(8,128)(2,1)S(1)}, u32[]{:S(2)}, u32[]{:S(2)}) collective-permute-start(bf16[128,2048]{1,0:T(8,128)(2,1)S(1)} %get-tuple-element.31), channel_id=1, source_target_pairs={{0,2},{1,3},{2,0},{3,1},{4,6},{5,7},{6,4},{7,5},{8,10},{9,11},{10,... | collective-permute-start | bytes 1572872 | tf_op jit(solution)/shard_map/ppermute | solution.py:127
  63.7 2.0 %collective-permute-start.8 = (bf16[128,2048]{1,0:T(8,128)(2,1)S(1)}, bf16[128,2048]{1,0:T(8,128)(2,1)S(1)}, u32[]{:S(2)}, u32[]{:S(2)}) collective-permute-start(bf16[128,2048]{1,0:T(8,128)(2,1)S(1)} %add_convert_fusion), channel_id=1, source_target_pairs={{0,1},{1,0},{2,3},{3,2},{4,5},{5,4},{6,7},{7,6},{8,9},{9,8},{10,11... | collective-permute-start | bytes 1572872 | tf_op jit(solution)/shard_map/ppermute | solution.py:127

commit v10 on v9

--- a/solution.py
+++ b/solution.py
@@ -114,10 +114,48 @@
         out_specs=vmem,
         scratch_shapes=[pltpu.VMEM((length, length), BF16) for _ in range(4)]
         + [pltpu.SemaphoreType.DMA((4,))],
-        compiler_params=pltpu.CompilerParams(vmem_limit_bytes=56 * 1024 * 1024),
+        compiler_params=pltpu.CompilerParams(vmem_limit_bytes=24 * 1024 * 1024),
         cost_estimate=pl.CostEstimate(flops=flops, transcendentals=0,
                                       bytes_accessed=4 * length * length * 2 + 8 * length * per),
     )(*pieces, m0, m1, *spec1, *spec2, *mats)
+
+def proj_kernel(*refs, nseq):
+    src_ref = refs[0]
+    pieces = refs[1:1 + nseq]
+    w_hbm = refs[1 + nseq]
+    o_ref = refs[2 + nseq]
+    bufs = refs[3 + nseq:3 + 2 * nseq]
+    sem = refs[3 + 2 * nseq]
+    per = bufs[0].shape[0]
+    copies = [pltpu.make_async_copy(w_hbm.at[pl.ds(src_ref[k] * per, per), :], bufs[k], sem.at[k])
+              for k in range(nseq)]
+    for c in copies:
+        c.start()
+    acc = None
+    for k in range(nseq):
+        copies[k].wait()
+        term = jnp.dot(pieces[k][...], bufs[k][...], preferred_element_type=F32)
+        acc = term if acc is None else acc + term
+    o_ref[...] = acc
+
+
+def proj_call(srcs, pieces, out_weight):
+    nseq = len(pieces)
+    rows, per = pieces[0].shape
+    out_cols = out_weight.shape[1]
+    vmem = pl.BlockSpec(memory_space=pltpu.VMEM)
+    return pl.pallas_call(
+        functools.partial(proj_kernel, nseq=nseq),
+        out_shape=jax.ShapeDtypeStruct((rows, out_cols), F32),
+        in_specs=[pl.BlockSpec(memory_space=pltpu.SMEM)] + [vmem] * nseq + [pl.BlockSpec(memory_space=pl.ANY)],
+        out_specs=vmem,
+        scratch_shapes=[pltpu.VMEM((per, out_cols), BF16) for _ in range(nseq)]
+        + [pltpu.SemaphoreType.DMA((nseq,))],
+        compiler_params=pltpu.CompilerParams(vmem_limit_bytes=32 * 1024 * 1024),
+        cost_estimate=pl.CostEstimate(flops=2 * rows * per * nseq * out_cols, transcendentals=0,
+                                      bytes_accessed=per * nseq * out_cols * 2 + rows * out_cols * 4),
+    )(srcs, *pieces, out_weight)
+
 
 def mm(a, b):
     return jnp.dot(a, b, preferred_element_type=F32)
@@ -178,21 +216,16 @@
                                          [(i, (i + k) % nseq) for i in range(nseq)])
         out_cols = out_weight.shape[1]
 
-        def project(cols_lo, width):
-            acc = None
-            for k in order:
-                w = lax.dynamic_slice(out_weight, (((me - k) % nseq) * per, cols_lo), (per, width))
-                term = mm(mix_pieces[k], w)
-                acc = term if acc is None else acc + term
-            return acc
+        srcs = jnp.stack([((me - k) % nseq).astype(jnp.int32) for k in range(nseq)])
+        partial_out = proj_call(srcs, [mix_pieces[k] for k in range(nseq)], out_weight)
 
         if nchan != 4:
-            return lax.psum(project(0, out_cols), "chan").astype(BF16)
+            return lax.psum(partial_out, "chan").astype(BF16)
         core = lax.axis_index("chan") % 2
         width = out_cols // 2
-        other = project((1 - core) * width, width)
+        other = lax.dynamic_slice_in_dim(partial_out, (1 - core) * width, width, 1)
         got_other = swap(other.astype(BF16), 1)
-        mine = project(core * width, width)
+        mine = lax.dynamic_slice_in_dim(partial_out, core * width, width, 1)
         chip = mine + got_other.astype(F32)
         total = (chip + swap(chip.astype(BF16), 2).astype(F32)).astype(BF16)
         peer = swap(total, 1)

time: 67.7 us -> 64.1 us (0.947)
  matrix products: 16.9 us -> 2.91 us
  local copies, waits for them, and re-layouts: 4.51 us -> 10.2 us
  waiting for transfers between devices: 20.4 us -> 24.8 us
  starting transfers between devices: 12.6 us -> 13.3 us
    dot_general x12 -> x4, matrix products: 16.9 us -> 2.91 us  [mm(): return jnp.dot(a, b, preferred_element_type=F32)]
    unnamed x14 -> x24, local copies, waits for them, and re-layouts: 0.07 us -> 8.01 us
    pallas_call x1, Pallas kernels: 7.23 us -> 3.98 us  [hyena_call(): pl.pallas_call(functools.partial(hyena_kernel, nseq=nseq, rows=rows), out...]
    pallas_call x0 -> x1, Pallas kernels: none -> 2.68 us  [proj_call(): pl.pallas_call(functools.partial(proj_kernel, nseq=nseq), out_shape=jax.S...]
    ppermute x3, waiting for transfers between devices: 14.7 us -> 16.3 us  [swap(): return lax.ppermute(x, 'chan', [(c, c ^ bit) for c in range(4)])]
    ppermute x3, waiting for transfers between devices: 4.28 us -> 5.77 us  [local(): lax.ppermute(block_for((me + k) % nseq), 'seq', [(i, (i + k) % nseq) for...]
    ppermute x3, waiting for transfers between devices: 1.35 us -> 2.78 us  [local(): lax.ppermute(second_mix[k * rows:(k + 1) * rows], 'seq', [(i, (i + k) % n...]
    slice x1, local copies, waits for them, and re-layouts: 0.92 us -> 0.02 us  [local(): second_mix[k * rows:(k + 1) * rows]]
  transfers between devices with their start and end apart: 9 -> 9, of which waited for: 4 -> 6; matrix products, arithmetic and copies ran while one was open for 21% -> 8% of each run, Pallas kernels for 0% -> 0%
where the time goes in v10:
time: 64.1 us; the launch traced here: 63.7 us
  waiting for transfers between devices  24.8 us (39%)
  starting transfers between devices  13.3 us (21%)
  local copies, waits for them, and re-layouts  10.2 us (16%)
  Pallas kernels  6.66 us (10%)
  other arithmetic  5.45 us (9%)
  matrix products  2.91 us (5%)
    ppermute x3, waiting for transfers between devices, swap(): return lax.ppermute(x, 'chan', [(c, c ^ bit) for c in range(4)])  16.3 us
    unnamed x24, local copies, waits for them, and re-layouts  8.01 us
    ppermute x3, starting transfers between devices, local(): lax.ppermute(block_for((me + k) % nseq), 'seq', [(i, (i + k) % nseq) for...  6.09 us
    ppermute x3, waiting for transfers between devices, local(): lax.ppermute(block_for((me + k) % nseq), 'seq', [(i, (i + k) % nseq) for...  5.77 us
    ppermute x3, starting transfers between devices, local(): lax.ppermute(second_mix[k * rows:(k + 1) * rows], 'seq', [(i, (i + k) % n...  5.5 us
    pallas_call x1, Pallas kernels, hyena_call(): pl.pallas_call(functools.partial(hyena_kernel, nseq=nseq, rows=rows), out...  3.98 us
    dot_general x4, matrix products, mm(): return jnp.dot(a, b, preferred_element_type=F32)  2.91 us
    ppermute x3, waiting for transfers between devices, local(): lax.ppermute(second_mix[k * rows:(k + 1) * rows], 'seq', [(i, (i + k) % n...  2.78 us
  transfers between devices with their start and end apart: 9, of which 6 were waited for; matrix products, arithmetic and copies ran while one was open for 8% of the time, Pallas kernels for 0%

profile of v10, /device:TPU:0, one launch (start us, length us, event | category | flops | bytes accessed | tf_op | source)
XLA Modules:
  0.0 63.7 jit_solution(3343731661955471541)
XLA Ops:
  0.0 0.0 copy-start.2
  0.0 0.7 %convert_element_type.58 = bf16[128]{0:T(256)(128)(2,1)S(1)} convert(s32[128]{0:T(128)} %param.17) | non-fusion elementwise | flops 128 | bytes 768 | tf_op jit(solution)/shard_map/convert_element_type | solution.py:198
  0.8 1.1 %multiply_convert_fusion = bf16[128,1024]{1,0:T(8,128)(2,1)S(1)} fusion(bf16[128,1024]{1,0:T(8,128)(2,1)} %param.11, bf16[128,1024]{1,0:T(8,128)(2,1)} %param.12), kind=kLoop, calls=%fused_computation.9 | loop fusion | flops 524288 | bytes 786432 | tf_op jit(solution)/shard_map/convert_element_type | solution.py:195
  1.9 1.0 %constant_dynamic-slice_fusion = (bf16[128,256]{1,0:T(8,128)(2,1)S(1)}, bf16[128,256]{1,0:T(8,128)(2,1)S(1)}, bf16[128,256]{1,0:T(8,128)(2,1)S(1)}, bf16[128,256...) fusion(bf16[128,1024]{1,0:T(8,128)(2,1)} %param.13, ...), kind=kLoop, calls=%fused_computation.23 | loop fusion | bytes 1048592 | tf_op jit(solution)/shard_map/dynamic_slice | solution.py:201
  2.9 0.0 copy-start.1
  2.9 0.7 %pad_maximum_fusion = (bf16[272,256]{1,0:T(8,128)(2,1)}, bf16[272,256]{1,0:T(8,128)(2,1)S(1)}, bf16[272,256]{1,0:T(8,128)(2,1)S(1)}, bf16[272,256]{1,0:T(8,128)(2,1)S(1)}) fusion(bf16[16,256]{1,0:T(8,128)(2,1)S(1)} %reshape.53, bf16[128,256]{1,0:T(8,128)(2,1)S(1)} %get-tuple-element.21, bf16[128,256]{1,0:T(8,128)(2,1)S(1)} %get-tuple-element.37, ...), kind=kLoop, calls=%fused_computation.10 | loop fusion | flops 1462272 | bytes 1089536 | tf_op jit(solution)/shard_map/concatenate | solution.py:202
  3.6 5.1 %collective-permute-start.2 = (bf16[272,256]{1,0:T(8,128)(2,1)}, bf16[272,256]{1,0:T(8,128)(2,1)S(1)}, u32[]{:S(2)}, u32[]{:S(2)}) collective-permute-start(bf16[272,256]{1,0:T(8,128)(2,1)} %get-tuple-element.25), channel_id=1, source_target_pairs={{0,12},{4,0},{8,4},{12,8},{1,13},{5,1},{9,5},{13,9},{2,14},{6,2},{... | collective-permute-start | bytes 417800 | tf_op jit(solution)/shard_map/ppermute | solution.py:206
  8.7 0.0 collective-permute-start.1
  8.7 1.0 %collective-permute-start = (bf16[272,256]{1,0:T(8,128)(2,1)S(1)}, bf16[272,256]{1,0:T(8,128)(2,1)S(1)}, u32[]{:S(2)}, u32[]{:S(2)}) collective-permute-start(bf16[272,256]{1,0:T(8,128)(2,1)S(1)} %get-tuple-element.26), channel_id=1, source_target_pairs={{0,4},{4,8},{8,12},{12,0},{1,5},{5,9},{9,13},{13,1},{2,6},{6,10},{... | collective-permute-start | bytes 417800 | tf_op jit(solution)/shard_map/ppermute | solution.py:206
  9.8 0.7 %dynamic-slice_bitcast_fusion = (bf16[512,16]{0,1:T(8,128)(2,1)S(1)}, bf16[512,16]{0,1:T(8,128)(2,1)S(1)}) fusion(bf16[64,512]{1,0:T(8,128)(2,1)} %param.15, s32[]{:T(128)S(6)} %select_n.96, bf16[64,512]{1,0:T(8,128)(2,1)} %param.14), kind=kLoop, calls=%fused_computation.18 | loop fusion | bytes 65540 | tf_op jit(solution)/shard_map/transpose | solution.py:181
  10.5 0.0 copy-done.2
  10.5 0.3 fusion.5
  10.9 0.3 fusion.4
  11.2 0.0 copy-done.1
  11.2 1.1 %fusion = f32[512,256]{1,0:T(8,128)} fusion(f32[256,512]{0,1:T(8,128)S(1)} %fusion.5, bf16[512,256]{0,1:T(8,128)(2,1)S(1)} %bitcast.37, bf16[512,512]{1,0:T(8,128)(2,1)S(1)} %copy-done.1), kind=kOutput, calls=%fused_computation.1 | convolution fusion | flops 134348800 | bytes 1835008 | tf_op jit(solution)/shard_map/dot_general | solution.py:161
  12.4 1.1 %fusion.1 = f32[512,256]{1,0:T(8,128)} fusion(f32[256,512]{0,1:T(8,128)S(1)} %fusion.4, bf16[512,256]{0,1:T(8,128)(2,1)S(1)} %bitcast.39, bf16[512,512]{1,0:T(8,128)(2,1)S(1)} %copy-done.1), kind=kOutput, calls=%fused_computation.3 | convolution fusion | flops 134348800 | bytes 1835008 | tf_op jit(solution)/shard_map/dot_general | solution.py:161
  13.5 1.3 %slice_select_fusion = (f32[256,256]{1,0:T(8,128)S(1)}, f32[256,256]{1,0:T(8,128)S(1)}, f32[256,256]{1,0:T(8,128)S(1)}, f32[256,256]{1,0:T(8,128)S(1)}, f32[256,256]{1,0:T(8,128)S(1)}, /*index=5*/f32[256,256]{1,0:T(8,128)S(1)}) fusion(f32[512,256]{1,0:T(8,128)} %fusion, pred[256]{0:T(512)(128)(4,1)S(1)} %iota_compare_fusion, f32[512,256]{1,0:T(8,128)} %fusion.1), kind=kLoop, calls=%fused_computation.14 | loop fusion | flops 262144 | bytes 2621696 | tf_op jit(solution)/shard_map/jit(_where)/select_n | solution.py:187
  14.8 0.0 collective-permute-done.2.refs_3_
  14.9 5.8 %collective-permute-done.1.refs_2_ = bf16[272,256]{1,0:T(8,128)(2,1)S(1)} collective-permute-done((bf16[272,256]{1,0:T(8,128)(2,1)S(1)}, bf16[272,256]{1,0:T(8,128)(2,1)S(1)}, u32[]{:S(2)}, u32[]{:S(2)}) %collective-permute-start.1) | collective-permute-done | bytes 139296 | tf_op jit(solution)/shard_map/ppermute | solution.py:206
  20.6 0.0 copy-start.3
  20.7 0.0 collective-permute-done.refs_1_
  20.7 0.0 copy-start.5
  20.7 0.7 %copy-done.5 = bf16[272,256]{1,0:T(8,128)(2,1)} copy-done((bf16[272,256]{1,0:T(8,128)(2,1)}, bf16[272,256]{1,0:T(8,128)(2,1)S(1)}, u32[]{:S(2)}) %copy-start.5) | copy-done | bytes 139288
  21.4 0.0 copy-done.3
  21.4 0.1 copy.22.refs_4_
  21.6 0.1 copy.23.refs_5_
  21.7 0.0 copy-start.4
  21.7 0.9 %copy-done.4 = bf16[272,256]{1,0:T(8,128)(2,1)S(1)} copy-done((bf16[272,256]{1,0:T(8,128)(2,1)S(1)}, bf16[272,256]{1,0:T(8,128)(2,1)}, u32[]{:S(2)}) %copy-start.4) | copy-done | bytes 139288
  22.6 0.0 copy-start.6
  22.7 0.9 %copy-done.6 = bf16[272,256]{1,0:T(8,128)(2,1)S(1)} copy-done((bf16[272,256]{1,0:T(8,128)(2,1)S(1)}, bf16[272,256]{1,0:T(8,128)(2,1)}, u32[]{:S(2)}) %copy-start.6) | copy-done | bytes 139288
  23.6 0.0 copy-start.7
  23.6 1.0 %copy-done.7 = bf16[512,512]{1,0:T(8,128)(2,1)S(1)} copy-done((bf16[512,512]{1,0:T(8,128)(2,1)S(1)}, bf16[512,512]{1,0:T(8,128)(2,1)}, u32[]{:S(2)}) %copy-start.7) | copy-done | bytes 524312
  24.6 0.0 copy-start.8
  24.6 1.0 %copy-done.8 = bf16[512,512]{1,0:T(8,128)(2,1)S(1)} copy-done((bf16[512,512]{1,0:T(8,128)(2,1)S(1)}, bf16[512,512]{1,0:T(8,128)(2,1)}, u32[]{:S(2)}) %copy-start.8) | copy-done | bytes 524312
  25.6 4.0 %shard_map.109 = bf16[512,256]{1,0:T(8,128)(2,1)S(1)} custom-call(bf16[272,256]{1,0:T(8,128)(2,1)S(1)} %get-tuple-element.28.refs_0_, bf16[272,256]{1,0:T(8,128)(2,1)S(1)} %copy-done.6, bf16[272,256]{1,0:T(8,128)(2,1)S(1)} %copy-done.4, bf16[272,256]{1,0:T(8,128)(2,1)S(1)} %collective-permute-done.2.refs_3_, f32[512,1]{1,0:T(8,128)S(1)} %copy.22.refs_4_, ...), custom_call_target="tpu_custom_call" | custom-call | flops 2684354560 | bytes 3145728 | tf_op jit(solution)/shard_map/pallas_call | solution.py:110
  29.7 0.7 %collective-permute-start.3 = (bf16[128,256]{1,0:T(8,128)(2,1)S(1)}, bf16[128,256]{1,0:T(8,128)(2,1)S(1)}, u32[]{:S(2)}, u32[]{:S(2)}) collective-permute-start(bf16[128,256]{1,0:T(8,128)(2,1)S(1)} %get-tuple-element.15), channel_id=1, source_target_pairs={{0,4},{4,8},{8,12},{12,0},{1,5},{5,9},{9,13},{13,1},{2,6},{6,10},{... | collective-permute-start | bytes 196616 | tf_op jit(solution)/shard_map/ppermute | solution.py:215
  30.3 2.0 %collective-permute-start.4 = (bf16[128,256]{1,0:T(8,128)(2,1)S(1)}, bf16[128,256]{1,0:T(8,128)(2,1)S(1)}, u32[]{:S(2)}, u32[]{:S(2)}) collective-permute-start(bf16[128,256]{1,0:T(8,128)(2,1)S(1)} %get-tuple-element.14), channel_id=1, source_target_pairs={{0,8},{4,12},{8,0},{12,4},{1,9},{5,13},{9,1},{13,5},{2,10},{6,14},... | collective-permute-start | bytes 196616 | tf_op jit(solution)/shard_map/ppermute | solution.py:215
  32.3 2.8 %collective-permute-start.5 = (bf16[128,256]{1,0:T(8,128)(2,1)S(1)}, bf16[128,256]{1,0:T(8,128)(2,1)S(1)}, u32[]{:S(2)}, u32[]{:S(2)}) collective-permute-start(bf16[128,256]{1,0:T(8,128)(2,1)S(1)} %get-tuple-element.13), channel_id=1, source_target_pairs={{0,12},{4,0},{8,4},{12,8},{1,13},{5,1},{9,5},{13,9},{2,14},{6,2},{... | collective-permute-start | bytes 196616 | tf_op jit(solution)/shard_map/ppermute | solution.py:215
  35.2 0.1 pad_add_fusion.refs_0_
  35.2 1.2 %collective-permute-done.3.refs_2_ = bf16[128,256]{1,0:T(8,128)(2,1)S(1)} collective-permute-done((bf16[128,256]{1,0:T(8,128)(2,1)S(1)}, bf16[128,256]{1,0:T(8,128)(2,1)S(1)}, u32[]{:S(2)}, u32[]{:S(2)}) %collective-permute-start.3) | collective-permute-done | bytes 65568 | tf_op jit(solution)/shard_map/ppermute | solution.py:215
  36.5 1.5 %collective-permute-done.4.refs_3_ = bf16[128,256]{1,0:T(8,128)(2,1)S(1)} collective-permute-done((bf16[128,256]{1,0:T(8,128)(2,1)S(1)}, bf16[128,256]{1,0:T(8,128)(2,1)S(1)}, u32[]{:S(2)}, u32[]{:S(2)}) %collective-permute-start.4) | collective-permute-done | bytes 65568 | tf_op jit(solution)/shard_map/ppermute | solution.py:215
  38.0 0.0 collective-permute-done.5.refs_4_
  38.0 0.0 copy-start
  38.0 3.4 %copy-done = bf16[1024,4096]{1,0:T(8,128)(2,1)S(1)} copy-done((bf16[1024,4096]{1,0:T(8,128)(2,1)S(1)}, bf16[1024,4096]{1,0:T(8,128)(2,1)}, u32[]{:S(2)}) %copy-start) | copy-done | bytes 8388632
  41.4 2.7 %shard_map.110 = f32[128,4096]{1,0:T(8,128)S(1)} custom-call(s32[4]{0:T(128)S(1)} %pad_add_fusion.refs_0_, bf16[128,256]{1,0:T(8,128)(2,1)S(1)} %get-tuple-element.16.refs_1_, bf16[128,256]{1,0:T(8,128)(2,1)S(1)} %collective-permute-done.3.refs_2_, bf16[128,256]{1,0:T(8,128)(2,1)S(1)} %collective-permute-done.4.refs_3_, ...), custom_call_target="tpu_custom_call" | custom-call | flops 1073741824 | bytes 10485760 | tf_op jit(solution)/shard_map/pallas_call | solution.py:147
  44.1 0.1 dynamic-slice_convert_fusion
  44.2 0.1 collective-permute-start.6
  44.3 1.9 %collective-permute-done.6 = bf16[128,2048]{1,0:T(8,128)(2,1)S(1)} collective-permute-done((bf16[128,2048]{1,0:T(8,128)(2,1)S(1)}, bf16[128,2048]{1,0:T(8,128)(2,1)S(1)}, u32[]{:S(2)}, u32[]{:S(2)}) %collective-permute-start.6) | collective-permute-done | bytes 524320 | tf_op jit(solution)/shard_map/ppermute | solution.py:165
  46.1 0.1 fusion.2
  46.3 1.5 %collective-permute-start.7 = (bf16[128,2048]{1,0:T(8,128)(2,1)S(1)}, bf16[128,2048]{1,0:T(8,128)(2,1)S(1)}, u32[]{:S(2)}, u32[]{:S(2)}) collective-permute-start(bf16[128,2048]{1,0:T(8,128)(2,1)S(1)} %fusion.2), channel_id=1, source_target_pairs={{0,2},{1,3},{2,0},{3,1},{4,6},{5,7},{6,4},{7,5},{8,10},{9,11},{10,... | collective-permute-start | bytes 1572872 | tf_op jit(solution)/shard_map/ppermute | solution.py:165
  47.8 12.5 %collective-permute-done.7 = bf16[128,2048]{1,0:T(8,128)(2,1)S(1)} collective-permute-done((bf16[128,2048]{1,0:T(8,128)(2,1)S(1)}, bf16[128,2048]{1,0:T(8,128)(2,1)S(1)}, u32[]{:S(2)}, u32[]{:S(2)}) %collective-permute-start.7) | collective-permute-done | bytes 524320 | tf_op jit(solution)/shard_map/ppermute | solution.py:165
  60.3 0.2 add_convert_fusion
  60.5 0.1 collective-permute-start.8
  60.6 1.9 %collective-permute-done.8 = bf16[128,2048]{1,0:T(8,128)(2,1)S(1)} collective-permute-done((bf16[128,2048]{1,0:T(8,128)(2,1)S(1)}, bf16[128,2048]{1,0:T(8,128)(2,1)S(1)}, u32[]{:S(2)}, u32[]{:S(2)}) %collective-permute-start.8) | collective-permute-done | bytes 524320 | tf_op jit(solution)/shard_map/ppermute | solution.py:165
  62.5 1.2 %maximum_select_fusion = bf16[128,4096]{1,0:T(8,128)(2,1)} fusion(bf16[128,2048]{1,0:T(8,128)(2,1)S(1)} %collective-permute-done.8, bf16[128,2048]{1,0:T(8,128)(2,1)S(1)} %add_convert_fusion, pred[]{:T(512)S(6)} %eq.51), kind=kLoop, calls=%fused_computation.4 | loop fusion | flops 4718592 | bytes 2097153 | tf_op jit(solution)/shard_map/jit(_where)/select_n | solution.py:232
  (15 shorter events, 0.2 us)
Async XLA Ops:
  0.0 10.5 %copy-start.2 = (bf16[512,512]{1,0:T(8,128)(2,1)S(1)}, bf16[512,512]{1,0:T(8,128)(2,1)}, u32[]{:S(2)}) copy-start(bf16[512,512]{1,0:T(8,128)(2,1)} %constant.91.clone.refs_12_) | copy-start | bytes 1572868
  2.9 8.4 %copy-start.1 = (bf16[512,512]{1,0:T(8,128)(2,1)S(1)}, bf16[512,512]{1,0:T(8,128)(2,1)}, u32[]{:S(2)}) copy-start(bf16[512,512]{1,0:T(8,128)(2,1)} %constant.92.clone.refs_13_) | copy-start | bytes 1572868
  3.6 11.3 %collective-permute-start.2 = (bf16[272,256]{1,0:T(8,128)(2,1)}, bf16[272,256]{1,0:T(8,128)(2,1)S(1)}, u32[]{:S(2)}, u32[]{:S(2)}) collective-permute-start(bf16[272,256]{1,0:T(8,128)(2,1)} %get-tuple-element.25), channel_id=1, source_target_pairs={{0,12},{4,0},{8,4},{12,8},{1,13},{5,1},{9,5},{13,9},{2,14},{6,2},{... | collective-permute-start | bytes 417800 | tf_op jit(solution)/shard_map/ppermute | solution.py:206
  8.7 12.0 %collective-permute-start.1 = (bf16[272,256]{1,0:T(8,128)(2,1)S(1)}, bf16[272,256]{1,0:T(8,128)(2,1)S(1)}, u32[]{:S(2)}, u32[]{:S(2)}) collective-permute-start(bf16[272,256]{1,0:T(8,128)(2,1)S(1)} %get-tuple-element.27), channel_id=1, source_target_pairs={{0,8},{4,12},{8,0},{12,4},{1,9},{5,13},{9,1},{13,5},{2,10},{6,14},... | collective-permute-start | bytes 417800 | tf_op jit(solution)/shard_map/ppermute | solution.py:206
  8.7 12.0 %collective-permute-start = (bf16[272,256]{1,0:T(8,128)(2,1)S(1)}, bf16[272,256]{1,0:T(8,128)(2,1)S(1)}, u32[]{:S(2)}, u32[]{:S(2)}) collective-permute-start(bf16[272,256]{1,0:T(8,128)(2,1)S(1)} %get-tuple-element.26), channel_id=1, source_target_pairs={{0,4},{4,8},{8,12},{12,0},{1,5},{5,9},{9,13},{13,1},{2,6},{6,10},{... | collective-permute-start | bytes 417800 | tf_op jit(solution)/shard_map/ppermute | solution.py:206
  20.6 0.8 %copy-start.3 = (bf16[272,256]{1,0:T(8,128)(2,1)}, bf16[272,256]{1,0:T(8,128)(2,1)S(1)}, u32[]{:S(2)}) copy-start(bf16[272,256]{1,0:T(8,128)(2,1)S(1)} %collective-permute-done.1.refs_2_) | copy-start | bytes 417796
  20.7 0.7 %copy-start.5 = (bf16[272,256]{1,0:T(8,128)(2,1)}, bf16[272,256]{1,0:T(8,128)(2,1)S(1)}, u32[]{:S(2)}) copy-start(bf16[272,256]{1,0:T(8,128)(2,1)S(1)} %collective-permute-done.refs_1_) | copy-start | bytes 417796
  21.7 0.9 %copy-start.4 = (bf16[272,256]{1,0:T(8,128)(2,1)S(1)}, bf16[272,256]{1,0:T(8,128)(2,1)}, u32[]{:S(2)}) copy-start(bf16[272,256]{1,0:T(8,128)(2,1)} %copy-done.3) | copy-start | bytes 417796
  22.6 0.9 %copy-start.6 = (bf16[272,256]{1,0:T(8,128)(2,1)S(1)}, bf16[272,256]{1,0:T(8,128)(2,1)}, u32[]{:S(2)}) copy-start(bf16[272,256]{1,0:T(8,128)(2,1)} %copy-done.5) | copy-start | bytes 417796
  23.6 1.0 %copy-start.7 = (bf16[512,512]{1,0:T(8,128)(2,1)S(1)}, bf16[512,512]{1,0:T(8,128)(2,1)}, u32[]{:S(2)}) copy-start(bf16[512,512]{1,0:T(8,128)(2,1)} %constant.93.clone.refs_14_) | copy-start | bytes 1572868
  24.6 1.0 %copy-start.8 = (bf16[512,512]{1,0:T(8,128)(2,1)S(1)}, bf16[512,512]{1,0:T(8,128)(2,1)}, u32[]{:S(2)}) copy-start(bf16[512,512]{1,0:T(8,128)(2,1)} %constant.94.clone.refs_15_) | copy-start | bytes 1572868
  29.7 6.8 %collective-permute-start.3 = (bf16[128,256]{1,0:T(8,128)(2,1)S(1)}, bf16[128,256]{1,0:T(8,128)(2,1)S(1)}, u32[]{:S(2)}, u32[]{:S(2)}) collective-permute-start(bf16[128,256]{1,0:T(8,128)(2,1)S(1)} %get-tuple-element.15), channel_id=1, source_target_pairs={{0,4},{4,8},{8,12},{12,0},{1,5},{5,9},{9,13},{13,1},{2,6},{6,10},{... | collective-permute-start | bytes 196616 | tf_op jit(solution)/shard_map/ppermute | solution.py:215
  30.3 7.7 %collective-permute-start.4 = (bf16[128,256]{1,0:T(8,128)(2,1)S(1)}, bf16[128,256]{1,0:T(8,128)(2,1)S(1)}, u32[]{:S(2)}, u32[]{:S(2)}) collective-permute-start(bf16[128,256]{1,0:T(8,128)(2,1)S(1)} %get-tuple-element.14), channel_id=1, source_target_pairs={{0,8},{4,12},{8,0},{12,4},{1,9},{5,13},{9,1},{13,5},{2,10},{6,14},... | collective-permute-start | bytes 196616 | tf_op jit(solution)/shard_map/ppermute | solution.py:215
  32.3 5.7 %collective-permute-start.5 = (bf16[128,256]{1,0:T(8,128)(2,1)S(1)}, bf16[128,256]{1,0:T(8,128)(2,1)S(1)}, u32[]{:S(2)}, u32[]{:S(2)}) collective-permute-start(bf16[128,256]{1,0:T(8,128)(2,1)S(1)} %get-tuple-element.13), channel_id=1, source_target_pairs={{0,12},{4,0},{8,4},{12,8},{1,13},{5,1},{9,5},{13,9},{2,14},{6,2},{... | collective-permute-start | bytes 196616 | tf_op jit(solution)/shard_map/ppermute | solution.py:215
  38.0 3.4 %copy-start = (bf16[1024,4096]{1,0:T(8,128)(2,1)S(1)}, bf16[1024,4096]{1,0:T(8,128)(2,1)}, u32[]{:S(2)}) copy-start(bf16[1024,4096]{1,0:T(8,128)(2,1)} %refs_5_.1) | copy-start | bytes 25165828
  44.2 2.0 %collective-permute-start.6 = (bf16[128,2048]{1,0:T(8,128)(2,1)S(1)}, bf16[128,2048]{1,0:T(8,128)(2,1)S(1)}, u32[]{:S(2)}, u32[]{:S(2)}) collective-permute-start(bf16[128,2048]{1,0:T(8,128)(2,1)S(1)} %dynamic-slice_convert_fusion), channel_id=1, source_target_pairs={{0,1},{1,0},{2,3},{3,2},{4,5},{5,4},{6,7},{7,6},{8,9},{9,8},{10,11... | collective-permute-start | bytes 1572872 | tf_op jit(solution)/shard_map/ppermute | solution.py:165
  46.3 14.0 %collective-permute-start.7 = (bf16[128,2048]{1,0:T(8,128)(2,1)S(1)}, bf16[128,2048]{1,0:T(8,128)(2,1)S(1)}, u32[]{:S(2)}, u32[]{:S(2)}) collective-permute-start(bf16[128,2048]{1,0:T(8,128)(2,1)S(1)} %fusion.2), channel_id=1, source_target_pairs={{0,2},{1,3},{2,0},{3,1},{4,6},{5,7},{6,4},{7,5},{8,10},{9,11},{10,... | collective-permute-start | bytes 1572872 | tf_op jit(solution)/shard_map/ppermute | solution.py:165
  60.5 2.0 %collective-permute-start.8 = (bf16[128,2048]{1,0:T(8,128)(2,1)S(1)}, bf16[128,2048]{1,0:T(8,128)(2,1)S(1)}, u32[]{:S(2)}, u32[]{:S(2)}) collective-permute-start(bf16[128,2048]{1,0:T(8,128)(2,1)S(1)} %add_convert_fusion), channel_id=1, source_target_pairs={{0,1},{1,0},{2,3},{3,2},{4,5},{5,4},{6,7},{7,6},{8,9},{9,8},{10,11... | collective-permute-start | bytes 1572872 | tf_op jit(solution)/shard_map/ppermute | solution.py:165

commit v11 on v10

--- a/solution.py
+++ b/solution.py
@@ -83,58 +83,57 @@
     m0_ref, m1_ref = refs[nseq:nseq + 2]
     spec_refs = refs[nseq + 2:nseq + 8]
     mats_hbm = refs[nseq + 8:nseq + 12]
-    o_ref = refs[nseq + 12]
-    mats = refs[nseq + 13:nseq + 17]
-    sem = refs[nseq + 17]
+    w_hbm = refs[nseq + 12]
+    o_ref, w_out = refs[nseq + 13:nseq + 15]
+    mats = refs[nseq + 15:nseq + 19]
+    sem = refs[nseq + 19]
     copies = [pltpu.make_async_copy(mats_hbm[i], mats[i], sem.at[i]) for i in range(4)]
+    w_copy = pltpu.make_async_copy(w_hbm, w_out, sem.at[4])
     for c in copies:
         c.start()
+    w_copy.start()
     loader = lambda r: (lambda: r[...])
     spec1 = [loader(r) for r in spec_refs[:3]]
     spec2 = [loader(r) for r in spec_refs[3:]]
     o_ref[...] = hyena_math(pieces, m0_ref[...], m1_ref[...], spec1, spec2,
                             [loader(r) for r in mats], rows, lambda i: copies[i].wait(), True)
-
-
-def hyena_call(pieces, m0, m1, spec1, spec2, mats, rows):
+    w_copy.wait()
+
+
+def hyena_call(pieces, m0, m1, spec1, spec2, mats, rows, out_weight):
     nseq = len(pieces)
     length = m0.shape[0]
     per = pieces[0].shape[1]
     if 4 * length * length * 2 > 8 * 1024 * 1024:
         const = lambda v: (lambda: v)
         return hyena_math(pieces, m0, m1, [const(v) for v in spec1], [const(v) for v in spec2],
-                          [const(v) for v in mats], rows, lambda i: None, False)
+                          [const(v) for v in mats], rows, lambda i: None, False), out_weight
     vmem = pl.BlockSpec(memory_space=pltpu.VMEM)
-    hbm = pl.BlockSpec(memory_space=pl.ANY)
+    hbm = pl.BlockSpec(memory_space=pltpu.MemorySpace.HBM)
     flops = 2 * (2 * length * length * 2 * per * 5)
     return pl.pallas_call(
         functools.partial(hyena_kernel, nseq=nseq, rows=rows),
-        out_shape=jax.ShapeDtypeStruct((length, per), BF16),
-        in_specs=[vmem] * (nseq + 8) + [hbm] * 4,
-        out_specs=vmem,
+        out_shape=(jax.ShapeDtypeStruct((length, per), BF16),
+                   jax.ShapeDtypeStruct(out_weight.shape, out_weight.dtype)),
+        in_specs=[vmem] * (nseq + 8) + [hbm] * 5,
+        out_specs=(vmem, vmem),
         scratch_shapes=[pltpu.VMEM((length, length), BF16) for _ in range(4)]
-        + [pltpu.SemaphoreType.DMA((4,))],
-        compiler_params=pltpu.CompilerParams(vmem_limit_bytes=24 * 1024 * 1024),
+        + [pltpu.SemaphoreType.DMA((5,))],
+        compiler_params=pltpu.CompilerParams(vmem_limit_bytes=40 * 1024 * 1024),
         cost_estimate=pl.CostEstimate(flops=flops, transcendentals=0,
                                       bytes_accessed=4 * length * length * 2 + 8 * length * per),
-    )(*pieces, m0, m1, *spec1, *spec2, *mats)
+    )(*pieces, m0, m1, *spec1, *spec2, *mats, out_weight)
 
 def proj_kernel(*refs, nseq):
     src_ref = refs[0]
     pieces = refs[1:1 + nseq]
-    w_hbm = refs[1 + nseq]
+    w_ref = refs[1 + nseq]
     o_ref = refs[2 + nseq]
-    bufs = refs[3 + nseq:3 + 2 * nseq]
-    sem = refs[3 + 2 * nseq]
-    per = bufs[0].shape[0]
-    copies = [pltpu.make_async_copy(w_hbm.at[pl.ds(src_ref[k] * per, per), :], bufs[k], sem.at[k])
-              for k in range(nseq)]
-    for c in copies:
-        c.start()
+    per = pieces[0].shape[1]
     acc = None
     for k in range(nseq):
-        copies[k].wait()
-        term = jnp.dot(pieces[k][...], bufs[k][...], preferred_element_type=F32)
+        start = pl.multiple_of(src_ref[k] * per, per)
+        term = jnp.dot(pieces[k][...], w_ref[pl.ds(start, per), :], preferred_element_type=F32)
         acc = term if acc is None else acc + term
     o_ref[...] = acc
 
@@ -147,11 +146,9 @@
     return pl.pallas_call(
         functools.partial(proj_kernel, nseq=nseq),
         out_shape=jax.ShapeDtypeStruct((rows, out_cols), F32),
-        in_specs=[pl.BlockSpec(memory_space=pltpu.SMEM)] + [vmem] * nseq + [pl.BlockSpec(memory_space=pl.ANY)],
+        in_specs=[pl.BlockSpec(memory_space=pltpu.SMEM)] + [vmem] * (nseq + 1),
         out_specs=vmem,
-        scratch_shapes=[pltpu.VMEM((per, out_cols), BF16) for _ in range(nseq)]
-        + [pltpu.SemaphoreType.DMA((nseq,))],
-        compiler_params=pltpu.CompilerParams(vmem_limit_bytes=32 * 1024 * 1024),
+        compiler_params=pltpu.CompilerParams(vmem_limit_bytes=24 * 1024 * 1024),
         cost_estimate=pl.CostEstimate(flops=2 * rows * per * nseq * out_cols, transcendentals=0,
                                       bytes_accessed=per * nseq * out_cols * 2 + rows * out_cols * 4),
     )(srcs, *pieces, out_weight)
@@ -208,8 +205,9 @@
         segs = seg_blocks.reshape(nseq, pad_rows * per)[:, :rows].reshape(nseq * rows)
         in0 = (segs == 0).astype(F32)[:, None]
         in1 = (segs == 1).astype(F32)[:, None]
-        second_mix = hyena_call([got[k] for k in range(nseq)], in0, in1, spectrum(first_filter),
-                                spectrum(second_filter), (f_hi, f_lo, i_hi, i_lo), rows)
+        second_mix, staged_weight = hyena_call(
+            [got[k] for k in range(nseq)], in0, in1, spectrum(first_filter),
+            spectrum(second_filter), (f_hi, f_lo, i_hi, i_lo), rows, out_weight)
         mix_pieces = {0: second_mix[:rows]}
         for k in order[1:]:
             mix_pieces[k] = lax.ppermute(second_mix[k * rows:(k + 1) * rows], "seq",
@@ -217,7 +215,7 @@
         out_cols = out_weight.shape[1]
 
         srcs = jnp.stack([((me - k) % nseq).astype(jnp.int32) for k in range(nseq)])
-        partial_out = proj_call(srcs, [mix_pieces[k] for k in range(nseq)], out_weight)
+        partial_out = proj_call(srcs, [mix_pieces[k] for k in range(nseq)], staged_weight)
 
         if nchan != 4:
             return lax.psum(partial_out, "chan").astype(BF16)

time: 64.1 us -> 59.8 us (0.933)
  local copies, waits for them, and re-layouts: 10.2 us -> 6.84 us
  Pallas kernels: 6.66 us -> 5.8 us
    unnamed x24 -> x22, local copies, waits for them, and re-layouts: 8.01 us -> 4.63 us
    pallas_call x1, Pallas kernels: 2.68 us -> 1.81 us  [proj_call(): pl.pallas_call(functools.partial(proj_kernel, nseq=nseq), out_shape=jax.S...]
  transfers between devices with their start and end apart: 9 -> 9, of which waited for: 6 -> 6; matrix products, arithmetic and copies ran while one was open for 8% -> 9% of each run, Pallas kernels for 0% -> 0%
where the time goes in v11:
time: 59.8 us; the launch traced here: 59.4 us
  waiting for transfers between devices  24.8 us (41%)
  starting transfers between devices  13.3 us (22%)
  local copies, waits for them, and re-layouts  6.84 us (11%)
  Pallas kernels  5.8 us (10%)
  other arithmetic  5.45 us (9%)
  matrix products  2.91 us (5%)
    ppermute x3, waiting for transfers between devices, swap(): return lax.ppermute(x, 'chan', [(c, c ^ bit) for c in range(4)])  16.3 us
    ppermute x3, starting transfers between devices, local(): lax.ppermute(block_for((me + k) % nseq), 'seq', [(i, (i + k) % nseq) for...  6.09 us
    ppermute x3, waiting for transfers between devices, local(): lax.ppermute(block_for((me + k) % nseq), 'seq', [(i, (i + k) % nseq) for...  5.77 us
    ppermute x3, starting transfers between devices, local(): lax.ppermute(second_mix[k * rows:(k + 1) * rows], 'seq', [(i, (i + k) % n...  5.51 us
    unnamed x22, local copies, waits for them, and re-layouts  4.63 us
    pallas_call x1, Pallas kernels, hyena_call(): pl.pallas_call(functools.partial(hyena_kernel, nseq=nseq, rows=rows), out...  3.99 us
    dot_general x4, matrix products, mm(): return jnp.dot(a, b, preferred_element_type=F32)  2.91 us
    ppermute x3, waiting for transfers between devices, local(): lax.ppermute(second_mix[k * rows:(k + 1) * rows], 'seq', [(i, (i + k) % n...  2.77 us
  transfers between devices with their start and end apart: 9, of which 6 were waited for; matrix products, arithmetic and copies ran while one was open for 9% of the time, Pallas kernels for 0%

profile of v11, /device:TPU:0, one launch (start us, length us, event | category | flops | bytes accessed | tf_op | source)
XLA Modules:
  0.0 59.4 jit_solution(10219340472691725958)
XLA Ops:
  0.0 0.0 copy-start.1
  0.0 0.7 %convert_element_type.58 = bf16[128]{0:T(256)(128)(2,1)S(1)} convert(s32[128]{0:T(128)} %param.17) | non-fusion elementwise | flops 128 | bytes 768 | tf_op jit(solution)/shard_map/convert_element_type | solution.py:195
  0.8 1.1 %multiply_convert_fusion = bf16[128,1024]{1,0:T(8,128)(2,1)S(1)} fusion(bf16[128,1024]{1,0:T(8,128)(2,1)} %param.11, bf16[128,1024]{1,0:T(8,128)(2,1)} %param.12), kind=kLoop, calls=%fused_computation.9 | loop fusion | flops 524288 | bytes 786432 | tf_op jit(solution)/shard_map/convert_element_type | solution.py:192
  1.9 1.0 %constant_dynamic-slice_fusion = (bf16[128,256]{1,0:T(8,128)(2,1)S(1)}, bf16[128,256]{1,0:T(8,128)(2,1)S(1)}, bf16[128,256]{1,0:T(8,128)(2,1)S(1)}, bf16[128,256...) fusion(bf16[128,1024]{1,0:T(8,128)(2,1)} %param.13, ...), kind=kLoop, calls=%fused_computation.23 | loop fusion | bytes 1048592 | tf_op jit(solution)/shard_map/dynamic_slice | solution.py:198
  2.9 0.0 copy-start
  2.9 0.7 %pad_maximum_fusion = (bf16[272,256]{1,0:T(8,128)(2,1)}, bf16[272,256]{1,0:T(8,128)(2,1)S(1)}, bf16[272,256]{1,0:T(8,128)(2,1)S(1)}, bf16[272,256]{1,0:T(8,128)(2,1)S(1)}) fusion(bf16[16,256]{1,0:T(8,128)(2,1)S(1)} %reshape.53, bf16[128,256]{1,0:T(8,128)(2,1)S(1)} %get-tuple-element.25, bf16[128,256]{1,0:T(8,128)(2,1)S(1)} %get-tuple-element.39, ...), kind=kLoop, calls=%fused_computation.10 | loop fusion | flops 1462272 | bytes 1089536 | tf_op jit(solution)/shard_map/concatenate | solution.py:199
  3.6 5.1 %collective-permute-start.2 = (bf16[272,256]{1,0:T(8,128)(2,1)}, bf16[272,256]{1,0:T(8,128)(2,1)S(1)}, u32[]{:S(2)}, u32[]{:S(2)}) collective-permute-start(bf16[272,256]{1,0:T(8,128)(2,1)} %get-tuple-element.29), channel_id=1, source_target_pairs={{0,12},{4,0},{8,4},{12,8},{1,13},{5,1},{9,5},{13,9},{2,14},{6,2},{... | collective-permute-start | bytes 417800 | tf_op jit(solution)/shard_map/ppermute | solution.py:203
  8.7 0.0 collective-permute-start.1
  8.7 1.0 %collective-permute-start = (bf16[272,256]{1,0:T(8,128)(2,1)S(1)}, bf16[272,256]{1,0:T(8,128)(2,1)S(1)}, u32[]{:S(2)}, u32[]{:S(2)}) collective-permute-start(bf16[272,256]{1,0:T(8,128)(2,1)S(1)} %get-tuple-element.30), channel_id=1, source_target_pairs={{0,4},{4,8},{8,12},{12,0},{1,5},{5,9},{9,13},{13,1},{2,6},{6,10},{... | collective-permute-start | bytes 417800 | tf_op jit(solution)/shard_map/ppermute | solution.py:203
  9.8 0.7 %dynamic-slice_bitcast_fusion = (bf16[512,16]{0,1:T(8,128)(2,1)S(1)}, bf16[512,16]{0,1:T(8,128)(2,1)S(1)}) fusion(bf16[64,512]{1,0:T(8,128)(2,1)} %param.15, s32[]{:T(128)S(6)} %select_n.96, bf16[64,512]{1,0:T(8,128)(2,1)} %param.14), kind=kLoop, calls=%fused_computation.18 | loop fusion | bytes 65540 | tf_op jit(solution)/shard_map/transpose | solution.py:178
  10.5 0.0 copy-done.1
  10.5 0.3 fusion.5
  10.9 0.3 fusion.4
  11.2 0.0 copy-done
  11.2 1.1 %fusion = f32[512,256]{1,0:T(8,128)} fusion(f32[256,512]{0,1:T(8,128)S(1)} %fusion.5, bf16[512,256]{0,1:T(8,128)(2,1)S(1)} %bitcast.37, bf16[512,512]{1,0:T(8,128)(2,1)S(1)} %copy-done), kind=kOutput, calls=%fused_computation.1 | convolution fusion | flops 134348800 | bytes 1835008 | tf_op jit(solution)/shard_map/dot_general | solution.py:158
  12.4 1.1 %fusion.1 = f32[512,256]{1,0:T(8,128)} fusion(f32[256,512]{0,1:T(8,128)S(1)} %fusion.4, bf16[512,256]{0,1:T(8,128)(2,1)S(1)} %bitcast.39, bf16[512,512]{1,0:T(8,128)(2,1)S(1)} %copy-done), kind=kOutput, calls=%fused_computation.3 | convolution fusion | flops 134348800 | bytes 1835008 | tf_op jit(solution)/shard_map/dot_general | solution.py:158
  13.5 1.3 %slice_select_fusion = (f32[256,256]{1,0:T(8,128)S(1)}, f32[256,256]{1,0:T(8,128)S(1)}, f32[256,256]{1,0:T(8,128)S(1)}, f32[256,256]{1,0:T(8,128)S(1)}, f32[256,256]{1,0:T(8,128)S(1)}, /*index=5*/f32[256,256]{1,0:T(8,128)S(1)}) fusion(f32[512,256]{1,0:T(8,128)} %fusion, pred[256]{0:T(512)(128)(4,1)S(1)} %iota_compare_fusion, f32[512,256]{1,0:T(8,128)} %fusion.1), kind=kLoop, calls=%fused_computation.14 | loop fusion | flops 262144 | bytes 2621696 | tf_op jit(solution)/shard_map/jit(_where)/select_n | solution.py:184
  14.8 0.0 collective-permute-done.2.refs_3_
  14.9 5.8 %collective-permute-done.1.refs_2_ = bf16[272,256]{1,0:T(8,128)(2,1)S(1)} collective-permute-done((bf16[272,256]{1,0:T(8,128)(2,1)S(1)}, bf16[272,256]{1,0:T(8,128)(2,1)S(1)}, u32[]{:S(2)}, u32[]{:S(2)}) %collective-permute-start.1) | collective-permute-done | bytes 139296 | tf_op jit(solution)/shard_map/ppermute | solution.py:203
  20.6 0.0 copy-start.4
  20.7 0.0 collective-permute-done.refs_1_
  20.7 0.0 copy-start.6
  20.7 0.7 %copy-done.6 = bf16[272,256]{1,0:T(8,128)(2,1)} copy-done((bf16[272,256]{1,0:T(8,128)(2,1)}, bf16[272,256]{1,0:T(8,128)(2,1)S(1)}, u32[]{:S(2)}) %copy-start.6) | copy-done | bytes 139288
  21.4 0.0 copy-done.4
  21.4 0.1 copy.22.refs_4_
  21.6 0.1 copy.23.refs_5_
  21.7 0.0 copy-start.2
  21.7 1.0 %copy-done.2 = bf16[512,512]{1,0:T(8,128)(2,1)S(1)} copy-done((bf16[512,512]{1,0:T(8,128)(2,1)S(1)}, bf16[512,512]{1,0:T(8,128)(2,1)}, u32[]{:S(2)}) %copy-start.2) | copy-done | bytes 524312
  22.8 0.0 copy-start.3
  22.8 1.0 %copy-done.3 = bf16[512,512]{1,0:T(8,128)(2,1)S(1)} copy-done((bf16[512,512]{1,0:T(8,128)(2,1)S(1)}, bf16[512,512]{1,0:T(8,128)(2,1)}, u32[]{:S(2)}) %copy-start.3) | copy-done | bytes 524312
  23.8 0.0 copy-start.5
  23.8 0.9 %copy-done.5 = bf16[272,256]{1,0:T(8,128)(2,1)S(1)} copy-done((bf16[272,256]{1,0:T(8,128)(2,1)S(1)}, bf16[272,256]{1,0:T(8,128)(2,1)}, u32[]{:S(2)}) %copy-start.5) | copy-done | bytes 139288
  24.7 0.0 copy-start.7
  24.7 0.9 %copy-done.7 = bf16[272,256]{1,0:T(8,128)(2,1)S(1)} copy-done((bf16[272,256]{1,0:T(8,128)(2,1)S(1)}, bf16[272,256]{1,0:T(8,128)(2,1)}, u32[]{:S(2)}) %copy-start.7) | copy-done | bytes 139288
  25.6 4.0 %shard_map.109 = (bf16[512,256]{1,0:T(8,128)(2,1)S(1)}, bf16[1024,4096]{1,0:T(8,128)(2,1)S(1)}) custom-call(bf16[272,256]{1,0:T(8,128)(2,1)S(1)} %get-tuple-element.32.refs_0_, bf16[272,256]{1,0:T(8,128)(2,1)S(1)} %copy-done.7, bf16[272,256]{1,0:T(8,128)(2,1)S(1)} %copy-done.5, bf16[272,256]{1,0:T(8,128)(2,1)S(1)} %collective-permute-done.2.refs_3_, ...), custom_call_target="tpu_custom_call" | custom-call | flops 2684354560 | bytes 3145728 | tf_op jit(solution)/shard_map/pallas_call | solution.py:114
  29.7 0.7 %collective-permute-start.3 = (bf16[128,256]{1,0:T(8,128)(2,1)S(1)}, bf16[128,256]{1,0:T(8,128)(2,1)S(1)}, u32[]{:S(2)}, u32[]{:S(2)}) collective-permute-start(bf16[128,256]{1,0:T(8,128)(2,1)S(1)} %get-tuple-element.19), channel_id=1, source_target_pairs={{0,4},{4,8},{8,12},{12,0},{1,5},{5,9},{9,13},{13,1},{2,6},{6,10},{... | collective-permute-start | bytes 196616 | tf_op jit(solution)/shard_map/ppermute | solution.py:213
  30.3 2.0 %collective-permute-start.4 = (bf16[128,256]{1,0:T(8,128)(2,1)S(1)}, bf16[128,256]{1,0:T(8,128)(2,1)S(1)}, u32[]{:S(2)}, u32[]{:S(2)}) collective-permute-start(bf16[128,256]{1,0:T(8,128)(2,1)S(1)} %get-tuple-element.18), channel_id=1, source_target_pairs={{0,8},{4,12},{8,0},{12,4},{1,9},{5,13},{9,1},{13,5},{2,10},{6,14},... | collective-permute-start | bytes 196616 | tf_op jit(solution)/shard_map/ppermute | solution.py:213
  32.3 2.8 %collective-permute-start.5 = (bf16[128,256]{1,0:T(8,128)(2,1)S(1)}, bf16[128,256]{1,0:T(8,128)(2,1)S(1)}, u32[]{:S(2)}, u32[]{:S(2)}) collective-permute-start(bf16[128,256]{1,0:T(8,128)(2,1)S(1)} %get-tuple-element.17), channel_id=1, source_target_pairs={{0,12},{4,0},{8,4},{12,8},{1,13},{5,1},{9,5},{13,9},{2,14},{6,2},{... | collective-permute-start | bytes 196616 | tf_op jit(solution)/shard_map/ppermute | solution.py:213
  35.2 0.1 pad_add_fusion.refs_0_
  35.3 1.2 %collective-permute-done.3.refs_2_ = bf16[128,256]{1,0:T(8,128)(2,1)S(1)} collective-permute-done((bf16[128,256]{1,0:T(8,128)(2,1)S(1)}, bf16[128,256]{1,0:T(8,128)(2,1)S(1)}, u32[]{:S(2)}, u32[]{:S(2)}) %collective-permute-start.3) | collective-permute-done | bytes 65568 | tf_op jit(solution)/shard_map/ppermute | solution.py:213
  36.5 1.5 %collective-permute-done.4.refs_3_ = bf16[128,256]{1,0:T(8,128)(2,1)S(1)} collective-permute-done((bf16[128,256]{1,0:T(8,128)(2,1)S(1)}, bf16[128,256]{1,0:T(8,128)(2,1)S(1)}, u32[]{:S(2)}, u32[]{:S(2)}) %collective-permute-start.4) | collective-permute-done | bytes 65568 | tf_op jit(solution)/shard_map/ppermute | solution.py:213
  38.0 0.0 collective-permute-done.5.refs_4_
  38.0 1.8 %shard_map.110 = f32[128,4096]{1,0:T(8,128)S(1)} custom-call(s32[4]{0:T(128)S(1)} %pad_add_fusion.refs_0_, bf16[128,256]{1,0:T(8,128)(2,1)S(1)} %get-tuple-element.20.refs_1_, bf16[128,256]{1,0:T(8,128)(2,1)S(1)} %collective-permute-done.3.refs_2_, bf16[128,256]{1,0:T(8,128)(2,1)S(1)} %collective-permute-done.4.refs_3_, ...), custom_call_target="tpu_custom_call" | custom-call | flops 1073741824 | bytes 10485760 | tf_op jit(solution)/shard_map/pallas_call | solution.py:146
  39.8 0.1 dynamic-slice_convert_fusion
  39.9 0.1 collective-permute-start.6
  40.0 1.9 %collective-permute-done.6 = bf16[128,2048]{1,0:T(8,128)(2,1)S(1)} collective-permute-done((bf16[128,2048]{1,0:T(8,128)(2,1)S(1)}, bf16[128,2048]{1,0:T(8,128)(2,1)S(1)}, u32[]{:S(2)}, u32[]{:S(2)}) %collective-permute-start.6) | collective-permute-done | bytes 524320 | tf_op jit(solution)/shard_map/ppermute | solution.py:162
  41.9 0.1 fusion.2
  42.0 1.6 %collective-permute-start.7 = (bf16[128,2048]{1,0:T(8,128)(2,1)S(1)}, bf16[128,2048]{1,0:T(8,128)(2,1)S(1)}, u32[]{:S(2)}, u32[]{:S(2)}) collective-permute-start(bf16[128,2048]{1,0:T(8,128)(2,1)S(1)} %fusion.2), channel_id=1, source_target_pairs={{0,2},{1,3},{2,0},{3,1},{4,6},{5,7},{6,4},{7,5},{8,10},{9,11},{10,... | collective-permute-start | bytes 1572872 | tf_op jit(solution)/shard_map/ppermute | solution.py:162
  43.6 12.5 %collective-permute-done.7 = bf16[128,2048]{1,0:T(8,128)(2,1)S(1)} collective-permute-done((bf16[128,2048]{1,0:T(8,128)(2,1)S(1)}, bf16[128,2048]{1,0:T(8,128)(2,1)S(1)}, u32[]{:S(2)}, u32[]{:S(2)}) %collective-permute-start.7) | collective-permute-done | bytes 524320 | tf_op jit(solution)/shard_map/ppermute | solution.py:162
  56.0 0.2 add_convert_fusion
  56.2 0.1 collective-permute-start.8
  56.3 1.9 %collective-permute-done.8 = bf16[128,2048]{1,0:T(8,128)(2,1)S(1)} collective-permute-done((bf16[128,2048]{1,0:T(8,128)(2,1)S(1)}, bf16[128,2048]{1,0:T(8,128)(2,1)S(1)}, u32[]{:S(2)}, u32[]{:S(2)}) %collective-permute-start.8) | collective-permute-done | bytes 524320 | tf_op jit(solution)/shard_map/ppermute | solution.py:162
  58.2 1.2 %maximum_select_fusion = bf16[128,4096]{1,0:T(8,128)(2,1)} fusion(bf16[128,2048]{1,0:T(8,128)(2,1)S(1)} %collective-permute-done.8, bf16[128,2048]{1,0:T(8,128)(2,1)S(1)} %add_convert_fusion, pred[]{:T(512)S(6)} %eq.51), kind=kLoop, calls=%fused_computation.4 | loop fusion | flops 4718592 | bytes 2097153 | tf_op jit(solution)/shard_map/jit(_where)/select_n | solution.py:230
  (15 shorter events, 0.2 us)
Async XLA Ops:
  0.0 10.5 %copy-start.1 = (bf16[512,512]{1,0:T(8,128)(2,1)S(1)}, bf16[512,512]{1,0:T(8,128)(2,1)}, u32[]{:S(2)}) copy-start(bf16[512,512]{1,0:T(8,128)(2,1)} %constant.91.clone.refs_12_) | copy-start | bytes 1572868
  2.9 8.4 %copy-start = (bf16[512,512]{1,0:T(8,128)(2,1)S(1)}, bf16[512,512]{1,0:T(8,128)(2,1)}, u32[]{:S(2)}) copy-start(bf16[512,512]{1,0:T(8,128)(2,1)} %constant.92.clone.refs_13_) | copy-start | bytes 1572868
  3.6 11.3 %collective-permute-start.2 = (bf16[272,256]{1,0:T(8,128)(2,1)}, bf16[272,256]{1,0:T(8,128)(2,1)S(1)}, u32[]{:S(2)}, u32[]{:S(2)}) collective-permute-start(bf16[272,256]{1,0:T(8,128)(2,1)} %get-tuple-element.29), channel_id=1, source_target_pairs={{0,12},{4,0},{8,4},{12,8},{1,13},{5,1},{9,5},{13,9},{2,14},{6,2},{... | collective-permute-start | bytes 417800 | tf_op jit(solution)/shard_map/ppermute | solution.py:203
  8.7 12.0 %collective-permute-start.1 = (bf16[272,256]{1,0:T(8,128)(2,1)S(1)}, bf16[272,256]{1,0:T(8,128)(2,1)S(1)}, u32[]{:S(2)}, u32[]{:S(2)}) collective-permute-start(bf16[272,256]{1,0:T(8,128)(2,1)S(1)} %get-tuple-element.31), channel_id=1, source_target_pairs={{0,8},{4,12},{8,0},{12,4},{1,9},{5,13},{9,1},{13,5},{2,10},{6,14},... | collective-permute-start | bytes 417800 | tf_op jit(solution)/shard_map/ppermute | solution.py:203
  8.7 12.0 %collective-permute-start = (bf16[272,256]{1,0:T(8,128)(2,1)S(1)}, bf16[272,256]{1,0:T(8,128)(2,1)S(1)}, u32[]{:S(2)}, u32[]{:S(2)}) collective-permute-start(bf16[272,256]{1,0:T(8,128)(2,1)S(1)} %get-tuple-element.30), channel_id=1, source_target_pairs={{0,4},{4,8},{8,12},{12,0},{1,5},{5,9},{9,13},{13,1},{2,6},{6,10},{... | collective-permute-start | bytes 417800 | tf_op jit(solution)/shard_map/ppermute | solution.py:203
  20.6 0.8 %copy-start.4 = (bf16[272,256]{1,0:T(8,128)(2,1)}, bf16[272,256]{1,0:T(8,128)(2,1)S(1)}, u32[]{:S(2)}) copy-start(bf16[272,256]{1,0:T(8,128)(2,1)S(1)} %collective-permute-done.1.refs_2_) | copy-start | bytes 417796
  20.7 0.7 %copy-start.6 = (bf16[272,256]{1,0:T(8,128)(2,1)}, bf16[272,256]{1,0:T(8,128)(2,1)S(1)}, u32[]{:S(2)}) copy-start(bf16[272,256]{1,0:T(8,128)(2,1)S(1)} %collective-permute-done.refs_1_) | copy-start | bytes 417796
  21.7 1.0 %copy-start.2 = (bf16[512,512]{1,0:T(8,128)(2,1)S(1)}, bf16[512,512]{1,0:T(8,128)(2,1)}, u32[]{:S(2)}) copy-start(bf16[512,512]{1,0:T(8,128)(2,1)} %constant.93.clone.refs_14_) | copy-start | bytes 1572868
  22.8 1.0 %copy-start.3 = (bf16[512,512]{1,0:T(8,128)(2,1)S(1)}, bf16[512,512]{1,0:T(8,128)(2,1)}, u32[]{:S(2)}) copy-start(bf16[512,512]{1,0:T(8,128)(2,1)} %constant.94.clone.refs_15_) | copy-start | bytes 1572868
  23.8 0.9 %copy-start.5 = (bf16[272,256]{1,0:T(8,128)(2,1)S(1)}, bf16[272,256]{1,0:T(8,128)(2,1)}, u32[]{:S(2)}) copy-start(bf16[272,256]{1,0:T(8,128)(2,1)} %copy-done.4) | copy-start | bytes 417796
  24.7 0.9 %copy-start.7 = (bf16[272,256]{1,0:T(8,128)(2,1)S(1)}, bf16[272,256]{1,0:T(8,128)(2,1)}, u32[]{:S(2)}) copy-start(bf16[272,256]{1,0:T(8,128)(2,1)} %copy-done.6) | copy-start | bytes 417796
  29.7 6.8 %collective-permute-start.3 = (bf16[128,256]{1,0:T(8,128)(2,1)S(1)}, bf16[128,256]{1,0:T(8,128)(2,1)S(1)}, u32[]{:S(2)}, u32[]{:S(2)}) collective-permute-start(bf16[128,256]{1,0:T(8,128)(2,1)S(1)} %get-tuple-element.19), channel_id=1, source_target_pairs={{0,4},{4,8},{8,12},{12,0},{1,5},{5,9},{9,13},{13,1},{2,6},{6,10},{... | collective-permute-start | bytes 196616 | tf_op jit(solution)/shard_map/ppermute | solution.py:213
  30.3 7.7 %collective-permute-start.4 = (bf16[128,256]{1,0:T(8,128)(2,1)S(1)}, bf16[128,256]{1,0:T(8,128)(2,1)S(1)}, u32[]{:S(2)}, u32[]{:S(2)}) collective-permute-start(bf16[128,256]{1,0:T(8,128)(2,1)S(1)} %get-tuple-element.18), channel_id=1, source_target_pairs={{0,8},{4,12},{8,0},{12,4},{1,9},{5,13},{9,1},{13,5},{2,10},{6,14},... | collective-permute-start | bytes 196616 | tf_op jit(solution)/shard_map/ppermute | solution.py:213
  32.3 5.7 %collective-permute-start.5 = (bf16[128,256]{1,0:T(8,128)(2,1)S(1)}, bf16[128,256]{1,0:T(8,128)(2,1)S(1)}, u32[]{:S(2)}, u32[]{:S(2)}) collective-permute-start(bf16[128,256]{1,0:T(8,128)(2,1)S(1)} %get-tuple-element.17), channel_id=1, source_target_pairs={{0,12},{4,0},{8,4},{12,8},{1,13},{5,1},{9,5},{13,9},{2,14},{6,2},{... | collective-permute-start | bytes 196616 | tf_op jit(solution)/shard_map/ppermute | solution.py:213
  39.9 2.0 %collective-permute-start.6 = (bf16[128,2048]{1,0:T(8,128)(2,1)S(1)}, bf16[128,2048]{1,0:T(8,128)(2,1)S(1)}, u32[]{:S(2)}, u32[]{:S(2)}) collective-permute-start(bf16[128,2048]{1,0:T(8,128)(2,1)S(1)} %dynamic-slice_convert_fusion), channel_id=1, source_target_pairs={{0,1},{1,0},{2,3},{3,2},{4,5},{5,4},{6,7},{7,6},{8,9},{9,8},{10,11... | collective-permute-start | bytes 1572872 | tf_op jit(solution)/shard_map/ppermute | solution.py:162
  42.0 14.0 %collective-permute-start.7 = (bf16[128,2048]{1,0:T(8,128)(2,1)S(1)}, bf16[128,2048]{1,0:T(8,128)(2,1)S(1)}, u32[]{:S(2)}, u32[]{:S(2)}) collective-permute-start(bf16[128,2048]{1,0:T(8,128)(2,1)S(1)} %fusion.2), channel_id=1, source_target_pairs={{0,2},{1,3},{2,0},{3,1},{4,6},{5,7},{6,4},{7,5},{8,10},{9,11},{10,... | collective-permute-start | bytes 1572872 | tf_op jit(solution)/shard_map/ppermute | solution.py:162
  56.2 2.0 %collective-permute-start.8 = (bf16[128,2048]{1,0:T(8,128)(2,1)S(1)}, bf16[128,2048]{1,0:T(8,128)(2,1)S(1)}, u32[]{:S(2)}, u32[]{:S(2)}) collective-permute-start(bf16[128,2048]{1,0:T(8,128)(2,1)S(1)} %add_convert_fusion), channel_id=1, source_target_pairs={{0,1},{1,0},{2,3},{3,2},{4,5},{5,4},{6,7},{7,6},{8,9},{9,8},{10,11... | collective-permute-start | bytes 1572872 | tf_op jit(solution)/shard_map/ppermute | solution.py:162

commit v12 on v11

--- a/solution.py
+++ b/solution.py
@@ -208,26 +208,33 @@
         second_mix, staged_weight = hyena_call(
             [got[k] for k in range(nseq)], in0, in1, spectrum(first_filter),
             spectrum(second_filter), (f_hi, f_lo, i_hi, i_lo), rows, out_weight)
-        mix_pieces = {0: second_mix[:rows]}
-        for k in order[1:]:
-            mix_pieces[k] = lax.ppermute(second_mix[k * rows:(k + 1) * rows], "seq",
-                                         [(i, (i + k) % nseq) for i in range(nseq)])
         out_cols = out_weight.shape[1]
-
         srcs = jnp.stack([((me - k) % nseq).astype(jnp.int32) for k in range(nseq)])
-        partial_out = proj_call(srcs, [mix_pieces[k] for k in range(nseq)], staged_weight)
-
-        if nchan != 4:
-            return lax.psum(partial_out, "chan").astype(BF16)
         core = lax.axis_index("chan") % 2
         width = out_cols // 2
-        other = lax.dynamic_slice_in_dim(partial_out, (1 - core) * width, width, 1)
-        got_other = swap(other.astype(BF16), 1)
-        mine = lax.dynamic_slice_in_dim(partial_out, core * width, width, 1)
-        chip = mine + got_other.astype(F32)
-        total = (chip + swap(chip.astype(BF16), 2).astype(F32)).astype(BF16)
-        peer = swap(total, 1)
-        return jnp.where(core == 0, jnp.concatenate([total, peer], 1), jnp.concatenate([peer, total], 1))
+        chunks = 2 if (nchan == 4 and rows % 32 == 0) else 1
+        step = rows // chunks
+        results = []
+        for c in range(chunks):
+            lo = c * step
+            pieces = {0: second_mix[lo:lo + step]}
+            for k in order[1:]:
+                base = k * rows + lo
+                pieces[k] = lax.ppermute(second_mix[base:base + step], "seq",
+                                         [(i, (i + k) % nseq) for i in range(nseq)])
+            partial_out = proj_call(srcs, [pieces[k] for k in range(nseq)], staged_weight)
+            if nchan != 4:
+                results.append(lax.psum(partial_out, "chan").astype(BF16))
+                continue
+            other = lax.dynamic_slice_in_dim(partial_out, (1 - core) * width, width, 1)
+            got_other = swap(other.astype(BF16), 1)
+            mine = lax.dynamic_slice_in_dim(partial_out, core * width, width, 1)
+            chip = mine + got_other.astype(F32)
+            total = (chip + swap(chip.astype(BF16), 2).astype(F32)).astype(BF16)
+            peer = swap(total, 1)
+            results.append(jnp.where(core == 0, jnp.concatenate([total, peer], 1),
+                                     jnp.concatenate([peer, total], 1)))
+        return jnp.concatenate(results, axis=0)
 
     return local
 

time: 59.8 us -> 66.6 us (1.11)
  local copies, waits for them, and re-layouts: 6.84 us -> 13.5 us
  waiting for transfers between devices: 24.8 us -> 18.2 us
  starting transfers between devices: 13.3 us -> 17.5 us
  Pallas kernels: 5.8 us -> 8.21 us
    unnamed x22 -> x26, local copies, waits for them, and re-layouts: 4.63 us -> 11.3 us
    ppermute x3 -> x6, waiting for transfers between devices: 16.3 us -> 12.4 us  [swap(): return lax.ppermute(x, 'chan', [(c, c ^ bit) for c in range(4)])]
    ppermute x3 -> x6, waiting for transfers between devices: 2.77 us -> 0.02 us  [local(): lax.ppermute(second_mix[base:base + step], 'seq', [(i, (i + k) % nseq) fo...]
    ppermute x3 -> x6, starting transfers between devices: 5.51 us -> 7.95 us  [local(): lax.ppermute(second_mix[base:base + step], 'seq', [(i, (i + k) % nseq) fo...]
    pallas_call x1 -> x2, Pallas kernels: 1.81 us -> 4.22 us  [proj_call(): pl.pallas_call(functools.partial(proj_kernel, nseq=nseq), out_shape=jax.S...]
    ppermute x3 -> x6, starting transfers between devices: 1.7 us -> 3.41 us  [swap(): return lax.ppermute(x, 'chan', [(c, c ^ bit) for c in range(4)])]
    concatenate x0 -> x1, other arithmetic: none -> 1.06 us  [local(): return jnp.concatenate(results, axis=0)]
    select_n x1 -> x2, other arithmetic: 1.21 us -> 0.25 us  [local(): jnp.where(core == 0, jnp.concatenate([total, peer], 1), jnp.concatenate([...]
  transfers between devices with their start and end apart: 9 -> 15, of which waited for: 6 -> 4; matrix products, arithmetic and copies ran while one was open for 9% -> 9% of each run, Pallas kernels for 0% -> 6%
where the time goes in v12:
time: 66.6 us; the launch traced here: 66.2 us
  waiting for transfers between devices  18.2 us (27%)
  starting transfers between devices  17.5 us (26%)
  local copies, waits for them, and re-layouts  13.5 us (20%)
  Pallas kernels  8.21 us (12%)
  other arithmetic  5.52 us (8%)
  matrix products  2.94 us (4%)
    ppermute x6, waiting for transfers between devices, swap(): return lax.ppermute(x, 'chan', [(c, c ^ bit) for c in range(4)])  12.4 us
    unnamed x26, local copies, waits for them, and re-layouts  11.3 us
    ppermute x6, starting transfers between devices, local(): lax.ppermute(second_mix[base:base + step], 'seq', [(i, (i + k) % nseq) fo...  7.95 us
    ppermute x3, starting transfers between devices, local(): lax.ppermute(block_for((me + k) % nseq), 'seq', [(i, (i + k) % nseq) for...  6.09 us
    ppermute x3, waiting for transfers between devices, local(): lax.ppermute(block_for((me + k) % nseq), 'seq', [(i, (i + k) % nseq) for...  5.75 us
    pallas_call x2, Pallas kernels, proj_call(): pl.pallas_call(functools.partial(proj_kernel, nseq=nseq), out_shape=jax.S...  4.22 us
    pallas_call x1, Pallas kernels, hyena_call(): pl.pallas_call(functools.partial(hyena_kernel, nseq=nseq, rows=rows), out...  3.99 us
    ppermute x6, starting transfers between devices, swap(): return lax.ppermute(x, 'chan', [(c, c ^ bit) for c in range(4)])  3.41 us
  transfers between devices with their start and end apart: 15, of which 4 were waited for; matrix products, arithmetic and copies ran while one was open for 9% of the time, Pallas kernels for 6%

profile of v12, /device:TPU:0, one launch (start us, length us, event | category | flops | bytes accessed | tf_op | source)
XLA Modules:
  0.0 66.2 jit_solution(10347729807759544699)
XLA Ops:
  0.0 0.7 %convert_element_type.73 = bf16[128]{0:T(256)(128)(2,1)S(1)} convert(s32[128]{0:T(128)} %param.17) | non-fusion elementwise | flops 128 | bytes 768 | tf_op jit(solution)/shard_map/convert_element_type | solution.py:195
  0.8 1.1 %multiply_convert_fusion = bf16[128,1024]{1,0:T(8,128)(2,1)S(1)} fusion(bf16[128,1024]{1,0:T(8,128)(2,1)} %param.11, bf16[128,1024]{1,0:T(8,128)(2,1)} %param.12), kind=kLoop, calls=%fused_computation.13 | loop fusion | flops 524288 | bytes 786432 | tf_op jit(solution)/shard_map/convert_element_type | solution.py:192
  1.9 1.0 %constant_dynamic-slice_fusion = (bf16[128,256]{1,0:T(8,128)(2,1)S(1)}, bf16[128,256]{1,0:T(8,128)(2,1)S(1)}, bf16[128,256]{1,0:T(8,128)(2,1)S(1)}, bf16[128,256...) fusion(bf16[128,1024]{1,0:T(8,128)(2,1)} %param.13, ...), kind=kLoop, calls=%fused_computation.29 | loop fusion | bytes 1048592 | tf_op jit(solution)/shard_map/dynamic_slice | solution.py:198
  2.9 0.0 copy-start.2
  2.9 0.7 %pad_maximum_fusion.1 = (bf16[272,256]{1,0:T(8,128)(2,1)}, bf16[272,256]{1,0:T(8,128)(2,1)S(1)}, bf16[272,256]{1,0:T(8,128)(2,1)S(1)}, bf16[272,256]{1,0:T(8,128)(2,1)S(1)}) fusion(bf16[16,256]{1,0:T(8,128)(2,1)S(1)} %reshape.53, bf16[128,256]{1,0:T(8,128)(2,1)S(1)} %get-tuple-element.29, bf16[128,256]{1,0:T(8,128)(2,1)S(1)} %get-tuple-element.43, ...), kind=kLoop, calls=%fused_computation.16 | loop fusion | flops 1462272 | bytes 1089536 | tf_op jit(solution)/shard_map/concatenate | solution.py:199
  3.6 5.1 %collective-permute-start.2 = (bf16[272,256]{1,0:T(8,128)(2,1)}, bf16[272,256]{1,0:T(8,128)(2,1)S(1)}, u32[]{:S(2)}, u32[]{:S(2)}) collective-permute-start(bf16[272,256]{1,0:T(8,128)(2,1)} %get-tuple-element.33), channel_id=1, source_target_pairs={{0,12},{4,0},{8,4},{12,8},{1,13},{5,1},{9,5},{13,9},{2,14},{6,2},{... | collective-permute-start | bytes 417800 | tf_op jit(solution)/shard_map/ppermute | solution.py:203
  8.7 0.0 collective-permute-start.1
  8.7 1.0 %collective-permute-start = (bf16[272,256]{1,0:T(8,128)(2,1)S(1)}, bf16[272,256]{1,0:T(8,128)(2,1)S(1)}, u32[]{:S(2)}, u32[]{:S(2)}) collective-permute-start(bf16[272,256]{1,0:T(8,128)(2,1)S(1)} %get-tuple-element.34), channel_id=1, source_target_pairs={{0,4},{4,8},{8,12},{12,0},{1,5},{5,9},{9,13},{13,1},{2,6},{6,10},{... | collective-permute-start | bytes 417800 | tf_op jit(solution)/shard_map/ppermute | solution.py:203
  9.8 0.7 %dynamic-slice_bitcast_fusion = (bf16[512,16]{0,1:T(8,128)(2,1)S(1)}, bf16[512,16]{0,1:T(8,128)(2,1)S(1)}) fusion(bf16[64,512]{1,0:T(8,128)(2,1)} %param.15, s32[]{:T(128)S(6)} %select_n.102, bf16[64,512]{1,0:T(8,128)(2,1)} %param.14), kind=kLoop, calls=%fused_computation.24 | loop fusion | bytes 65540 | tf_op jit(solution)/shard_map/transpose | solution.py:178
  10.5 0.0 copy-done.3
  10.5 0.3 fusion.6
  10.9 0.3 fusion.5
  11.2 0.0 copy-done.2
  11.3 1.1 %fusion = f32[512,256]{1,0:T(8,128)} fusion(f32[256,512]{0,1:T(8,128)S(1)} %fusion.6, bf16[512,256]{0,1:T(8,128)(2,1)S(1)} %bitcast.37, bf16[512,512]{1,0:T(8,128)(2,1)S(1)} %copy-done.2), kind=kOutput, calls=%fused_computation.1 | convolution fusion | flops 134348800 | bytes 1835008 | tf_op jit(solution)/shard_map/dot_general | solution.py:158
  12.4 1.1 %fusion.1 = f32[512,256]{1,0:T(8,128)} fusion(f32[256,512]{0,1:T(8,128)S(1)} %fusion.5, bf16[512,256]{0,1:T(8,128)(2,1)S(1)} %bitcast.39, bf16[512,512]{1,0:T(8,128)(2,1)S(1)} %copy-done.2), kind=kOutput, calls=%fused_computation.3 | convolution fusion | flops 134348800 | bytes 1835008 | tf_op jit(solution)/shard_map/dot_general | solution.py:158
  13.5 1.3 %slice_select_fusion = (f32[256,256]{1,0:T(8,128)S(1)}, f32[256,256]{1,0:T(8,128)S(1)}, f32[256,256]{1,0:T(8,128)S(1)}, f32[256,256]{1,0:T(8,128)S(1)}, f32[256,256]{1,0:T(8,128)S(1)}, /*index=5*/f32[256,256]{1,0:T(8,128)S(1)}) fusion(f32[512,256]{1,0:T(8,128)} %fusion, pred[256]{0:T(512)(128)(4,1)S(1)} %iota_compare_fusion, f32[512,256]{1,0:T(8,128)} %fusion.1), kind=kLoop, calls=%fused_computation.20 | loop fusion | flops 262144 | bytes 2621696 | tf_op jit(solution)/shard_map/jit(_where)/select_n | solution.py:184
  14.9 0.0 collective-permute-done.2.refs_3_
  14.9 5.7 %collective-permute-done.1.refs_2_ = bf16[272,256]{1,0:T(8,128)(2,1)S(1)} collective-permute-done((bf16[272,256]{1,0:T(8,128)(2,1)S(1)}, bf16[272,256]{1,0:T(8,128)(2,1)S(1)}, u32[]{:S(2)}, u32[]{:S(2)}) %collective-permute-start.1) | collective-permute-done | bytes 139296 | tf_op jit(solution)/shard_map/ppermute | solution.py:203
  20.7 0.0 collective-permute-done.refs_1_
  20.7 0.0 copy-start.8
  20.7 0.7 copy-done.8
  21.4 0.0 copy-done.6
  21.4 0.1 copy.22.refs_4_
  21.6 0.1 copy.23.refs_5_
  21.7 0.0 copy-start.4
  21.7 1.0 %copy-done.4 = bf16[512,512]{1,0:T(8,128)(2,1)S(1)} copy-done((bf16[512,512]{1,0:T(8,128)(2,1)S(1)}, bf16[512,512]{1,0:T(8,128)(2,1)}, u32[]{:S(2)}) %copy-start.4) | copy-done | bytes 524312
  22.8 1.0 %copy-done.5 = bf16[512,512]{1,0:T(8,128)(2,1)S(1)} copy-done((bf16[512,512]{1,0:T(8,128)(2,1)S(1)}, bf16[512,512]{1,0:T(8,128)(2,1)}, u32[]{:S(2)}) %copy-start.5) | copy-done | bytes 524312
  23.8 0.9 %copy-done.7 = bf16[272,256]{1,0:T(8,128)(2,1)S(1)} copy-done((bf16[272,256]{1,0:T(8,128)(2,1)S(1)}, bf16[272,256]{1,0:T(8,128)(2,1)}, u32[]{:S(2)}) %copy-start.7) | copy-done | bytes 139288
  24.7 0.9 %copy-done.9 = bf16[272,256]{1,0:T(8,128)(2,1)S(1)} copy-done((bf16[272,256]{1,0:T(8,128)(2,1)S(1)}, bf16[272,256]{1,0:T(8,128)(2,1)}, u32[]{:S(2)}) %copy-start.9) | copy-done | bytes 139288
  25.6 4.0 %shard_map.109 = (bf16[512,256]{1,0:T(8,128)(2,1)S(1)}, bf16[1024,4096]{1,0:T(8,128)(2,1)S(1)}) custom-call(bf16[272,256]{1,0:T(8,128)(2,1)S(1)} %get-tuple-element.36.refs_0_, bf16[272,256]{1,0:T(8,128)(2,1)S(1)} %copy-done.9, bf16[272,256]{1,0:T(8,128)(2,1)S(1)} %copy-done.7, bf16[272,256]{1,0:T(8,128)(2,1)S(1)} %collective-permute-done.2.refs_3_, ...), custom_call_target="tpu_custom_call" | custom-call | flops 2684354560 | bytes 3145728 | tf_op jit(solution)/shard_map/pallas_call | solution.py:114
  29.6 3.3 %copy-done = bf16[1024,4096]{1,0:T(8,128)(2,1)} copy-done((bf16[1024,4096]{1,0:T(8,128)(2,1)}, bf16[1024,4096]{1,0:T(8,128)(2,1)S(1)}, u32[]{:S(2)}) %copy-start) | copy-done | bytes 8388632
  32.9 0.7 collective-permute-start.3
  33.6 2.0 %collective-permute-start.4 = (bf16[64,256]{1,0:T(8,128)(2,1)S(1)}, bf16[64,256]{1,0:T(8,128)(2,1)S(1)}, u32[]{:S(2)}, u32[]{:S(2)}) collective-permute-start(bf16[64,256]{1,0:T(8,128)(2,1)S(1)} %get-tuple-element.22), channel_id=1, source_target_pairs={{0,8},{4,12},{8,0},{12,4},{1,9},{5,13},{9,1},{13,5},{2,10},{6,14},... | collective-permute-start | bytes 98312 | tf_op jit(solution)/shard_map/ppermute | solution.py:223
  35.6 2.8 %collective-permute-start.5 = (bf16[64,256]{1,0:T(8,128)(2,1)S(1)}, bf16[64,256]{1,0:T(8,128)(2,1)S(1)}, u32[]{:S(2)}, u32[]{:S(2)}) collective-permute-start(bf16[64,256]{1,0:T(8,128)(2,1)S(1)} %get-tuple-element.17), channel_id=1, source_target_pairs={{0,12},{4,0},{8,4},{12,8},{1,13},{5,1},{9,5},{13,9},{2,14},{6,2},{... | collective-permute-start | bytes 98312 | tf_op jit(solution)/shard_map/ppermute | solution.py:223
  38.4 0.1 pad_add_fusion.refs_0_
  38.5 0.4 collective-permute-start.10
  38.9 1.1 %collective-permute-start.11 = (bf16[64,256]{1,0:T(8,128)(2,1)S(1)}, bf16[64,256]{1,0:T(8,128)(2,1)S(1)}, u32[]{:S(2)}, u32[]{:S(2)}) collective-permute-start(bf16[64,256]{1,0:T(8,128)(2,1)S(1)} %get-tuple-element.18), channel_id=1, source_target_pairs={{0,12},{4,0},{8,4},{12,8},{1,13},{5,1},{9,5},{13,9},{2,14},{6,2},{... | collective-permute-start | bytes 98312 | tf_op jit(solution)/shard_map/ppermute | solution.py:223
  40.1 0.0 collective-permute-done.3.refs_2_
  40.1 0.9 %collective-permute-start.9 = (bf16[64,256]{1,0:T(8,128)(2,1)S(1)}, bf16[64,256]{1,0:T(8,128)(2,1)S(1)}, u32[]{:S(2)}, u32[]{:S(2)}) collective-permute-start(bf16[64,256]{1,0:T(8,128)(2,1)S(1)} %get-tuple-element.20), channel_id=1, source_target_pairs={{0,4},{4,8},{8,12},{12,0},{1,5},{5,9},{9,13},{13,1},{2,6},{6,10},{... | collective-permute-start | bytes 98312 | tf_op jit(solution)/shard_map/ppermute | solution.py:223
  41.0 0.0 collective-permute-done.4.refs_3_
  41.0 0.0 collective-permute-done.5.refs_4_
  41.0 3.4 %copy-done.1 = bf16[1024,4096]{1,0:T(8,128)(2,1)S(1)} copy-done((bf16[1024,4096]{1,0:T(8,128)(2,1)S(1)}, bf16[1024,4096]{1,0:T(8,128)(2,1)}, u32[]{:S(2)}) %copy-start.1) | copy-done | bytes 8388632
  44.4 2.1 %shard_map.110 = f32[64,4096]{1,0:T(8,128)S(1)} custom-call(s32[4]{0:T(128)S(1)} %pad_add_fusion.refs_0_, bf16[64,256]{1,0:T(8,128)(2,1)S(1)} %get-tuple-element.24.refs_1_, bf16[64,256]{1,0:T(8,128)(2,1)S(1)} %collective-permute-done.3.refs_2_, bf16[64,256]{1,0:T(8,128)(2,1)S(1)} %collective-permute-done.4.refs_3_, ...), custom_call_target="tpu_custom_call" | custom-call | flops 536870912 | bytes 9437184 | tf_op jit(solution)/shard_map/pallas_call | solution.py:146
  46.5 0.1 collective-permute-start.6
  46.6 0.0 collective-permute-done.10.refs_3_
  46.6 0.0 collective-permute-done.11.refs_4_
  46.6 0.0 collective-permute-done.9.refs_2_
  46.6 2.1 %shard_map.111 = f32[64,4096]{1,0:T(8,128)S(1)} custom-call(s32[4]{0:T(128)S(1)} %pad_add_fusion.refs_0_, bf16[64,256]{1,0:T(8,128)(2,1)S(1)} %get-tuple-element.21.refs_1_, bf16[64,256]{1,0:T(8,128)(2,1)S(1)} %collective-permute-done.9.refs_2_, bf16[64,256]{1,0:T(8,128)(2,1)S(1)} %collective-permute-done.10.refs_3_, ...), custom_call_target="tpu_custom_call" | custom-call | flops 536870912 | bytes 9437184 | tf_op jit(solution)/shard_map/pallas_call | solution.py:146
  48.8 0.5 collective-permute-start.12
  49.3 0.0 collective-permute-done.6
  49.4 1.6 %collective-permute-start.7 = (bf16[64,2048]{1,0:T(8,128)(2,1)S(1)}, bf16[64,2048]{1,0:T(8,128)(2,1)S(1)}, u32[]{:S(2)}, u32[]{:S(2)}) collective-permute-start(bf16[64,2048]{1,0:T(8,128)(2,1)S(1)} %fusion.2), channel_id=1, source_target_pairs={{0,2},{1,3},{2,0},{3,1},{4,6},{5,7},{6,4},{7,5},{8,10},{9,11},{10,... | collective-permute-start | bytes 786440 | tf_op jit(solution)/shard_map/ppermute | solution.py:162
  50.9 0.0 collective-permute-done.12
  51.0 1.1 %collective-permute-start.13 = (bf16[64,2048]{1,0:T(8,128)(2,1)S(1)}, bf16[64,2048]{1,0:T(8,128)(2,1)S(1)}, u32[]{:S(2)}, u32[]{:S(2)}) collective-permute-start(bf16[64,2048]{1,0:T(8,128)(2,1)S(1)} %fusion.3), channel_id=1, source_target_pairs={{0,2},{1,3},{2,0},{3,1},{4,6},{5,7},{6,4},{7,5},{8,10},{9,11},{10,... | collective-permute-start | bytes 786440 | tf_op jit(solution)/shard_map/ppermute | solution.py:162
  52.1 6.5 %collective-permute-done.7 = bf16[64,2048]{1,0:T(8,128)(2,1)S(1)} collective-permute-done((bf16[64,2048]{1,0:T(8,128)(2,1)S(1)}, bf16[64,2048]{1,0:T(8,128)(2,1)S(1)}, u32[]{:S(2)}, u32[]{:S(2)}) %collective-permute-start.7) | collective-permute-done | bytes 262176 | tf_op jit(solution)/shard_map/ppermute | solution.py:162
  58.6 0.1 add_convert_fusion.1
  58.7 0.1 collective-permute-start.8
  58.8 4.5 %collective-permute-done.13 = bf16[64,2048]{1,0:T(8,128)(2,1)S(1)} collective-permute-done((bf16[64,2048]{1,0:T(8,128)(2,1)S(1)}, bf16[64,2048]{1,0:T(8,128)(2,1)S(1)}, u32[]{:S(2)}, u32[]{:S(2)}) %collective-permute-start.13) | collective-permute-done | bytes 262176 | tf_op jit(solution)/shard_map/ppermute | solution.py:162
  63.3 0.1 add_convert_fusion
  63.4 0.1 collective-permute-start.14
  63.5 0.0 collective-permute-done.8
  63.5 0.1 maximum_select_fusion
  63.6 1.4 %collective-permute-done.14 = bf16[64,2048]{1,0:T(8,128)(2,1)S(1)} collective-permute-done((bf16[64,2048]{1,0:T(8,128)(2,1)S(1)}, bf16[64,2048]{1,0:T(8,128)(2,1)S(1)}, u32[]{:S(2)}, u32[]{:S(2)}) %collective-permute-start.14) | collective-permute-done | bytes 262176 | tf_op jit(solution)/shard_map/ppermute | solution.py:162
  65.0 0.1 maximum_select_fusion.1
  65.1 1.1 %pad_maximum_fusion = bf16[128,4096]{1,0:T(8,128)(2,1)} fusion(bf16[64,4096]{1,0:T(8,128)(2,1)S(1)} %maximum_select_fusion.1, bf16[64,4096]{1,0:T(8,128)(2,1)S(1)} %maximum_select_fusion), kind=kLoop, calls=%fused_computation.4 | loop fusion | flops 2097152 | bytes 2097152 | tf_op jit(solution)/shard_map/concatenate | solution.py:237
  (26 shorter events, 0.4 us)
Async XLA Ops:
  0.0 10.5 %copy-start.3 = (bf16[512,512]{1,0:T(8,128)(2,1)S(1)}, bf16[512,512]{1,0:T(8,128)(2,1)}, u32[]{:S(2)}) copy-start(bf16[512,512]{1,0:T(8,128)(2,1)} %constant.91.clone.refs_12_) | copy-start | bytes 1572868
  2.9 8.4 %copy-start.2 = (bf16[512,512]{1,0:T(8,128)(2,1)S(1)}, bf16[512,512]{1,0:T(8,128)(2,1)}, u32[]{:S(2)}) copy-start(bf16[512,512]{1,0:T(8,128)(2,1)} %constant.92.clone.refs_13_) | copy-start | bytes 1572868
  3.6 11.3 %collective-permute-start.2 = (bf16[272,256]{1,0:T(8,128)(2,1)}, bf16[272,256]{1,0:T(8,128)(2,1)S(1)}, u32[]{:S(2)}, u32[]{:S(2)}) collective-permute-start(bf16[272,256]{1,0:T(8,128)(2,1)} %get-tuple-element.33), channel_id=1, source_target_pairs={{0,12},{4,0},{8,4},{12,8},{1,13},{5,1},{9,5},{13,9},{2,14},{6,2},{... | collective-permute-start | bytes 417800 | tf_op jit(solution)/shard_map/ppermute | solution.py:203
  8.7 12.0 %collective-permute-start.1 = (bf16[272,256]{1,0:T(8,128)(2,1)S(1)}, bf16[272,256]{1,0:T(8,128)(2,1)S(1)}, u32[]{:S(2)}, u32[]{:S(2)}) collective-permute-start(bf16[272,256]{1,0:T(8,128)(2,1)S(1)} %get-tuple-element.35), channel_id=1, source_target_pairs={{0,8},{4,12},{8,0},{12,4},{1,9},{5,13},{9,1},{13,5},{2,10},{6,14},... | collective-permute-start | bytes 417800 | tf_op jit(solution)/shard_map/ppermute | solution.py:203
  8.7 12.0 %collective-permute-start = (bf16[272,256]{1,0:T(8,128)(2,1)S(1)}, bf16[272,256]{1,0:T(8,128)(2,1)S(1)}, u32[]{:S(2)}, u32[]{:S(2)}) collective-permute-start(bf16[272,256]{1,0:T(8,128)(2,1)S(1)} %get-tuple-element.34), channel_id=1, source_target_pairs={{0,4},{4,8},{8,12},{12,0},{1,5},{5,9},{9,13},{13,1},{2,6},{6,10},{... | collective-permute-start | bytes 417800 | tf_op jit(solution)/shard_map/ppermute | solution.py:203
  20.6 0.8 %copy-start.6 = (bf16[272,256]{1,0:T(8,128)(2,1)}, bf16[272,256]{1,0:T(8,128)(2,1)S(1)}, u32[]{:S(2)}) copy-start(bf16[272,256]{1,0:T(8,128)(2,1)S(1)} %collective-permute-done.1.refs_2_) | copy-start | bytes 417796
  20.7 0.7 %copy-start.8 = (bf16[272,256]{1,0:T(8,128)(2,1)}, bf16[272,256]{1,0:T(8,128)(2,1)S(1)}, u32[]{:S(2)}) copy-start(bf16[272,256]{1,0:T(8,128)(2,1)S(1)} %collective-permute-done.refs_1_) | copy-start | bytes 417796
  21.7 1.0 %copy-start.4 = (bf16[512,512]{1,0:T(8,128)(2,1)S(1)}, bf16[512,512]{1,0:T(8,128)(2,1)}, u32[]{:S(2)}) copy-start(bf16[512,512]{1,0:T(8,128)(2,1)} %constant.93.clone.refs_14_) | copy-start | bytes 1572868
  22.8 1.0 %copy-start.5 = (bf16[512,512]{1,0:T(8,128)(2,1)S(1)}, bf16[512,512]{1,0:T(8,128)(2,1)}, u32[]{:S(2)}) copy-start(bf16[512,512]{1,0:T(8,128)(2,1)} %constant.94.clone.refs_15_) | copy-start | bytes 1572868
  23.8 0.9 %copy-start.7 = (bf16[272,256]{1,0:T(8,128)(2,1)S(1)}, bf16[272,256]{1,0:T(8,128)(2,1)}, u32[]{:S(2)}) copy-start(bf16[272,256]{1,0:T(8,128)(2,1)} %copy-done.6) | copy-start | bytes 417796
  24.7 0.9 %copy-start.9 = (bf16[272,256]{1,0:T(8,128)(2,1)S(1)}, bf16[272,256]{1,0:T(8,128)(2,1)}, u32[]{:S(2)}) copy-start(bf16[272,256]{1,0:T(8,128)(2,1)} %copy-done.8) | copy-start | bytes 417796
  29.6 3.3 %copy-start = (bf16[1024,4096]{1,0:T(8,128)(2,1)}, bf16[1024,4096]{1,0:T(8,128)(2,1)S(1)}, u32[]{:S(2)}) copy-start(bf16[1024,4096]{1,0:T(8,128)(2,1)S(1)} %get-tuple-element.8.refs_5_) | copy-start | bytes 25165828
  32.9 7.2 %collective-permute-start.3 = (bf16[64,256]{1,0:T(8,128)(2,1)S(1)}, bf16[64,256]{1,0:T(8,128)(2,1)S(1)}, u32[]{:S(2)}, u32[]{:S(2)}) collective-permute-start(bf16[64,256]{1,0:T(8,128)(2,1)S(1)} %get-tuple-element.23), channel_id=1, source_target_pairs={{0,4},{4,8},{8,12},{12,0},{1,5},{5,9},{9,13},{13,1},{2,6},{6,10},{... | collective-permute-start | bytes 98312 | tf_op jit(solution)/shard_map/ppermute | solution.py:223
  33.6 7.4 %collective-permute-start.4 = (bf16[64,256]{1,0:T(8,128)(2,1)S(1)}, bf16[64,256]{1,0:T(8,128)(2,1)S(1)}, u32[]{:S(2)}, u32[]{:S(2)}) collective-permute-start(bf16[64,256]{1,0:T(8,128)(2,1)S(1)} %get-tuple-element.22), channel_id=1, source_target_pairs={{0,8},{4,12},{8,0},{12,4},{1,9},{5,13},{9,1},{13,5},{2,10},{6,14},... | collective-permute-start | bytes 98312 | tf_op jit(solution)/shard_map/ppermute | solution.py:223
  35.6 5.4 %collective-permute-start.5 = (bf16[64,256]{1,0:T(8,128)(2,1)S(1)}, bf16[64,256]{1,0:T(8,128)(2,1)S(1)}, u32[]{:S(2)}, u32[]{:S(2)}) collective-permute-start(bf16[64,256]{1,0:T(8,128)(2,1)S(1)} %get-tuple-element.17), channel_id=1, source_target_pairs={{0,12},{4,0},{8,4},{12,8},{1,13},{5,1},{9,5},{13,9},{2,14},{6,2},{... | collective-permute-start | bytes 98312 | tf_op jit(solution)/shard_map/ppermute | solution.py:223
  38.5 8.1 %collective-permute-start.10 = (bf16[64,256]{1,0:T(8,128)(2,1)S(1)}, bf16[64,256]{1,0:T(8,128)(2,1)S(1)}, u32[]{:S(2)}, u32[]{:S(2)}) collective-permute-start(bf16[64,256]{1,0:T(8,128)(2,1)S(1)} %get-tuple-element.19), channel_id=1, source_target_pairs={{0,8},{4,12},{8,0},{12,4},{1,9},{5,13},{9,1},{13,5},{2,10},{6,14},... | collective-permute-start | bytes 98312 | tf_op jit(solution)/shard_map/ppermute | solution.py:223
  38.9 7.7 %collective-permute-start.11 = (bf16[64,256]{1,0:T(8,128)(2,1)S(1)}, bf16[64,256]{1,0:T(8,128)(2,1)S(1)}, u32[]{:S(2)}, u32[]{:S(2)}) collective-permute-start(bf16[64,256]{1,0:T(8,128)(2,1)S(1)} %get-tuple-element.18), channel_id=1, source_target_pairs={{0,12},{4,0},{8,4},{12,8},{1,13},{5,1},{9,5},{13,9},{2,14},{6,2},{... | collective-permute-start | bytes 98312 | tf_op jit(solution)/shard_map/ppermute | solution.py:223
  40.1 6.5 %collective-permute-start.9 = (bf16[64,256]{1,0:T(8,128)(2,1)S(1)}, bf16[64,256]{1,0:T(8,128)(2,1)S(1)}, u32[]{:S(2)}, u32[]{:S(2)}) collective-permute-start(bf16[64,256]{1,0:T(8,128)(2,1)S(1)} %get-tuple-element.20), channel_id=1, source_target_pairs={{0,4},{4,8},{8,12},{12,0},{1,5},{5,9},{9,13},{13,1},{2,6},{6,10},{... | collective-permute-start | bytes 98312 | tf_op jit(solution)/shard_map/ppermute | solution.py:223
  41.0 3.4 %copy-start.1 = (bf16[1024,4096]{1,0:T(8,128)(2,1)S(1)}, bf16[1024,4096]{1,0:T(8,128)(2,1)}, u32[]{:S(2)}) copy-start(bf16[1024,4096]{1,0:T(8,128)(2,1)} %copy-done) | copy-start | bytes 25165828
  46.5 2.8 %collective-permute-start.6 = (bf16[64,2048]{1,0:T(8,128)(2,1)S(1)}, bf16[64,2048]{1,0:T(8,128)(2,1)S(1)}, u32[]{:S(2)}, u32[]{:S(2)}) collective-permute-start(bf16[64,2048]{1,0:T(8,128)(2,1)S(1)} %dynamic-slice_convert_fusion.1), channel_id=1, source_target_pairs={{0,1},{1,0},{2,3},{3,2},{4,5},{5,4},{6,7},{7,6},{8,9},{9,8},{10,11... | collective-permute-start | bytes 786440 | tf_op jit(solution)/shard_map/ppermute | solution.py:162
  48.8 2.2 %collective-permute-start.12 = (bf16[64,2048]{1,0:T(8,128)(2,1)S(1)}, bf16[64,2048]{1,0:T(8,128)(2,1)S(1)}, u32[]{:S(2)}, u32[]{:S(2)}) collective-permute-start(bf16[64,2048]{1,0:T(8,128)(2,1)S(1)} %dynamic-slice_convert_fusion), channel_id=1, source_target_pairs={{0,1},{1,0},{2,3},{3,2},{4,5},{5,4},{6,7},{7,6},{8,9},{9,8},{10,11... | collective-permute-start | bytes 786440 | tf_op jit(solution)/shard_map/ppermute | solution.py:162
  49.4 9.2 %collective-permute-start.7 = (bf16[64,2048]{1,0:T(8,128)(2,1)S(1)}, bf16[64,2048]{1,0:T(8,128)(2,1)S(1)}, u32[]{:S(2)}, u32[]{:S(2)}) collective-permute-start(bf16[64,2048]{1,0:T(8,128)(2,1)S(1)} %fusion.2), channel_id=1, source_target_pairs={{0,2},{1,3},{2,0},{3,1},{4,6},{5,7},{6,4},{7,5},{8,10},{9,11},{10,... | collective-permute-start | bytes 786440 | tf_op jit(solution)/shard_map/ppermute | solution.py:162
  51.0 12.3 %collective-permute-start.13 = (bf16[64,2048]{1,0:T(8,128)(2,1)S(1)}, bf16[64,2048]{1,0:T(8,128)(2,1)S(1)}, u32[]{:S(2)}, u32[]{:S(2)}) collective-permute-start(bf16[64,2048]{1,0:T(8,128)(2,1)S(1)} %fusion.3), channel_id=1, source_target_pairs={{0,2},{1,3},{2,0},{3,1},{4,6},{5,7},{6,4},{7,5},{8,10},{9,11},{10,... | collective-permute-start | bytes 786440 | tf_op jit(solution)/shard_map/ppermute | solution.py:162
  58.7 4.8 %collective-permute-start.8 = (bf16[64,2048]{1,0:T(8,128)(2,1)S(1)}, bf16[64,2048]{1,0:T(8,128)(2,1)S(1)}, u32[]{:S(2)}, u32[]{:S(2)}) collective-permute-start(bf16[64,2048]{1,0:T(8,128)(2,1)S(1)} %add_convert_fusion.1), channel_id=1, source_target_pairs={{0,1},{1,0},{2,3},{3,2},{4,5},{5,4},{6,7},{7,6},{8,9},{9,8},{10,11... | collective-permute-start | bytes 786440 | tf_op jit(solution)/shard_map/ppermute | solution.py:162
  63.4 1.6 %collective-permute-start.14 = (bf16[64,2048]{1,0:T(8,128)(2,1)S(1)}, bf16[64,2048]{1,0:T(8,128)(2,1)S(1)}, u32[]{:S(2)}, u32[]{:S(2)}) collective-permute-start(bf16[64,2048]{1,0:T(8,128)(2,1)S(1)} %add_convert_fusion), channel_id=1, source_target_pairs={{0,1},{1,0},{2,3},{3,2},{4,5},{5,4},{6,7},{7,6},{8,9},{9,8},{10,11... | collective-permute-start | bytes 786440 | tf_op jit(solution)/shard_map/ppermute | solution.py:162

commit v13 on v11

--- a/solution.py
+++ b/solution.py
@@ -35,6 +35,10 @@
     return split_bf16(fwd), split_bf16(inv)
 
 
+def mm_t(a, b):
+    return lax.dot_general(a, b, (((0,), (0,)), ((), ())), preferred_element_type=F32)
+
+
 def round_bf16(x, in_kernel):
     if in_kernel:
         return x.astype(BF16).astype(F32)
@@ -60,17 +64,14 @@
         a, b, d = (jnp.concatenate([v, v], axis=1) for v in (f() for f in spec))
         xr = x[:half]
         xi = x[half:]
-        y = jnp.concatenate([xr * a - xi * b, xr * b + xi * d], axis=0)
+        row = lax.broadcasted_iota(jnp.int32, (length, 1), 0)
+        weight = jnp.where((row == 0) | (row == half), 1.0 / length, 2.0 / length).astype(F32)
+        y = jnp.concatenate([xr * a - xi * b, xr * b + xi * d], axis=0) * weight
         y_hi32 = round_bf16(y, in_kernel)
         y_hi = y_hi32.astype(BF16)
         y_lo = (y - y_hi32).astype(BF16)
-        if first_call:
-            wait(2)
-            wait(3)
-        ihi = mats[2]()
-        both = (jnp.dot(ihi, y_hi, preferred_element_type=F32)
-                + jnp.dot(ihi, y_lo, preferred_element_type=F32)
-                + jnp.dot(mats[3](), y_hi, preferred_element_type=F32))
+        fhi = mats[0]()
+        both = mm_t(fhi, y_hi) + mm_t(fhi, y_lo) + mm_t(mats[1](), y_hi)
         return both[:, :per] * m0 + both[:, per:] * m1
 
     first_mix = conv(first, spec1, True)
@@ -82,13 +83,13 @@
     pieces = [r[...] for r in refs[:nseq]]
     m0_ref, m1_ref = refs[nseq:nseq + 2]
     spec_refs = refs[nseq + 2:nseq + 8]
-    mats_hbm = refs[nseq + 8:nseq + 12]
-    w_hbm = refs[nseq + 12]
-    o_ref, w_out = refs[nseq + 13:nseq + 15]
-    mats = refs[nseq + 15:nseq + 19]
-    sem = refs[nseq + 19]
-    copies = [pltpu.make_async_copy(mats_hbm[i], mats[i], sem.at[i]) for i in range(4)]
-    w_copy = pltpu.make_async_copy(w_hbm, w_out, sem.at[4])
+    mats_hbm = refs[nseq + 8:nseq + 10]
+    w_hbm = refs[nseq + 10]
+    o_ref, w_out = refs[nseq + 11:nseq + 13]
+    mats = refs[nseq + 13:nseq + 15]
+    sem = refs[nseq + 15]
+    copies = [pltpu.make_async_copy(mats_hbm[i], mats[i], sem.at[i]) for i in range(2)]
+    w_copy = pltpu.make_async_copy(w_hbm, w_out, sem.at[2])
     for c in copies:
         c.start()
     w_copy.start()
@@ -115,10 +116,10 @@
         functools.partial(hyena_kernel, nseq=nseq, rows=rows),
         out_shape=(jax.ShapeDtypeStruct((length, per), BF16),
                    jax.ShapeDtypeStruct(out_weight.shape, out_weight.dtype)),
-        in_specs=[vmem] * (nseq + 8) + [hbm] * 5,
+        in_specs=[vmem] * (nseq + 8) + [hbm] * 3,
         out_specs=(vmem, vmem),
-        scratch_shapes=[pltpu.VMEM((length, length), BF16) for _ in range(4)]
-        + [pltpu.SemaphoreType.DMA((5,))],
+        scratch_shapes=[pltpu.VMEM((length, length), BF16) for _ in range(2)]
+        + [pltpu.SemaphoreType.DMA((3,))],
         compiler_params=pltpu.CompilerParams(vmem_limit_bytes=40 * 1024 * 1024),
         cost_estimate=pl.CostEstimate(flops=flops, transcendentals=0,
                                       bytes_accessed=4 * length * length * 2 + 8 * length * per),
@@ -207,7 +208,7 @@
         in1 = (segs == 1).astype(F32)[:, None]
         second_mix, staged_weight = hyena_call(
             [got[k] for k in range(nseq)], in0, in1, spectrum(first_filter),
-            spectrum(second_filter), (f_hi, f_lo, i_hi, i_lo), rows, out_weight)
+            spectrum(second_filter), (f_hi, f_lo), rows, out_weight)
         mix_pieces = {0: second_mix[:rows]}
         for k in order[1:]:
             mix_pieces[k] = lax.ppermute(second_mix[k * rows:(k + 1) * rows], "seq",

time: 59.8 us -> 57.5 us (0.962)
  local copies, waits for them, and re-layouts: 6.84 us -> 4.75 us
    unnamed x22 -> x18, local copies, waits for them, and re-layouts: 4.63 us -> 2.54 us
where the time goes in v13:
time: 57.5 us; the launch traced here: 57.2 us
  waiting for transfers between devices  24.8 us (43%)
  starting transfers between devices  13.3 us (23%)
  Pallas kernels  5.67 us (10%)
  other arithmetic  5.44 us (9%)
  local copies, waits for them, and re-layouts  4.75 us (8%)
  matrix products  2.92 us (5%)
    ppermute x3, waiting for transfers between devices, swap(): return lax.ppermute(x, 'chan', [(c, c ^ bit) for c in range(4)])  16.2 us
    ppermute x3, starting transfers between devices, local(): lax.ppermute(block_for((me + k) % nseq), 'seq', [(i, (i + k) % nseq) for...  6.09 us
    ppermute x3, waiting for transfers between devices, local(): lax.ppermute(block_for((me + k) % nseq), 'seq', [(i, (i + k) % nseq) for...  5.77 us
    ppermute x3, starting transfers between devices, local(): lax.ppermute(second_mix[k * rows:(k + 1) * rows], 'seq', [(i, (i + k) % n...  5.51 us
    pallas_call x1, Pallas kernels, hyena_call(): pl.pallas_call(functools.partial(hyena_kernel, nseq=nseq, rows=rows), out...  3.86 us
    dot_general x4, matrix products, mm(): return jnp.dot(a, b, preferred_element_type=F32)  2.92 us
    ppermute x3, waiting for transfers between devices, local(): lax.ppermute(second_mix[k * rows:(k + 1) * rows], 'seq', [(i, (i + k) % n...  2.77 us
    unnamed x18, local copies, waits for them, and re-layouts  2.54 us
  transfers between devices with their start and end apart: 9, of which 6 were waited for; matrix products, arithmetic and copies ran while one was open for 9% of the time, Pallas kernels for 0%

profile of v13, /device:TPU:0, one launch (start us, length us, event | category | flops | bytes accessed | tf_op | source)
XLA Modules:
  0.0 57.2 jit_solution(4226190379014001207)
XLA Ops:
  0.0 0.0 copy-start.1
  0.0 0.7 %convert_element_type.58 = bf16[128]{0:T(256)(128)(2,1)S(1)} convert(s32[128]{0:T(128)} %param.15) | non-fusion elementwise | flops 128 | bytes 768 | tf_op jit(solution)/shard_map/convert_element_type | solution.py:196
  0.8 1.1 %multiply_convert_fusion = bf16[128,1024]{1,0:T(8,128)(2,1)S(1)} fusion(bf16[128,1024]{1,0:T(8,128)(2,1)} %param.9, bf16[128,1024]{1,0:T(8,128)(2,1)} %param.10), kind=kLoop, calls=%fused_computation.9 | loop fusion | flops 524288 | bytes 786432 | tf_op jit(solution)/shard_map/convert_element_type | solution.py:193
  1.9 1.0 %constant_dynamic-slice_fusion = (bf16[128,256]{1,0:T(8,128)(2,1)S(1)}, bf16[128,256]{1,0:T(8,128)(2,1)S(1)}, bf16[128,256]{1,0:T(8,128)(2,1)S(1)}, bf16[128,256...) fusion(bf16[128,1024]{1,0:T(8,128)(2,1)} %param.11, ...), kind=kLoop, calls=%fused_computation.23 | loop fusion | bytes 1048592 | tf_op jit(solution)/shard_map/dynamic_slice | solution.py:199
  2.9 0.0 copy-start
  2.9 0.7 %pad_maximum_fusion = (bf16[272,256]{1,0:T(8,128)(2,1)}, bf16[272,256]{1,0:T(8,128)(2,1)S(1)}, bf16[272,256]{1,0:T(8,128)(2,1)S(1)}, bf16[272,256]{1,0:T(8,128)(2,1)S(1)}) fusion(bf16[16,256]{1,0:T(8,128)(2,1)S(1)} %reshape.53, bf16[128,256]{1,0:T(8,128)(2,1)S(1)} %get-tuple-element.25, bf16[128,256]{1,0:T(8,128)(2,1)S(1)} %get-tuple-element.39, ...), kind=kLoop, calls=%fused_computation.10 | loop fusion | flops 1462272 | bytes 1089536 | tf_op jit(solution)/shard_map/concatenate | solution.py:200
  3.6 5.1 %collective-permute-start.2 = (bf16[272,256]{1,0:T(8,128)(2,1)}, bf16[272,256]{1,0:T(8,128)(2,1)S(1)}, u32[]{:S(2)}, u32[]{:S(2)}) collective-permute-start(bf16[272,256]{1,0:T(8,128)(2,1)} %get-tuple-element.29), channel_id=1, source_target_pairs={{0,12},{4,0},{8,4},{12,8},{1,13},{5,1},{9,5},{13,9},{2,14},{6,2},{... | collective-permute-start | bytes 417800 | tf_op jit(solution)/shard_map/ppermute | solution.py:204
  8.6 0.0 collective-permute-start.1
  8.7 1.0 %collective-permute-start = (bf16[272,256]{1,0:T(8,128)(2,1)S(1)}, bf16[272,256]{1,0:T(8,128)(2,1)S(1)}, u32[]{:S(2)}, u32[]{:S(2)}) collective-permute-start(bf16[272,256]{1,0:T(8,128)(2,1)S(1)} %get-tuple-element.30), channel_id=1, source_target_pairs={{0,4},{4,8},{8,12},{12,0},{1,5},{5,9},{9,13},{13,1},{2,6},{6,10},{... | collective-permute-start | bytes 417800 | tf_op jit(solution)/shard_map/ppermute | solution.py:204
  9.7 0.7 %dynamic-slice_bitcast_fusion = (bf16[512,16]{0,1:T(8,128)(2,1)S(1)}, bf16[512,16]{0,1:T(8,128)(2,1)S(1)}) fusion(bf16[64,512]{1,0:T(8,128)(2,1)} %param.13, s32[]{:T(128)S(6)} %select_n.96, bf16[64,512]{1,0:T(8,128)(2,1)} %param.12), kind=kLoop, calls=%fused_computation.18 | loop fusion | bytes 65540 | tf_op jit(solution)/shard_map/transpose | solution.py:179
  10.5 0.0 copy-done.1
  10.5 0.3 fusion.5
  10.9 0.3 fusion.4
  11.2 0.0 copy-done
  11.2 1.1 %fusion = f32[512,256]{1,0:T(8,128)} fusion(f32[256,512]{0,1:T(8,128)S(1)} %fusion.5, bf16[512,256]{0,1:T(8,128)(2,1)S(1)} %bitcast.37, bf16[512,512]{1,0:T(8,128)(2,1)S(1)} %copy-done), kind=kOutput, calls=%fused_computation.1 | convolution fusion | flops 134348800 | bytes 1835008 | tf_op jit(solution)/shard_map/dot_general | solution.py:159
  12.4 1.1 %fusion.1 = f32[512,256]{1,0:T(8,128)} fusion(f32[256,512]{0,1:T(8,128)S(1)} %fusion.4, bf16[512,256]{0,1:T(8,128)(2,1)S(1)} %bitcast.39, bf16[512,512]{1,0:T(8,128)(2,1)S(1)} %copy-done), kind=kOutput, calls=%fused_computation.3 | convolution fusion | flops 134348800 | bytes 1835008 | tf_op jit(solution)/shard_map/dot_general | solution.py:159
  13.5 1.3 %slice_select_fusion = (f32[256,256]{1,0:T(8,128)S(1)}, f32[256,256]{1,0:T(8,128)S(1)}, f32[256,256]{1,0:T(8,128)S(1)}, f32[256,256]{1,0:T(8,128)S(1)}, f32[256,256]{1,0:T(8,128)S(1)}, /*index=5*/f32[256,256]{1,0:T(8,128)S(1)}) fusion(f32[512,256]{1,0:T(8,128)} %fusion, pred[256]{0:T(512)(128)(4,1)S(1)} %iota_compare_fusion, f32[512,256]{1,0:T(8,128)} %fusion.1), kind=kLoop, calls=%fused_computation.14 | loop fusion | flops 262144 | bytes 2621696 | tf_op jit(solution)/shard_map/jit(_where)/select_n | solution.py:185
  14.8 0.0 collective-permute-done.2.refs_3_
  14.9 5.8 %collective-permute-done.1.refs_2_ = bf16[272,256]{1,0:T(8,128)(2,1)S(1)} collective-permute-done((bf16[272,256]{1,0:T(8,128)(2,1)S(1)}, bf16[272,256]{1,0:T(8,128)(2,1)S(1)}, u32[]{:S(2)}, u32[]{:S(2)}) %collective-permute-start.1) | collective-permute-done | bytes 139296 | tf_op jit(solution)/shard_map/ppermute | solution.py:204
  20.6 0.0 copy-start.2
  20.7 0.0 collective-permute-done.refs_1_
  20.7 0.0 copy-start.4
  20.7 0.7 %copy-done.4 = bf16[272,256]{1,0:T(8,128)(2,1)} copy-done((bf16[272,256]{1,0:T(8,128)(2,1)}, bf16[272,256]{1,0:T(8,128)(2,1)S(1)}, u32[]{:S(2)}) %copy-start.4) | copy-done | bytes 139288
  21.4 0.0 copy-done.2
  21.4 0.1 copy.20.refs_4_
  21.6 0.1 copy.21.refs_5_
  21.7 0.0 copy-start.3
  21.7 0.9 %copy-done.3 = bf16[272,256]{1,0:T(8,128)(2,1)S(1)} copy-done((bf16[272,256]{1,0:T(8,128)(2,1)S(1)}, bf16[272,256]{1,0:T(8,128)(2,1)}, u32[]{:S(2)}) %copy-start.3) | copy-done | bytes 139288
  22.6 0.0 copy-start.5
  22.6 0.9 %copy-done.5 = bf16[272,256]{1,0:T(8,128)(2,1)S(1)} copy-done((bf16[272,256]{1,0:T(8,128)(2,1)S(1)}, bf16[272,256]{1,0:T(8,128)(2,1)}, u32[]{:S(2)}) %copy-start.5) | copy-done | bytes 139288
  23.5 3.9 %shard_map.91 = (bf16[512,256]{1,0:T(8,128)(2,1)S(1)}, bf16[1024,4096]{1,0:T(8,128)(2,1)S(1)}) custom-call(bf16[272,256]{1,0:T(8,128)(2,1)S(1)} %get-tuple-element.32.refs_0_, bf16[272,256]{1,0:T(8,128)(2,1)S(1)} %copy-done.5, bf16[272,256]{1,0:T(8,128)(2,1)S(1)} %copy-done.3, bf16[272,256]{1,0:T(8,128)(2,1)S(1)} %collective-permute-done.2.refs_3_, ...), custom_call_target="tpu_custom_call" | custom-call | flops 2684354560 | bytes 3145728 | tf_op jit(solution)/shard_map/pallas_call | solution.py:115
  27.4 0.7 %collective-permute-start.3 = (bf16[128,256]{1,0:T(8,128)(2,1)S(1)}, bf16[128,256]{1,0:T(8,128)(2,1)S(1)}, u32[]{:S(2)}, u32[]{:S(2)}) collective-permute-start(bf16[128,256]{1,0:T(8,128)(2,1)S(1)} %get-tuple-element.19), channel_id=1, source_target_pairs={{0,4},{4,8},{8,12},{12,0},{1,5},{5,9},{9,13},{13,1},{2,6},{6,10},{... | collective-permute-start | bytes 196616 | tf_op jit(solution)/shard_map/ppermute | solution.py:214
  28.1 2.0 %collective-permute-start.4 = (bf16[128,256]{1,0:T(8,128)(2,1)S(1)}, bf16[128,256]{1,0:T(8,128)(2,1)S(1)}, u32[]{:S(2)}, u32[]{:S(2)}) collective-permute-start(bf16[128,256]{1,0:T(8,128)(2,1)S(1)} %get-tuple-element.18), channel_id=1, source_target_pairs={{0,8},{4,12},{8,0},{12,4},{1,9},{5,13},{9,1},{13,5},{2,10},{6,14},... | collective-permute-start | bytes 196616 | tf_op jit(solution)/shard_map/ppermute | solution.py:214
  30.1 2.8 %collective-permute-start.5 = (bf16[128,256]{1,0:T(8,128)(2,1)S(1)}, bf16[128,256]{1,0:T(8,128)(2,1)S(1)}, u32[]{:S(2)}, u32[]{:S(2)}) collective-permute-start(bf16[128,256]{1,0:T(8,128)(2,1)S(1)} %get-tuple-element.17), channel_id=1, source_target_pairs={{0,12},{4,0},{8,4},{12,8},{1,13},{5,1},{9,5},{13,9},{2,14},{6,2},{... | collective-permute-start | bytes 196616 | tf_op jit(solution)/shard_map/ppermute | solution.py:214
  32.9 0.1 pad_add_fusion.refs_0_
  33.0 1.2 %collective-permute-done.3.refs_2_ = bf16[128,256]{1,0:T(8,128)(2,1)S(1)} collective-permute-done((bf16[128,256]{1,0:T(8,128)(2,1)S(1)}, bf16[128,256]{1,0:T(8,128)(2,1)S(1)}, u32[]{:S(2)}, u32[]{:S(2)}) %collective-permute-start.3) | collective-permute-done | bytes 65568 | tf_op jit(solution)/shard_map/ppermute | solution.py:214
  34.3 1.5 %collective-permute-done.4.refs_3_ = bf16[128,256]{1,0:T(8,128)(2,1)S(1)} collective-permute-done((bf16[128,256]{1,0:T(8,128)(2,1)S(1)}, bf16[128,256]{1,0:T(8,128)(2,1)S(1)}, u32[]{:S(2)}, u32[]{:S(2)}) %collective-permute-start.4) | collective-permute-done | bytes 65568 | tf_op jit(solution)/shard_map/ppermute | solution.py:214
  35.8 0.0 collective-permute-done.5.refs_4_
  35.8 1.8 %shard_map.92 = f32[128,4096]{1,0:T(8,128)S(1)} custom-call(s32[4]{0:T(128)S(1)} %pad_add_fusion.refs_0_, bf16[128,256]{1,0:T(8,128)(2,1)S(1)} %get-tuple-element.20.refs_1_, bf16[128,256]{1,0:T(8,128)(2,1)S(1)} %collective-permute-done.3.refs_2_, bf16[128,256]{1,0:T(8,128)(2,1)S(1)} %collective-permute-done.4.refs_3_, ...), custom_call_target="tpu_custom_call" | custom-call | flops 1073741824 | bytes 10485760 | tf_op jit(solution)/shard_map/pallas_call | solution.py:147
  37.6 0.1 dynamic-slice_convert_fusion
  37.7 0.1 collective-permute-start.6
  37.8 1.9 %collective-permute-done.6 = bf16[128,2048]{1,0:T(8,128)(2,1)S(1)} collective-permute-done((bf16[128,2048]{1,0:T(8,128)(2,1)S(1)}, bf16[128,2048]{1,0:T(8,128)(2,1)S(1)}, u32[]{:S(2)}, u32[]{:S(2)}) %collective-permute-start.6) | collective-permute-done | bytes 524320 | tf_op jit(solution)/shard_map/ppermute | solution.py:163
  39.7 0.1 fusion.2
  39.8 1.6 %collective-permute-start.7 = (bf16[128,2048]{1,0:T(8,128)(2,1)S(1)}, bf16[128,2048]{1,0:T(8,128)(2,1)S(1)}, u32[]{:S(2)}, u32[]{:S(2)}) collective-permute-start(bf16[128,2048]{1,0:T(8,128)(2,1)S(1)} %fusion.2), channel_id=1, source_target_pairs={{0,2},{1,3},{2,0},{3,1},{4,6},{5,7},{6,4},{7,5},{8,10},{9,11},{10,... | collective-permute-start | bytes 1572872 | tf_op jit(solution)/shard_map/ppermute | solution.py:163
  41.3 12.5 %collective-permute-done.7 = bf16[128,2048]{1,0:T(8,128)(2,1)S(1)} collective-permute-done((bf16[128,2048]{1,0:T(8,128)(2,1)S(1)}, bf16[128,2048]{1,0:T(8,128)(2,1)S(1)}, u32[]{:S(2)}, u32[]{:S(2)}) %collective-permute-start.7) | collective-permute-done | bytes 524320 | tf_op jit(solution)/shard_map/ppermute | solution.py:163
  53.8 0.2 add_convert_fusion
  54.0 0.1 collective-permute-start.8
  54.1 1.9 %collective-permute-done.8 = bf16[128,2048]{1,0:T(8,128)(2,1)S(1)} collective-permute-done((bf16[128,2048]{1,0:T(8,128)(2,1)S(1)}, bf16[128,2048]{1,0:T(8,128)(2,1)S(1)}, u32[]{:S(2)}, u32[]{:S(2)}) %collective-permute-start.8) | collective-permute-done | bytes 524320 | tf_op jit(solution)/shard_map/ppermute | solution.py:163
  56.0 1.2 %maximum_select_fusion = bf16[128,4096]{1,0:T(8,128)(2,1)} fusion(bf16[128,2048]{1,0:T(8,128)(2,1)S(1)} %collective-permute-done.8, bf16[128,2048]{1,0:T(8,128)(2,1)S(1)} %add_convert_fusion, pred[]{:T(512)S(6)} %eq.51), kind=kLoop, calls=%fused_computation.4 | loop fusion | flops 4718592 | bytes 2097153 | tf_op jit(solution)/shard_map/jit(_where)/select_n | solution.py:231
  (15 shorter events, 0.2 us)
Async XLA Ops:
  0.0 10.5 %copy-start.1 = (bf16[512,512]{1,0:T(8,128)(2,1)S(1)}, bf16[512,512]{1,0:T(8,128)(2,1)}, u32[]{:S(2)}) copy-start(bf16[512,512]{1,0:T(8,128)(2,1)} %constant.87.clone.refs_12_) | copy-start | bytes 1572868
  2.9 8.4 %copy-start = (bf16[512,512]{1,0:T(8,128)(2,1)S(1)}, bf16[512,512]{1,0:T(8,128)(2,1)}, u32[]{:S(2)}) copy-start(bf16[512,512]{1,0:T(8,128)(2,1)} %constant.88.clone.refs_13_) | copy-start | bytes 1572868
  3.6 11.3 %collective-permute-start.2 = (bf16[272,256]{1,0:T(8,128)(2,1)}, bf16[272,256]{1,0:T(8,128)(2,1)S(1)}, u32[]{:S(2)}, u32[]{:S(2)}) collective-permute-start(bf16[272,256]{1,0:T(8,128)(2,1)} %get-tuple-element.29), channel_id=1, source_target_pairs={{0,12},{4,0},{8,4},{12,8},{1,13},{5,1},{9,5},{13,9},{2,14},{6,2},{... | collective-permute-start | bytes 417800 | tf_op jit(solution)/shard_map/ppermute | solution.py:204
  8.6 12.0 %collective-permute-start.1 = (bf16[272,256]{1,0:T(8,128)(2,1)S(1)}, bf16[272,256]{1,0:T(8,128)(2,1)S(1)}, u32[]{:S(2)}, u32[]{:S(2)}) collective-permute-start(bf16[272,256]{1,0:T(8,128)(2,1)S(1)} %get-tuple-element.31), channel_id=1, source_target_pairs={{0,8},{4,12},{8,0},{12,4},{1,9},{5,13},{9,1},{13,5},{2,10},{6,14},... | collective-permute-start | bytes 417800 | tf_op jit(solution)/shard_map/ppermute | solution.py:204
  8.7 12.0 %collective-permute-start = (bf16[272,256]{1,0:T(8,128)(2,1)S(1)}, bf16[272,256]{1,0:T(8,128)(2,1)S(1)}, u32[]{:S(2)}, u32[]{:S(2)}) collective-permute-start(bf16[272,256]{1,0:T(8,128)(2,1)S(1)} %get-tuple-element.30), channel_id=1, source_target_pairs={{0,4},{4,8},{8,12},{12,0},{1,5},{5,9},{9,13},{13,1},{2,6},{6,10},{... | collective-permute-start | bytes 417800 | tf_op jit(solution)/shard_map/ppermute | solution.py:204
  20.6 0.8 %copy-start.2 = (bf16[272,256]{1,0:T(8,128)(2,1)}, bf16[272,256]{1,0:T(8,128)(2,1)S(1)}, u32[]{:S(2)}) copy-start(bf16[272,256]{1,0:T(8,128)(2,1)S(1)} %collective-permute-done.1.refs_2_) | copy-start | bytes 417796
  20.7 0.7 %copy-start.4 = (bf16[272,256]{1,0:T(8,128)(2,1)}, bf16[272,256]{1,0:T(8,128)(2,1)S(1)}, u32[]{:S(2)}) copy-start(bf16[272,256]{1,0:T(8,128)(2,1)S(1)} %collective-permute-done.refs_1_) | copy-start | bytes 417796
  21.7 0.9 %copy-start.3 = (bf16[272,256]{1,0:T(8,128)(2,1)S(1)}, bf16[272,256]{1,0:T(8,128)(2,1)}, u32[]{:S(2)}) copy-start(bf16[272,256]{1,0:T(8,128)(2,1)} %copy-done.2) | copy-start | bytes 417796
  22.6 0.9 %copy-start.5 = (bf16[272,256]{1,0:T(8,128)(2,1)S(1)}, bf16[272,256]{1,0:T(8,128)(2,1)}, u32[]{:S(2)}) copy-start(bf16[272,256]{1,0:T(8,128)(2,1)} %copy-done.4) | copy-start | bytes 417796
  27.4 6.8 %collective-permute-start.3 = (bf16[128,256]{1,0:T(8,128)(2,1)S(1)}, bf16[128,256]{1,0:T(8,128)(2,1)S(1)}, u32[]{:S(2)}, u32[]{:S(2)}) collective-permute-start(bf16[128,256]{1,0:T(8,128)(2,1)S(1)} %get-tuple-element.19), channel_id=1, source_target_pairs={{0,4},{4,8},{8,12},{12,0},{1,5},{5,9},{9,13},{13,1},{2,6},{6,10},{... | collective-permute-start | bytes 196616 | tf_op jit(solution)/shard_map/ppermute | solution.py:214
  28.1 7.7 %collective-permute-start.4 = (bf16[128,256]{1,0:T(8,128)(2,1)S(1)}, bf16[128,256]{1,0:T(8,128)(2,1)S(1)}, u32[]{:S(2)}, u32[]{:S(2)}) collective-permute-start(bf16[128,256]{1,0:T(8,128)(2,1)S(1)} %get-tuple-element.18), channel_id=1, source_target_pairs={{0,8},{4,12},{8,0},{12,4},{1,9},{5,13},{9,1},{13,5},{2,10},{6,14},... | collective-permute-start | bytes 196616 | tf_op jit(solution)/shard_map/ppermute | solution.py:214
  30.1 5.7 %collective-permute-start.5 = (bf16[128,256]{1,0:T(8,128)(2,1)S(1)}, bf16[128,256]{1,0:T(8,128)(2,1)S(1)}, u32[]{:S(2)}, u32[]{:S(2)}) collective-permute-start(bf16[128,256]{1,0:T(8,128)(2,1)S(1)} %get-tuple-element.17), channel_id=1, source_target_pairs={{0,12},{4,0},{8,4},{12,8},{1,13},{5,1},{9,5},{13,9},{2,14},{6,2},{... | collective-permute-start | bytes 196616 | tf_op jit(solution)/shard_map/ppermute | solution.py:214
  37.7 2.0 %collective-permute-start.6 = (bf16[128,2048]{1,0:T(8,128)(2,1)S(1)}, bf16[128,2048]{1,0:T(8,128)(2,1)S(1)}, u32[]{:S(2)}, u32[]{:S(2)}) collective-permute-start(bf16[128,2048]{1,0:T(8,128)(2,1)S(1)} %dynamic-slice_convert_fusion), channel_id=1, source_target_pairs={{0,1},{1,0},{2,3},{3,2},{4,5},{5,4},{6,7},{7,6},{8,9},{9,8},{10,11... | collective-permute-start | bytes 1572872 | tf_op jit(solution)/shard_map/ppermute | solution.py:163
  39.8 14.0 %collective-permute-start.7 = (bf16[128,2048]{1,0:T(8,128)(2,1)S(1)}, bf16[128,2048]{1,0:T(8,128)(2,1)S(1)}, u32[]{:S(2)}, u32[]{:S(2)}) collective-permute-start(bf16[128,2048]{1,0:T(8,128)(2,1)S(1)} %fusion.2), channel_id=1, source_target_pairs={{0,2},{1,3},{2,0},{3,1},{4,6},{5,7},{6,4},{7,5},{8,10},{9,11},{10,... | collective-permute-start | bytes 1572872 | tf_op jit(solution)/shard_map/ppermute | solution.py:163
  54.0 2.0 %collective-permute-start.8 = (bf16[128,2048]{1,0:T(8,128)(2,1)S(1)}, bf16[128,2048]{1,0:T(8,128)(2,1)S(1)}, u32[]{:S(2)}, u32[]{:S(2)}) collective-permute-start(bf16[128,2048]{1,0:T(8,128)(2,1)S(1)} %add_convert_fusion), channel_id=1, source_target_pairs={{0,1},{1,0},{2,3},{3,2},{4,5},{5,4},{6,7},{7,6},{8,9},{9,8},{10,11... | collective-permute-start | bytes 1572872 | tf_op jit(solution)/shard_map/ppermute | solution.py:163

commit v14 on v13

--- a/solution.py
+++ b/solution.py
@@ -45,12 +45,24 @@
     return lax.reduce_precision(x, exponent_bits=8, mantissa_bits=7)
 
 
-def hyena_math(pieces, m0, m1, spec1, spec2, mats, rows, wait, in_kernel):
+def id_column(ids, rows, in_kernel):
+    if in_kernel:
+        shape = (rows, ids.shape[1])
+        eye = (lax.broadcasted_iota(jnp.int32, shape, 0) == lax.broadcasted_iota(jnp.int32, shape, 1))
+        cols = lax.dot_general(eye.astype(BF16), ids, (((1,), (1,)), ((), ())), preferred_element_type=F32)
+        return cols[:, 0:1]
+    return ids.reshape(-1)[:rows].astype(F32)[:, None]
+
+
+def hyena_math(pieces, spec1, spec2, mats, rows, wait, in_kernel):
     nseq = len(pieces)
     per = pieces[0].shape[1]
-    length = m0.shape[0]
+    length = nseq * rows
     half = length // 2
     order = [(nseq - j) % nseq for j in range(nseq)]
+    segs = jnp.concatenate([id_column(pieces[k][2 * rows:, :], rows, in_kernel) for k in order], axis=0)
+    m0 = (segs == 0).astype(F32)
+    m1 = (segs == 1).astype(F32)
     first = jnp.concatenate([pieces[k][0:rows, :] for k in order], axis=0).astype(F32)
     gate = jnp.concatenate([pieces[k][rows:2 * rows, :] for k in order], axis=0).astype(F32)
 
@@ -81,13 +93,12 @@
 
 def hyena_kernel(*refs, nseq, rows):
     pieces = [r[...] for r in refs[:nseq]]
-    m0_ref, m1_ref = refs[nseq:nseq + 2]
-    spec_refs = refs[nseq + 2:nseq + 8]
-    mats_hbm = refs[nseq + 8:nseq + 10]
-    w_hbm = refs[nseq + 10]
-    o_ref, w_out = refs[nseq + 11:nseq + 13]
-    mats = refs[nseq + 13:nseq + 15]
-    sem = refs[nseq + 15]
+    spec_refs = refs[nseq:nseq + 6]
+    mats_hbm = refs[nseq + 6:nseq + 8]
+    w_hbm = refs[nseq + 8]
+    o_ref, w_out = refs[nseq + 9:nseq + 11]
+    mats = refs[nseq + 11:nseq + 13]
+    sem = refs[nseq + 13]
     copies = [pltpu.make_async_copy(mats_hbm[i], mats[i], sem.at[i]) for i in range(2)]
     w_copy = pltpu.make_async_copy(w_hbm, w_out, sem.at[2])
     for c in copies:
@@ -96,18 +107,18 @@
     loader = lambda r: (lambda: r[...])
     spec1 = [loader(r) for r in spec_refs[:3]]
     spec2 = [loader(r) for r in spec_refs[3:]]
-    o_ref[...] = hyena_math(pieces, m0_ref[...], m1_ref[...], spec1, spec2,
+    o_ref[...] = hyena_math(pieces, spec1, spec2,
                             [loader(r) for r in mats], rows, lambda i: copies[i].wait(), True)
     w_copy.wait()
 
 
-def hyena_call(pieces, m0, m1, spec1, spec2, mats, rows, out_weight):
+def hyena_call(pieces, spec1, spec2, mats, rows, out_weight):
     nseq = len(pieces)
-    length = m0.shape[0]
+    length = nseq * rows
     per = pieces[0].shape[1]
-    if 4 * length * length * 2 > 8 * 1024 * 1024:
+    if 4 * length * length * 2 > 8 * 1024 * 1024 or per < rows:
         const = lambda v: (lambda: v)
-        return hyena_math(pieces, m0, m1, [const(v) for v in spec1], [const(v) for v in spec2],
+        return hyena_math(pieces, [const(v) for v in spec1], [const(v) for v in spec2],
                           [const(v) for v in mats], rows, lambda i: None, False), out_weight
     vmem = pl.BlockSpec(memory_space=pltpu.VMEM)
     hbm = pl.BlockSpec(memory_space=pltpu.MemorySpace.HBM)
@@ -116,14 +127,14 @@
         functools.partial(hyena_kernel, nseq=nseq, rows=rows),
         out_shape=(jax.ShapeDtypeStruct((length, per), BF16),
                    jax.ShapeDtypeStruct(out_weight.shape, out_weight.dtype)),
-        in_specs=[vmem] * (nseq + 8) + [hbm] * 3,
+        in_specs=[vmem] * (nseq + 6) + [hbm] * 3,
         out_specs=(vmem, vmem),
         scratch_shapes=[pltpu.VMEM((length, length), BF16) for _ in range(2)]
         + [pltpu.SemaphoreType.DMA((3,))],
         compiler_params=pltpu.CompilerParams(vmem_limit_bytes=40 * 1024 * 1024),
         cost_estimate=pl.CostEstimate(flops=flops, transcendentals=0,
                                       bytes_accessed=4 * length * length * 2 + 8 * length * per),
-    )(*pieces, m0, m1, *spec1, *spec2, *mats, out_weight)
+    )(*pieces, *spec1, *spec2, *mats, out_weight)
 
 def proj_kernel(*refs, nseq):
     src_ref = refs[0]
@@ -202,12 +213,8 @@
         got = {0: block_for(me)}
         for k in order[1:]:
             got[k] = lax.ppermute(block_for((me + k) % nseq), "seq", [(i, (i + k) % nseq) for i in range(nseq)])
-        seg_blocks = jnp.stack([got[(nseq - j) % nseq][2 * rows:] for j in range(nseq)])
-        segs = seg_blocks.reshape(nseq, pad_rows * per)[:, :rows].reshape(nseq * rows)
-        in0 = (segs == 0).astype(F32)[:, None]
-        in1 = (segs == 1).astype(F32)[:, None]
         second_mix, staged_weight = hyena_call(
-            [got[k] for k in range(nseq)], in0, in1, spectrum(first_filter),
+            [got[k] for k in range(nseq)], spectrum(first_filter),
             spectrum(second_filter), (f_hi, f_lo), rows, out_weight)
         mix_pieces = {0: second_mix[:rows]}
         for k in order[1:]:

time: 57.5 us -> 53.8 us (0.936)
  local copies, waits for them, and re-layouts: 4.75 us -> 1.9 us
  other arithmetic: 5.44 us -> 3.59 us
  matrix products: 2.92 us -> 1.31 us
  starting transfers between devices: 13.3 us -> 14.7 us
  waiting for transfers between devices: 24.8 us -> 26 us
    unnamed x18 -> x4, local copies, waits for them, and re-layouts: 2.54 us -> 0.01 us
    dot_general x4, matrix products: 2.92 us -> 1.31 us  [mm(): return jnp.dot(a, b, preferred_element_type=F32)]
    ppermute x3, waiting for transfers between devices: 2.77 us -> 4.3 us  [local(): lax.ppermute(second_mix[k * rows:(k + 1) * rows], 'seq', [(i, (i + k) % n...]
    select_n x1, other arithmetic: 1.32 us -> 0.14 us  [spectrum(): d = jnp.where(row0, im, re)]
    ppermute x3, starting transfers between devices: 6.09 us -> 7.04 us  [local(): lax.ppermute(block_for((me + k) % nseq), 'seq', [(i, (i + k) % nseq) for...]
    concatenate x1, other arithmetic: 0.69 us -> 0.04 us  [block_for(): return jnp.concatenate([cols(first_input), cols(second_gate), ids], axis=0)]
  transfers between devices with their start and end apart: 9 -> 9, of which waited for: 6 -> 8; matrix products, arithmetic and copies ran while one was open for 9% -> 4% of each run, Pallas kernels for 0% -> 0%
where the time goes in v14:
time: 53.8 us; the launch traced here: 53.5 us
  waiting for transfers between devices  26 us (48%)
  starting transfers between devices  14.7 us (27%)
  Pallas kernels  5.78 us (11%)
  other arithmetic  3.59 us (7%)
  local copies, waits for them, and re-layouts  1.9 us (4%)
  matrix products  1.31 us (2%)
    ppermute x3, waiting for transfers between devices, swap(): return lax.ppermute(x, 'chan', [(c, c ^ bit) for c in range(4)])  16.3 us
    ppermute x3, starting transfers between devices, local(): lax.ppermute(block_for((me + k) % nseq), 'seq', [(i, (i + k) % nseq) for...  7.04 us
    ppermute x3, starting transfers between devices, local(): lax.ppermute(second_mix[k * rows:(k + 1) * rows], 'seq', [(i, (i + k) % n...  5.95 us
    ppermute x3, waiting for transfers between devices, local(): lax.ppermute(block_for((me + k) % nseq), 'seq', [(i, (i + k) % nseq) for...  5.46 us
    ppermute x3, waiting for transfers between devices, local(): lax.ppermute(second_mix[k * rows:(k + 1) * rows], 'seq', [(i, (i + k) % n...  4.3 us
    pallas_call x1, Pallas kernels, hyena_call(): pl.pallas_call(functools.partial(hyena_kernel, nseq=nseq, rows=rows), out...  3.95 us
    pallas_call x1, Pallas kernels, proj_call(): pl.pallas_call(functools.partial(proj_kernel, nseq=nseq), out_shape=jax.S...  1.83 us
    ppermute x3, starting transfers between devices, swap(): return lax.ppermute(x, 'chan', [(c, c ^ bit) for c in range(4)])  1.7 us
  transfers between devices with their start and end apart: 9, of which 8 were waited for; matrix products, arithmetic and copies ran while one was open for 4% of the time, Pallas kernels for 0%

profile of v14, /device:TPU:0, one launch (start us, length us, event | category | flops | bytes accessed | tf_op | source)
XLA Modules:
  0.0 53.5 jit_solution(16883445010912650632)
XLA Ops:
  0.0 0.0 copy-start.1
  0.0 0.7 %convert_element_type.32 = bf16[128]{0:T(256)(128)(2,1)S(1)} convert(s32[128]{0:T(128)} %param.15) | non-fusion elementwise | flops 128 | bytes 768 | tf_op jit(solution)/shard_map/convert_element_type | solution.py:207
  0.8 1.1 %multiply_convert_fusion = bf16[128,1024]{1,0:T(8,128)(2,1)S(1)} fusion(bf16[128,1024]{1,0:T(8,128)(2,1)} %param.9, bf16[128,1024]{1,0:T(8,128)(2,1)} %param.10), kind=kLoop, calls=%fused_computation.9 | loop fusion | flops 524288 | bytes 786432 | tf_op jit(solution)/shard_map/convert_element_type | solution.py:204
  1.9 1.0 %constant_dynamic-slice_fusion = (bf16[128,256]{1,0:T(8,128)(2,1)S(1)}, bf16[128,256]{1,0:T(8,128)(2,1)S(1)}, bf16[128,256]{1,0:T(8,128)(2,1)S(1)}, bf16[128,256...) fusion(bf16[128,1024]{1,0:T(8,128)(2,1)} %param.11, ...), kind=kLoop, calls=%fused_computation.20 | loop fusion | bytes 1048592 | tf_op jit(solution)/shard_map/dynamic_slice | solution.py:210
  2.9 0.0 copy-start
  2.9 3.1 %collective-permute-start = (bf16[272,256]{1,0:T(8,128)(2,1)S(1)}, bf16[272,256]{1,0:T(8,128)(2,1)S(1)}, u32[]{:S(2)}, u32[]{:S(2)}) collective-permute-start(bf16[272,256]{1,0:T(8,128)(2,1)S(1)} %get-tuple-element.28), channel_id=1, source_target_pairs={{0,4},{4,8},{8,12},{12,0},{1,5},{5,9},{9,13},{13,1},{2,6},{6,10},{... | collective-permute-start | bytes 417800 | tf_op jit(solution)/shard_map/ppermute | solution.py:215
  6.0 2.6 %collective-permute-start.1 = (bf16[272,256]{1,0:T(8,128)(2,1)S(1)}, bf16[272,256]{1,0:T(8,128)(2,1)S(1)}, u32[]{:S(2)}, u32[]{:S(2)}) collective-permute-start(bf16[272,256]{1,0:T(8,128)(2,1)S(1)} %get-tuple-element.29), channel_id=1, source_target_pairs={{0,8},{4,12},{8,0},{12,4},{1,9},{5,13},{9,1},{13,5},{2,10},{6,14},... | collective-permute-start | bytes 417800 | tf_op jit(solution)/shard_map/ppermute | solution.py:215
  8.6 1.3 %collective-permute-start.2 = (bf16[272,256]{1,0:T(8,128)(2,1)S(1)}, bf16[272,256]{1,0:T(8,128)(2,1)S(1)}, u32[]{:S(2)}, u32[]{:S(2)}) collective-permute-start(bf16[272,256]{1,0:T(8,128)(2,1)S(1)} %get-tuple-element.27), channel_id=1, source_target_pairs={{0,12},{4,0},{8,4},{12,8},{1,13},{5,1},{9,5},{13,9},{2,14},{6,2},{... | collective-permute-start | bytes 417800 | tf_op jit(solution)/shard_map/ppermute | solution.py:215
  10.0 0.7 %dynamic-slice_bitcast_fusion = (bf16[512,16]{0,1:T(8,128)(2,1)S(1)}, bf16[512,16]{0,1:T(8,128)(2,1)S(1)}) fusion(bf16[64,512]{1,0:T(8,128)(2,1)} %param.13, s32[]{:T(128)S(6)} %select_n.96, bf16[64,512]{1,0:T(8,128)(2,1)} %param.12), kind=kLoop, calls=%fused_computation.18 | loop fusion | bytes 65540 | tf_op jit(solution)/shard_map/transpose | solution.py:190
  10.7 0.0 copy-done.1
  10.7 0.3 fusion.5
  11.1 0.3 fusion.4
  11.4 0.0 copy-done
  11.5 0.3 fusion
  11.8 0.3 fusion.1
  12.2 0.1 slice_select_fusion
  12.3 0.3 collective-permute-done.refs_1_
  12.7 5.1 %collective-permute-done.1.refs_2_ = bf16[272,256]{1,0:T(8,128)(2,1)S(1)} collective-permute-done((bf16[272,256]{1,0:T(8,128)(2,1)S(1)}, bf16[272,256]{1,0:T(8,128)(2,1)S(1)}, u32[]{:S(2)}, u32[]{:S(2)}) %collective-permute-start.1) | collective-permute-done | bytes 139296 | tf_op jit(solution)/shard_map/ppermute | solution.py:215
  17.8 0.0 collective-permute-done.2.refs_3_
  17.8 4.0 %shard_map.91 = (bf16[512,256]{1,0:T(8,128)(2,1)S(1)}, bf16[1024,4096]{1,0:T(8,128)(2,1)S(1)}) custom-call(bf16[272,256]{1,0:T(8,128)(2,1)S(1)} %get-tuple-element.30.refs_0_, bf16[272,256]{1,0:T(8,128)(2,1)S(1)} %collective-permute-done.refs_1_, bf16[272,256]{1,0:T(8,128)(2,1)S(1)} %collective-permute-done.1.refs_2_, ...), custom_call_target="tpu_custom_call" | custom-call | flops 2684354560 | bytes 3145728 | tf_op jit(solution)/shard_map/pallas_call | solution.py:126
  21.8 3.5 %collective-permute-start.3 = (bf16[128,256]{1,0:T(8,128)(2,1)S(1)}, bf16[128,256]{1,0:T(8,128)(2,1)S(1)}, u32[]{:S(2)}, u32[]{:S(2)}) collective-permute-start(bf16[128,256]{1,0:T(8,128)(2,1)S(1)} %get-tuple-element.17), channel_id=1, source_target_pairs={{0,4},{4,8},{8,12},{12,0},{1,5},{5,9},{9,13},{13,1},{2,6},{6,10},{... | collective-permute-start | bytes 196616 | tf_op jit(solution)/shard_map/ppermute | solution.py:221
  25.3 1.6 %collective-permute-start.4 = (bf16[128,256]{1,0:T(8,128)(2,1)S(1)}, bf16[128,256]{1,0:T(8,128)(2,1)S(1)}, u32[]{:S(2)}, u32[]{:S(2)}) collective-permute-start(bf16[128,256]{1,0:T(8,128)(2,1)S(1)} %get-tuple-element.16), channel_id=1, source_target_pairs={{0,8},{4,12},{8,0},{12,4},{1,9},{5,13},{9,1},{13,5},{2,10},{6,14},... | collective-permute-start | bytes 196616 | tf_op jit(solution)/shard_map/ppermute | solution.py:221
  26.9 0.8 %collective-permute-start.5 = (bf16[128,256]{1,0:T(8,128)(2,1)S(1)}, bf16[128,256]{1,0:T(8,128)(2,1)S(1)}, u32[]{:S(2)}, u32[]{:S(2)}) collective-permute-start(bf16[128,256]{1,0:T(8,128)(2,1)S(1)} %get-tuple-element.15), channel_id=1, source_target_pairs={{0,12},{4,0},{8,4},{12,8},{1,13},{5,1},{9,5},{13,9},{2,14},{6,2},{... | collective-permute-start | bytes 196616 | tf_op jit(solution)/shard_map/ppermute | solution.py:221
  27.7 0.1 pad_add_fusion.refs_0_
  27.8 1.1 %collective-permute-done.3.refs_2_ = bf16[128,256]{1,0:T(8,128)(2,1)S(1)} collective-permute-done((bf16[128,256]{1,0:T(8,128)(2,1)S(1)}, bf16[128,256]{1,0:T(8,128)(2,1)S(1)}, u32[]{:S(2)}, u32[]{:S(2)}) %collective-permute-start.3) | collective-permute-done | bytes 65568 | tf_op jit(solution)/shard_map/ppermute | solution.py:221
  28.9 2.6 %collective-permute-done.4.refs_3_ = bf16[128,256]{1,0:T(8,128)(2,1)S(1)} collective-permute-done((bf16[128,256]{1,0:T(8,128)(2,1)S(1)}, bf16[128,256]{1,0:T(8,128)(2,1)S(1)}, u32[]{:S(2)}, u32[]{:S(2)}) %collective-permute-start.4) | collective-permute-done | bytes 65568 | tf_op jit(solution)/shard_map/ppermute | solution.py:221
  31.5 0.6 %collective-permute-done.5.refs_4_ = bf16[128,256]{1,0:T(8,128)(2,1)S(1)} collective-permute-done((bf16[128,256]{1,0:T(8,128)(2,1)S(1)}, bf16[128,256]{1,0:T(8,128)(2,1)S(1)}, u32[]{:S(2)}, u32[]{:S(2)}) %collective-permute-start.5) | collective-permute-done | bytes 65568 | tf_op jit(solution)/shard_map/ppermute | solution.py:221
  32.1 1.8 %shard_map.92 = f32[128,4096]{1,0:T(8,128)S(1)} custom-call(s32[4]{0:T(128)S(1)} %pad_add_fusion.refs_0_, bf16[128,256]{1,0:T(8,128)(2,1)S(1)} %get-tuple-element.18.refs_1_, bf16[128,256]{1,0:T(8,128)(2,1)S(1)} %collective-permute-done.3.refs_2_, bf16[128,256]{1,0:T(8,128)(2,1)S(1)} %collective-permute-done.4.refs_3_, ...), custom_call_target="tpu_custom_call" | custom-call | flops 1073741824 | bytes 10485760 | tf_op jit(solution)/shard_map/pallas_call | solution.py:158
  33.9 0.1 dynamic-slice_convert_fusion
  34.0 0.1 collective-permute-start.6
  34.1 1.9 %collective-permute-done.6 = bf16[128,2048]{1,0:T(8,128)(2,1)S(1)} collective-permute-done((bf16[128,2048]{1,0:T(8,128)(2,1)S(1)}, bf16[128,2048]{1,0:T(8,128)(2,1)S(1)}, u32[]{:S(2)}, u32[]{:S(2)}) %collective-permute-start.6) | collective-permute-done | bytes 524320 | tf_op jit(solution)/shard_map/ppermute | solution.py:174
  36.0 0.1 fusion.2
  36.1 1.6 %collective-permute-start.7 = (bf16[128,2048]{1,0:T(8,128)(2,1)S(1)}, bf16[128,2048]{1,0:T(8,128)(2,1)S(1)}, u32[]{:S(2)}, u32[]{:S(2)}) collective-permute-start(bf16[128,2048]{1,0:T(8,128)(2,1)S(1)} %fusion.2), channel_id=1, source_target_pairs={{0,2},{1,3},{2,0},{3,1},{4,6},{5,7},{6,4},{7,5},{8,10},{9,11},{10,... | collective-permute-start | bytes 1572872 | tf_op jit(solution)/shard_map/ppermute | solution.py:174
  37.7 12.5 %collective-permute-done.7 = bf16[128,2048]{1,0:T(8,128)(2,1)S(1)} collective-permute-done((bf16[128,2048]{1,0:T(8,128)(2,1)S(1)}, bf16[128,2048]{1,0:T(8,128)(2,1)S(1)}, u32[]{:S(2)}, u32[]{:S(2)}) %collective-permute-start.7) | collective-permute-done | bytes 524320 | tf_op jit(solution)/shard_map/ppermute | solution.py:174
  50.1 0.2 add_convert_fusion
  50.3 0.1 collective-permute-start.8
  50.4 1.9 %collective-permute-done.8 = bf16[128,2048]{1,0:T(8,128)(2,1)S(1)} collective-permute-done((bf16[128,2048]{1,0:T(8,128)(2,1)S(1)}, bf16[128,2048]{1,0:T(8,128)(2,1)S(1)}, u32[]{:S(2)}, u32[]{:S(2)}) %collective-permute-start.8) | collective-permute-done | bytes 524320 | tf_op jit(solution)/shard_map/ppermute | solution.py:174
  52.3 1.2 %maximum_select_fusion = bf16[128,4096]{1,0:T(8,128)(2,1)} fusion(bf16[128,2048]{1,0:T(8,128)(2,1)S(1)} %collective-permute-done.8, bf16[128,2048]{1,0:T(8,128)(2,1)S(1)} %add_convert_fusion, pred[]{:T(512)S(6)} %eq.23), kind=kLoop, calls=%fused_computation.4 | loop fusion | flops 4718592 | bytes 2097153 | tf_op jit(solution)/shard_map/jit(_where)/select_n | solution.py:238
  (7 shorter events, 0.1 us)
Async XLA Ops:
  0.0 10.7 %copy-start.1 = (bf16[512,512]{1,0:T(8,128)(2,1)S(1)}, bf16[512,512]{1,0:T(8,128)(2,1)}, u32[]{:S(2)}) copy-start(bf16[512,512]{1,0:T(8,128)(2,1)} %constant.84.clone.refs_10_) | copy-start | bytes 1572868
  2.9 8.6 %copy-start = (bf16[512,512]{1,0:T(8,128)(2,1)S(1)}, bf16[512,512]{1,0:T(8,128)(2,1)}, u32[]{:S(2)}) copy-start(bf16[512,512]{1,0:T(8,128)(2,1)} %constant.85.clone.refs_11_) | copy-start | bytes 1572868
  2.9 9.8 %collective-permute-start = (bf16[272,256]{1,0:T(8,128)(2,1)S(1)}, bf16[272,256]{1,0:T(8,128)(2,1)S(1)}, u32[]{:S(2)}, u32[]{:S(2)}) collective-permute-start(bf16[272,256]{1,0:T(8,128)(2,1)S(1)} %get-tuple-element.28), channel_id=1, source_target_pairs={{0,4},{4,8},{8,12},{12,0},{1,5},{5,9},{9,13},{13,1},{2,6},{6,10},{... | collective-permute-start | bytes 417800 | tf_op jit(solution)/shard_map/ppermute | solution.py:215
  6.0 11.8 %collective-permute-start.1 = (bf16[272,256]{1,0:T(8,128)(2,1)S(1)}, bf16[272,256]{1,0:T(8,128)(2,1)S(1)}, u32[]{:S(2)}, u32[]{:S(2)}) collective-permute-start(bf16[272,256]{1,0:T(8,128)(2,1)S(1)} %get-tuple-element.29), channel_id=1, source_target_pairs={{0,8},{4,12},{8,0},{12,4},{1,9},{5,13},{9,1},{13,5},{2,10},{6,14},... | collective-permute-start | bytes 417800 | tf_op jit(solution)/shard_map/ppermute | solution.py:215
  8.6 9.2 %collective-permute-start.2 = (bf16[272,256]{1,0:T(8,128)(2,1)S(1)}, bf16[272,256]{1,0:T(8,128)(2,1)S(1)}, u32[]{:S(2)}, u32[]{:S(2)}) collective-permute-start(bf16[272,256]{1,0:T(8,128)(2,1)S(1)} %get-tuple-element.27), channel_id=1, source_target_pairs={{0,12},{4,0},{8,4},{12,8},{1,13},{5,1},{9,5},{13,9},{2,14},{6,2},{... | collective-permute-start | bytes 417800 | tf_op jit(solution)/shard_map/ppermute | solution.py:215
  21.8 7.2 %collective-permute-start.3 = (bf16[128,256]{1,0:T(8,128)(2,1)S(1)}, bf16[128,256]{1,0:T(8,128)(2,1)S(1)}, u32[]{:S(2)}, u32[]{:S(2)}) collective-permute-start(bf16[128,256]{1,0:T(8,128)(2,1)S(1)} %get-tuple-element.17), channel_id=1, source_target_pairs={{0,4},{4,8},{8,12},{12,0},{1,5},{5,9},{9,13},{13,1},{2,6},{6,10},{... | collective-permute-start | bytes 196616 | tf_op jit(solution)/shard_map/ppermute | solution.py:221
  25.3 6.2 %collective-permute-start.4 = (bf16[128,256]{1,0:T(8,128)(2,1)S(1)}, bf16[128,256]{1,0:T(8,128)(2,1)S(1)}, u32[]{:S(2)}, u32[]{:S(2)}) collective-permute-start(bf16[128,256]{1,0:T(8,128)(2,1)S(1)} %get-tuple-element.16), channel_id=1, source_target_pairs={{0,8},{4,12},{8,0},{12,4},{1,9},{5,13},{9,1},{13,5},{2,10},{6,14},... | collective-permute-start | bytes 196616 | tf_op jit(solution)/shard_map/ppermute | solution.py:221
  26.9 5.2 %collective-permute-start.5 = (bf16[128,256]{1,0:T(8,128)(2,1)S(1)}, bf16[128,256]{1,0:T(8,128)(2,1)S(1)}, u32[]{:S(2)}, u32[]{:S(2)}) collective-permute-start(bf16[128,256]{1,0:T(8,128)(2,1)S(1)} %get-tuple-element.15), channel_id=1, source_target_pairs={{0,12},{4,0},{8,4},{12,8},{1,13},{5,1},{9,5},{13,9},{2,14},{6,2},{... | collective-permute-start | bytes 196616 | tf_op jit(solution)/shard_map/ppermute | solution.py:221
  34.0 2.0 %collective-permute-start.6 = (bf16[128,2048]{1,0:T(8,128)(2,1)S(1)}, bf16[128,2048]{1,0:T(8,128)(2,1)S(1)}, u32[]{:S(2)}, u32[]{:S(2)}) collective-permute-start(bf16[128,2048]{1,0:T(8,128)(2,1)S(1)} %dynamic-slice_convert_fusion), channel_id=1, source_target_pairs={{0,1},{1,0},{2,3},{3,2},{4,5},{5,4},{6,7},{7,6},{8,9},{9,8},{10,11... | collective-permute-start | bytes 1572872 | tf_op jit(solution)/shard_map/ppermute | solution.py:174
  36.1 14.0 %collective-permute-start.7 = (bf16[128,2048]{1,0:T(8,128)(2,1)S(1)}, bf16[128,2048]{1,0:T(8,128)(2,1)S(1)}, u32[]{:S(2)}, u32[]{:S(2)}) collective-permute-start(bf16[128,2048]{1,0:T(8,128)(2,1)S(1)} %fusion.2), channel_id=1, source_target_pairs={{0,2},{1,3},{2,0},{3,1},{4,6},{5,7},{6,4},{7,5},{8,10},{9,11},{10,... | collective-permute-start | bytes 1572872 | tf_op jit(solution)/shard_map/ppermute | solution.py:174
  50.3 2.0 %collective-permute-start.8 = (bf16[128,2048]{1,0:T(8,128)(2,1)S(1)}, bf16[128,2048]{1,0:T(8,128)(2,1)S(1)}, u32[]{:S(2)}, u32[]{:S(2)}) collective-permute-start(bf16[128,2048]{1,0:T(8,128)(2,1)S(1)} %add_convert_fusion), channel_id=1, source_target_pairs={{0,1},{1,0},{2,3},{3,2},{4,5},{5,4},{6,7},{7,6},{8,9},{9,8},{10,11... | collective-permute-start | bytes 1572872 | tf_op jit(solution)/shard_map/ppermute | solution.py:174

commit v15 on v14

--- a/solution.py
+++ b/solution.py
@@ -201,14 +201,14 @@
         order = [0] + [k for k in (1, nseq - 1) if k < nseq] + [k for k in range(2, nseq - 1)]
         order = list(dict.fromkeys(order))
 
-        first_input = (first_gate.astype(F32) * value.astype(F32)).astype(BF16)
         id_rows = -(-rows // per)
         pad_rows = -(-id_rows // 16) * 16
-        ids = jnp.pad(segment_ids.astype(BF16), (0, pad_rows * per - rows)).reshape(pad_rows, per)
 
         def block_for(dest):
             cols = lambda x: lax.dynamic_slice_in_dim(x, dest * per, per, 1)
-            return jnp.concatenate([cols(first_input), cols(second_gate), ids], axis=0)
+            first_input = (cols(first_gate).astype(F32) * cols(value).astype(F32)).astype(BF16)
+            ids = jnp.pad(segment_ids.astype(BF16), (0, pad_rows * per - rows)).reshape(pad_rows, per)
+            return jnp.concatenate([first_input, cols(second_gate), ids], axis=0)
 
         got = {0: block_for(me)}
         for k in order[1:]:

time: 53.8 us -> 53.8 us (level)
  no operation moved by 1% of the time
where the time goes in v15:
time: 53.8 us; the launch traced here: 53.5 us
  waiting for transfers between devices  26 us (48%)
  starting transfers between devices  14.7 us (27%)
  Pallas kernels  5.79 us (11%)
  other arithmetic  3.64 us (7%)
  local copies, waits for them, and re-layouts  1.87 us (3%)
  matrix products  1.32 us (2%)
    ppermute x3, waiting for transfers between devices, swap(): return lax.ppermute(x, 'chan', [(c, c ^ bit) for c in range(4)])  16.3 us
    ppermute x3, starting transfers between devices, local(): lax.ppermute(block_for((me + k) % nseq), 'seq', [(i, (i + k) % nseq) for...  7.04 us
    ppermute x3, starting transfers between devices, local(): lax.ppermute(second_mix[k * rows:(k + 1) * rows], 'seq', [(i, (i + k) % n...  5.93 us
    ppermute x3, waiting for transfers between devices, local(): lax.ppermute(block_for((me + k) % nseq), 'seq', [(i, (i + k) % nseq) for...  5.46 us
    ppermute x3, waiting for transfers between devices, local(): lax.ppermute(second_mix[k * rows:(k + 1) * rows], 'seq', [(i, (i + k) % n...  4.31 us
    pallas_call x1, Pallas kernels, hyena_call(): pl.pallas_call(functools.partial(hyena_kernel, nseq=nseq, rows=rows), out...  3.96 us
    pallas_call x1, Pallas kernels, proj_call(): pl.pallas_call(functools.partial(proj_kernel, nseq=nseq), out_shape=jax.S...  1.83 us
    ppermute x3, starting transfers between devices, swap(): return lax.ppermute(x, 'chan', [(c, c ^ bit) for c in range(4)])  1.7 us
  transfers between devices with their start and end apart: 9, of which 8 were waited for; matrix products, arithmetic and copies ran while one was open for 4% of the time, Pallas kernels for 0%

profile of v15, /device:TPU:0, one launch (start us, length us, event | category | flops | bytes accessed | tf_op | source)
XLA Modules:
  0.0 53.5 jit_solution(6167371821313177246)
XLA Ops:
  0.0 0.0 copy-start.1
  0.0 0.7 %convert_element_type.65 = bf16[128]{0:T(256)(128)(2,1)S(1)} convert(s32[128]{0:T(128)} %param.15) | non-fusion elementwise | flops 128 | bytes 768 | tf_op jit(solution)/shard_map/convert_element_type | solution.py:210
  0.8 1.0 %constant_dynamic-slice_fusion = (bf16[128,256]{1,0:T(8,128)(2,1)S(1)}, bf16[128,256]{1,0:T(8,128)(2,1)S(1)}, bf16[128,256]{1,0:T(8,128)(2,1)S(1)}, bf16[128,256]{1,0:T(8,128)(2,1)S(1)}) fusion(bf16[128,1024]{1,0:T(8,128)(2,1)} %param.11, s32[]{:T(128)S(6)} %select_n.99, s32[]{:T(128)S(6)} %select_n.95, s32[]{:T(128)S(6)} %select_n.93, s32[]{:T(128)S(6)} %select_n.97), kind=kLoop, calls=%fused_computation.23 | loop fusion | bytes 524304 | tf_op jit(solution)/shard_map/dynamic_slice | solution.py:208
  1.7 1.1 %multiply_convert_fusion = (bf16[128,256]{1,0:T(8,128)(2,1)S(1)}, bf16[128,256]{1,0:T(8,128)(2,1)S(1)}, bf16[128,256]{1,0:T(8,128)(2,1)S(1)}, bf16[128,256]{1,0:T(8,128)(2,1)S(1)}) fusion(bf16[128,1024]{1,0:T(8,128)(2,1)} %param.9, s32[]{:T(128)S(6)} %select_n.99, bf16[128,1024]{1,0:T(8,128)(2,1)} %param.10, s32[]{:T(128)S(6)} %select_n.95, ...), kind=kLoop, calls=%fused_computation.17 | loop fusion | flops 524288 | bytes 786448 | tf_op jit(solution)/shard_map/convert_element_type | solution.py:209
  2.9 0.0 copy-start
  2.9 3.1 %collective-permute-start = (bf16[272,256]{1,0:T(8,128)(2,1)S(1)}, bf16[272,256]{1,0:T(8,128)(2,1)S(1)}, u32[]{:S(2)}, u32[]{:S(2)}) collective-permute-start(bf16[272,256]{1,0:T(8,128)(2,1)S(1)} %get-tuple-element.28), channel_id=1, source_target_pairs={{0,4},{4,8},{8,12},{12,0},{1,5},{5,9},{9,13},{13,1},{2,6},{6,10},{... | collective-permute-start | bytes 417800 | tf_op jit(solution)/shard_map/ppermute | solution.py:215
  6.0 2.6 %collective-permute-start.1 = (bf16[272,256]{1,0:T(8,128)(2,1)S(1)}, bf16[272,256]{1,0:T(8,128)(2,1)S(1)}, u32[]{:S(2)}, u32[]{:S(2)}) collective-permute-start(bf16[272,256]{1,0:T(8,128)(2,1)S(1)} %get-tuple-element.29), channel_id=1, source_target_pairs={{0,8},{4,12},{8,0},{12,4},{1,9},{5,13},{9,1},{13,5},{2,10},{6,14},... | collective-permute-start | bytes 417800 | tf_op jit(solution)/shard_map/ppermute | solution.py:215
  8.6 1.3 %collective-permute-start.2 = (bf16[272,256]{1,0:T(8,128)(2,1)S(1)}, bf16[272,256]{1,0:T(8,128)(2,1)S(1)}, u32[]{:S(2)}, u32[]{:S(2)}) collective-permute-start(bf16[272,256]{1,0:T(8,128)(2,1)S(1)} %get-tuple-element.27), channel_id=1, source_target_pairs={{0,12},{4,0},{8,4},{12,8},{1,13},{5,1},{9,5},{13,9},{2,14},{6,2},{... | collective-permute-start | bytes 417800 | tf_op jit(solution)/shard_map/ppermute | solution.py:215
  10.0 0.7 %dynamic-slice_bitcast_fusion = (bf16[512,16]{0,1:T(8,128)(2,1)S(1)}, bf16[512,16]{0,1:T(8,128)(2,1)S(1)}) fusion(bf16[64,512]{1,0:T(8,128)(2,1)} %param.13, s32[]{:T(128)S(6)} %select_n.100, bf16[64,512]{1,0:T(8,128)(2,1)} %param.12), kind=kLoop, calls=%fused_computation.21 | loop fusion | bytes 65540 | tf_op jit(solution)/shard_map/transpose | solution.py:190
  10.8 0.0 copy-done.1
  10.8 0.3 fusion.5
  11.1 0.3 fusion.4
  11.5 0.0 copy-done
  11.5 0.3 fusion
  11.8 0.3 fusion.1
  12.2 0.1 slice_select_fusion
  12.3 0.3 collective-permute-done.refs_1_
  12.7 5.1 %collective-permute-done.1.refs_2_ = bf16[272,256]{1,0:T(8,128)(2,1)S(1)} collective-permute-done((bf16[272,256]{1,0:T(8,128)(2,1)S(1)}, bf16[272,256]{1,0:T(8,128)(2,1)S(1)}, u32[]{:S(2)}, u32[]{:S(2)}) %collective-permute-start.1) | collective-permute-done | bytes 139296 | tf_op jit(solution)/shard_map/ppermute | solution.py:215
  17.8 0.0 collective-permute-done.2.refs_3_
  17.8 4.0 %shard_map.91 = (bf16[512,256]{1,0:T(8,128)(2,1)S(1)}, bf16[1024,4096]{1,0:T(8,128)(2,1)S(1)}) custom-call(bf16[272,256]{1,0:T(8,128)(2,1)S(1)} %get-tuple-element.30.refs_0_, bf16[272,256]{1,0:T(8,128)(2,1)S(1)} %collective-permute-done.refs_1_, bf16[272,256]{1,0:T(8,128)(2,1)S(1)} %collective-permute-done.1.refs_2_, ...), custom_call_target="tpu_custom_call" | custom-call | flops 2684354560 | bytes 3145728 | tf_op jit(solution)/shard_map/pallas_call | solution.py:126
  21.8 3.5 %collective-permute-start.3 = (bf16[128,256]{1,0:T(8,128)(2,1)S(1)}, bf16[128,256]{1,0:T(8,128)(2,1)S(1)}, u32[]{:S(2)}, u32[]{:S(2)}) collective-permute-start(bf16[128,256]{1,0:T(8,128)(2,1)S(1)} %get-tuple-element.21), channel_id=1, source_target_pairs={{0,4},{4,8},{8,12},{12,0},{1,5},{5,9},{9,13},{13,1},{2,6},{6,10},{... | collective-permute-start | bytes 196616 | tf_op jit(solution)/shard_map/ppermute | solution.py:221
  25.3 1.6 %collective-permute-start.4 = (bf16[128,256]{1,0:T(8,128)(2,1)S(1)}, bf16[128,256]{1,0:T(8,128)(2,1)S(1)}, u32[]{:S(2)}, u32[]{:S(2)}) collective-permute-start(bf16[128,256]{1,0:T(8,128)(2,1)S(1)} %get-tuple-element.20), channel_id=1, source_target_pairs={{0,8},{4,12},{8,0},{12,4},{1,9},{5,13},{9,1},{13,5},{2,10},{6,14},... | collective-permute-start | bytes 196616 | tf_op jit(solution)/shard_map/ppermute | solution.py:221
  26.9 0.8 %collective-permute-start.5 = (bf16[128,256]{1,0:T(8,128)(2,1)S(1)}, bf16[128,256]{1,0:T(8,128)(2,1)S(1)}, u32[]{:S(2)}, u32[]{:S(2)}) collective-permute-start(bf16[128,256]{1,0:T(8,128)(2,1)S(1)} %get-tuple-element.19), channel_id=1, source_target_pairs={{0,12},{4,0},{8,4},{12,8},{1,13},{5,1},{9,5},{13,9},{2,14},{6,2},{... | collective-permute-start | bytes 196616 | tf_op jit(solution)/shard_map/ppermute | solution.py:221
  27.7 0.1 pad_add_fusion.refs_0_
  27.8 1.1 %collective-permute-done.3.refs_2_ = bf16[128,256]{1,0:T(8,128)(2,1)S(1)} collective-permute-done((bf16[128,256]{1,0:T(8,128)(2,1)S(1)}, bf16[128,256]{1,0:T(8,128)(2,1)S(1)}, u32[]{:S(2)}, u32[]{:S(2)}) %collective-permute-start.3) | collective-permute-done | bytes 65568 | tf_op jit(solution)/shard_map/ppermute | solution.py:221
  28.9 2.6 %collective-permute-done.4.refs_3_ = bf16[128,256]{1,0:T(8,128)(2,1)S(1)} collective-permute-done((bf16[128,256]{1,0:T(8,128)(2,1)S(1)}, bf16[128,256]{1,0:T(8,128)(2,1)S(1)}, u32[]{:S(2)}, u32[]{:S(2)}) %collective-permute-start.4) | collective-permute-done | bytes 65568 | tf_op jit(solution)/shard_map/ppermute | solution.py:221
  31.5 0.6 %collective-permute-done.5.refs_4_ = bf16[128,256]{1,0:T(8,128)(2,1)S(1)} collective-permute-done((bf16[128,256]{1,0:T(8,128)(2,1)S(1)}, bf16[128,256]{1,0:T(8,128)(2,1)S(1)}, u32[]{:S(2)}, u32[]{:S(2)}) %collective-permute-start.5) | collective-permute-done | bytes 65568 | tf_op jit(solution)/shard_map/ppermute | solution.py:221
  32.1 1.8 %shard_map.92 = f32[128,4096]{1,0:T(8,128)S(1)} custom-call(s32[4]{0:T(128)S(1)} %pad_add_fusion.refs_0_, bf16[128,256]{1,0:T(8,128)(2,1)S(1)} %get-tuple-element.22.refs_1_, bf16[128,256]{1,0:T(8,128)(2,1)S(1)} %collective-permute-done.3.refs_2_, bf16[128,256]{1,0:T(8,128)(2,1)S(1)} %collective-permute-done.4.refs_3_, ...), custom_call_target="tpu_custom_call" | custom-call | flops 1073741824 | bytes 10485760 | tf_op jit(solution)/shard_map/pallas_call | solution.py:158
  34.0 0.1 dynamic-slice_convert_fusion
  34.0 0.1 collective-permute-start.6
  34.1 1.9 %collective-permute-done.6 = bf16[128,2048]{1,0:T(8,128)(2,1)S(1)} collective-permute-done((bf16[128,2048]{1,0:T(8,128)(2,1)S(1)}, bf16[128,2048]{1,0:T(8,128)(2,1)S(1)}, u32[]{:S(2)}, u32[]{:S(2)}) %collective-permute-start.6) | collective-permute-done | bytes 524320 | tf_op jit(solution)/shard_map/ppermute | solution.py:174
  36.0 0.1 fusion.2
  36.1 1.6 %collective-permute-start.7 = (bf16[128,2048]{1,0:T(8,128)(2,1)S(1)}, bf16[128,2048]{1,0:T(8,128)(2,1)S(1)}, u32[]{:S(2)}, u32[]{:S(2)}) collective-permute-start(bf16[128,2048]{1,0:T(8,128)(2,1)S(1)} %fusion.2), channel_id=1, source_target_pairs={{0,2},{1,3},{2,0},{3,1},{4,6},{5,7},{6,4},{7,5},{8,10},{9,11},{10,... | collective-permute-start | bytes 1572872 | tf_op jit(solution)/shard_map/ppermute | solution.py:174
  37.7 12.5 %collective-permute-done.7 = bf16[128,2048]{1,0:T(8,128)(2,1)S(1)} collective-permute-done((bf16[128,2048]{1,0:T(8,128)(2,1)S(1)}, bf16[128,2048]{1,0:T(8,128)(2,1)S(1)}, u32[]{:S(2)}, u32[]{:S(2)}) %collective-permute-start.7) | collective-permute-done | bytes 524320 | tf_op jit(solution)/shard_map/ppermute | solution.py:174
  50.2 0.2 add_convert_fusion
  50.4 0.1 collective-permute-start.8
  50.4 1.9 %collective-permute-done.8 = bf16[128,2048]{1,0:T(8,128)(2,1)S(1)} collective-permute-done((bf16[128,2048]{1,0:T(8,128)(2,1)S(1)}, bf16[128,2048]{1,0:T(8,128)(2,1)S(1)}, u32[]{:S(2)}, u32[]{:S(2)}) %collective-permute-start.8) | collective-permute-done | bytes 524320 | tf_op jit(solution)/shard_map/ppermute | solution.py:174
  52.3 1.2 %maximum_select_fusion = bf16[128,4096]{1,0:T(8,128)(2,1)} fusion(bf16[128,2048]{1,0:T(8,128)(2,1)S(1)} %collective-permute-done.8, bf16[128,2048]{1,0:T(8,128)(2,1)S(1)} %add_convert_fusion, pred[]{:T(512)S(6)} %eq.23), kind=kLoop, calls=%fused_computation.4 | loop fusion | flops 4718592 | bytes 2097153 | tf_op jit(solution)/shard_map/jit(_where)/select_n | solution.py:238
  (7 shorter events, 0.1 us)
Async XLA Ops:
  0.0 10.8 %copy-start.1 = (bf16[512,512]{1,0:T(8,128)(2,1)S(1)}, bf16[512,512]{1,0:T(8,128)(2,1)}, u32[]{:S(2)}) copy-start(bf16[512,512]{1,0:T(8,128)(2,1)} %constant.84.clone.refs_10_) | copy-start | bytes 1572868
  2.9 8.6 %copy-start = (bf16[512,512]{1,0:T(8,128)(2,1)S(1)}, bf16[512,512]{1,0:T(8,128)(2,1)}, u32[]{:S(2)}) copy-start(bf16[512,512]{1,0:T(8,128)(2,1)} %constant.85.clone.refs_11_) | copy-start | bytes 1572868
  2.9 9.8 %collective-permute-start = (bf16[272,256]{1,0:T(8,128)(2,1)S(1)}, bf16[272,256]{1,0:T(8,128)(2,1)S(1)}, u32[]{:S(2)}, u32[]{:S(2)}) collective-permute-start(bf16[272,256]{1,0:T(8,128)(2,1)S(1)} %get-tuple-element.28), channel_id=1, source_target_pairs={{0,4},{4,8},{8,12},{12,0},{1,5},{5,9},{9,13},{13,1},{2,6},{6,10},{... | collective-permute-start | bytes 417800 | tf_op jit(solution)/shard_map/ppermute | solution.py:215
  6.0 11.8 %collective-permute-start.1 = (bf16[272,256]{1,0:T(8,128)(2,1)S(1)}, bf16[272,256]{1,0:T(8,128)(2,1)S(1)}, u32[]{:S(2)}, u32[]{:S(2)}) collective-permute-start(bf16[272,256]{1,0:T(8,128)(2,1)S(1)} %get-tuple-element.29), channel_id=1, source_target_pairs={{0,8},{4,12},{8,0},{12,4},{1,9},{5,13},{9,1},{13,5},{2,10},{6,14},... | collective-permute-start | bytes 417800 | tf_op jit(solution)/shard_map/ppermute | solution.py:215
  8.6 9.2 %collective-permute-start.2 = (bf16[272,256]{1,0:T(8,128)(2,1)S(1)}, bf16[272,256]{1,0:T(8,128)(2,1)S(1)}, u32[]{:S(2)}, u32[]{:S(2)}) collective-permute-start(bf16[272,256]{1,0:T(8,128)(2,1)S(1)} %get-tuple-element.27), channel_id=1, source_target_pairs={{0,12},{4,0},{8,4},{12,8},{1,13},{5,1},{9,5},{13,9},{2,14},{6,2},{... | collective-permute-start | bytes 417800 | tf_op jit(solution)/shard_map/ppermute | solution.py:215
  21.8 7.1 %collective-permute-start.3 = (bf16[128,256]{1,0:T(8,128)(2,1)S(1)}, bf16[128,256]{1,0:T(8,128)(2,1)S(1)}, u32[]{:S(2)}, u32[]{:S(2)}) collective-permute-start(bf16[128,256]{1,0:T(8,128)(2,1)S(1)} %get-tuple-element.21), channel_id=1, source_target_pairs={{0,4},{4,8},{8,12},{12,0},{1,5},{5,9},{9,13},{13,1},{2,6},{6,10},{... | collective-permute-start | bytes 196616 | tf_op jit(solution)/shard_map/ppermute | solution.py:221
  25.3 6.2 %collective-permute-start.4 = (bf16[128,256]{1,0:T(8,128)(2,1)S(1)}, bf16[128,256]{1,0:T(8,128)(2,1)S(1)}, u32[]{:S(2)}, u32[]{:S(2)}) collective-permute-start(bf16[128,256]{1,0:T(8,128)(2,1)S(1)} %get-tuple-element.20), channel_id=1, source_target_pairs={{0,8},{4,12},{8,0},{12,4},{1,9},{5,13},{9,1},{13,5},{2,10},{6,14},... | collective-permute-start | bytes 196616 | tf_op jit(solution)/shard_map/ppermute | solution.py:221
  26.9 5.2 %collective-permute-start.5 = (bf16[128,256]{1,0:T(8,128)(2,1)S(1)}, bf16[128,256]{1,0:T(8,128)(2,1)S(1)}, u32[]{:S(2)}, u32[]{:S(2)}) collective-permute-start(bf16[128,256]{1,0:T(8,128)(2,1)S(1)} %get-tuple-element.19), channel_id=1, source_target_pairs={{0,12},{4,0},{8,4},{12,8},{1,13},{5,1},{9,5},{13,9},{2,14},{6,2},{... | collective-permute-start | bytes 196616 | tf_op jit(solution)/shard_map/ppermute | solution.py:221
  34.0 2.0 %collective-permute-start.6 = (bf16[128,2048]{1,0:T(8,128)(2,1)S(1)}, bf16[128,2048]{1,0:T(8,128)(2,1)S(1)}, u32[]{:S(2)}, u32[]{:S(2)}) collective-permute-start(bf16[128,2048]{1,0:T(8,128)(2,1)S(1)} %dynamic-slice_convert_fusion), channel_id=1, source_target_pairs={{0,1},{1,0},{2,3},{3,2},{4,5},{5,4},{6,7},{7,6},{8,9},{9,8},{10,11... | collective-permute-start | bytes 1572872 | tf_op jit(solution)/shard_map/ppermute | solution.py:174
  36.1 14.0 %collective-permute-start.7 = (bf16[128,2048]{1,0:T(8,128)(2,1)S(1)}, bf16[128,2048]{1,0:T(8,128)(2,1)S(1)}, u32[]{:S(2)}, u32[]{:S(2)}) collective-permute-start(bf16[128,2048]{1,0:T(8,128)(2,1)S(1)} %fusion.2), channel_id=1, source_target_pairs={{0,2},{1,3},{2,0},{3,1},{4,6},{5,7},{6,4},{7,5},{8,10},{9,11},{10,... | collective-permute-start | bytes 1572872 | tf_op jit(solution)/shard_map/ppermute | solution.py:174
  50.4 2.0 %collective-permute-start.8 = (bf16[128,2048]{1,0:T(8,128)(2,1)S(1)}, bf16[128,2048]{1,0:T(8,128)(2,1)S(1)}, u32[]{:S(2)}, u32[]{:S(2)}) collective-permute-start(bf16[128,2048]{1,0:T(8,128)(2,1)S(1)} %add_convert_fusion), channel_id=1, source_target_pairs={{0,1},{1,0},{2,3},{3,2},{4,5},{5,4},{6,7},{7,6},{8,9},{9,8},{10,11... | collective-permute-start | bytes 1572872 | tf_op jit(solution)/shard_map/ppermute | solution.py:174

commit v16 on v15

--- a/solution.py
+++ b/solution.py
@@ -142,18 +142,26 @@
     w_ref = refs[1 + nseq]
     o_ref = refs[2 + nseq]
     per = pieces[0].shape[1]
+    width = o_ref.shape[1]
+    col = pl.multiple_of(src_ref[nseq] * width, width)
     acc = None
     for k in range(nseq):
         start = pl.multiple_of(src_ref[k] * per, per)
-        term = jnp.dot(pieces[k][...], w_ref[pl.ds(start, per), :], preferred_element_type=F32)
+        term = jnp.dot(pieces[k][...], w_ref[pl.ds(start, per), pl.ds(col, width)],
+                       preferred_element_type=F32)
         acc = term if acc is None else acc + term
     o_ref[...] = acc
 
 
-def proj_call(srcs, pieces, out_weight):
+def proj_call(srcs, pieces, out_weight, half=None):
     nseq = len(pieces)
     rows, per = pieces[0].shape
     out_cols = out_weight.shape[1]
+    if half is None:
+        srcs = jnp.concatenate([srcs, jnp.zeros((1,), jnp.int32)])
+    else:
+        out_cols = out_cols // 2
+        srcs = jnp.concatenate([srcs, jnp.reshape(half, (1,)).astype(jnp.int32)])
     vmem = pl.BlockSpec(memory_space=pltpu.VMEM)
     return pl.pallas_call(
         functools.partial(proj_kernel, nseq=nseq),
@@ -223,15 +231,13 @@
         out_cols = out_weight.shape[1]
 
         srcs = jnp.stack([((me - k) % nseq).astype(jnp.int32) for k in range(nseq)])
-        partial_out = proj_call(srcs, [mix_pieces[k] for k in range(nseq)], staged_weight)
-
+        received = [mix_pieces[k] for k in range(nseq)]
         if nchan != 4:
-            return lax.psum(partial_out, "chan").astype(BF16)
+            return lax.psum(proj_call(srcs, received, staged_weight), "chan").astype(BF16)
         core = lax.axis_index("chan") % 2
-        width = out_cols // 2
-        other = lax.dynamic_slice_in_dim(partial_out, (1 - core) * width, width, 1)
+        other = proj_call(srcs, received, staged_weight, 1 - core)
         got_other = swap(other.astype(BF16), 1)
-        mine = lax.dynamic_slice_in_dim(partial_out, core * width, width, 1)
+        mine = proj_call(srcs, received, staged_weight, core)
         chip = mine + got_other.astype(F32)
         total = (chip + swap(chip.astype(BF16), 2).astype(F32)).astype(BF16)
         peer = swap(total, 1)

time: 53.8 us -> 63.2 us (1.17)
  local copies, waits for them, and re-layouts: 1.87 us -> 12 us
  waiting for transfers between devices: 26 us -> 24.5 us
  Pallas kernels: 5.79 us -> 6.49 us
    unnamed x4 -> x10, local copies, waits for them, and re-layouts: 0.01 us -> 10 us
    ppermute x3, waiting for transfers between devices: 16.3 us -> 14.7 us  [swap(): return lax.ppermute(x, 'chan', [(c, c ^ bit) for c in range(4)])]
    pallas_call x1 -> x2, Pallas kernels: 1.83 us -> 2.53 us  [proj_call(): pl.pallas_call(functools.partial(proj_kernel, nseq=nseq), out_shape=jax.S...]
  transfers between devices with their start and end apart: 9 -> 9, of which waited for: 8 -> 7; matrix products, arithmetic and copies ran while one was open for 4% -> 4% of each run, Pallas kernels for 0% -> 2%
where the time goes in v16:
time: 63.2 us; the launch traced here: 62.8 us
  waiting for transfers between devices  24.5 us (39%)
  starting transfers between devices  14.7 us (23%)
  local copies, waits for them, and re-layouts  12 us (19%)
  Pallas kernels  6.49 us (10%)
  other arithmetic  3.66 us (6%)
  matrix products  1.32 us (2%)
    ppermute x3, waiting for transfers between devices, swap(): return lax.ppermute(x, 'chan', [(c, c ^ bit) for c in range(4)])  14.7 us
    unnamed x10, local copies, waits for them, and re-layouts  10 us
    ppermute x3, starting transfers between devices, local(): lax.ppermute(block_for((me + k) % nseq), 'seq', [(i, (i + k) % nseq) for...  7.04 us
    ppermute x3, starting transfers between devices, local(): lax.ppermute(second_mix[k * rows:(k + 1) * rows], 'seq', [(i, (i + k) % n...  5.93 us
    ppermute x3, waiting for transfers between devices, local(): lax.ppermute(block_for((me + k) % nseq), 'seq', [(i, (i + k) % nseq) for...  5.51 us
    ppermute x3, waiting for transfers between devices, local(): lax.ppermute(second_mix[k * rows:(k + 1) * rows], 'seq', [(i, (i + k) % n...  4.3 us
    pallas_call x1, Pallas kernels, hyena_call(): pl.pallas_call(functools.partial(hyena_kernel, nseq=nseq, rows=rows), out...  3.96 us
    pallas_call x2, Pallas kernels, proj_call(): pl.pallas_call(functools.partial(proj_kernel, nseq=nseq), out_shape=jax.S...  2.53 us
  transfers between devices with their start and end apart: 9, of which 7 were waited for; matrix products, arithmetic and copies ran while one was open for 4% of the time, Pallas kernels for 2%

profile of v16, /device:TPU:0, one launch (start us, length us, event | category | flops | bytes accessed | tf_op | source)
XLA Modules:
  0.0 62.8 jit_solution(6785177303440950723)
XLA Ops:
  0.0 0.0 copy-start.4
  0.0 0.7 %convert_element_type.65 = bf16[128]{0:T(256)(128)(2,1)S(1)} convert(s32[128]{0:T(128)} %param.15) | non-fusion elementwise | flops 128 | bytes 768 | tf_op jit(solution)/shard_map/convert_element_type | solution.py:218
  0.8 1.0 %constant_dynamic-slice_fusion = (bf16[128,256]{1,0:T(8,128)(2,1)S(1)}, bf16[128,256]{1,0:T(8,128)(2,1)S(1)}, bf16[128,256]{1,0:T(8,128)(2,1)S(1)}, bf16[128,256]{1,0:T(8,128)(2,1)S(1)}) fusion(bf16[128,1024]{1,0:T(8,128)(2,1)} %param.11, s32[]{:T(128)S(6)} %select_n.93, s32[]{:T(128)S(6)} %select_n.89, s32[]{:T(128)S(6)} %select_n.87, s32[]{:T(128)S(6)} %select_n.91), kind=kLoop, calls=%fused_computation.22 | loop fusion | bytes 524304 | tf_op jit(solution)/shard_map/dynamic_slice | solution.py:216
  1.7 1.1 %multiply_convert_fusion = (bf16[128,256]{1,0:T(8,128)(2,1)S(1)}, bf16[128,256]{1,0:T(8,128)(2,1)S(1)}, bf16[128,256]{1,0:T(8,128)(2,1)S(1)}, bf16[128,256]{1,0:T(8,128)(2,1)S(1)}) fusion(bf16[128,1024]{1,0:T(8,128)(2,1)} %param.9, s32[]{:T(128)S(6)} %select_n.93, bf16[128,1024]{1,0:T(8,128)(2,1)} %param.10, s32[]{:T(128)S(6)} %select_n.89, ...), kind=kLoop, calls=%fused_computation.16 | loop fusion | flops 524288 | bytes 786448 | tf_op jit(solution)/shard_map/convert_element_type | solution.py:217
  2.9 0.0 copy-start.3
  2.9 3.1 %collective-permute-start = (bf16[272,256]{1,0:T(8,128)(2,1)S(1)}, bf16[272,256]{1,0:T(8,128)(2,1)S(1)}, u32[]{:S(2)}, u32[]{:S(2)}) collective-permute-start(bf16[272,256]{1,0:T(8,128)(2,1)S(1)} %get-tuple-element.28), channel_id=1, source_target_pairs={{0,4},{4,8},{8,12},{12,0},{1,5},{5,9},{9,13},{13,1},{2,6},{6,10},{... | collective-permute-start | bytes 417800 | tf_op jit(solution)/shard_map/ppermute | solution.py:223
  6.0 2.6 %collective-permute-start.1 = (bf16[272,256]{1,0:T(8,128)(2,1)S(1)}, bf16[272,256]{1,0:T(8,128)(2,1)S(1)}, u32[]{:S(2)}, u32[]{:S(2)}) collective-permute-start(bf16[272,256]{1,0:T(8,128)(2,1)S(1)} %get-tuple-element.29), channel_id=1, source_target_pairs={{0,8},{4,12},{8,0},{12,4},{1,9},{5,13},{9,1},{13,5},{2,10},{6,14},... | collective-permute-start | bytes 417800 | tf_op jit(solution)/shard_map/ppermute | solution.py:223
  8.6 1.3 %collective-permute-start.2 = (bf16[272,256]{1,0:T(8,128)(2,1)S(1)}, bf16[272,256]{1,0:T(8,128)(2,1)S(1)}, u32[]{:S(2)}, u32[]{:S(2)}) collective-permute-start(bf16[272,256]{1,0:T(8,128)(2,1)S(1)} %get-tuple-element.27), channel_id=1, source_target_pairs={{0,12},{4,0},{8,4},{12,8},{1,13},{5,1},{9,5},{13,9},{2,14},{6,2},{... | collective-permute-start | bytes 417800 | tf_op jit(solution)/shard_map/ppermute | solution.py:223
  10.0 0.7 %dynamic-slice_bitcast_fusion = (bf16[512,16]{0,1:T(8,128)(2,1)S(1)}, bf16[512,16]{0,1:T(8,128)(2,1)S(1)}) fusion(bf16[64,512]{1,0:T(8,128)(2,1)} %param.13, s32[]{:T(128)S(6)} %select_n.94, bf16[64,512]{1,0:T(8,128)(2,1)} %param.12), kind=kLoop, calls=%fused_computation.20 | loop fusion | bytes 65540 | tf_op jit(solution)/shard_map/transpose | solution.py:198
  10.8 0.0 copy-done.4
  10.8 0.3 fusion.5
  11.1 0.3 fusion.4
  11.5 0.0 copy-done.3
  11.5 0.3 fusion
  11.8 0.3 fusion.1
  12.1 0.1 slice_select_fusion
  12.3 0.4 collective-permute-done.refs_1_
  12.7 5.1 %collective-permute-done.1.refs_2_ = bf16[272,256]{1,0:T(8,128)(2,1)S(1)} collective-permute-done((bf16[272,256]{1,0:T(8,128)(2,1)S(1)}, bf16[272,256]{1,0:T(8,128)(2,1)S(1)}, u32[]{:S(2)}, u32[]{:S(2)}) %collective-permute-start.1) | collective-permute-done | bytes 139296 | tf_op jit(solution)/shard_map/ppermute | solution.py:223
  17.8 0.0 collective-permute-done.2.refs_3_
  17.8 4.0 %shard_map.91 = (bf16[512,256]{1,0:T(8,128)(2,1)S(1)}, bf16[1024,4096]{1,0:T(8,128)(2,1)S(1)}) custom-call(bf16[272,256]{1,0:T(8,128)(2,1)S(1)} %get-tuple-element.30.refs_0_, bf16[272,256]{1,0:T(8,128)(2,1)S(1)} %collective-permute-done.refs_1_, bf16[272,256]{1,0:T(8,128)(2,1)S(1)} %collective-permute-done.1.refs_2_, ...), custom_call_target="tpu_custom_call" | custom-call | flops 2684354560 | bytes 3145728 | tf_op jit(solution)/shard_map/pallas_call | solution.py:126
  21.8 0.0 copy-start
  21.8 3.2 %copy-done = bf16[1024,4096]{1,0:T(8,128)(2,1)} copy-done((bf16[1024,4096]{1,0:T(8,128)(2,1)}, bf16[1024,4096]{1,0:T(8,128)(2,1)S(1)}, u32[]{:S(2)}) %copy-start) | copy-done | bytes 8388632
  25.0 3.5 %collective-permute-start.3 = (bf16[128,256]{1,0:T(8,128)(2,1)S(1)}, bf16[128,256]{1,0:T(8,128)(2,1)S(1)}, u32[]{:S(2)}, u32[]{:S(2)}) collective-permute-start(bf16[128,256]{1,0:T(8,128)(2,1)S(1)} %get-tuple-element.21), channel_id=1, source_target_pairs={{0,4},{4,8},{8,12},{12,0},{1,5},{5,9},{9,13},{13,1},{2,6},{6,10},{... | collective-permute-start | bytes 196616 | tf_op jit(solution)/shard_map/ppermute | solution.py:229
  28.5 1.6 %collective-permute-start.4 = (bf16[128,256]{1,0:T(8,128)(2,1)S(1)}, bf16[128,256]{1,0:T(8,128)(2,1)S(1)}, u32[]{:S(2)}, u32[]{:S(2)}) collective-permute-start(bf16[128,256]{1,0:T(8,128)(2,1)S(1)} %get-tuple-element.20), channel_id=1, source_target_pairs={{0,8},{4,12},{8,0},{12,4},{1,9},{5,13},{9,1},{13,5},{2,10},{6,14},... | collective-permute-start | bytes 196616 | tf_op jit(solution)/shard_map/ppermute | solution.py:229
  30.2 0.8 %collective-permute-start.5 = (bf16[128,256]{1,0:T(8,128)(2,1)S(1)}, bf16[128,256]{1,0:T(8,128)(2,1)S(1)}, u32[]{:S(2)}, u32[]{:S(2)}) collective-permute-start(bf16[128,256]{1,0:T(8,128)(2,1)S(1)} %get-tuple-element.19), channel_id=1, source_target_pairs={{0,12},{4,0},{8,4},{12,8},{1,13},{5,1},{9,5},{13,9},{2,14},{6,2},{... | collective-permute-start | bytes 196616 | tf_op jit(solution)/shard_map/ppermute | solution.py:229
  31.0 0.1 concatenate.31.refs_0_
  31.1 1.1 %collective-permute-done.3.refs_2_ = bf16[128,256]{1,0:T(8,128)(2,1)S(1)} collective-permute-done((bf16[128,256]{1,0:T(8,128)(2,1)S(1)}, bf16[128,256]{1,0:T(8,128)(2,1)S(1)}, u32[]{:S(2)}, u32[]{:S(2)}) %collective-permute-start.3) | collective-permute-done | bytes 65568 | tf_op jit(solution)/shard_map/ppermute | solution.py:229
  32.2 2.6 %collective-permute-done.4.refs_3_ = bf16[128,256]{1,0:T(8,128)(2,1)S(1)} collective-permute-done((bf16[128,256]{1,0:T(8,128)(2,1)S(1)}, bf16[128,256]{1,0:T(8,128)(2,1)S(1)}, u32[]{:S(2)}, u32[]{:S(2)}) %collective-permute-start.4) | collective-permute-done | bytes 65568 | tf_op jit(solution)/shard_map/ppermute | solution.py:229
  34.7 0.6 collective-permute-done.5.refs_4_
  35.3 0.0 copy-start.1
  35.4 3.4 %copy-done.1 = bf16[1024,4096]{1,0:T(8,128)(2,1)S(1)} copy-done((bf16[1024,4096]{1,0:T(8,128)(2,1)S(1)}, bf16[1024,4096]{1,0:T(8,128)(2,1)}, u32[]{:S(2)}) %copy-start.1) | copy-done | bytes 8388632
  38.7 1.3 %shard_map.93 = f32[128,2048]{1,0:T(8,128)S(1)} custom-call(s32[5]{0:T(128)S(1)} %concatenate.31.refs_0_, bf16[128,256]{1,0:T(8,128)(2,1)S(1)} %get-tuple-element.22.refs_1_, bf16[128,256]{1,0:T(8,128)(2,1)S(1)} %collective-permute-done.3.refs_2_, bf16[128,256]{1,0:T(8,128)(2,1)S(1)} %collective-permute-done.4.refs_3_, ...), custom_call_target="tpu_custom_call" | custom-call | flops 536870912 | bytes 5242880 | tf_op jit(solution)/shard_map/pallas_call | solution.py:166
  40.0 0.1 convert_element_type.75
  40.1 0.1 collective-permute-start.6
  40.1 0.1 concatenate.26.refs_0_
  40.2 0.0 copy-start.2
  40.2 3.4 %copy-done.2 = bf16[1024,4096]{1,0:T(8,128)(2,1)S(1)} copy-done((bf16[1024,4096]{1,0:T(8,128)(2,1)S(1)}, bf16[1024,4096]{1,0:T(8,128)(2,1)}, u32[]{:S(2)}) %copy-start.2) | copy-done | bytes 8388632
  43.6 1.3 %shard_map.92 = f32[128,2048]{1,0:T(8,128)S(1)} custom-call(s32[5]{0:T(128)S(1)} %concatenate.26.refs_0_, bf16[128,256]{1,0:T(8,128)(2,1)S(1)} %get-tuple-element.22.refs_1_, bf16[128,256]{1,0:T(8,128)(2,1)S(1)} %collective-permute-done.3.refs_2_, bf16[128,256]{1,0:T(8,128)(2,1)S(1)} %collective-permute-done.4.refs_3_, ...), custom_call_target="tpu_custom_call" | custom-call | flops 536870912 | bytes 5242880 | tf_op jit(solution)/shard_map/pallas_call | solution.py:166
  44.9 0.0 collective-permute-done.6
  44.9 0.1 fusion.2
  45.0 1.6 %collective-permute-start.7 = (bf16[128,2048]{1,0:T(8,128)(2,1)S(1)}, bf16[128,2048]{1,0:T(8,128)(2,1)S(1)}, u32[]{:S(2)}, u32[]{:S(2)}) collective-permute-start(bf16[128,2048]{1,0:T(8,128)(2,1)S(1)} %fusion.2), channel_id=1, source_target_pairs={{0,2},{1,3},{2,0},{3,1},{4,6},{5,7},{6,4},{7,5},{8,10},{9,11},{10,... | collective-permute-start | bytes 1572872 | tf_op jit(solution)/shard_map/ppermute | solution.py:182
  46.6 12.8 %collective-permute-done.7 = bf16[128,2048]{1,0:T(8,128)(2,1)S(1)} collective-permute-done((bf16[128,2048]{1,0:T(8,128)(2,1)S(1)}, bf16[128,2048]{1,0:T(8,128)(2,1)S(1)}, u32[]{:S(2)}, u32[]{:S(2)}) %collective-permute-start.7) | collective-permute-done | bytes 524320 | tf_op jit(solution)/shard_map/ppermute | solution.py:182
  59.4 0.2 add_convert_fusion
  59.6 0.1 collective-permute-start.8
  59.7 1.9 %collective-permute-done.8 = bf16[128,2048]{1,0:T(8,128)(2,1)S(1)} collective-permute-done((bf16[128,2048]{1,0:T(8,128)(2,1)S(1)}, bf16[128,2048]{1,0:T(8,128)(2,1)S(1)}, u32[]{:S(2)}, u32[]{:S(2)}) %collective-permute-start.8) | collective-permute-done | bytes 524320 | tf_op jit(solution)/shard_map/ppermute | solution.py:182
  61.6 1.2 %maximum_select_fusion = bf16[128,4096]{1,0:T(8,128)(2,1)} fusion(bf16[128,2048]{1,0:T(8,128)(2,1)S(1)} %collective-permute-done.8, bf16[128,2048]{1,0:T(8,128)(2,1)S(1)} %add_convert_fusion, pred[]{:T(512)S(6)} %eq.23), kind=kLoop, calls=%fused_computation.4 | loop fusion | flops 4718592 | bytes 2097153 | tf_op jit(solution)/shard_map/jit(_where)/select_n | solution.py:244
  (7 shorter events, 0.1 us)
Async XLA Ops:
  0.0 10.8 %copy-start.4 = (bf16[512,512]{1,0:T(8,128)(2,1)S(1)}, bf16[512,512]{1,0:T(8,128)(2,1)}, u32[]{:S(2)}) copy-start(bf16[512,512]{1,0:T(8,128)(2,1)} %constant.80.clone.refs_10_) | copy-start | bytes 1572868
  2.9 8.6 %copy-start.3 = (bf16[512,512]{1,0:T(8,128)(2,1)S(1)}, bf16[512,512]{1,0:T(8,128)(2,1)}, u32[]{:S(2)}) copy-start(bf16[512,512]{1,0:T(8,128)(2,1)} %constant.81.clone.refs_11_) | copy-start | bytes 1572868
  2.9 9.8 %collective-permute-start = (bf16[272,256]{1,0:T(8,128)(2,1)S(1)}, bf16[272,256]{1,0:T(8,128)(2,1)S(1)}, u32[]{:S(2)}, u32[]{:S(2)}) collective-permute-start(bf16[272,256]{1,0:T(8,128)(2,1)S(1)} %get-tuple-element.28), channel_id=1, source_target_pairs={{0,4},{4,8},{8,12},{12,0},{1,5},{5,9},{9,13},{13,1},{2,6},{6,10},{... | collective-permute-start | bytes 417800 | tf_op jit(solution)/shard_map/ppermute | solution.py:223
  6.0 11.8 %collective-permute-start.1 = (bf16[272,256]{1,0:T(8,128)(2,1)S(1)}, bf16[272,256]{1,0:T(8,128)(2,1)S(1)}, u32[]{:S(2)}, u32[]{:S(2)}) collective-permute-start(bf16[272,256]{1,0:T(8,128)(2,1)S(1)} %get-tuple-element.29), channel_id=1, source_target_pairs={{0,8},{4,12},{8,0},{12,4},{1,9},{5,13},{9,1},{13,5},{2,10},{6,14},... | collective-permute-start | bytes 417800 | tf_op jit(solution)/shard_map/ppermute | solution.py:223
  8.6 9.2 %collective-permute-start.2 = (bf16[272,256]{1,0:T(8,128)(2,1)S(1)}, bf16[272,256]{1,0:T(8,128)(2,1)S(1)}, u32[]{:S(2)}, u32[]{:S(2)}) collective-permute-start(bf16[272,256]{1,0:T(8,128)(2,1)S(1)} %get-tuple-element.27), channel_id=1, source_target_pairs={{0,12},{4,0},{8,4},{12,8},{1,13},{5,1},{9,5},{13,9},{2,14},{6,2},{... | collective-permute-start | bytes 417800 | tf_op jit(solution)/shard_map/ppermute | solution.py:223
  21.8 3.2 %copy-start = (bf16[1024,4096]{1,0:T(8,128)(2,1)}, bf16[1024,4096]{1,0:T(8,128)(2,1)S(1)}, u32[]{:S(2)}) copy-start(bf16[1024,4096]{1,0:T(8,128)(2,1)S(1)} %get-tuple-element.8.refs_5_) | copy-start | bytes 25165828
  25.0 7.1 %collective-permute-start.3 = (bf16[128,256]{1,0:T(8,128)(2,1)S(1)}, bf16[128,256]{1,0:T(8,128)(2,1)S(1)}, u32[]{:S(2)}, u32[]{:S(2)}) collective-permute-start(bf16[128,256]{1,0:T(8,128)(2,1)S(1)} %get-tuple-element.21), channel_id=1, source_target_pairs={{0,4},{4,8},{8,12},{12,0},{1,5},{5,9},{9,13},{13,1},{2,6},{6,10},{... | collective-permute-start | bytes 196616 | tf_op jit(solution)/shard_map/ppermute | solution.py:229
  28.5 6.2 %collective-permute-start.4 = (bf16[128,256]{1,0:T(8,128)(2,1)S(1)}, bf16[128,256]{1,0:T(8,128)(2,1)S(1)}, u32[]{:S(2)}, u32[]{:S(2)}) collective-permute-start(bf16[128,256]{1,0:T(8,128)(2,1)S(1)} %get-tuple-element.20), channel_id=1, source_target_pairs={{0,8},{4,12},{8,0},{12,4},{1,9},{5,13},{9,1},{13,5},{2,10},{6,14},... | collective-permute-start | bytes 196616 | tf_op jit(solution)/shard_map/ppermute | solution.py:229
  30.2 5.2 %collective-permute-start.5 = (bf16[128,256]{1,0:T(8,128)(2,1)S(1)}, bf16[128,256]{1,0:T(8,128)(2,1)S(1)}, u32[]{:S(2)}, u32[]{:S(2)}) collective-permute-start(bf16[128,256]{1,0:T(8,128)(2,1)S(1)} %get-tuple-element.19), channel_id=1, source_target_pairs={{0,12},{4,0},{8,4},{12,8},{1,13},{5,1},{9,5},{13,9},{2,14},{6,2},{... | collective-permute-start | bytes 196616 | tf_op jit(solution)/shard_map/ppermute | solution.py:229
  35.3 3.4 %copy-start.1 = (bf16[1024,4096]{1,0:T(8,128)(2,1)S(1)}, bf16[1024,4096]{1,0:T(8,128)(2,1)}, u32[]{:S(2)}) copy-start(bf16[1024,4096]{1,0:T(8,128)(2,1)} %copy-done) | copy-start | bytes 25165828
  40.1 4.8 %collective-permute-start.6 = (bf16[128,2048]{1,0:T(8,128)(2,1)S(1)}, bf16[128,2048]{1,0:T(8,128)(2,1)S(1)}, u32[]{:S(2)}, u32[]{:S(2)}) collective-permute-start(bf16[128,2048]{1,0:T(8,128)(2,1)S(1)} %convert_element_type.75), channel_id=1, source_target_pairs={{0,1},{1,0},{2,3},{3,2},{4,5},{5,4},{6,7},{7,6},{8,9},{9,8},{10,11... | collective-permute-start | bytes 1572872 | tf_op jit(solution)/shard_map/ppermute | solution.py:182
  40.2 3.4 %copy-start.2 = (bf16[1024,4096]{1,0:T(8,128)(2,1)S(1)}, bf16[1024,4096]{1,0:T(8,128)(2,1)}, u32[]{:S(2)}) copy-start(bf16[1024,4096]{1,0:T(8,128)(2,1)} %copy-done) | copy-start | bytes 25165828
  45.0 14.4 %collective-permute-start.7 = (bf16[128,2048]{1,0:T(8,128)(2,1)S(1)}, bf16[128,2048]{1,0:T(8,128)(2,1)S(1)}, u32[]{:S(2)}, u32[]{:S(2)}) collective-permute-start(bf16[128,2048]{1,0:T(8,128)(2,1)S(1)} %fusion.2), channel_id=1, source_target_pairs={{0,2},{1,3},{2,0},{3,1},{4,6},{5,7},{6,4},{7,5},{8,10},{9,11},{10,... | collective-permute-start | bytes 1572872 | tf_op jit(solution)/shard_map/ppermute | solution.py:182
  59.6 2.0 %collective-permute-start.8 = (bf16[128,2048]{1,0:T(8,128)(2,1)S(1)}, bf16[128,2048]{1,0:T(8,128)(2,1)S(1)}, u32[]{:S(2)}, u32[]{:S(2)}) collective-permute-start(bf16[128,2048]{1,0:T(8,128)(2,1)S(1)} %add_convert_fusion), channel_id=1, source_target_pairs={{0,1},{1,0},{2,3},{3,2},{4,5},{5,4},{6,7},{7,6},{8,9},{9,8},{10,11... | collective-permute-start | bytes 1572872 | tf_op jit(solution)/shard_map/ppermute | solution.py:182

commit v17 on v15

--- a/solution.py
+++ b/solution.py
@@ -235,7 +235,8 @@
         chip = mine + got_other.astype(F32)
         total = (chip + swap(chip.astype(BF16), 2).astype(F32)).astype(BF16)
         peer = swap(total, 1)
-        return jnp.where(core == 0, jnp.concatenate([total, peer], 1), jnp.concatenate([peer, total], 1))
+        first_half = core == 0
+        return jnp.concatenate([jnp.where(first_half, total, peer), jnp.where(first_half, peer, total)], 1)
 
     return local
 

time: 53.8 us -> 53.7 us (level)
    select_n x1, other arithmetic: 1.21 us -> 0.07 us  [local(): jnp.where(first_half, total, peer)]
    concatenate x0 -> x1, other arithmetic: none -> 1.06 us  [local(): jnp.concatenate([jnp.where(first_half, total, peer), jnp.where(first_half...]
where the time goes in v17:
time: 53.7 us; the launch traced here: 53.5 us
  waiting for transfers between devices  26 us (48%)
  starting transfers between devices  14.7 us (27%)
  Pallas kernels  5.79 us (11%)
  other arithmetic  3.56 us (7%)
  local copies, waits for them, and re-layouts  1.87 us (3%)
  matrix products  1.32 us (2%)
    ppermute x3, waiting for transfers between devices, swap(): return lax.ppermute(x, 'chan', [(c, c ^ bit) for c in range(4)])  16.3 us
    ppermute x3, starting transfers between devices, local(): lax.ppermute(block_for((me + k) % nseq), 'seq', [(i, (i + k) % nseq) for...  7.04 us
    ppermute x3, starting transfers between devices, local(): lax.ppermute(second_mix[k * rows:(k + 1) * rows], 'seq', [(i, (i + k) % n...  5.93 us
    ppermute x3, waiting for transfers between devices, local(): lax.ppermute(block_for((me + k) % nseq), 'seq', [(i, (i + k) % nseq) for...  5.46 us
    ppermute x3, waiting for transfers between devices, local(): lax.ppermute(second_mix[k * rows:(k + 1) * rows], 'seq', [(i, (i + k) % n...  4.31 us
    pallas_call x1, Pallas kernels, hyena_call(): pl.pallas_call(functools.partial(hyena_kernel, nseq=nseq, rows=rows), out...  3.96 us
    pallas_call x1, Pallas kernels, proj_call(): pl.pallas_call(functools.partial(proj_kernel, nseq=nseq), out_shape=jax.S...  1.83 us
    ppermute x3, starting transfers between devices, swap(): return lax.ppermute(x, 'chan', [(c, c ^ bit) for c in range(4)])  1.7 us
  transfers between devices with their start and end apart: 9, of which 8 were waited for; matrix products, arithmetic and copies ran while one was open for 4% of the time, Pallas kernels for 0%

profile of v17, /device:TPU:0, one launch (start us, length us, event | category | flops | bytes accessed | tf_op | source)
XLA Modules:
  0.0 53.5 jit_solution(2732548069166472689)
XLA Ops:
  0.0 0.0 copy-start.1
  0.0 0.7 %convert_element_type.65 = bf16[128]{0:T(256)(128)(2,1)S(1)} convert(s32[128]{0:T(128)} %param.15) | non-fusion elementwise | flops 128 | bytes 768 | tf_op jit(solution)/shard_map/convert_element_type | solution.py:210
  0.8 1.0 %constant_dynamic-slice_fusion = (bf16[128,256]{1,0:T(8,128)(2,1)S(1)}, bf16[128,256]{1,0:T(8,128)(2,1)S(1)}, bf16[128,256]{1,0:T(8,128)(2,1)S(1)}, bf16[128,256]{1,0:T(8,128)(2,1)S(1)}) fusion(bf16[128,1024]{1,0:T(8,128)(2,1)} %param.11, s32[]{:T(128)S(6)} %select_n.103, s32[]{:T(128)S(6)} %select_n.99, s32[]{:T(128)S(6)} %select_n.97, s32[]{:T(128)S(6)} %select_n.101), kind=kLoop, calls=%fused_computation.25 | loop fusion | bytes 524304 | tf_op jit(solution)/shard_map/dynamic_slice | solution.py:208
  1.7 1.1 %multiply_convert_fusion = (bf16[128,256]{1,0:T(8,128)(2,1)S(1)}, bf16[128,256]{1,0:T(8,128)(2,1)S(1)}, bf16[128,256]{1,0:T(8,128)(2,1)S(1)}, bf16[128,256]{1,0:T(8,128)(2,1)S(1)}) fusion(bf16[128,1024]{1,0:T(8,128)(2,1)} %param.9, s32[]{:T(128)S(6)} %select_n.103, bf16[128,1024]{1,0:T(8,128)(2,1)} %param.10, s32[]{:T(128)S(6)} %select_n.99, ...), kind=kLoop, calls=%fused_computation.19 | loop fusion | flops 524288 | bytes 786448 | tf_op jit(solution)/shard_map/convert_element_type | solution.py:209
  2.9 0.0 copy-start
  2.9 3.1 %collective-permute-start = (bf16[272,256]{1,0:T(8,128)(2,1)S(1)}, bf16[272,256]{1,0:T(8,128)(2,1)S(1)}, u32[]{:S(2)}, u32[]{:S(2)}) collective-permute-start(bf16[272,256]{1,0:T(8,128)(2,1)S(1)} %get-tuple-element.30), channel_id=1, source_target_pairs={{0,4},{4,8},{8,12},{12,0},{1,5},{5,9},{9,13},{13,1},{2,6},{6,10},{... | collective-permute-start | bytes 417800 | tf_op jit(solution)/shard_map/ppermute | solution.py:215
  6.0 2.6 %collective-permute-start.1 = (bf16[272,256]{1,0:T(8,128)(2,1)S(1)}, bf16[272,256]{1,0:T(8,128)(2,1)S(1)}, u32[]{:S(2)}, u32[]{:S(2)}) collective-permute-start(bf16[272,256]{1,0:T(8,128)(2,1)S(1)} %get-tuple-element.31), channel_id=1, source_target_pairs={{0,8},{4,12},{8,0},{12,4},{1,9},{5,13},{9,1},{13,5},{2,10},{6,14},... | collective-permute-start | bytes 417800 | tf_op jit(solution)/shard_map/ppermute | solution.py:215
  8.6 1.3 %collective-permute-start.2 = (bf16[272,256]{1,0:T(8,128)(2,1)S(1)}, bf16[272,256]{1,0:T(8,128)(2,1)S(1)}, u32[]{:S(2)}, u32[]{:S(2)}) collective-permute-start(bf16[272,256]{1,0:T(8,128)(2,1)S(1)} %get-tuple-element.29), channel_id=1, source_target_pairs={{0,12},{4,0},{8,4},{12,8},{1,13},{5,1},{9,5},{13,9},{2,14},{6,2},{... | collective-permute-start | bytes 417800 | tf_op jit(solution)/shard_map/ppermute | solution.py:215
  10.0 0.7 %dynamic-slice_bitcast_fusion = (bf16[512,16]{0,1:T(8,128)(2,1)S(1)}, bf16[512,16]{0,1:T(8,128)(2,1)S(1)}) fusion(bf16[64,512]{1,0:T(8,128)(2,1)} %param.13, s32[]{:T(128)S(6)} %select_n.104, bf16[64,512]{1,0:T(8,128)(2,1)} %param.12), kind=kLoop, calls=%fused_computation.23 | loop fusion | bytes 65540 | tf_op jit(solution)/shard_map/transpose | solution.py:190
  10.8 0.0 copy-done.1
  10.8 0.3 fusion.5
  11.1 0.3 fusion.4
  11.5 0.0 copy-done
  11.5 0.3 fusion
  11.8 0.3 fusion.1
  12.2 0.1 slice_select_fusion
  12.3 0.3 collective-permute-done.refs_1_
  12.7 5.1 %collective-permute-done.1.refs_2_ = bf16[272,256]{1,0:T(8,128)(2,1)S(1)} collective-permute-done((bf16[272,256]{1,0:T(8,128)(2,1)S(1)}, bf16[272,256]{1,0:T(8,128)(2,1)S(1)}, u32[]{:S(2)}, u32[]{:S(2)}) %collective-permute-start.1) | collective-permute-done | bytes 139296 | tf_op jit(solution)/shard_map/ppermute | solution.py:215
  17.8 0.0 collective-permute-done.2.refs_3_
  17.8 4.0 %shard_map.91 = (bf16[512,256]{1,0:T(8,128)(2,1)S(1)}, bf16[1024,4096]{1,0:T(8,128)(2,1)S(1)}) custom-call(bf16[272,256]{1,0:T(8,128)(2,1)S(1)} %get-tuple-element.32.refs_0_, bf16[272,256]{1,0:T(8,128)(2,1)S(1)} %collective-permute-done.refs_1_, bf16[272,256]{1,0:T(8,128)(2,1)S(1)} %collective-permute-done.1.refs_2_, ...), custom_call_target="tpu_custom_call" | custom-call | flops 2684354560 | bytes 3145728 | tf_op jit(solution)/shard_map/pallas_call | solution.py:126
  21.8 3.5 %collective-permute-start.3 = (bf16[128,256]{1,0:T(8,128)(2,1)S(1)}, bf16[128,256]{1,0:T(8,128)(2,1)S(1)}, u32[]{:S(2)}, u32[]{:S(2)}) collective-permute-start(bf16[128,256]{1,0:T(8,128)(2,1)S(1)} %get-tuple-element.23), channel_id=1, source_target_pairs={{0,4},{4,8},{8,12},{12,0},{1,5},{5,9},{9,13},{13,1},{2,6},{6,10},{... | collective-permute-start | bytes 196616 | tf_op jit(solution)/shard_map/ppermute | solution.py:221
  25.3 1.6 %collective-permute-start.4 = (bf16[128,256]{1,0:T(8,128)(2,1)S(1)}, bf16[128,256]{1,0:T(8,128)(2,1)S(1)}, u32[]{:S(2)}, u32[]{:S(2)}) collective-permute-start(bf16[128,256]{1,0:T(8,128)(2,1)S(1)} %get-tuple-element.22), channel_id=1, source_target_pairs={{0,8},{4,12},{8,0},{12,4},{1,9},{5,13},{9,1},{13,5},{2,10},{6,14},... | collective-permute-start | bytes 196616 | tf_op jit(solution)/shard_map/ppermute | solution.py:221
  26.9 0.8 %collective-permute-start.5 = (bf16[128,256]{1,0:T(8,128)(2,1)S(1)}, bf16[128,256]{1,0:T(8,128)(2,1)S(1)}, u32[]{:S(2)}, u32[]{:S(2)}) collective-permute-start(bf16[128,256]{1,0:T(8,128)(2,1)S(1)} %get-tuple-element.21), channel_id=1, source_target_pairs={{0,12},{4,0},{8,4},{12,8},{1,13},{5,1},{9,5},{13,9},{2,14},{6,2},{... | collective-permute-start | bytes 196616 | tf_op jit(solution)/shard_map/ppermute | solution.py:221
  27.7 0.1 pad_add_fusion.refs_0_
  27.8 1.1 %collective-permute-done.3.refs_2_ = bf16[128,256]{1,0:T(8,128)(2,1)S(1)} collective-permute-done((bf16[128,256]{1,0:T(8,128)(2,1)S(1)}, bf16[128,256]{1,0:T(8,128)(2,1)S(1)}, u32[]{:S(2)}, u32[]{:S(2)}) %collective-permute-start.3) | collective-permute-done | bytes 65568 | tf_op jit(solution)/shard_map/ppermute | solution.py:221
  28.9 2.6 %collective-permute-done.4.refs_3_ = bf16[128,256]{1,0:T(8,128)(2,1)S(1)} collective-permute-done((bf16[128,256]{1,0:T(8,128)(2,1)S(1)}, bf16[128,256]{1,0:T(8,128)(2,1)S(1)}, u32[]{:S(2)}, u32[]{:S(2)}) %collective-permute-start.4) | collective-permute-done | bytes 65568 | tf_op jit(solution)/shard_map/ppermute | solution.py:221
  31.5 0.6 %collective-permute-done.5.refs_4_ = bf16[128,256]{1,0:T(8,128)(2,1)S(1)} collective-permute-done((bf16[128,256]{1,0:T(8,128)(2,1)S(1)}, bf16[128,256]{1,0:T(8,128)(2,1)S(1)}, u32[]{:S(2)}, u32[]{:S(2)}) %collective-permute-start.5) | collective-permute-done | bytes 65568 | tf_op jit(solution)/shard_map/ppermute | solution.py:221
  32.1 1.8 %shard_map.92 = f32[128,4096]{1,0:T(8,128)S(1)} custom-call(s32[4]{0:T(128)S(1)} %pad_add_fusion.refs_0_, bf16[128,256]{1,0:T(8,128)(2,1)S(1)} %get-tuple-element.24.refs_1_, bf16[128,256]{1,0:T(8,128)(2,1)S(1)} %collective-permute-done.3.refs_2_, bf16[128,256]{1,0:T(8,128)(2,1)S(1)} %collective-permute-done.4.refs_3_, ...), custom_call_target="tpu_custom_call" | custom-call | flops 1073741824 | bytes 10485760 | tf_op jit(solution)/shard_map/pallas_call | solution.py:158
  34.0 0.1 dynamic-slice_convert_fusion
  34.0 0.1 collective-permute-start.6
  34.1 1.9 %collective-permute-done.6 = bf16[128,2048]{1,0:T(8,128)(2,1)S(1)} collective-permute-done((bf16[128,2048]{1,0:T(8,128)(2,1)S(1)}, bf16[128,2048]{1,0:T(8,128)(2,1)S(1)}, u32[]{:S(2)}, u32[]{:S(2)}) %collective-permute-start.6) | collective-permute-done | bytes 524320 | tf_op jit(solution)/shard_map/ppermute | solution.py:174
  36.0 0.1 fusion.2
  36.1 1.6 %collective-permute-start.7 = (bf16[128,2048]{1,0:T(8,128)(2,1)S(1)}, bf16[128,2048]{1,0:T(8,128)(2,1)S(1)}, u32[]{:S(2)}, u32[]{:S(2)}) collective-permute-start(bf16[128,2048]{1,0:T(8,128)(2,1)S(1)} %fusion.2), channel_id=1, source_target_pairs={{0,2},{1,3},{2,0},{3,1},{4,6},{5,7},{6,4},{7,5},{8,10},{9,11},{10,... | collective-permute-start | bytes 1572872 | tf_op jit(solution)/shard_map/ppermute | solution.py:174
  37.7 12.5 %collective-permute-done.7 = bf16[128,2048]{1,0:T(8,128)(2,1)S(1)} collective-permute-done((bf16[128,2048]{1,0:T(8,128)(2,1)S(1)}, bf16[128,2048]{1,0:T(8,128)(2,1)S(1)}, u32[]{:S(2)}, u32[]{:S(2)}) %collective-permute-start.7) | collective-permute-done | bytes 524320 | tf_op jit(solution)/shard_map/ppermute | solution.py:174
  50.2 0.2 add_convert_fusion
  50.4 0.1 collective-permute-start.8
  50.4 1.9 %collective-permute-done.8 = bf16[128,2048]{1,0:T(8,128)(2,1)S(1)} collective-permute-done((bf16[128,2048]{1,0:T(8,128)(2,1)S(1)}, bf16[128,2048]{1,0:T(8,128)(2,1)S(1)}, u32[]{:S(2)}, u32[]{:S(2)}) %collective-permute-start.8) | collective-permute-done | bytes 524320 | tf_op jit(solution)/shard_map/ppermute | solution.py:174
  52.3 0.1 broadcast_select_fusion.1
  52.4 1.1 %pad_maximum_fusion = bf16[128,4096]{1,0:T(8,128)(2,1)} fusion(bf16[128,2048]{1,0:T(8,128)(2,1)S(1)} %get-tuple-element.10, bf16[128,2048]{1,0:T(8,128)(2,1)S(1)} %get-tuple-element.9), kind=kLoop, calls=%fused_computation.4 | loop fusion | flops 2097152 | bytes 2097152 | tf_op jit(solution)/shard_map/concatenate | solution.py:239
  (7 shorter events, 0.1 us)
Async XLA Ops:
  0.0 10.8 %copy-start.1 = (bf16[512,512]{1,0:T(8,128)(2,1)S(1)}, bf16[512,512]{1,0:T(8,128)(2,1)}, u32[]{:S(2)}) copy-start(bf16[512,512]{1,0:T(8,128)(2,1)} %constant.84.clone.refs_10_) | copy-start | bytes 1572868
  2.9 8.6 %copy-start = (bf16[512,512]{1,0:T(8,128)(2,1)S(1)}, bf16[512,512]{1,0:T(8,128)(2,1)}, u32[]{:S(2)}) copy-start(bf16[512,512]{1,0:T(8,128)(2,1)} %constant.85.clone.refs_11_) | copy-start | bytes 1572868
  2.9 9.8 %collective-permute-start = (bf16[272,256]{1,0:T(8,128)(2,1)S(1)}, bf16[272,256]{1,0:T(8,128)(2,1)S(1)}, u32[]{:S(2)}, u32[]{:S(2)}) collective-permute-start(bf16[272,256]{1,0:T(8,128)(2,1)S(1)} %get-tuple-element.30), channel_id=1, source_target_pairs={{0,4},{4,8},{8,12},{12,0},{1,5},{5,9},{9,13},{13,1},{2,6},{6,10},{... | collective-permute-start | bytes 417800 | tf_op jit(solution)/shard_map/ppermute | solution.py:215
  6.0 11.8 %collective-permute-start.1 = (bf16[272,256]{1,0:T(8,128)(2,1)S(1)}, bf16[272,256]{1,0:T(8,128)(2,1)S(1)}, u32[]{:S(2)}, u32[]{:S(2)}) collective-permute-start(bf16[272,256]{1,0:T(8,128)(2,1)S(1)} %get-tuple-element.31), channel_id=1, source_target_pairs={{0,8},{4,12},{8,0},{12,4},{1,9},{5,13},{9,1},{13,5},{2,10},{6,14},... | collective-permute-start | bytes 417800 | tf_op jit(solution)/shard_map/ppermute | solution.py:215
  8.6 9.2 %collective-permute-start.2 = (bf16[272,256]{1,0:T(8,128)(2,1)S(1)}, bf16[272,256]{1,0:T(8,128)(2,1)S(1)}, u32[]{:S(2)}, u32[]{:S(2)}) collective-permute-start(bf16[272,256]{1,0:T(8,128)(2,1)S(1)} %get-tuple-element.29), channel_id=1, source_target_pairs={{0,12},{4,0},{8,4},{12,8},{1,13},{5,1},{9,5},{13,9},{2,14},{6,2},{... | collective-permute-start | bytes 417800 | tf_op jit(solution)/shard_map/ppermute | solution.py:215
  21.8 7.1 %collective-permute-start.3 = (bf16[128,256]{1,0:T(8,128)(2,1)S(1)}, bf16[128,256]{1,0:T(8,128)(2,1)S(1)}, u32[]{:S(2)}, u32[]{:S(2)}) collective-permute-start(bf16[128,256]{1,0:T(8,128)(2,1)S(1)} %get-tuple-element.23), channel_id=1, source_target_pairs={{0,4},{4,8},{8,12},{12,0},{1,5},{5,9},{9,13},{13,1},{2,6},{6,10},{... | collective-permute-start | bytes 196616 | tf_op jit(solution)/shard_map/ppermute | solution.py:221
  25.3 6.2 %collective-permute-start.4 = (bf16[128,256]{1,0:T(8,128)(2,1)S(1)}, bf16[128,256]{1,0:T(8,128)(2,1)S(1)}, u32[]{:S(2)}, u32[]{:S(2)}) collective-permute-start(bf16[128,256]{1,0:T(8,128)(2,1)S(1)} %get-tuple-element.22), channel_id=1, source_target_pairs={{0,8},{4,12},{8,0},{12,4},{1,9},{5,13},{9,1},{13,5},{2,10},{6,14},... | collective-permute-start | bytes 196616 | tf_op jit(solution)/shard_map/ppermute | solution.py:221
  26.9 5.2 %collective-permute-start.5 = (bf16[128,256]{1,0:T(8,128)(2,1)S(1)}, bf16[128,256]{1,0:T(8,128)(2,1)S(1)}, u32[]{:S(2)}, u32[]{:S(2)}) collective-permute-start(bf16[128,256]{1,0:T(8,128)(2,1)S(1)} %get-tuple-element.21), channel_id=1, source_target_pairs={{0,12},{4,0},{8,4},{12,8},{1,13},{5,1},{9,5},{13,9},{2,14},{6,2},{... | collective-permute-start | bytes 196616 | tf_op jit(solution)/shard_map/ppermute | solution.py:221
  34.0 2.0 %collective-permute-start.6 = (bf16[128,2048]{1,0:T(8,128)(2,1)S(1)}, bf16[128,2048]{1,0:T(8,128)(2,1)S(1)}, u32[]{:S(2)}, u32[]{:S(2)}) collective-permute-start(bf16[128,2048]{1,0:T(8,128)(2,1)S(1)} %dynamic-slice_convert_fusion), channel_id=1, source_target_pairs={{0,1},{1,0},{2,3},{3,2},{4,5},{5,4},{6,7},{7,6},{8,9},{9,8},{10,11... | collective-permute-start | bytes 1572872 | tf_op jit(solution)/shard_map/ppermute | solution.py:174
  36.1 14.0 %collective-permute-start.7 = (bf16[128,2048]{1,0:T(8,128)(2,1)S(1)}, bf16[128,2048]{1,0:T(8,128)(2,1)S(1)}, u32[]{:S(2)}, u32[]{:S(2)}) collective-permute-start(bf16[128,2048]{1,0:T(8,128)(2,1)S(1)} %fusion.2), channel_id=1, source_target_pairs={{0,2},{1,3},{2,0},{3,1},{4,6},{5,7},{6,4},{7,5},{8,10},{9,11},{10,... | collective-permute-start | bytes 1572872 | tf_op jit(solution)/shard_map/ppermute | solution.py:174
  50.4 2.0 %collective-permute-start.8 = (bf16[128,2048]{1,0:T(8,128)(2,1)S(1)}, bf16[128,2048]{1,0:T(8,128)(2,1)S(1)}, u32[]{:S(2)}, u32[]{:S(2)}) collective-permute-start(bf16[128,2048]{1,0:T(8,128)(2,1)S(1)} %add_convert_fusion), channel_id=1, source_target_pairs={{0,1},{1,0},{2,3},{3,2},{4,5},{5,4},{6,7},{7,6},{8,9},{9,8},{10,11... | collective-permute-start | bytes 1572872 | tf_op jit(solution)/shard_map/ppermute | solution.py:174
